TPU v7x, 32 devices: a whole 2x2x4 slice. The times are simulated.
32 devices in a mesh: tm: 8 (over y, x, core), space: 4 (over z).
Axes of the slice: x: 2, y: 2, z: 4, core: 2. Of those that a mesh axis runs over, the one named last changes fastest.
Arguments:
- starts: float32 [8, 32, 128, 128], P('tm', 'space'), may hold values from -6 to 6
- diffusivity: float32 [32, 128, 128], P('space'), may hold values from 0.04 to 0.2
- velocity: float32 [2, 32, 128, 128], P(None, 'space'), may hold values from -0.1 to 0.1
- obstacle: int32 [32, 128, 128], P('space'), may hold values from 0 to 1, as said below
- substep_scale: float32 [12], replicated, may hold values from 0.5 to 1
- neighbors: int32 [32, 4], P('space'), may hold values from 0 to 32, as said below
- coarse_x: float32 [32, 64, 64], P('space'), may hold values from -1 to 1
- coarse_y: float32 [32, 128, 128], P('space'), may hold values from -1 to 1
Outputs:
- slice_ends: float32 [8, 32, 128, 128], P('tm', 'space')
- increment: float32 [8, 32, 128, 128], P('tm', 'space')
Inputs may be any that keep to these rules, and one draw needn't show every extreme that they name: `neighbors`: tiles form a grid of 4 by 8; each entry names the tile beside a tile in the given direction, or 32 on the grid's edge. The tiles 8 * k to 8 * (k + 1) - 1 fill grid row k, in any order within it, so a neighbour's number differs from the tile's block k by at most one block. `obstacle`: each tile holds one tube, a disc of radius 128 // 8 to 32 cells.
All inputs are finite; a program needn't handle non-finite values.
Results may differ from a plain program's by a relative error of at most 0.0002.
Values sent between devices are 32-bit elements; how exact they have to be, the bound alone decides.
No kernel may reach another device: no remote copies, remote signals or barrier semaphores. Data moves between devices by JAX's collectives and lax.ppermute only.
A program may use at most 128 MiB of HBM per device.

v0:
```python
import jax
import jax.numpy as jnp
from jax import lax
from jax.sharding import PartitionSpec as P

SUB = 12


exact_precision = lax.Precision.HIGHEST


def padded(block, sides, width):
    for axis, dim in sides:
        count = lax.axis_size(axis)
        forward = [(i, i + 1) for i in range(count - 1)]
        backward = [(target, source) for source, target in forward]
        low = lax.ppermute(
            lax.slice_in_dim(block, block.shape[dim] - width, None, axis=dim), axis, forward
        )
        high = lax.ppermute(lax.slice_in_dim(block, 0, width, axis=dim), axis, backward)
        block = jnp.concatenate([low, block, high], axis=dim)
    return block


def spread(value, axis, source):
    kept = jnp.where(lax.axis_index(axis) == source, value, 0).astype(value.dtype)
    return lax.psum(kept, axis)


def passed_along(block, axis, distance):
    devices = range(lax.axis_size(axis))
    route = [(i - distance, i) for i in devices if i - distance in devices]
    return lax.ppermute(block, axis, route)


def restrict(values):
    return 0.5 * (values[..., 0::2, :] + values[..., 1::2, :])


def prolong(coarse_values):
    return jnp.repeat(coarse_values, 2, axis=-2)


def apply_coarse(coarse_values, matrix_x, matrix_y):
    mixed_x = jnp.einsum("tij,...tjk->...tik", matrix_x, coarse_values, precision=exact_precision)
    return jnp.einsum("...tik,tlk->...til", mixed_x, matrix_y, precision=exact_precision)


def on_device(
    starts, diffusivity, velocity, obstacle, substep_scale, neighbors, coarse_x, coarse_y
):
    slice_count = starts.shape[0]
    tile_count = starts.shape[1]
    all_tiles = tile_count * lax.axis_size("space")
    block_base = lax.axis_index("space") * tile_count
    open_cells = 1.0 - obstacle.astype(jnp.float32)
    speed_x = velocity[0]
    speed_y = velocity[1]
    shifted = neighbors - block_base + tile_count
    lookup_index = jnp.where(neighbors == all_tiles, 3 * tile_count, shifted)

    def advance(substep_index, current):
        strength = substep_scale[substep_index]
        own_faces = jnp.stack(
            [current[:, :, 0, :], current[:, :, -1, :], current[:, :, :, 0], current[:, :, :, -1]],
            axis=2,
        )
        gathered = padded(own_faces, (("space", 1),), tile_count)
        gathered = jnp.concatenate([gathered, jnp.zeros_like(gathered[:, :1])], axis=1)
        west_face = gathered[:, lookup_index[:, 0], 1]
        east_face = gathered[:, lookup_index[:, 1], 0]
        south_face = gathered[:, lookup_index[:, 2], 3]
        north_face = gathered[:, lookup_index[:, 3], 2]
        from_west = jnp.concatenate([west_face[:, :, None, :], current[:, :, :-1, :]], axis=2)
        from_east = jnp.concatenate([current[:, :, 1:, :], east_face[:, :, None, :]], axis=2)
        from_south = jnp.concatenate([south_face[:, :, :, None], current[:, :, :, :-1]], axis=3)
        from_north = jnp.concatenate([current[:, :, :, 1:], north_face[:, :, :, None]], axis=3)
        laplace = from_west + from_east + from_south + from_north - 4.0 * current
        transport = speed_x * (from_east - from_west) + speed_y * (from_north - from_south)
        return open_cells * (current + strength * diffusivity * laplace - 0.5 * transport)

    fine_ends = lax.fori_loop(0, SUB, advance, starts)
    correction = fine_ends - prolong(apply_coarse(restrict(starts), coarse_x, coarse_y))
    coarse_jump = restrict(correction)
    first_coarse = spread(restrict(starts[0]), "tm", 0)
    every_jump = lax.all_gather(coarse_jump, "tm", axis=0, tiled=True)

    def sweep(state_now, jump):
        return (apply_coarse(state_now, coarse_x, coarse_y) + jump, state_now)

    last_state, history = lax.scan(sweep, first_coarse, every_jump)
    own_coarse = lax.dynamic_slice_in_dim(
        history, lax.axis_index("tm") * slice_count, slice_count, 0
    )
    slice_ends = prolong(apply_coarse(own_coarse, coarse_x, coarse_y)) + correction
    previous = passed_along(slice_ends[-1], "tm", 1)
    first_step = jnp.where(
        lax.axis_index("tm") == 0, jnp.zeros_like(previous), previous - starts[0]
    )
    increment = jnp.concatenate([first_step[None], slice_ends[:-1] - starts[1:]], axis=0)
    return (slice_ends, increment)


def solution(mesh):
    placed = (
        P("tm", "space", None, None),
        P("space", None, None),
        P(None, "space", None, None),
        P("space", None, None),
        P(),
        P("space", None),
        P("space", None, None),
        P("space", None, None),
    )
    return jax.shard_map(
        on_device,
        mesh=mesh,
        in_specs=placed,
        out_specs=(P("tm", "space", None, None), P("tm", "space", None, None)),
        check_vma=False,
    )
```

profile of v0, /device:TPU:12, one launch (start us, length us, event | category | flops | bytes accessed | tf_op | source)
XLA Modules:
  0.0 285.5 jit_solution(6165159158150083791)
XLA Ops:
  16.3 169.3 %while.25 = (s32[]{:T(128)}, f32[1,8,128,128]{2,1,3,0:T(8,128)S(1)}, f32[8,128,128]{1,0,2:T(8,128)}, f32[12]{0:T(128)S(1)}, f32[8,128,128]{1,0,2:T(8,128)}, /*in...) while((s32[]{:T(128)}, ...), condition=%wide.region_2.3_spmd, body=%wide.region_1.2_spmd.sunk | while | flops 2710714 | bytes 10800037 | solution.py:82
  16.6 3.5 %collective-permute-start.1 = (f32[1,8,4,128]{3,2,1,0:T(4,128)S(1)}, f32[1,8,4,128]{3,2,1,0:T(4,128)S(1)}, u32[]{:S(2)}, u32[]{:S(2)}) collective-permute-start(f32[1,8,4,128]{3,2,1,0:T(4,128)S(1)} %pad_maximum_fusion.6), channel_id=1, source_target_pairs={{0,1},{1,2},{2,3},{4,5},{5,6},{6,7},{8,9},{9,10},{10,11},{12,13},{... | collective-permute-start | bytes 49160 | tf_op jit(solution)/shard_map/while/body/eval_jaxpr/ppermute | solution.py:17
  28.7 3.0 %fusion.60 = f32[1,8,128,128]{2,1,3,0:T(8,128)S(1)} fusion(f32[1,8,128,128]{2,1,3,0:T(8,128)S(1)} %get-tuple-element.355, f32[8,128,128]{1,0,2:T(8,128)} %get-tuple-element.367, f32[1,8,128,128]{2,1,3,0:T(8,128)} %get-tuple-element.372, f32[1,8,128,128]{2,1,3,0:T(8,128)} %get-tuple-element.371, f32[1,8,128,1]{2,1,3,0:T(8,128)S(1)} %bitcast.113, ...), kind=kLoop, calls=%fused_computation.13.clone.1 | loop fusion | flops 2621440 | bytes 5242884 | tf_op jit(solution)/shard_map/while/body/eval_jaxpr/mul | solution.py:80
  31.9 3.5 %collective-permute-start.1 = (f32[1,8,4,128]{3,2,1,0:T(4,128)S(1)}, f32[1,8,4,128]{3,2,1,0:T(4,128)S(1)}, u32[]{:S(2)}, u32[]{:S(2)}) collective-permute-start(f32[1,8,4,128]{3,2,1,0:T(4,128)S(1)} %pad_maximum_fusion.6), channel_id=1, source_target_pairs={{0,1},{1,2},{2,3},{4,5},{5,6},{6,7},{8,9},{9,10},{10,11},{12,13},{... | collective-permute-start | bytes 49160 | tf_op jit(solution)/shard_map/while/body/eval_jaxpr/ppermute | solution.py:17
  44.0 3.0 %fusion.60 = f32[1,8,128,128]{2,1,3,0:T(8,128)S(1)} fusion(f32[1,8,128,128]{2,1,3,0:T(8,128)S(1)} %get-tuple-element.355, f32[8,128,128]{1,0,2:T(8,128)} %get-tuple-element.367, f32[1,8,128,128]{2,1,3,0:T(8,128)} %get-tuple-element.372, f32[1,8,128,128]{2,1,3,0:T(8,128)} %get-tuple-element.371, f32[1,8,128,1]{2,1,3,0:T(8,128)S(1)} %bitcast.113, ...), kind=kLoop, calls=%fused_computation.13.clone.1 | loop fusion | flops 2621440 | bytes 5242884 | tf_op jit(solution)/shard_map/while/body/eval_jaxpr/mul | solution.py:80
  49.3 3.8 %collective-permute-start = (f32[1,8,4,128]{3,2,1,0:T(4,128)S(1)}, f32[1,8,4,128]{3,2,1,0:T(4,128)S(1)}, u32[]{:S(2)}, u32[]{:S(2)}) collective-permute-start(f32[1,8,4,128]{3,2,1,0:T(4,128)S(1)} %pad_maximum_fusion.6), channel_id=1, source_target_pairs={{1,0},{2,1},{3,2},{5,4},{6,5},{7,6},{9,8},{10,9},{11,10},{13,12},{... | collective-permute-start | bytes 49160 | tf_op jit(solution)/shard_map/while/body/eval_jaxpr/ppermute | solution.py:20
  57.9 3.0 %fusion.60 = f32[1,8,128,128]{2,1,3,0:T(8,128)S(1)} fusion(f32[1,8,128,128]{2,1,3,0:T(8,128)S(1)} %get-tuple-element.355, f32[8,128,128]{1,0,2:T(8,128)} %get-tuple-element.367, f32[1,8,128,128]{2,1,3,0:T(8,128)} %get-tuple-element.372, f32[1,8,128,128]{2,1,3,0:T(8,128)} %get-tuple-element.371, f32[1,8,128,1]{2,1,3,0:T(8,128)S(1)} %bitcast.113, ...), kind=kLoop, calls=%fused_computation.13.clone.1 | loop fusion | flops 2621440 | bytes 5242884 | tf_op jit(solution)/shard_map/while/body/eval_jaxpr/mul | solution.py:80
  63.2 3.9 %collective-permute-start = (f32[1,8,4,128]{3,2,1,0:T(4,128)S(1)}, f32[1,8,4,128]{3,2,1,0:T(4,128)S(1)}, u32[]{:S(2)}, u32[]{:S(2)}) collective-permute-start(f32[1,8,4,128]{3,2,1,0:T(4,128)S(1)} %pad_maximum_fusion.6), channel_id=1, source_target_pairs={{1,0},{2,1},{3,2},{5,4},{6,5},{7,6},{9,8},{10,9},{11,10},{13,12},{... | collective-permute-start | bytes 49160 | tf_op jit(solution)/shard_map/while/body/eval_jaxpr/ppermute | solution.py:20
  71.8 3.0 %fusion.60 = f32[1,8,128,128]{2,1,3,0:T(8,128)S(1)} fusion(f32[1,8,128,128]{2,1,3,0:T(8,128)S(1)} %get-tuple-element.355, f32[8,128,128]{1,0,2:T(8,128)} %get-tuple-element.367, f32[1,8,128,128]{2,1,3,0:T(8,128)} %get-tuple-element.372, f32[1,8,128,128]{2,1,3,0:T(8,128)} %get-tuple-element.371, f32[1,8,128,1]{2,1,3,0:T(8,128)S(1)} %bitcast.113, ...), kind=kLoop, calls=%fused_computation.13.clone.1 | loop fusion | flops 2621440 | bytes 5242884 | tf_op jit(solution)/shard_map/while/body/eval_jaxpr/mul | solution.py:80
  77.0 3.8 %collective-permute-start = (f32[1,8,4,128]{3,2,1,0:T(4,128)S(1)}, f32[1,8,4,128]{3,2,1,0:T(4,128)S(1)}, u32[]{:S(2)}, u32[]{:S(2)}) collective-permute-start(f32[1,8,4,128]{3,2,1,0:T(4,128)S(1)} %pad_maximum_fusion.6), channel_id=1, source_target_pairs={{1,0},{2,1},{3,2},{5,4},{6,5},{7,6},{9,8},{10,9},{11,10},{13,12},{... | collective-permute-start | bytes 49160 | tf_op jit(solution)/shard_map/while/body/eval_jaxpr/ppermute | solution.py:20
  85.6 3.0 %fusion.60 = f32[1,8,128,128]{2,1,3,0:T(8,128)S(1)} fusion(f32[1,8,128,128]{2,1,3,0:T(8,128)S(1)} %get-tuple-element.355, f32[8,128,128]{1,0,2:T(8,128)} %get-tuple-element.367, f32[1,8,128,128]{2,1,3,0:T(8,128)} %get-tuple-element.372, f32[1,8,128,128]{2,1,3,0:T(8,128)} %get-tuple-element.371, f32[1,8,128,1]{2,1,3,0:T(8,128)S(1)} %bitcast.113, ...), kind=kLoop, calls=%fused_computation.13.clone.1 | loop fusion | flops 2621440 | bytes 5242884 | tf_op jit(solution)/shard_map/while/body/eval_jaxpr/mul | solution.py:80
  90.9 3.9 %collective-permute-start = (f32[1,8,4,128]{3,2,1,0:T(4,128)S(1)}, f32[1,8,4,128]{3,2,1,0:T(4,128)S(1)}, u32[]{:S(2)}, u32[]{:S(2)}) collective-permute-start(f32[1,8,4,128]{3,2,1,0:T(4,128)S(1)} %pad_maximum_fusion.6), channel_id=1, source_target_pairs={{1,0},{2,1},{3,2},{5,4},{6,5},{7,6},{9,8},{10,9},{11,10},{13,12},{... | collective-permute-start | bytes 49160 | tf_op jit(solution)/shard_map/while/body/eval_jaxpr/ppermute | solution.py:20
  99.5 3.0 %fusion.60 = f32[1,8,128,128]{2,1,3,0:T(8,128)S(1)} fusion(f32[1,8,128,128]{2,1,3,0:T(8,128)S(1)} %get-tuple-element.355, f32[8,128,128]{1,0,2:T(8,128)} %get-tuple-element.367, f32[1,8,128,128]{2,1,3,0:T(8,128)} %get-tuple-element.372, f32[1,8,128,128]{2,1,3,0:T(8,128)} %get-tuple-element.371, f32[1,8,128,1]{2,1,3,0:T(8,128)S(1)} %bitcast.113, ...), kind=kLoop, calls=%fused_computation.13.clone.1 | loop fusion | flops 2621440 | bytes 5242884 | tf_op jit(solution)/shard_map/while/body/eval_jaxpr/mul | solution.py:80
  104.8 3.9 %collective-permute-start = (f32[1,8,4,128]{3,2,1,0:T(4,128)S(1)}, f32[1,8,4,128]{3,2,1,0:T(4,128)S(1)}, u32[]{:S(2)}, u32[]{:S(2)}) collective-permute-start(f32[1,8,4,128]{3,2,1,0:T(4,128)S(1)} %pad_maximum_fusion.6), channel_id=1, source_target_pairs={{1,0},{2,1},{3,2},{5,4},{6,5},{7,6},{9,8},{10,9},{11,10},{13,12},{... | collective-permute-start | bytes 49160 | tf_op jit(solution)/shard_map/while/body/eval_jaxpr/ppermute | solution.py:20
  113.4 3.0 %fusion.60 = f32[1,8,128,128]{2,1,3,0:T(8,128)S(1)} fusion(f32[1,8,128,128]{2,1,3,0:T(8,128)S(1)} %get-tuple-element.355, f32[8,128,128]{1,0,2:T(8,128)} %get-tuple-element.367, f32[1,8,128,128]{2,1,3,0:T(8,128)} %get-tuple-element.372, f32[1,8,128,128]{2,1,3,0:T(8,128)} %get-tuple-element.371, f32[1,8,128,1]{2,1,3,0:T(8,128)S(1)} %bitcast.113, ...), kind=kLoop, calls=%fused_computation.13.clone.1 | loop fusion | flops 2621440 | bytes 5242884 | tf_op jit(solution)/shard_map/while/body/eval_jaxpr/mul | solution.py:80
  118.6 3.9 %collective-permute-start = (f32[1,8,4,128]{3,2,1,0:T(4,128)S(1)}, f32[1,8,4,128]{3,2,1,0:T(4,128)S(1)}, u32[]{:S(2)}, u32[]{:S(2)}) collective-permute-start(f32[1,8,4,128]{3,2,1,0:T(4,128)S(1)} %pad_maximum_fusion.6), channel_id=1, source_target_pairs={{1,0},{2,1},{3,2},{5,4},{6,5},{7,6},{9,8},{10,9},{11,10},{13,12},{... | collective-permute-start | bytes 49160 | tf_op jit(solution)/shard_map/while/body/eval_jaxpr/ppermute | solution.py:20
  127.2 3.0 %fusion.60 = f32[1,8,128,128]{2,1,3,0:T(8,128)S(1)} fusion(f32[1,8,128,128]{2,1,3,0:T(8,128)S(1)} %get-tuple-element.355, f32[8,128,128]{1,0,2:T(8,128)} %get-tuple-element.367, f32[1,8,128,128]{2,1,3,0:T(8,128)} %get-tuple-element.372, f32[1,8,128,128]{2,1,3,0:T(8,128)} %get-tuple-element.371, f32[1,8,128,1]{2,1,3,0:T(8,128)S(1)} %bitcast.113, ...), kind=kLoop, calls=%fused_computation.13.clone.1 | loop fusion | flops 2621440 | bytes 5242884 | tf_op jit(solution)/shard_map/while/body/eval_jaxpr/mul | solution.py:80
  132.5 3.9 %collective-permute-start = (f32[1,8,4,128]{3,2,1,0:T(4,128)S(1)}, f32[1,8,4,128]{3,2,1,0:T(4,128)S(1)}, u32[]{:S(2)}, u32[]{:S(2)}) collective-permute-start(f32[1,8,4,128]{3,2,1,0:T(4,128)S(1)} %pad_maximum_fusion.6), channel_id=1, source_target_pairs={{1,0},{2,1},{3,2},{5,4},{6,5},{7,6},{9,8},{10,9},{11,10},{13,12},{... | collective-permute-start | bytes 49160 | tf_op jit(solution)/shard_map/while/body/eval_jaxpr/ppermute | solution.py:20
  141.1 3.0 %fusion.60 = f32[1,8,128,128]{2,1,3,0:T(8,128)S(1)} fusion(f32[1,8,128,128]{2,1,3,0:T(8,128)S(1)} %get-tuple-element.355, f32[8,128,128]{1,0,2:T(8,128)} %get-tuple-element.367, f32[1,8,128,128]{2,1,3,0:T(8,128)} %get-tuple-element.372, f32[1,8,128,128]{2,1,3,0:T(8,128)} %get-tuple-element.371, f32[1,8,128,1]{2,1,3,0:T(8,128)S(1)} %bitcast.113, ...), kind=kLoop, calls=%fused_computation.13.clone.1 | loop fusion | flops 2621440 | bytes 5242884 | tf_op jit(solution)/shard_map/while/body/eval_jaxpr/mul | solution.py:80
  146.3 3.9 %collective-permute-start = (f32[1,8,4,128]{3,2,1,0:T(4,128)S(1)}, f32[1,8,4,128]{3,2,1,0:T(4,128)S(1)}, u32[]{:S(2)}, u32[]{:S(2)}) collective-permute-start(f32[1,8,4,128]{3,2,1,0:T(4,128)S(1)} %pad_maximum_fusion.6), channel_id=1, source_target_pairs={{1,0},{2,1},{3,2},{5,4},{6,5},{7,6},{9,8},{10,9},{11,10},{13,12},{... | collective-permute-start | bytes 49160 | tf_op jit(solution)/shard_map/while/body/eval_jaxpr/ppermute | solution.py:20
  154.9 3.0 %fusion.60 = f32[1,8,128,128]{2,1,3,0:T(8,128)S(1)} fusion(f32[1,8,128,128]{2,1,3,0:T(8,128)S(1)} %get-tuple-element.355, f32[8,128,128]{1,0,2:T(8,128)} %get-tuple-element.367, f32[1,8,128,128]{2,1,3,0:T(8,128)} %get-tuple-element.372, f32[1,8,128,128]{2,1,3,0:T(8,128)} %get-tuple-element.371, f32[1,8,128,1]{2,1,3,0:T(8,128)S(1)} %bitcast.113, ...), kind=kLoop, calls=%fused_computation.13.clone.1 | loop fusion | flops 2621440 | bytes 5242884 | tf_op jit(solution)/shard_map/while/body/eval_jaxpr/mul | solution.py:80
  160.2 3.9 %collective-permute-start = (f32[1,8,4,128]{3,2,1,0:T(4,128)S(1)}, f32[1,8,4,128]{3,2,1,0:T(4,128)S(1)}, u32[]{:S(2)}, u32[]{:S(2)}) collective-permute-start(f32[1,8,4,128]{3,2,1,0:T(4,128)S(1)} %pad_maximum_fusion.6), channel_id=1, source_target_pairs={{1,0},{2,1},{3,2},{5,4},{6,5},{7,6},{9,8},{10,9},{11,10},{13,12},{... | collective-permute-start | bytes 49160 | tf_op jit(solution)/shard_map/while/body/eval_jaxpr/ppermute | solution.py:20
  168.8 3.0 %fusion.60 = f32[1,8,128,128]{2,1,3,0:T(8,128)S(1)} fusion(f32[1,8,128,128]{2,1,3,0:T(8,128)S(1)} %get-tuple-element.355, f32[8,128,128]{1,0,2:T(8,128)} %get-tuple-element.367, f32[1,8,128,128]{2,1,3,0:T(8,128)} %get-tuple-element.372, f32[1,8,128,128]{2,1,3,0:T(8,128)} %get-tuple-element.371, f32[1,8,128,1]{2,1,3,0:T(8,128)S(1)} %bitcast.113, ...), kind=kLoop, calls=%fused_computation.13.clone.1 | loop fusion | flops 2621440 | bytes 5242884 | tf_op jit(solution)/shard_map/while/body/eval_jaxpr/mul | solution.py:80
  174.1 3.9 %collective-permute-start = (f32[1,8,4,128]{3,2,1,0:T(4,128)S(1)}, f32[1,8,4,128]{3,2,1,0:T(4,128)S(1)}, u32[]{:S(2)}, u32[]{:S(2)}) collective-permute-start(f32[1,8,4,128]{3,2,1,0:T(4,128)S(1)} %pad_maximum_fusion.6), channel_id=1, source_target_pairs={{1,0},{2,1},{3,2},{5,4},{6,5},{7,6},{9,8},{10,9},{11,10},{13,12},{... | collective-permute-start | bytes 49160 | tf_op jit(solution)/shard_map/while/body/eval_jaxpr/ppermute | solution.py:20
  182.7 3.0 %fusion.60 = f32[1,8,128,128]{2,1,3,0:T(8,128)S(1)} fusion(f32[1,8,128,128]{2,1,3,0:T(8,128)S(1)} %get-tuple-element.355, f32[8,128,128]{1,0,2:T(8,128)} %get-tuple-element.367, f32[1,8,128,128]{2,1,3,0:T(8,128)} %get-tuple-element.372, f32[1,8,128,128]{2,1,3,0:T(8,128)} %get-tuple-element.371, f32[1,8,128,1]{2,1,3,0:T(8,128)S(1)} %bitcast.113, ...), kind=kLoop, calls=%fused_computation.13.clone.1 | loop fusion | flops 2621440 | bytes 5242884 | tf_op jit(solution)/shard_map/while/body/eval_jaxpr/mul | solution.py:80
  189.8 27.4 %all-gather.2.cloned.1.call-done = f32[8,8,64,128]{3,2,1,0:T(8,128)} async-done(((f32[1,8,64,128]{3,2,1,0:T(8,128)}), f32[8,8,64,128]{3,2,1,0:T(8,128)}) %all-gather.2.cloned.1.call-update) | async-done | bytes 2097168 | tf_op jit(solution)/shard_map/all_gather | solution.py:86
  217.2 46.5 %while.26 = (s32[]{:T(128)}, f32[8,64,128]{2,1,0:T(8,128)}, f32[8,8,64,128]{3,2,1,0:T(8,128)}, f32[8,64,64]{2,1,0:T(8,128)S(1)}, f32[8,128,128]{2,1,0:T(8,128)S(1)}, /*index=5*/f32[8,8,64,128]{3,2,1,0:T(8,128)}, s32[]{:T(128)}) while((s32[]{:T(128)}, f32[8,64,128]{2,1,0:T(8,128)}, f32[8,8,64,128]{3,2,1,0:T(8,128)}, ...), condition=%wide.region_4.5_spmd, body=%wide.region_3.4_spmd.sunk | while | flops 151060480 | bytes 2490461 | solution.py:91
  220.2 2.8 convolution_add_fusion.2
  226.0 2.8 convolution_add_fusion.2
  243.4 2.8 convolution_add_fusion.2
  260.8 2.8 convolution_add_fusion.2
  268.5 9.3 %collective-permute-done.2 = f32[8,128,128]{2,1,0:T(8,128)S(1)} collective-permute-done((f32[8,128,128]{2,1,0:T(8,128)S(1)}, f32[8,128,128]{2,1,0:T(8,128)S(1)}, u32[]{:S(2)}, u32[]{:S(2)}) %collective-permute-start.2) | collective-permute-done | bytes 524320 | tf_op jit(solution)/shard_map/ppermute | solution.py:33
  (301 shorter events, 141.1 us)
Async XLA Ops:
  7.2 182.6 %all-reduce.6.cloned.1.call-start = ((), (), s32[]{:S(2)}) async-start(), calls=%async_computation | async-start | bytes 524288 | tf_op jit(solution)/shard_map/psum | solution.py:27
  7.2 4.8 %copy-start.6 = (f32[8,128,128]{2,1,0:T(8,128)S(1)}, f32[8,128,128]{2,1,0:T(8,128)}, u32[]{:S(2)}) copy-start(f32[8,128,128]{2,1,0:T(8,128)} %param.13) | copy-start | bytes 1572868
  9.4 3.6 %copy-start.7 = (s32[8,128,128]{2,1,0:T(8,128)S(1)}, s32[8,128,128]{2,1,0:T(8,128)}, u32[]{:S(2)}) copy-start(s32[8,128,128]{2,1,0:T(8,128)} %param.15) | copy-start | bytes 1572868
  10.2 206.9 %all-gather.2.cloned.1.call-start = ((), (), s32[]{:S(2)}) async-start(), calls=%async_computation.1 | async-start | bytes 2359296 | tf_op jit(solution)/shard_map/all_gather | solution.py:86
  16.3 169.6 %copy-start.1 = (f32[8,64,64]{2,1,0:T(8,128)S(1)}, f32[8,64,64]{2,1,0:T(8,128)}, u32[]{:S(2)}) copy-start(f32[8,64,64]{2,1,0:T(8,128)} %param.18) | copy-start | bytes 393220
  16.6 7.6 %collective-permute-start.1 = (f32[1,8,4,128]{3,2,1,0:T(4,128)S(1)}, f32[1,8,4,128]{3,2,1,0:T(4,128)S(1)}, u32[]{:S(2)}, u32[]{:S(2)}) collective-permute-start(f32[1,8,4,128]{3,2,1,0:T(4,128)S(1)} %pad_maximum_fusion.6), channel_id=1, source_target_pairs={{0,1},{1,2},{2,3},{4,5},{5,6},{6,7},{8,9},{9,10},{10,11},{12,13},{... | collective-permute-start | bytes 49160 | tf_op jit(solution)/shard_map/while/body/eval_jaxpr/ppermute | solution.py:17
  20.1 5.6 %collective-permute-start = (f32[1,8,4,128]{3,2,1,0:T(4,128)S(1)}, f32[1,8,4,128]{3,2,1,0:T(4,128)S(1)}, u32[]{:S(2)}, u32[]{:S(2)}) collective-permute-start(f32[1,8,4,128]{3,2,1,0:T(4,128)S(1)} %pad_maximum_fusion.6), channel_id=1, source_target_pairs={{1,0},{2,1},{3,2},{5,4},{6,5},{7,6},{9,8},{10,9},{11,10},{13,12},{... | collective-permute-start | bytes 49160 | tf_op jit(solution)/shard_map/while/body/eval_jaxpr/ppermute | solution.py:20
  31.9 7.6 %collective-permute-start.1 = (f32[1,8,4,128]{3,2,1,0:T(4,128)S(1)}, f32[1,8,4,128]{3,2,1,0:T(4,128)S(1)}, u32[]{:S(2)}, u32[]{:S(2)}) collective-permute-start(f32[1,8,4,128]{3,2,1,0:T(4,128)S(1)} %pad_maximum_fusion.6), channel_id=1, source_target_pairs={{0,1},{1,2},{2,3},{4,5},{5,6},{6,7},{8,9},{9,10},{10,11},{12,13},{... | collective-permute-start | bytes 49160 | tf_op jit(solution)/shard_map/while/body/eval_jaxpr/ppermute | solution.py:17
  35.4 5.6 %collective-permute-start = (f32[1,8,4,128]{3,2,1,0:T(4,128)S(1)}, f32[1,8,4,128]{3,2,1,0:T(4,128)S(1)}, u32[]{:S(2)}, u32[]{:S(2)}) collective-permute-start(f32[1,8,4,128]{3,2,1,0:T(4,128)S(1)} %pad_maximum_fusion.6), channel_id=1, source_target_pairs={{1,0},{2,1},{3,2},{5,4},{6,5},{7,6},{9,8},{10,9},{11,10},{13,12},{... | collective-permute-start | bytes 49160 | tf_op jit(solution)/shard_map/while/body/eval_jaxpr/ppermute | solution.py:20
  47.3 7.6 %collective-permute-start.1 = (f32[1,8,4,128]{3,2,1,0:T(4,128)S(1)}, f32[1,8,4,128]{3,2,1,0:T(4,128)S(1)}, u32[]{:S(2)}, u32[]{:S(2)}) collective-permute-start(f32[1,8,4,128]{3,2,1,0:T(4,128)S(1)} %pad_maximum_fusion.6), channel_id=1, source_target_pairs={{0,1},{1,2},{2,3},{4,5},{5,6},{6,7},{8,9},{9,10},{10,11},{12,13},{... | collective-permute-start | bytes 49160 | tf_op jit(solution)/shard_map/while/body/eval_jaxpr/ppermute | solution.py:17
  49.3 5.6 %collective-permute-start = (f32[1,8,4,128]{3,2,1,0:T(4,128)S(1)}, f32[1,8,4,128]{3,2,1,0:T(4,128)S(1)}, u32[]{:S(2)}, u32[]{:S(2)}) collective-permute-start(f32[1,8,4,128]{3,2,1,0:T(4,128)S(1)} %pad_maximum_fusion.6), channel_id=1, source_target_pairs={{1,0},{2,1},{3,2},{5,4},{6,5},{7,6},{9,8},{10,9},{11,10},{13,12},{... | collective-permute-start | bytes 49160 | tf_op jit(solution)/shard_map/while/body/eval_jaxpr/ppermute | solution.py:20
  61.2 7.6 %collective-permute-start.1 = (f32[1,8,4,128]{3,2,1,0:T(4,128)S(1)}, f32[1,8,4,128]{3,2,1,0:T(4,128)S(1)}, u32[]{:S(2)}, u32[]{:S(2)}) collective-permute-start(f32[1,8,4,128]{3,2,1,0:T(4,128)S(1)} %pad_maximum_fusion.6), channel_id=1, source_target_pairs={{0,1},{1,2},{2,3},{4,5},{5,6},{6,7},{8,9},{9,10},{10,11},{12,13},{... | collective-permute-start | bytes 49160 | tf_op jit(solution)/shard_map/while/body/eval_jaxpr/ppermute | solution.py:17
  63.2 5.6 %collective-permute-start = (f32[1,8,4,128]{3,2,1,0:T(4,128)S(1)}, f32[1,8,4,128]{3,2,1,0:T(4,128)S(1)}, u32[]{:S(2)}, u32[]{:S(2)}) collective-permute-start(f32[1,8,4,128]{3,2,1,0:T(4,128)S(1)} %pad_maximum_fusion.6), channel_id=1, source_target_pairs={{1,0},{2,1},{3,2},{5,4},{6,5},{7,6},{9,8},{10,9},{11,10},{13,12},{... | collective-permute-start | bytes 49160 | tf_op jit(solution)/shard_map/while/body/eval_jaxpr/ppermute | solution.py:20
  75.0 7.6 %collective-permute-start.1 = (f32[1,8,4,128]{3,2,1,0:T(4,128)S(1)}, f32[1,8,4,128]{3,2,1,0:T(4,128)S(1)}, u32[]{:S(2)}, u32[]{:S(2)}) collective-permute-start(f32[1,8,4,128]{3,2,1,0:T(4,128)S(1)} %pad_maximum_fusion.6), channel_id=1, source_target_pairs={{0,1},{1,2},{2,3},{4,5},{5,6},{6,7},{8,9},{9,10},{10,11},{12,13},{... | collective-permute-start | bytes 49160 | tf_op jit(solution)/shard_map/while/body/eval_jaxpr/ppermute | solution.py:17
  77.0 5.6 %collective-permute-start = (f32[1,8,4,128]{3,2,1,0:T(4,128)S(1)}, f32[1,8,4,128]{3,2,1,0:T(4,128)S(1)}, u32[]{:S(2)}, u32[]{:S(2)}) collective-permute-start(f32[1,8,4,128]{3,2,1,0:T(4,128)S(1)} %pad_maximum_fusion.6), channel_id=1, source_target_pairs={{1,0},{2,1},{3,2},{5,4},{6,5},{7,6},{9,8},{10,9},{11,10},{13,12},{... | collective-permute-start | bytes 49160 | tf_op jit(solution)/shard_map/while/body/eval_jaxpr/ppermute | solution.py:20
  88.9 7.6 %collective-permute-start.1 = (f32[1,8,4,128]{3,2,1,0:T(4,128)S(1)}, f32[1,8,4,128]{3,2,1,0:T(4,128)S(1)}, u32[]{:S(2)}, u32[]{:S(2)}) collective-permute-start(f32[1,8,4,128]{3,2,1,0:T(4,128)S(1)} %pad_maximum_fusion.6), channel_id=1, source_target_pairs={{0,1},{1,2},{2,3},{4,5},{5,6},{6,7},{8,9},{9,10},{10,11},{12,13},{... | collective-permute-start | bytes 49160 | tf_op jit(solution)/shard_map/while/body/eval_jaxpr/ppermute | solution.py:17
  90.9 5.6 %collective-permute-start = (f32[1,8,4,128]{3,2,1,0:T(4,128)S(1)}, f32[1,8,4,128]{3,2,1,0:T(4,128)S(1)}, u32[]{:S(2)}, u32[]{:S(2)}) collective-permute-start(f32[1,8,4,128]{3,2,1,0:T(4,128)S(1)} %pad_maximum_fusion.6), channel_id=1, source_target_pairs={{1,0},{2,1},{3,2},{5,4},{6,5},{7,6},{9,8},{10,9},{11,10},{13,12},{... | collective-permute-start | bytes 49160 | tf_op jit(solution)/shard_map/while/body/eval_jaxpr/ppermute | solution.py:20
  102.8 7.6 %collective-permute-start.1 = (f32[1,8,4,128]{3,2,1,0:T(4,128)S(1)}, f32[1,8,4,128]{3,2,1,0:T(4,128)S(1)}, u32[]{:S(2)}, u32[]{:S(2)}) collective-permute-start(f32[1,8,4,128]{3,2,1,0:T(4,128)S(1)} %pad_maximum_fusion.6), channel_id=1, source_target_pairs={{0,1},{1,2},{2,3},{4,5},{5,6},{6,7},{8,9},{9,10},{10,11},{12,13},{... | collective-permute-start | bytes 49160 | tf_op jit(solution)/shard_map/while/body/eval_jaxpr/ppermute | solution.py:17
  104.8 5.6 %collective-permute-start = (f32[1,8,4,128]{3,2,1,0:T(4,128)S(1)}, f32[1,8,4,128]{3,2,1,0:T(4,128)S(1)}, u32[]{:S(2)}, u32[]{:S(2)}) collective-permute-start(f32[1,8,4,128]{3,2,1,0:T(4,128)S(1)} %pad_maximum_fusion.6), channel_id=1, source_target_pairs={{1,0},{2,1},{3,2},{5,4},{6,5},{7,6},{9,8},{10,9},{11,10},{13,12},{... | collective-permute-start | bytes 49160 | tf_op jit(solution)/shard_map/while/body/eval_jaxpr/ppermute | solution.py:20
  116.6 7.6 %collective-permute-start.1 = (f32[1,8,4,128]{3,2,1,0:T(4,128)S(1)}, f32[1,8,4,128]{3,2,1,0:T(4,128)S(1)}, u32[]{:S(2)}, u32[]{:S(2)}) collective-permute-start(f32[1,8,4,128]{3,2,1,0:T(4,128)S(1)} %pad_maximum_fusion.6), channel_id=1, source_target_pairs={{0,1},{1,2},{2,3},{4,5},{5,6},{6,7},{8,9},{9,10},{10,11},{12,13},{... | collective-permute-start | bytes 49160 | tf_op jit(solution)/shard_map/while/body/eval_jaxpr/ppermute | solution.py:17
  118.6 5.6 %collective-permute-start = (f32[1,8,4,128]{3,2,1,0:T(4,128)S(1)}, f32[1,8,4,128]{3,2,1,0:T(4,128)S(1)}, u32[]{:S(2)}, u32[]{:S(2)}) collective-permute-start(f32[1,8,4,128]{3,2,1,0:T(4,128)S(1)} %pad_maximum_fusion.6), channel_id=1, source_target_pairs={{1,0},{2,1},{3,2},{5,4},{6,5},{7,6},{9,8},{10,9},{11,10},{13,12},{... | collective-permute-start | bytes 49160 | tf_op jit(solution)/shard_map/while/body/eval_jaxpr/ppermute | solution.py:20
  130.5 7.6 %collective-permute-start.1 = (f32[1,8,4,128]{3,2,1,0:T(4,128)S(1)}, f32[1,8,4,128]{3,2,1,0:T(4,128)S(1)}, u32[]{:S(2)}, u32[]{:S(2)}) collective-permute-start(f32[1,8,4,128]{3,2,1,0:T(4,128)S(1)} %pad_maximum_fusion.6), channel_id=1, source_target_pairs={{0,1},{1,2},{2,3},{4,5},{5,6},{6,7},{8,9},{9,10},{10,11},{12,13},{... | collective-permute-start | bytes 49160 | tf_op jit(solution)/shard_map/while/body/eval_jaxpr/ppermute | solution.py:17
  132.5 5.6 %collective-permute-start = (f32[1,8,4,128]{3,2,1,0:T(4,128)S(1)}, f32[1,8,4,128]{3,2,1,0:T(4,128)S(1)}, u32[]{:S(2)}, u32[]{:S(2)}) collective-permute-start(f32[1,8,4,128]{3,2,1,0:T(4,128)S(1)} %pad_maximum_fusion.6), channel_id=1, source_target_pairs={{1,0},{2,1},{3,2},{5,4},{6,5},{7,6},{9,8},{10,9},{11,10},{13,12},{... | collective-permute-start | bytes 49160 | tf_op jit(solution)/shard_map/while/body/eval_jaxpr/ppermute | solution.py:20
  144.4 7.6 %collective-permute-start.1 = (f32[1,8,4,128]{3,2,1,0:T(4,128)S(1)}, f32[1,8,4,128]{3,2,1,0:T(4,128)S(1)}, u32[]{:S(2)}, u32[]{:S(2)}) collective-permute-start(f32[1,8,4,128]{3,2,1,0:T(4,128)S(1)} %pad_maximum_fusion.6), channel_id=1, source_target_pairs={{0,1},{1,2},{2,3},{4,5},{5,6},{6,7},{8,9},{9,10},{10,11},{12,13},{... | collective-permute-start | bytes 49160 | tf_op jit(solution)/shard_map/while/body/eval_jaxpr/ppermute | solution.py:17
  146.3 5.6 %collective-permute-start = (f32[1,8,4,128]{3,2,1,0:T(4,128)S(1)}, f32[1,8,4,128]{3,2,1,0:T(4,128)S(1)}, u32[]{:S(2)}, u32[]{:S(2)}) collective-permute-start(f32[1,8,4,128]{3,2,1,0:T(4,128)S(1)} %pad_maximum_fusion.6), channel_id=1, source_target_pairs={{1,0},{2,1},{3,2},{5,4},{6,5},{7,6},{9,8},{10,9},{11,10},{13,12},{... | collective-permute-start | bytes 49160 | tf_op jit(solution)/shard_map/while/body/eval_jaxpr/ppermute | solution.py:20
  158.2 7.6 %collective-permute-start.1 = (f32[1,8,4,128]{3,2,1,0:T(4,128)S(1)}, f32[1,8,4,128]{3,2,1,0:T(4,128)S(1)}, u32[]{:S(2)}, u32[]{:S(2)}) collective-permute-start(f32[1,8,4,128]{3,2,1,0:T(4,128)S(1)} %pad_maximum_fusion.6), channel_id=1, source_target_pairs={{0,1},{1,2},{2,3},{4,5},{5,6},{6,7},{8,9},{9,10},{10,11},{12,13},{... | collective-permute-start | bytes 49160 | tf_op jit(solution)/shard_map/while/body/eval_jaxpr/ppermute | solution.py:17
  160.2 5.6 %collective-permute-start = (f32[1,8,4,128]{3,2,1,0:T(4,128)S(1)}, f32[1,8,4,128]{3,2,1,0:T(4,128)S(1)}, u32[]{:S(2)}, u32[]{:S(2)}) collective-permute-start(f32[1,8,4,128]{3,2,1,0:T(4,128)S(1)} %pad_maximum_fusion.6), channel_id=1, source_target_pairs={{1,0},{2,1},{3,2},{5,4},{6,5},{7,6},{9,8},{10,9},{11,10},{13,12},{... | collective-permute-start | bytes 49160 | tf_op jit(solution)/shard_map/while/body/eval_jaxpr/ppermute | solution.py:20
  172.1 7.6 %collective-permute-start.1 = (f32[1,8,4,128]{3,2,1,0:T(4,128)S(1)}, f32[1,8,4,128]{3,2,1,0:T(4,128)S(1)}, u32[]{:S(2)}, u32[]{:S(2)}) collective-permute-start(f32[1,8,4,128]{3,2,1,0:T(4,128)S(1)} %pad_maximum_fusion.6), channel_id=1, source_target_pairs={{0,1},{1,2},{2,3},{4,5},{5,6},{6,7},{8,9},{9,10},{10,11},{12,13},{... | collective-permute-start | bytes 49160 | tf_op jit(solution)/shard_map/while/body/eval_jaxpr/ppermute | solution.py:17
  174.1 5.6 %collective-permute-start = (f32[1,8,4,128]{3,2,1,0:T(4,128)S(1)}, f32[1,8,4,128]{3,2,1,0:T(4,128)S(1)}, u32[]{:S(2)}, u32[]{:S(2)}) collective-permute-start(f32[1,8,4,128]{3,2,1,0:T(4,128)S(1)} %pad_maximum_fusion.6), channel_id=1, source_target_pairs={{1,0},{2,1},{3,2},{5,4},{6,5},{7,6},{9,8},{10,9},{11,10},{13,12},{... | collective-permute-start | bytes 49160 | tf_op jit(solution)/shard_map/while/body/eval_jaxpr/ppermute | solution.py:20
  263.6 14.2 %copy-start.3 = (f32[1,8,128,128]{3,2,1,0:T(8,128)S(1)}, f32[1,8,128,128]{3,2,1,0:T(8,128)}, u32[]{:S(2)}) copy-start(f32[1,8,128,128]{3,2,1,0:T(8,128)} %param.12) | copy-start | bytes 1572868
  266.4 12.3 %copy-start.5 = (f32[1,8,128,128]{3,2,1,0:T(8,128)}, f32[1,8,128,128]{3,2,1,0:T(8,128)S(1)}, u32[]{:S(2)}) copy-start(f32[1,8,128,128]{3,2,1,0:T(8,128)S(1)} %add.163) | copy-start | bytes 1572868
  266.4 11.4 %collective-permute-start.2 = (f32[8,128,128]{2,1,0:T(8,128)S(1)}, f32[8,128,128]{2,1,0:T(8,128)S(1)}, u32[]{:S(2)}, u32[]{:S(2)}) collective-permute-start(f32[8,128,128]{2,1,0:T(8,128)S(1)} %bitcast.111), channel_id=1, source_target_pairs={{0,4},{4,8},{8,12},{12,16},{16,20},{20,24},{24,28},{1,5},{5,9},{9,... | collective-permute-start | bytes 1572872 | tf_op jit(solution)/shard_map/ppermute | solution.py:33
  (5 other events, 11.4 us)
Sparse Core Ops, SparseCore 0:
  11.0 54.3 all-reduce.5
  189.8 27.2 all-gather.1
where the time goes:
time: 288 us; the launch traced here: 286 us
  local copies, waits for them, and re-layouts  79.5 us (28%)
  starting transfers between devices  72.3 us (25%)
  other arithmetic  40.4 us (14%)
  waiting for transfers between devices  39.8 us (14%)
  matrix products  38 us (13%)
  between operations  14.3 us (5%)
    ppermute x12, starting transfers between devices, padded(): lax.ppermute(lax.slice_in_dim(block, 0, width, axis=dim), axis, backward)  43.2 us
    mul x12, other arithmetic, advance(): open_cells * (current + strength * diffusivity * laplace - 0.5 * transport)  35.6 us
    all_gather x1, waiting for transfers between devices, on_device(): every_jump = lax.all_gather(coarse_jump, 'tm', axis=0, tiled=True)  27.4 us
    ppermute x12, starting transfers between devices, padded(): lax.ppermute(lax.slice_in_dim(block, block.shape[dim] - width, None, axis...  26.8 us
    dot_general x10, matrix products, apply_coarse(): jnp.einsum('...tik,tlk->...til', mixed_x, matrix_y, precision=exact_preci...  24.6 us
    dot_general x10, matrix products, apply_coarse(): jnp.einsum('tij,...tjk->...tik', matrix_x, coarse_values, precision=exact...  13.5 us
    dynamic_update_slice x8, local copies, waits for them, and re-layouts, on_device(): last_state, history = lax.scan(sweep, first_coarse, every_jump)  13.4 us
    slice x12, local copies, waits for them, and re-layouts, advance(): current[:, :, :, :-1]  10.3 us
  transfers between devices with their start and end apart: 27, of which 4 were waited for; matrix products, arithmetic and copies ran while one was open for 37% of the time, Pallas kernels for 0%

commit v1 on v0

v1 whole, which is shorter than its diff:
```python
import jax
import jax.numpy as jnp
from jax import lax
from jax.experimental import pallas as pl
from jax.experimental.pallas import tpu as pltpu
from jax.sharding import PartitionSpec as P

SUB = 12
HALO = 16


exact_precision = lax.Precision.HIGHEST


def spread(value, axis, source):
    kept = jnp.where(lax.axis_index(axis) == source, value, 0).astype(value.dtype)
    return lax.psum(kept, axis)


def passed_along(block, axis, distance):
    devices = range(lax.axis_size(axis))
    route = [(i - distance, i) for i in devices if i - distance in devices]
    return lax.ppermute(block, axis, route)


def restrict(values):
    return 0.5 * (values[..., 0::2, :] + values[..., 1::2, :])


def prolong(coarse_values):
    return jnp.repeat(coarse_values, 2, axis=-2)


def apply_coarse(coarse_values, matrix_x, matrix_y):
    mixed_x = jnp.einsum("tij,...tjk->...tik", matrix_x, coarse_values, precision=exact_precision)
    return jnp.einsum("...tik,tlk->...til", mixed_x, matrix_y, precision=exact_precision)


def fine_kernel(south_ref, north_ref, south_ok_ref, north_ok_ref, scale_ref,
                u_ref, fields_ref, west_ref, east_ref, out_ref, state_ref, field_ref):
    tiles = u_ref.shape[0]
    rows = u_ref.shape[1]
    total = rows + 2 * HALO
    for i in range(tiles):
        state_ref[0, i, pl.ds(0, HALO), :] = west_ref[0, i]
        state_ref[0, i, pl.ds(HALO, rows), :] = u_ref[i]
        state_ref[0, i, pl.ds(HALO + rows, HALO), :] = east_ref[0, i]
        for f in range(4):
            field_ref[f, i, pl.ds(0, HALO), :] = west_ref[f + 1, i]
            field_ref[f, i, pl.ds(HALO, rows), :] = fields_ref[f, i]
            field_ref[f, i, pl.ds(HALO + rows, HALO), :] = east_ref[f + 1, i]

    lanes = u_ref.shape[2]
    lane = lax.broadcasted_iota(jnp.int32, (total, lanes), 1)
    first_lane = lane == 0
    last_lane = lane == lanes - 1

    def substep(s, carry):
        src = s % 2
        dst = 1 - src
        strength = scale_ref[s]
        for i in range(tiles):
            current = state_ref[src, i]
            south_tile = state_ref[src, south_ref[i]]
            north_tile = state_ref[src, north_ref[i]]
            south_edge = jnp.where(south_ok_ref[i] > 0, pltpu.roll(south_tile, 1, 1), 0.0)
            north_edge = jnp.where(north_ok_ref[i] > 0, pltpu.roll(north_tile, lanes - 1, 1), 0.0)
            from_west = pltpu.roll(current, 1, 0)
            from_east = pltpu.roll(current, total - 1, 0)
            from_south = jnp.where(first_lane, south_edge, pltpu.roll(current, 1, 1))
            from_north = jnp.where(last_lane, north_edge, pltpu.roll(current, lanes - 1, 1))
            diffusivity = field_ref[0, i]
            speed_x = field_ref[1, i]
            speed_y = field_ref[2, i]
            open_cells = field_ref[3, i]
            laplace = from_west + from_east + from_south + from_north - 4.0 * current
            transport = speed_x * (from_east - from_west) + speed_y * (from_north - from_south)
            state_ref[dst, i] = open_cells * (
                current + strength * diffusivity * laplace - 0.5 * transport
            )
        return carry

    lax.fori_loop(0, SUB, substep, 0)
    last = SUB % 2
    for i in range(tiles):
        out_ref[i] = state_ref[last, i, pl.ds(HALO, rows), :]


def fine_propagate(u, fields, west, east, south, north, south_ok, north_ok, scale):
    tiles, rows, lanes = u.shape
    total = rows + 2 * HALO
    vmem = pltpu.MemorySpace.VMEM
    smem = pltpu.MemorySpace.SMEM
    return pl.pallas_call(
        fine_kernel,
        out_shape=jax.ShapeDtypeStruct(u.shape, u.dtype),
        in_specs=[pl.BlockSpec(memory_space=smem)] * 5 + [pl.BlockSpec(memory_space=vmem)] * 4,
        out_specs=pl.BlockSpec(memory_space=vmem),
        scratch_shapes=[
            pltpu.VMEM((2, tiles, total, lanes), jnp.float32),
            pltpu.VMEM((4, tiles, total, lanes), jnp.float32),
        ],
        compiler_params=pltpu.CompilerParams(vmem_limit_bytes=48 * 1024 * 1024),
    )(south, north, south_ok, north_ok, scale, u, fields, west, east)


def on_device(
    starts, diffusivity, velocity, obstacle, substep_scale, neighbors, coarse_x, coarse_y
):
    slice_count = starts.shape[0]
    tile_count = starts.shape[1]
    rows = starts.shape[2]
    all_tiles = tile_count * lax.axis_size("space")
    block_base = lax.axis_index("space") * tile_count
    open_cells = 1.0 - obstacle.astype(jnp.float32)

    fields = jnp.stack([diffusivity, velocity[0], velocity[1], open_cells], axis=0)
    layers = jnp.concatenate([starts, fields], axis=0)
    space_count = lax.axis_size("space")
    forward = [(i, i + 1) for i in range(space_count - 1)]
    backward = [(i + 1, i) for i in range(space_count - 1)]
    from_prev = lax.ppermute(layers[:, :, rows - HALO:, :], "space", forward)
    from_next = lax.ppermute(layers[:, :, :HALO, :], "space", backward)
    zero_tile = jnp.zeros_like(from_prev[:, :1])
    from_prev = jnp.concatenate([from_prev, zero_tile], axis=1)
    from_next = jnp.concatenate([from_next, zero_tile], axis=1)
    west_nb = neighbors[:, 0]
    east_nb = neighbors[:, 1]
    west_index = jnp.where(west_nb == all_tiles, tile_count, west_nb - (block_base - tile_count))
    east_index = jnp.where(east_nb == all_tiles, tile_count, east_nb - (block_base + tile_count))
    west_index = jnp.clip(west_index, 0, tile_count)
    east_index = jnp.clip(east_index, 0, tile_count)
    west = jnp.take(from_prev, west_index, axis=1)
    east = jnp.take(from_next, east_index, axis=1)

    south_nb = neighbors[:, 2]
    north_nb = neighbors[:, 3]
    south_ok = (south_nb != all_tiles).astype(jnp.int32)
    north_ok = (north_nb != all_tiles).astype(jnp.int32)
    south = jnp.clip(south_nb - block_base, 0, tile_count - 1) * south_ok
    north = jnp.clip(north_nb - block_base, 0, tile_count - 1) * north_ok

    fine_ends = jnp.stack(
        [
            fine_propagate(
                starts[n],
                fields,
                jnp.concatenate([west[n : n + 1], west[slice_count:]], axis=0),
                jnp.concatenate([east[n : n + 1], east[slice_count:]], axis=0),
                south,
                north,
                south_ok,
                north_ok,
                substep_scale,
            )
            for n in range(slice_count)
        ],
        axis=0,
    )
    correction = fine_ends - prolong(apply_coarse(restrict(starts), coarse_x, coarse_y))
    coarse_jump = restrict(correction)
    first_coarse = spread(restrict(starts[0]), "tm", 0)
    every_jump = lax.all_gather(coarse_jump, "tm", axis=0, tiled=True)

    def sweep(state_now, jump):
        return (apply_coarse(state_now, coarse_x, coarse_y) + jump, state_now)

    last_state, history = lax.scan(sweep, first_coarse, every_jump)
    own_coarse = lax.dynamic_slice_in_dim(
        history, lax.axis_index("tm") * slice_count, slice_count, 0
    )
    slice_ends = prolong(apply_coarse(own_coarse, coarse_x, coarse_y)) + correction
    previous = passed_along(slice_ends[-1], "tm", 1)
    first_step = jnp.where(
        lax.axis_index("tm") == 0, jnp.zeros_like(previous), previous - starts[0]
    )
    increment = jnp.concatenate([first_step[None], slice_ends[:-1] - starts[1:]], axis=0)
    return (slice_ends, increment)


def solution(mesh):
    placed = (
        P("tm", "space", None, None),
        P("space", None, None),
        P(None, "space", None, None),
        P("space", None, None),
        P(),
        P("space", None),
        P("space", None, None),
        P("space", None, None),
    )
    return jax.shard_map(
        on_device,
        mesh=mesh,
        in_specs=placed,
        out_specs=(P("tm", "space", None, None), P("tm", "space", None, None)),
        check_vma=False,
    )
```

time: 288 us -> 165 us (0.57)
  starting transfers between devices: 72.3 us -> 8.04 us
  local copies, waits for them, and re-layouts: 79.5 us -> 25.9 us
  other arithmetic: 40.4 us -> 6.49 us
  Pallas kernels: 0 us -> 19.5 us
  waiting for transfers between devices: 39.8 us -> 50.9 us
    ppermute x24 -> x2, starting transfers between devices: 70.1 us -> 5.83 us  [the longest x1 3.49 us: on_device(): from_prev = lax.ppermute(layers[:, :, rows - HALO:, :], 'space', forward)]
    mul x12 -> x1, other arithmetic: 35.6 us -> 0.01 us  [on_device(): north = jnp.clip(north_nb - block_base, 0, tile_count - 1) * north_ok]
    gather x48 -> x2, local copies, waits for them, and re-layouts: 28 us -> 4.54 us  [the longest x1 2.28 us: on_device(): east = jnp.take(from_next, east_index, axis=1)]
    pallas_call x0 -> x1, Pallas kernels: none -> 19.5 us  [fine_propagate(): pl.pallas_call(fine_kernel, out_shape=jax.ShapeDtypeStruct(u.shape, u.dty...]
    slice x49 -> x0, local copies, waits for them, and re-layouts: 12.9 us -> none  [the longest x12 10.3 us: advance(): current[:, :, :, :-1]]
    psum x1, waiting for transfers between devices: 0.02 us -> 11.4 us  [spread(): return lax.psum(kept, axis)]
    dynamic_slice x12 -> x0, local copies, waits for them, and re-layouts: 7.33 us -> none  [advance(): strength = substep_scale[substep_index]]
    concatenate x36 -> x2, local copies, waits for them, and re-layouts: 7.07 us -> 3.49 us  [the longest x1 1.75 us: on_device(): from_next = jnp.concatenate([from_next, zero_tile], axis=1)]
  transfers between devices with their start and end apart: 27 -> 5, of which waited for: 4 -> 3; matrix products, arithmetic and copies ran while one was open for 37% -> 11% of each run, Pallas kernels for 0% -> 12%
where the time goes in v1:
time: 165 us; the launch traced here: 164 us
  waiting for transfers between devices  50.9 us (31%)
  matrix products  38.5 us (23%)
  local copies, waits for them, and re-layouts  25.9 us (16%)
  Pallas kernels  19.5 us (12%)
  between operations  14.4 us (9%)
  starting transfers between devices  8.04 us (5%)
  other arithmetic  6.49 us (4%)
    all_gather x1, waiting for transfers between devices, on_device(): every_jump = lax.all_gather(coarse_jump, 'tm', axis=0, tiled=True)  30.2 us
    dot_general x10, matrix products, apply_coarse(): jnp.einsum('...tik,tlk->...til', mixed_x, matrix_y, precision=exact_preci...  25.2 us
    pallas_call x1, Pallas kernels, fine_propagate(): pl.pallas_call(fine_kernel, out_shape=jax.ShapeDtypeStruct(u.shape, u.dty...  19.5 us
    dynamic_update_slice x8, local copies, waits for them, and re-layouts, on_device(): last_state, history = lax.scan(sweep, first_coarse, every_jump)  13.4 us
    dot_general x10, matrix products, apply_coarse(): jnp.einsum('tij,...tjk->...tik', matrix_x, coarse_values, precision=exact...  13.3 us
    psum x1, waiting for transfers between devices, spread(): return lax.psum(kept, axis)  11.4 us
    ppermute x1, waiting for transfers between devices, passed_along(): return lax.ppermute(block, axis, route)  9.26 us
    slice x6, local copies, waits for them, and re-layouts, restrict(): return 0.5 * (values[..., 0::2, :] + values[..., 1::2, :])  4.02 us
  transfers between devices with their start and end apart: 5, of which 3 were waited for; matrix products, arithmetic and copies ran while one was open for 11% of the time, Pallas kernels for 12%

profile of v1, /device:TPU:12, one launch (start us, length us, event | category | flops | bytes accessed | tf_op | source)
XLA Modules:
  0.0 163.8 jit_solution(9108012135017336262)
XLA Ops:
  11.4 2.3 %collective-permute-start.1 = (f32[5,8,16,128]{3,2,1,0:T(8,128)}, f32[5,8,16,128]{3,2,1,0:T(8,128)}, u32[]{:S(2)}, u32[]{:S(2)}) collective-permute-start(f32[5,8,16,128]{3,2,1,0:T(8,128)} %get-tuple-element.52), channel_id=1, source_target_pairs={{1,0},{2,1},{3,2},{5,4},{6,5},{7,6},{9,8},{10,9},{11,10},{13,12},{... | collective-permute-start | bytes 983048 | tf_op jit(solution)/shard_map/ppermute | solution.py:123
  13.8 3.5 %collective-permute-start = (f32[5,8,16,128]{3,2,1,0:T(8,128)}, f32[5,8,16,128]{3,2,1,0:T(8,128)}, u32[]{:S(2)}, u32[]{:S(2)}) collective-permute-start(f32[5,8,16,128]{3,2,1,0:T(8,128)} %get-tuple-element.53), channel_id=1, source_target_pairs={{0,1},{1,2},{2,3},{4,5},{5,6},{6,7},{8,9},{9,10},{10,11},{12,13},{... | collective-permute-start | bytes 983048 | tf_op jit(solution)/shard_map/ppermute | solution.py:122
  18.9 1.8 %pad_maximum_fusion.fields_ref = f32[4,8,128,128]{3,2,1,0:T(8,128)S(1)} fusion(f32[1,8,128,128]{3,2,1,0:T(8,128)} %copy-done.4, f32[2,8,128,128]{3,2,1,0:T(8,128)} %param.14, f32[1,8,128,128]{3,2,1,0:T(8,128)} %bitcast.80), kind=kLoop, calls=%fused_computation.4 | loop fusion | flops 1048576 | bytes 4194304 | tf_op jit(solution)/shard_map/stack | solution.py:117
  20.7 1.4 convolution_bitcast_fusion.1
  22.2 1.8 %fusion.17 = f32[8,64,128]{2,1,0:T(8,128)} fusion(f32[8,64,128]{2,1,0:T(8,128)S(1)} %convolution_bitcast_fusion.1, f32[8,128,128]{2,1,0:T(8,128)S(1)} %copy-done.2), kind=kOutput, calls=%fused_computation.46 | convolution fusion | flops 100663296 | bytes 1048576 | tf_op jit(solution)/shard_map/...tik,tlk->...til/dot_general | solution.py:36
  24.0 1.7 %concatenate.15 = f32[5,9,16,128]{3,2,1,0:T(8,128)} pad(f32[5,8,16,128]{3,2,1,0:T(8,128)} %collective-permute-done.1, f32[]{:T(128)} %constant.13.clone.1), padding=0_0x0_1x0_0x0_0 | pad | bytes 696324 | tf_op jit(solution)/shard_map/concatenate | solution.py:126
  25.8 2.3 %gather_fusion.1 = f32[8,5,16,128]{3,2,1,0:T(8,128)} fusion(f32[5,9,16,128]{3,2,1,0:T(8,128)} %concatenate.15, s32[1024]{0:T(1024)S(1)} %pad_clamp_fusion), kind=kCustom, calls=%fused_computation.1.clone | custom fusion | bytes 655392 | tf_op jit(solution)/shard_map/jit(_take)/gather | solution.py:134
  28.1 1.7 %concatenate.14 = f32[5,9,16,128]{3,2,1,0:T(8,128)} pad(f32[5,8,16,128]{3,2,1,0:T(8,128)} %collective-permute-done, f32[]{:T(128)} %constant.13.clone.1), padding=0_0x0_1x0_0x0_0 | pad | bytes 696324 | tf_op jit(solution)/shard_map/concatenate | solution.py:125
  29.8 2.3 %gather_fusion = f32[8,5,16,128]{3,2,1,0:T(8,128)} fusion(f32[5,9,16,128]{3,2,1,0:T(8,128)} %concatenate.14, s32[1024]{0:T(1024)S(1)} %pad_clamp_fusion.1), kind=kCustom, calls=%fused_computation.clone | custom fusion | bytes 655392 | tf_op jit(solution)/shard_map/jit(_take)/gather | solution.py:133
  33.3 19.5 %shard_map.95 = f32[8,128,128]{2,1,0:T(8,128)S(1)} custom-call(s32[8]{0:T(128)S(1)} %get-tuple-element.59.south_ref, s32[8]{0:T(128)S(1)} %get-tuple-element.58.north_ref, s32[8]{0:T(128)S(1)} %get-tuple-element.57.south_ok_ref, s32[8]{0:T(128)S(1)} %get-tuple-element.56.north_ok_ref, f32[12]{0:T(128)S(1)} %copy-done.1, f32[8,128,128]{2,1,0:T(8,128)S(1)} %bitcast.75, ...), custom_call_target="tpu_custom_call" | custom-call | tf_op jit(solution)/shard_map/pallas_call | solution.py:94
  54.1 11.4 %all-reduce.4.cloned.1.call-done = f32[8,64,128]{2,1,0:T(8,128)} async-done(((f32[8,64,128]{2,1,0:T(8,128)}), f32[8,64,128]{2,1,0:T(8,128)}) %all-reduce.4.cloned.1.call-update) | async-done | bytes 262160 | tf_op jit(solution)/shard_map/psum | solution.py:17
  65.4 30.2 %all-gather.2.cloned.1.call-done = f32[8,8,64,128]{3,2,1,0:T(8,128)} async-done(((f32[1,8,64,128]{3,2,1,0:T(8,128)}), f32[8,8,64,128]{3,2,1,0:T(8,128)}) %all-gather.2.cloned.1.call-update) | async-done | bytes 2097168 | tf_op jit(solution)/shard_map/all_gather | solution.py:163
  95.7 46.3 %while.12 = (s32[]{:T(128)}, f32[8,64,128]{2,1,0:T(8,128)}, f32[8,8,64,128]{3,2,1,0:T(8,128)}, f32[8,64,64]{2,1,0:T(8,128)S(1)}, f32[8,128,128]{2,1,0:T(8,128)S(1)}, /*index=5*/f32[8,8,64,128]{3,2,1,0:T(8,128)}, s32[]{:T(128)}) while((s32[]{:T(128)}, f32[8,64,128]{2,1,0:T(8,128)}, f32[8,8,64,128]{3,2,1,0:T(8,128)}, ...), condition=%wide.region_2.4_spmd, body=%wide.region_1.3_spmd.sunk | while | flops 151060480 | bytes 2490461 | solution.py:168
  97.0 1.7 %bitcast_dynamic-update-slice_fusion.2 = f32[8,8,64,128]{3,2,1,0:T(8,128)} fusion(f32[8,8,64,128]{3,2,1,0:T(8,128)} %get-tuple-element.108, s32[]{:T(128)S(6)} %copy.25, f32[8,64,128]{2,1,0:T(8,128)} %get-tuple-element.107), kind=kLoop, calls=%fused_computation.3.clone.1 | loop fusion | bytes 524292 | tf_op jit(solution)/shard_map/while/body/jit(dynamic_update_index_in_dim)/dynamic_update_slice | solution.py:168
  98.7 2.8 %convolution_add_fusion.2 = f32[8,64,128]{2,1,0:T(8,128)} fusion(f32[8,64,128]{2,1,0:T(8,128)S(1)} %fusion.38, f32[8,128,128]{2,1,0:T(8,128)S(1)} %get-tuple-element.117, f32[8,8,64,128]{3,2,1,0:T(8,128)} %get-tuple-element.118, s32[]{:T(128)S(6)} %copy.25), kind=kOutput, calls=%fused_computation.2.clone.1 | convolution fusion | flops 100728832 | bytes 1310724 | tf_op jit(solution)/shard_map/while/body/eval_jaxpr/...tik,tlk->...til/dot_general | solution.py:36
  101.4 1.3 fusion.38
  102.8 1.7 %bitcast_dynamic-update-slice_fusion.2 = f32[8,8,64,128]{3,2,1,0:T(8,128)} fusion(f32[8,8,64,128]{3,2,1,0:T(8,128)} %get-tuple-element.108, s32[]{:T(128)S(6)} %copy.25, f32[8,64,128]{2,1,0:T(8,128)} %get-tuple-element.107), kind=kLoop, calls=%fused_computation.3.clone.1 | loop fusion | bytes 524292 | tf_op jit(solution)/shard_map/while/body/jit(dynamic_update_index_in_dim)/dynamic_update_slice | solution.py:168
  104.5 2.8 %convolution_add_fusion.2 = f32[8,64,128]{2,1,0:T(8,128)} fusion(f32[8,64,128]{2,1,0:T(8,128)S(1)} %fusion.38, f32[8,128,128]{2,1,0:T(8,128)S(1)} %get-tuple-element.117, f32[8,8,64,128]{3,2,1,0:T(8,128)} %get-tuple-element.118, s32[]{:T(128)S(6)} %copy.25), kind=kOutput, calls=%fused_computation.2.clone.1 | convolution fusion | flops 100728832 | bytes 1310724 | tf_op jit(solution)/shard_map/while/body/eval_jaxpr/...tik,tlk->...til/dot_general | solution.py:36
  108.6 1.7 %bitcast_dynamic-update-slice_fusion.2 = f32[8,8,64,128]{3,2,1,0:T(8,128)} fusion(f32[8,8,64,128]{3,2,1,0:T(8,128)} %get-tuple-element.108, s32[]{:T(128)S(6)} %copy.25, f32[8,64,128]{2,1,0:T(8,128)} %get-tuple-element.107), kind=kLoop, calls=%fused_computation.3.clone.1 | loop fusion | bytes 524292 | tf_op jit(solution)/shard_map/while/body/jit(dynamic_update_index_in_dim)/dynamic_update_slice | solution.py:168
  110.3 2.8 %convolution_add_fusion.2 = f32[8,64,128]{2,1,0:T(8,128)} fusion(f32[8,64,128]{2,1,0:T(8,128)S(1)} %fusion.38, f32[8,128,128]{2,1,0:T(8,128)S(1)} %get-tuple-element.117, f32[8,8,64,128]{3,2,1,0:T(8,128)} %get-tuple-element.118, s32[]{:T(128)S(6)} %copy.25), kind=kOutput, calls=%fused_computation.2.clone.1 | convolution fusion | flops 100728832 | bytes 1310724 | tf_op jit(solution)/shard_map/while/body/eval_jaxpr/...tik,tlk->...til/dot_general | solution.py:36
  114.4 1.7 %bitcast_dynamic-update-slice_fusion.2 = f32[8,8,64,128]{3,2,1,0:T(8,128)} fusion(f32[8,8,64,128]{3,2,1,0:T(8,128)} %get-tuple-element.108, s32[]{:T(128)S(6)} %copy.25, f32[8,64,128]{2,1,0:T(8,128)} %get-tuple-element.107), kind=kLoop, calls=%fused_computation.3.clone.1 | loop fusion | bytes 524292 | tf_op jit(solution)/shard_map/while/body/jit(dynamic_update_index_in_dim)/dynamic_update_slice | solution.py:168
  116.1 2.8 %convolution_add_fusion.2 = f32[8,64,128]{2,1,0:T(8,128)} fusion(f32[8,64,128]{2,1,0:T(8,128)S(1)} %fusion.38, f32[8,128,128]{2,1,0:T(8,128)S(1)} %get-tuple-element.117, f32[8,8,64,128]{3,2,1,0:T(8,128)} %get-tuple-element.118, s32[]{:T(128)S(6)} %copy.25), kind=kOutput, calls=%fused_computation.2.clone.1 | convolution fusion | flops 100728832 | bytes 1310724 | tf_op jit(solution)/shard_map/while/body/eval_jaxpr/...tik,tlk->...til/dot_general | solution.py:36
  120.2 1.7 %bitcast_dynamic-update-slice_fusion.2 = f32[8,8,64,128]{3,2,1,0:T(8,128)} fusion(f32[8,8,64,128]{3,2,1,0:T(8,128)} %get-tuple-element.108, s32[]{:T(128)S(6)} %copy.25, f32[8,64,128]{2,1,0:T(8,128)} %get-tuple-element.107), kind=kLoop, calls=%fused_computation.3.clone.1 | loop fusion | bytes 524292 | tf_op jit(solution)/shard_map/while/body/jit(dynamic_update_index_in_dim)/dynamic_update_slice | solution.py:168
  121.8 2.8 %convolution_add_fusion.2 = f32[8,64,128]{2,1,0:T(8,128)} fusion(f32[8,64,128]{2,1,0:T(8,128)S(1)} %fusion.38, f32[8,128,128]{2,1,0:T(8,128)S(1)} %get-tuple-element.117, f32[8,8,64,128]{3,2,1,0:T(8,128)} %get-tuple-element.118, s32[]{:T(128)S(6)} %copy.25), kind=kOutput, calls=%fused_computation.2.clone.1 | convolution fusion | flops 100728832 | bytes 1310724 | tf_op jit(solution)/shard_map/while/body/eval_jaxpr/...tik,tlk->...til/dot_general | solution.py:36
  125.9 1.7 %bitcast_dynamic-update-slice_fusion.2 = f32[8,8,64,128]{3,2,1,0:T(8,128)} fusion(f32[8,8,64,128]{3,2,1,0:T(8,128)} %get-tuple-element.108, s32[]{:T(128)S(6)} %copy.25, f32[8,64,128]{2,1,0:T(8,128)} %get-tuple-element.107), kind=kLoop, calls=%fused_computation.3.clone.1 | loop fusion | bytes 524292 | tf_op jit(solution)/shard_map/while/body/jit(dynamic_update_index_in_dim)/dynamic_update_slice | solution.py:168
  127.6 2.8 %convolution_add_fusion.2 = f32[8,64,128]{2,1,0:T(8,128)} fusion(f32[8,64,128]{2,1,0:T(8,128)S(1)} %fusion.38, f32[8,128,128]{2,1,0:T(8,128)S(1)} %get-tuple-element.117, f32[8,8,64,128]{3,2,1,0:T(8,128)} %get-tuple-element.118, s32[]{:T(128)S(6)} %copy.25), kind=kOutput, calls=%fused_computation.2.clone.1 | convolution fusion | flops 100728832 | bytes 1310724 | tf_op jit(solution)/shard_map/while/body/eval_jaxpr/...tik,tlk->...til/dot_general | solution.py:36
  131.7 1.7 %bitcast_dynamic-update-slice_fusion.2 = f32[8,8,64,128]{3,2,1,0:T(8,128)} fusion(f32[8,8,64,128]{3,2,1,0:T(8,128)} %get-tuple-element.108, s32[]{:T(128)S(6)} %copy.25, f32[8,64,128]{2,1,0:T(8,128)} %get-tuple-element.107), kind=kLoop, calls=%fused_computation.3.clone.1 | loop fusion | bytes 524292 | tf_op jit(solution)/shard_map/while/body/jit(dynamic_update_index_in_dim)/dynamic_update_slice | solution.py:168
  133.4 2.8 %convolution_add_fusion.2 = f32[8,64,128]{2,1,0:T(8,128)} fusion(f32[8,64,128]{2,1,0:T(8,128)S(1)} %fusion.38, f32[8,128,128]{2,1,0:T(8,128)S(1)} %get-tuple-element.117, f32[8,8,64,128]{3,2,1,0:T(8,128)} %get-tuple-element.118, s32[]{:T(128)S(6)} %copy.25), kind=kOutput, calls=%fused_computation.2.clone.1 | convolution fusion | flops 100728832 | bytes 1310724 | tf_op jit(solution)/shard_map/while/body/eval_jaxpr/...tik,tlk->...til/dot_general | solution.py:36
  137.5 1.7 %bitcast_dynamic-update-slice_fusion.2 = f32[8,8,64,128]{3,2,1,0:T(8,128)} fusion(f32[8,8,64,128]{3,2,1,0:T(8,128)} %get-tuple-element.108, s32[]{:T(128)S(6)} %copy.25, f32[8,64,128]{2,1,0:T(8,128)} %get-tuple-element.107), kind=kLoop, calls=%fused_computation.3.clone.1 | loop fusion | bytes 524292 | tf_op jit(solution)/shard_map/while/body/jit(dynamic_update_index_in_dim)/dynamic_update_slice | solution.py:168
  139.2 2.8 %convolution_add_fusion.2 = f32[8,64,128]{2,1,0:T(8,128)} fusion(f32[8,64,128]{2,1,0:T(8,128)S(1)} %fusion.38, f32[8,128,128]{2,1,0:T(8,128)S(1)} %get-tuple-element.117, f32[8,8,64,128]{3,2,1,0:T(8,128)} %get-tuple-element.118, s32[]{:T(128)S(6)} %copy.25), kind=kOutput, calls=%fused_computation.2.clone.1 | convolution fusion | flops 100728832 | bytes 1310724 | tf_op jit(solution)/shard_map/while/body/eval_jaxpr/...tik,tlk->...til/dot_general | solution.py:36
  144.7 2.1 %collective-permute-start.2 = (f32[8,128,128]{2,1,0:T(8,128)S(1)}, f32[8,128,128]{2,1,0:T(8,128)S(1)}, u32[]{:S(2)}, u32[]{:S(2)}) collective-permute-start(f32[8,128,128]{2,1,0:T(8,128)S(1)} %add.42), channel_id=1, source_target_pairs={{0,4},{4,8},{8,12},{12,16},{16,20},{20,24},{24,28},{1,5},{5,9},{9,... | collective-permute-start | bytes 1572872 | tf_op jit(solution)/shard_map/ppermute | solution.py:23
  146.8 9.3 %collective-permute-done.2 = f32[8,128,128]{2,1,0:T(8,128)S(1)} collective-permute-done((f32[8,128,128]{2,1,0:T(8,128)S(1)}, f32[8,128,128]{2,1,0:T(8,128)S(1)}, u32[]{:S(2)}, u32[]{:S(2)}) %collective-permute-start.2) | collective-permute-done | bytes 524320 | tf_op jit(solution)/shard_map/ppermute | solution.py:23
  (59 shorter events, 21.0 us)
Async XLA Ops:
  7.2 3.3 %copy-start = (f32[1,8,128,128]{3,2,1,0:T(8,128)S(1)}, f32[1,8,128,128]{3,2,1,0:T(8,128)}, u32[]{:S(2)}) copy-start(f32[1,8,128,128]{3,2,1,0:T(8,128)} %param.12) | copy-start | bytes 1572868
  7.2 3.2 %copy-start.9 = (s32[8,128,128]{2,1,0:T(8,128)S(1)}, s32[8,128,128]{2,1,0:T(8,128)}, u32[]{:S(2)}) copy-start(s32[8,128,128]{2,1,0:T(8,128)} %param.15) | copy-start | bytes 1572868
  7.2 3.3 %copy-start.5 = (f32[2,8,128,128]{3,2,1,0:T(8,128)S(1)}, f32[2,8,128,128]{3,2,1,0:T(8,128)}, u32[]{:S(2)}) copy-start(f32[2,8,128,128]{3,2,1,0:T(8,128)} %param.14) | copy-start | bytes 3145732
  7.2 3.3 %copy-start.6 = (f32[8,128,128]{2,1,0:T(8,128)S(1)}, f32[8,128,128]{2,1,0:T(8,128)}, u32[]{:S(2)}) copy-start(f32[8,128,128]{2,1,0:T(8,128)} %param.13) | copy-start | bytes 1572868
  7.2 58.2 %all-reduce.4.cloned.1.call-start = ((), (), s32[]{:S(2)}) async-start(), calls=%async_computation | async-start | bytes 524288 | tf_op jit(solution)/shard_map/psum | solution.py:17
  10.3 7.0 %copy-start.10 = (s32[8,4]{0,1:T(4,128)S(1)}, s32[8,4]{0,1:T(4,128)}, u32[]{:S(2)}) copy-start(s32[8,4]{0,1:T(4,128)} %param.17) | copy-start | bytes 388
  10.3 85.3 %all-gather.2.cloned.1.call-start = ((), (), s32[]{:S(2)}) async-start(), calls=%async_computation.1 | async-start | bytes 2359296 | tf_op jit(solution)/shard_map/all_gather | solution.py:163
  10.4 7.7 %copy-start.4 = (f32[1,8,128,128]{3,2,1,0:T(8,128)}, f32[1,8,128,128]{3,2,1,0:T(8,128)S(1)}, u32[]{:S(2)}) copy-start(f32[1,8,128,128]{3,2,1,0:T(8,128)S(1)} %subtract_bitcast_fusion) | copy-start | bytes 1572868
  11.4 12.6 %collective-permute-start.1 = (f32[5,8,16,128]{3,2,1,0:T(8,128)}, f32[5,8,16,128]{3,2,1,0:T(8,128)}, u32[]{:S(2)}, u32[]{:S(2)}) collective-permute-start(f32[5,8,16,128]{3,2,1,0:T(8,128)} %get-tuple-element.52), channel_id=1, source_target_pairs={{1,0},{2,1},{3,2},{5,4},{6,5},{7,6},{9,8},{10,9},{11,10},{13,12},{... | collective-permute-start | bytes 983048 | tf_op jit(solution)/shard_map/ppermute | solution.py:123
  13.8 14.3 %collective-permute-start = (f32[5,8,16,128]{3,2,1,0:T(8,128)}, f32[5,8,16,128]{3,2,1,0:T(8,128)}, u32[]{:S(2)}, u32[]{:S(2)}) collective-permute-start(f32[5,8,16,128]{3,2,1,0:T(8,128)} %get-tuple-element.53), channel_id=1, source_target_pairs={{0,1},{1,2},{2,3},{4,5},{5,6},{6,7},{8,9},{9,10},{10,11},{12,13},{... | collective-permute-start | bytes 983048 | tf_op jit(solution)/shard_map/ppermute | solution.py:122
  18.9 1.9 %copy-start.3 = (f32[8,64,64]{2,1,0:T(8,128)S(1)}, f32[8,64,64]{2,1,0:T(8,128)}, u32[]{:S(2)}) copy-start(f32[8,64,64]{2,1,0:T(8,128)} %param.18) | copy-start | bytes 393220
  18.9 3.3 %copy-start.2 = (f32[8,128,128]{2,1,0:T(8,128)S(1)}, f32[8,128,128]{2,1,0:T(8,128)}, u32[]{:S(2)}) copy-start(f32[8,128,128]{2,1,0:T(8,128)} %param.19) | copy-start | bytes 1572868
  24.0 9.2 %copy-start.1 = (f32[12]{0:T(128)S(1)}, f32[12]{0:T(128)}, u32[]{:S(2)}) copy-start(f32[12]{0:T(128)} %scale_ref.1) | copy-start | bytes 148
  33.3 19.5 %copy-start.7 = (f32[8,64,128]{2,1,0:T(8,128)S(1)}, f32[8,64,128]{2,1,0:T(8,128)}, u32[]{:S(2)}) copy-start(f32[8,64,128]{2,1,0:T(8,128)} %fusion.17) | copy-start | bytes 786436
  144.7 12.3 %copy-start.8 = (f32[8,128,128]{2,1,0:T(8,128)}, f32[8,128,128]{2,1,0:T(8,128)S(1)}, u32[]{:S(2)}) copy-start(f32[8,128,128]{2,1,0:T(8,128)S(1)} %add.42) | copy-start | bytes 1572868
  144.7 11.4 %collective-permute-start.2 = (f32[8,128,128]{2,1,0:T(8,128)S(1)}, f32[8,128,128]{2,1,0:T(8,128)S(1)}, u32[]{:S(2)}, u32[]{:S(2)}) collective-permute-start(f32[8,128,128]{2,1,0:T(8,128)S(1)} %add.42), channel_id=1, source_target_pairs={{0,4},{4,8},{8,12},{12,16},{16,20},{20,24},{24,28},{1,5},{5,9},{9,... | collective-permute-start | bytes 1572872 | tf_op jit(solution)/shard_map/ppermute | solution.py:23
Sparse Core Ops, SparseCore 0:
  11.1 54.2 all-reduce.3
  67.9 27.7 all-gather.1

commit v2 on v1

--- a/solution.py
+++ b/solution.py
@@ -159,16 +159,45 @@
     )
     correction = fine_ends - prolong(apply_coarse(restrict(starts), coarse_x, coarse_y))
     coarse_jump = restrict(correction)
-    first_coarse = spread(restrict(starts[0]), "tm", 0)
-    every_jump = lax.all_gather(coarse_jump, "tm", axis=0, tiled=True)
-
-    def sweep(state_now, jump):
-        return (apply_coarse(state_now, coarse_x, coarse_y) + jump, state_now)
-
-    last_state, history = lax.scan(sweep, first_coarse, every_jump)
-    own_coarse = lax.dynamic_slice_in_dim(
-        history, lax.axis_index("tm") * slice_count, slice_count, 0
-    )
+    tm_index = lax.axis_index("tm")
+    tm_count = lax.axis_size("tm")
+    shifted_jump = jnp.concatenate(
+        [passed_along(coarse_jump[-1:], "tm", 1), coarse_jump[:-1]], axis=0
+    )
+    first_coarse = restrict(starts[:1])
+    head = jnp.where(tm_index == 0, first_coarse, shifted_jump[:1])
+    local = jnp.concatenate([head, shifted_jump[1:]], axis=0)
+
+    states = [local[0]]
+    for n in range(1, slice_count):
+        states.append(apply_coarse(states[-1], coarse_x, coarse_y) + local[n])
+    states = jnp.stack(states, axis=0)
+
+    power_x = coarse_x
+    power_y = coarse_y
+    for n in range(1, slice_count):
+        power_x = jnp.einsum("tij,tjk->tik", power_x, coarse_x, precision=exact_precision)
+        power_y = jnp.einsum("tij,tjk->tik", power_y, coarse_y, precision=exact_precision)
+    total = states[-1]
+    distance = 1
+    while distance < tm_count:
+        received = passed_along(total, "tm", distance)
+        total = total + jnp.where(
+            tm_index >= distance, apply_coarse(received, power_x, power_y), 0.0
+        )
+        distance *= 2
+        if distance < tm_count:
+            power_x = jnp.einsum("tij,tjk->tik", power_x, power_x, precision=exact_precision)
+            power_y = jnp.einsum("tij,tjk->tik", power_y, power_y, precision=exact_precision)
+    if slice_count == 1:
+        own_coarse = total[None]
+    else:
+        earlier = jnp.where(tm_index > 0, passed_along(total, "tm", 1), 0.0)
+        own_coarse = []
+        for n in range(slice_count):
+            earlier = apply_coarse(earlier, coarse_x, coarse_y)
+            own_coarse.append(states[n] + earlier)
+        own_coarse = jnp.stack(own_coarse, axis=0)
     slice_ends = prolong(apply_coarse(own_coarse, coarse_x, coarse_y)) + correction
     previous = passed_along(slice_ends[-1], "tm", 1)
     first_step = jnp.where(

time: 165 us -> 99.5 us (0.60)
  matrix products: 38.5 us -> 11.3 us
  waiting for transfers between devices: 50.9 us -> 34.9 us
  local copies, waits for them, and re-layouts: 25.9 us -> 11 us
  between operations: 14.4 us -> 1.06 us
  starting transfers between devices: 8.04 us -> 15.5 us
    all_gather x1 -> x0, waiting for transfers between devices: 30.2 us -> none  [on_device(): every_jump = lax.all_gather(coarse_jump, 'tm', axis=0, tiled=True)]
    ppermute x1 -> x5, waiting for transfers between devices: 9.26 us -> 34.9 us  [passed_along(): return lax.ppermute(block, axis, route)]
    dot_general x10 -> x5, matrix products: 25.2 us -> 6.32 us  [apply_coarse(): jnp.einsum('...tik,tlk->...til', mixed_x, matrix_y, precision=exact_preci...]
    dynamic_update_slice x8 -> x0, local copies, waits for them, and re-layouts: 13.4 us -> none  [on_device(): last_state, history = lax.scan(sweep, first_coarse, every_jump)]
    psum x1 -> x0, waiting for transfers between devices: 11.4 us -> none  [spread(): return lax.psum(kept, axis)]
    dot_general x10 -> x5, matrix products: 13.3 us -> 2.94 us  [apply_coarse(): jnp.einsum('tij,...tjk->...tik', matrix_x, coarse_values, precision=exact...]
    ppermute x1 -> x5, starting transfers between devices: 2.13 us -> 8.97 us  [passed_along(): return lax.ppermute(block, axis, route)]
    slice x6 -> x4, local copies, waits for them, and re-layouts: 4.02 us -> 1.79 us  [restrict(): return 0.5 * (values[..., 0::2, :] + values[..., 1::2, :])]
  transfers between devices with their start and end apart: 5 -> 7, of which waited for: 3 -> 5; matrix products, arithmetic and copies ran while one was open for 11% -> 11% of each run, Pallas kernels for 12% -> 0%
where the time goes in v2:
time: 99.5 us; the launch traced here: 99 us
  waiting for transfers between devices  34.9 us (35%)
  Pallas kernels  19.5 us (20%)
  starting transfers between devices  15.5 us (16%)
  matrix products  11.3 us (11%)
  local copies, waits for them, and re-layouts  11 us (11%)
  other arithmetic  5.69 us (6%)
  between operations  1.06 us (1%)
    ppermute x5, waiting for transfers between devices, passed_along(): return lax.ppermute(block, axis, route)  34.9 us
    pallas_call x1, Pallas kernels, fine_propagate(): pl.pallas_call(fine_kernel, out_shape=jax.ShapeDtypeStruct(u.shape, u.dty...  19.5 us
    ppermute x5, starting transfers between devices, passed_along(): return lax.ppermute(block, axis, route)  8.97 us
    dot_general x5, matrix products, apply_coarse(): jnp.einsum('...tik,tlk->...til', mixed_x, matrix_y, precision=exact_preci...  6.32 us
    ppermute x1, starting transfers between devices, on_device(): from_prev = lax.ppermute(layers[:, :, rows - HALO:, :], 'space', forward)  3.47 us
    ppermute x1, starting transfers between devices, on_device(): from_next = lax.ppermute(layers[:, :, :HALO, :], 'space', backward)  3.09 us
    dot_general x5, matrix products, apply_coarse(): jnp.einsum('tij,...tjk->...tik', matrix_x, coarse_values, precision=exact...  2.94 us
    gather x1, local copies, waits for them, and re-layouts, on_device(): west = jnp.take(from_prev, west_index, axis=1)  2.3 us
  transfers between devices with their start and end apart: 7, of which 5 were waited for; matrix products, arithmetic and copies ran while one was open for 11% of the time, Pallas kernels for 0%

profile of v2, /device:TPU:12, one launch (start us, length us, event | category | flops | bytes accessed | tf_op | source)
XLA Modules:
  0.0 99.0 jit_solution(14453474686029140166)
XLA Ops:
  0.7 1.2 %subtract_bitcast_fusion = f32[1,8,128,128]{3,2,1,0:T(8,128)S(1)} fusion(s32[8,128,128]{2,1,0:T(8,128)} %param.13), kind=kLoop, calls=%fused_computation.12 | loop fusion | flops 262144 | bytes 1048576 | tf_op jit(solution)/shard_map/stack | solution.py:117
  1.9 2.0 %pad_maximum_fusion.1 = (f32[5,8,16,128]{3,2,1,0:T(8,128)}, f32[5,8,16,128]{3,2,1,0:T(8,128)}) fusion(f32[1,8,128,128]{3,2,1,0:T(8,128)S(1)} %subtract_bitcast_fusion, f32[2,8,128,128]{3,2,1,0:T(8,128)} %param.12, f32[1,8,128,128]{3,2,1,0:T(8,128)} %bitcast.78, f32[1,8,128,128]{3,2,1,0:T(8,128)} %param.10), kind=kLoop, calls=%fused_computation.13 | loop fusion | flops 491520 | bytes 3276800 | tf_op jit(solution)/shard_map/concatenate | solution.py:118
  3.9 3.5 %collective-permute-start = (f32[5,8,16,128]{3,2,1,0:T(8,128)}, f32[5,8,16,128]{3,2,1,0:T(8,128)}, u32[]{:S(2)}, u32[]{:S(2)}) collective-permute-start(f32[5,8,16,128]{3,2,1,0:T(8,128)} %get-tuple-element.8), channel_id=1, source_target_pairs={{0,1},{1,2},{2,3},{4,5},{5,6},{6,7},{8,9},{9,10},{10,11},{12,13},{... | collective-permute-start | bytes 983048 | tf_op jit(solution)/shard_map/ppermute | solution.py:122
  7.3 3.1 %collective-permute-start.1 = (f32[5,8,16,128]{3,2,1,0:T(8,128)}, f32[5,8,16,128]{3,2,1,0:T(8,128)}, u32[]{:S(2)}, u32[]{:S(2)}) collective-permute-start(f32[5,8,16,128]{3,2,1,0:T(8,128)} %get-tuple-element.7), channel_id=1, source_target_pairs={{1,0},{2,1},{3,2},{5,4},{6,5},{7,6},{9,8},{10,9},{11,10},{13,12},{... | collective-permute-start | bytes 983048 | tf_op jit(solution)/shard_map/ppermute | solution.py:123
  10.7 0.4 copy-done.10
  11.5 0.8 slice.42
  12.3 0.8 slice.43
  13.1 1.4 %convolution_bitcast_fusion.1 = f32[8,64,128]{2,1,0:T(8,128)S(1)} fusion(f32[8,64,64]{2,1,0:T(8,128)S(1)} %copy-done.3, f32[1,8,64,128]{3,2,1,0:T(8,128)} %slice.42, f32[1,8,64,128]{3,2,1,0:T(8,128)} %slice.43), kind=kOutput, calls=%fused_computation.7 | convolution fusion | flops 50462720 | bytes 917504 | tf_op jit(solution)/shard_map/tij,...tjk->...tik/dot_general | solution.py:35
  14.6 1.8 %fusion.13 = f32[8,64,128]{2,1,0:T(8,128)} fusion(f32[8,64,128]{2,1,0:T(8,128)S(1)} %convolution_bitcast_fusion.1, f32[8,128,128]{2,1,0:T(8,128)S(1)} %copy-done), kind=kOutput, calls=%fused_computation.44 | convolution fusion | flops 100663296 | bytes 1048576 | tf_op jit(solution)/shard_map/...tik,tlk->...til/dot_general | solution.py:36
  16.4 1.7 %concatenate.14 = f32[5,9,16,128]{3,2,1,0:T(8,128)} pad(f32[5,8,16,128]{3,2,1,0:T(8,128)} %collective-permute-done, f32[]{:T(128)} %constant.19.clone.1), padding=0_0x0_1x0_0x0_0 | pad | bytes 696324 | tf_op jit(solution)/shard_map/concatenate | solution.py:125
  18.2 2.3 %gather_fusion = f32[8,5,16,128]{3,2,1,0:T(8,128)} fusion(f32[5,9,16,128]{3,2,1,0:T(8,128)} %concatenate.14, s32[1024]{0:T(1024)S(1)} %pad_clamp_fusion.1), kind=kCustom, calls=%fused_computation.clone | custom fusion | bytes 655392 | tf_op jit(solution)/shard_map/jit(_take)/gather | solution.py:133
  20.5 1.7 %concatenate.15 = f32[5,9,16,128]{3,2,1,0:T(8,128)} pad(f32[5,8,16,128]{3,2,1,0:T(8,128)} %collective-permute-done.1, f32[]{:T(128)} %constant.19.clone.1), padding=0_0x0_1x0_0x0_0 | pad | bytes 696324 | tf_op jit(solution)/shard_map/concatenate | solution.py:126
  22.2 2.3 %gather_fusion.1 = f32[8,5,16,128]{3,2,1,0:T(8,128)} fusion(f32[5,9,16,128]{3,2,1,0:T(8,128)} %concatenate.15, s32[1024]{0:T(1024)S(1)} %pad_clamp_fusion), kind=kCustom, calls=%fused_computation.1.clone | custom fusion | bytes 655392 | tf_op jit(solution)/shard_map/jit(_take)/gather | solution.py:134
  24.5 1.2 %fusion.3 = (f32[5,8,16,128]{3,2,1,0:T(8,128)S(1)}, f32[5,8,16,128]{3,2,1,0:T(8,128)S(1)}) fusion(f32[8,5,16,128]{3,2,1,0:T(8,128)} %gather_fusion.1, pred[8]{0:T(512)(128)(4,1)S(1)} %get-tuple-element.3, f32[8,5,16,128]{3,2,1,0:T(8,128)} %gather_fusion, pred[8]{0:T(512)(128)(4,1)S(1)} %get-tuple-element.9), kind=kLoop, calls=%fused_computation.18 | loop fusion | flops 163840 | bytes 1310736 | tf_op jit(solution)/shard_map/jit(_take)/select_n | solution.py:134
  25.7 19.5 %shard_map.95 = f32[8,128,128]{2,1,0:T(8,128)S(1)} custom-call(s32[8]{0:T(128)S(1)} %get-tuple-element.14.south_ref, s32[8]{0:T(128)S(1)} %get-tuple-element.13.north_ref, s32[8]{0:T(128)S(1)} %get-tuple-element.12.south_ok_ref, s32[8]{0:T(128)S(1)} %get-tuple-element.11.north_ok_ref, f32[12]{0:T(128)S(1)} %copy-done.2, f32[8,128,128]{2,1,0:T(8,128)S(1)} %bitcast.73, ...), custom_call_target="tpu_custom_call" | custom-call | tf_op jit(solution)/shard_map/pallas_call | solution.py:94
  45.7 1.9 %collective-permute-start.2 = (f32[1,8,64,128]{3,2,1,0:T(8,128)S(1)}, f32[1,8,64,128]{3,2,1,0:T(8,128)S(1)}, u32[]{:S(2)}, u32[]{:S(2)}) collective-permute-start(f32[1,8,64,128]{3,2,1,0:T(8,128)S(1)} %add_multiply_fusion), channel_id=1, source_target_pairs={{0,4},{4,8},{8,12},{12,16},{16,20},{20,24},{24,28},{1,5},{5,9},{9,... | collective-permute-start | bytes 786440 | tf_op jit(solution)/shard_map/ppermute | solution.py:23
  47.7 6.7 %collective-permute-done.2 = f32[1,8,64,128]{3,2,1,0:T(8,128)S(1)} collective-permute-done((f32[1,8,64,128]{3,2,1,0:T(8,128)S(1)}, f32[1,8,64,128]{3,2,1,0:T(8,128)S(1)}, u32[]{:S(2)}, u32[]{:S(2)}) %collective-permute-start.2) | collective-permute-done | bytes 262176 | tf_op jit(solution)/shard_map/ppermute | solution.py:23
  54.4 1.9 %collective-permute-start.3 = (f32[8,64,128]{2,1,0:T(8,128)S(1)}, f32[8,64,128]{2,1,0:T(8,128)S(1)}, u32[]{:S(2)}, u32[]{:S(2)}) collective-permute-start(f32[8,64,128]{2,1,0:T(8,128)S(1)} %select_bitcast_fusion.1), channel_id=1, source_target_pairs={{0,4},{4,8},{8,12},{12,16},{16,20},{20,24},{24,28},{1,5},{5,9},{9,... | collective-permute-start | bytes 786440 | tf_op jit(solution)/shard_map/ppermute | solution.py:23
  57.1 5.9 %collective-permute-done.3 = f32[8,64,128]{2,1,0:T(8,128)S(1)} collective-permute-done((f32[8,64,128]{2,1,0:T(8,128)S(1)}, f32[8,64,128]{2,1,0:T(8,128)S(1)}, u32[]{:S(2)}, u32[]{:S(2)}) %collective-permute-start.3) | collective-permute-done | bytes 262176 | tf_op jit(solution)/shard_map/ppermute | solution.py:23
  63.4 1.1 %fusion = f32[8,64,128]{2,1,0:T(8,128)S(1)} fusion(f32[8,64,128]{2,1,0:T(8,128)S(1)} %select_bitcast_fusion.1, f32[8,128,64]{1,2,0:T(8,128)S(1)} %fusion.14, f32[8,128,128]{2,1,0:T(8,128)S(1)} %copy-done, pred[]{:T(512)S(6)} %ge.13), kind=kOutput, calls=%fused_computation.8 | convolution fusion | flops 100794368 | bytes 1310721 | tf_op jit(solution)/shard_map/...tik,tlk->...til/dot_general | solution.py:36
  64.5 1.9 %collective-permute-start.4 = (f32[8,64,128]{2,1,0:T(8,128)S(1)}, f32[8,64,128]{2,1,0:T(8,128)S(1)}, u32[]{:S(2)}, u32[]{:S(2)}) collective-permute-start(f32[8,64,128]{2,1,0:T(8,128)S(1)} %fusion), channel_id=1, source_target_pairs={{0,8},{4,12},{8,16},{12,20},{16,24},{20,28},{1,9},{5,13},{9,17},{1... | collective-permute-start | bytes 786440 | tf_op jit(solution)/shard_map/ppermute | solution.py:23
  66.4 0.6 fusion.17
  67.0 6.6 %collective-permute-done.4 = f32[8,64,128]{2,1,0:T(8,128)S(1)} collective-permute-done((f32[8,64,128]{2,1,0:T(8,128)S(1)}, f32[8,64,128]{2,1,0:T(8,128)S(1)}, u32[]{:S(2)}, u32[]{:S(2)}) %collective-permute-start.4) | collective-permute-done | bytes 262176 | tf_op jit(solution)/shard_map/ppermute | solution.py:23
  74.1 1.1 %fusion.1 = f32[8,64,128]{2,1,0:T(8,128)S(1)} fusion(f32[8,64,128]{2,1,0:T(8,128)S(1)} %fusion, f32[8,64,128]{2,1,0:T(8,128)S(1)} %fusion.16, f32[8,128,128]{2,1,0:T(8,128)S(1)} %fusion.17, pred[]{:T(512)S(6)} %ge.14), kind=kOutput, calls=%fused_computation.9 | convolution fusion | flops 100794368 | bytes 1310721 | tf_op jit(solution)/shard_map/...tik,tlk->...til/dot_general | solution.py:36
  75.2 1.3 %collective-permute-start.5 = (f32[8,64,128]{2,1,0:T(8,128)S(1)}, f32[8,64,128]{2,1,0:T(8,128)S(1)}, u32[]{:S(2)}, u32[]{:S(2)}) collective-permute-start(f32[8,64,128]{2,1,0:T(8,128)S(1)} %fusion.1), channel_id=1, source_target_pairs={{0,16},{4,20},{8,24},{12,28},{1,17},{5,21},{9,25},{13,29},{2,18},{... | collective-permute-start | bytes 786440 | tf_op jit(solution)/shard_map/ppermute | solution.py:23
  76.5 0.6 fusion.20
  77.1 6.3 %collective-permute-done.5 = f32[8,64,128]{2,1,0:T(8,128)S(1)} collective-permute-done((f32[8,64,128]{2,1,0:T(8,128)S(1)}, f32[8,64,128]{2,1,0:T(8,128)S(1)}, u32[]{:S(2)}, u32[]{:S(2)}) %collective-permute-start.5) | collective-permute-done | bytes 262176 | tf_op jit(solution)/shard_map/ppermute | solution.py:23
  83.8 1.1 %fusion.2 = f32[8,64,128]{2,1,0:T(8,128)S(1)} fusion(f32[8,64,128]{2,1,0:T(8,128)S(1)} %fusion.1, f32[8,64,128]{2,1,0:T(8,128)S(1)} %fusion.19, f32[8,128,128]{2,1,0:T(8,128)S(1)} %fusion.20, pred[]{:T(512)S(6)} %ge.15), kind=kOutput, calls=%fused_computation.10 | convolution fusion | flops 100794368 | bytes 1310721 | tf_op jit(solution)/shard_map/...tik,tlk->...til/dot_general | solution.py:36
  85.4 1.1 %fusion.21 = f32[8,64,128]{2,1,0:T(8,128)S(1)} fusion(f32[8,64,128]{2,1,0:T(8,128)S(1)} %convolution_bitcast_fusion, f32[8,128,128]{2,1,0:T(8,128)S(1)} %copy-done), kind=kOutput, calls=%fused_computation.52 | convolution fusion | flops 100663296 | bytes 1048576 | tf_op jit(solution)/shard_map/...tik,tlk->...til/dot_general | solution.py:36
  86.7 1.9 %collective-permute-start.6 = (f32[8,128,128]{2,1,0:T(8,128)S(1)}, f32[8,128,128]{2,1,0:T(8,128)S(1)}, u32[]{:S(2)}, u32[]{:S(2)}) collective-permute-start(f32[8,128,128]{2,1,0:T(8,128)S(1)} %add.39), channel_id=1, source_target_pairs={{0,4},{4,8},{8,12},{12,16},{16,20},{20,24},{24,28},{1,5},{5,9},{9,... | collective-permute-start | bytes 1572872 | tf_op jit(solution)/shard_map/ppermute | solution.py:23
  88.7 9.5 %collective-permute-done.6 = f32[8,128,128]{2,1,0:T(8,128)S(1)} collective-permute-done((f32[8,128,128]{2,1,0:T(8,128)S(1)}, f32[8,128,128]{2,1,0:T(8,128)S(1)}, u32[]{:S(2)}, u32[]{:S(2)}) %collective-permute-start.6) | collective-permute-done | bytes 524320 | tf_op jit(solution)/shard_map/ppermute | solution.py:23
  98.1 0.9 select_bitcast_fusion
  (43 shorter events, 3.7 us)
Async XLA Ops:
  0.6 13.9 %copy-start = (f32[8,128,128]{2,1,0:T(8,128)S(1)}, f32[8,128,128]{2,1,0:T(8,128)}, u32[]{:S(2)}) copy-start(f32[8,128,128]{2,1,0:T(8,128)} %param.17) | copy-start | bytes 1572868
  0.6 9.8 %copy-start.7 = (f32[8,128,128]{2,1,0:T(8,128)S(1)}, f32[8,128,128]{2,1,0:T(8,128)}, u32[]{:S(2)}) copy-start(f32[8,128,128]{2,1,0:T(8,128)} %param.11) | copy-start | bytes 1572868
  0.7 9.8 %copy-start.4 = (f32[2,8,128,128]{3,2,1,0:T(8,128)S(1)}, f32[2,8,128,128]{3,2,1,0:T(8,128)}, u32[]{:S(2)}) copy-start(f32[2,8,128,128]{3,2,1,0:T(8,128)} %param.12) | copy-start | bytes 3145732
  3.9 12.6 %collective-permute-start = (f32[5,8,16,128]{3,2,1,0:T(8,128)}, f32[5,8,16,128]{3,2,1,0:T(8,128)}, u32[]{:S(2)}, u32[]{:S(2)}) collective-permute-start(f32[5,8,16,128]{3,2,1,0:T(8,128)} %get-tuple-element.8), channel_id=1, source_target_pairs={{0,1},{1,2},{2,3},{4,5},{5,6},{6,7},{8,9},{9,10},{10,11},{12,13},{... | collective-permute-start | bytes 983048 | tf_op jit(solution)/shard_map/ppermute | solution.py:122
  7.3 13.1 %collective-permute-start.1 = (f32[5,8,16,128]{3,2,1,0:T(8,128)}, f32[5,8,16,128]{3,2,1,0:T(8,128)}, u32[]{:S(2)}, u32[]{:S(2)}) collective-permute-start(f32[5,8,16,128]{3,2,1,0:T(8,128)} %get-tuple-element.7), channel_id=1, source_target_pairs={{1,0},{2,1},{3,2},{5,4},{6,5},{7,6},{9,8},{10,9},{11,10},{13,12},{... | collective-permute-start | bytes 983048 | tf_op jit(solution)/shard_map/ppermute | solution.py:123
  10.5 0.7 copy-start.10
  10.5 1.0 %copy-start.1 = (f32[1,8,128,128]{3,2,1,0:T(8,128)S(1)}, f32[1,8,128,128]{3,2,1,0:T(8,128)}, u32[]{:S(2)}) copy-start(f32[1,8,128,128]{3,2,1,0:T(8,128)} %param.10) | copy-start | bytes 1572868
  10.5 2.6 %copy-start.3 = (f32[8,64,64]{2,1,0:T(8,128)S(1)}, f32[8,64,64]{2,1,0:T(8,128)}, u32[]{:S(2)}) copy-start(f32[8,64,64]{2,1,0:T(8,128)} %param.16) | copy-start | bytes 393220
  16.4 9.3 %copy-start.2 = (f32[12]{0:T(128)S(1)}, f32[12]{0:T(128)}, u32[]{:S(2)}) copy-start(f32[12]{0:T(128)} %scale_ref.1) | copy-start | bytes 148
  25.7 19.5 %copy-start.8 = (f32[8,64,128]{2,1,0:T(8,128)S(1)}, f32[8,64,128]{2,1,0:T(8,128)}, u32[]{:S(2)}) copy-start(f32[8,64,128]{2,1,0:T(8,128)} %fusion.13) | copy-start | bytes 786436
  45.2 9.1 %copy-start.5 = (f32[1,8,64,128]{3,2,1,0:T(8,128)S(1)}, f32[1,8,64,128]{3,2,1,0:T(8,128)}, u32[]{:S(2)}) copy-start(f32[1,8,64,128]{3,2,1,0:T(8,128)} %slice.42) | copy-start | bytes 786436
  45.2 9.1 %copy-start.6 = (f32[1,8,64,128]{3,2,1,0:T(8,128)S(1)}, f32[1,8,64,128]{3,2,1,0:T(8,128)}, u32[]{:S(2)}) copy-start(f32[1,8,64,128]{3,2,1,0:T(8,128)} %slice.43) | copy-start | bytes 786436
  45.7 8.6 %collective-permute-start.2 = (f32[1,8,64,128]{3,2,1,0:T(8,128)S(1)}, f32[1,8,64,128]{3,2,1,0:T(8,128)S(1)}, u32[]{:S(2)}, u32[]{:S(2)}) collective-permute-start(f32[1,8,64,128]{3,2,1,0:T(8,128)S(1)} %add_multiply_fusion), channel_id=1, source_target_pairs={{0,4},{4,8},{8,12},{12,16},{16,20},{20,24},{24,28},{1,5},{5,9},{9,... | collective-permute-start | bytes 786440 | tf_op jit(solution)/shard_map/ppermute | solution.py:23
  54.4 8.6 %collective-permute-start.3 = (f32[8,64,128]{2,1,0:T(8,128)S(1)}, f32[8,64,128]{2,1,0:T(8,128)S(1)}, u32[]{:S(2)}, u32[]{:S(2)}) collective-permute-start(f32[8,64,128]{2,1,0:T(8,128)S(1)} %select_bitcast_fusion.1), channel_id=1, source_target_pairs={{0,4},{4,8},{8,12},{12,16},{16,20},{20,24},{24,28},{1,5},{5,9},{9,... | collective-permute-start | bytes 786440 | tf_op jit(solution)/shard_map/ppermute | solution.py:23
  64.5 9.2 %collective-permute-start.4 = (f32[8,64,128]{2,1,0:T(8,128)S(1)}, f32[8,64,128]{2,1,0:T(8,128)S(1)}, u32[]{:S(2)}, u32[]{:S(2)}) collective-permute-start(f32[8,64,128]{2,1,0:T(8,128)S(1)} %fusion), channel_id=1, source_target_pairs={{0,8},{4,12},{8,16},{12,20},{16,24},{20,28},{1,9},{5,13},{9,17},{1... | collective-permute-start | bytes 786440 | tf_op jit(solution)/shard_map/ppermute | solution.py:23
  75.2 8.3 %collective-permute-start.5 = (f32[8,64,128]{2,1,0:T(8,128)S(1)}, f32[8,64,128]{2,1,0:T(8,128)S(1)}, u32[]{:S(2)}, u32[]{:S(2)}) collective-permute-start(f32[8,64,128]{2,1,0:T(8,128)S(1)} %fusion.1), channel_id=1, source_target_pairs={{0,16},{4,20},{8,24},{12,28},{1,17},{5,21},{9,25},{13,29},{2,18},{... | collective-permute-start | bytes 786440 | tf_op jit(solution)/shard_map/ppermute | solution.py:23
  86.7 12.3 %copy-start.9 = (f32[8,128,128]{2,1,0:T(8,128)}, f32[8,128,128]{2,1,0:T(8,128)S(1)}, u32[]{:S(2)}) copy-start(f32[8,128,128]{2,1,0:T(8,128)S(1)} %add.39) | copy-start | bytes 1572868
  86.7 11.4 %collective-permute-start.6 = (f32[8,128,128]{2,1,0:T(8,128)S(1)}, f32[8,128,128]{2,1,0:T(8,128)S(1)}, u32[]{:S(2)}, u32[]{:S(2)}) collective-permute-start(f32[8,128,128]{2,1,0:T(8,128)S(1)} %add.39), channel_id=1, source_target_pairs={{0,4},{4,8},{8,12},{12,16},{16,20},{20,24},{24,28},{1,5},{5,9},{9,... | collective-permute-start | bytes 1572872 | tf_op jit(solution)/shard_map/ppermute | solution.py:23

commit v3 on v1

--- a/solution.py
+++ b/solution.py
@@ -1,3 +1,5 @@
+import functools
+
 import jax
 import jax.numpy as jnp
 from jax import lax
@@ -36,19 +38,32 @@
     return jnp.einsum("...tik,tlk->...til", mixed_x, matrix_y, precision=exact_precision)
 
 
-def fine_kernel(south_ref, north_ref, south_ok_ref, north_ok_ref, scale_ref,
-                u_ref, fields_ref, west_ref, east_ref, out_ref, state_ref, field_ref):
+def fine_kernel(slice_at, south_ref, north_ref, south_ok_ref, north_ok_ref, west_at_ref, east_at_ref,
+                west_ok_ref, east_ok_ref, scale_ref, u_ref, fields_ref, prev_ref, next_ref,
+                out_ref, state_ref, field_ref):
     tiles = u_ref.shape[0]
     rows = u_ref.shape[1]
     total = rows + 2 * HALO
+    layers = prev_ref.shape[0]
     for i in range(tiles):
-        state_ref[0, i, pl.ds(0, HALO), :] = west_ref[0, i]
+        west_at = west_at_ref[i]
+        east_at = east_at_ref[i]
+        west_ok = west_ok_ref[i] > 0
+        east_ok = east_ok_ref[i] > 0
+        state_ref[0, i, pl.ds(0, HALO), :] = jnp.where(west_ok, prev_ref[slice_at, west_at], 0.0)
         state_ref[0, i, pl.ds(HALO, rows), :] = u_ref[i]
-        state_ref[0, i, pl.ds(HALO + rows, HALO), :] = east_ref[0, i]
+        state_ref[0, i, pl.ds(HALO + rows, HALO), :] = jnp.where(
+            east_ok, next_ref[slice_at, east_at], 0.0
+        )
         for f in range(4):
-            field_ref[f, i, pl.ds(0, HALO), :] = west_ref[f + 1, i]
+            field_at = layers - 4 + f
+            field_ref[f, i, pl.ds(0, HALO), :] = jnp.where(
+                west_ok, prev_ref[field_at, west_at], 0.0
+            )
             field_ref[f, i, pl.ds(HALO, rows), :] = fields_ref[f, i]
-            field_ref[f, i, pl.ds(HALO + rows, HALO), :] = east_ref[f + 1, i]
+            field_ref[f, i, pl.ds(HALO + rows, HALO), :] = jnp.where(
+                east_ok, next_ref[field_at, east_at], 0.0
+            )
 
     lanes = u_ref.shape[2]
     lane = lax.broadcasted_iota(jnp.int32, (total, lanes), 1)
@@ -86,22 +101,22 @@
         out_ref[i] = state_ref[last, i, pl.ds(HALO, rows), :]
 
 
-def fine_propagate(u, fields, west, east, south, north, south_ok, north_ok, scale):
+def fine_propagate(slice_at, u, fields, from_prev, from_next, indices, scale):
     tiles, rows, lanes = u.shape
     total = rows + 2 * HALO
     vmem = pltpu.MemorySpace.VMEM
     smem = pltpu.MemorySpace.SMEM
     return pl.pallas_call(
-        fine_kernel,
+        functools.partial(fine_kernel, slice_at),
         out_shape=jax.ShapeDtypeStruct(u.shape, u.dtype),
-        in_specs=[pl.BlockSpec(memory_space=smem)] * 5 + [pl.BlockSpec(memory_space=vmem)] * 4,
+        in_specs=[pl.BlockSpec(memory_space=smem)] * 9 + [pl.BlockSpec(memory_space=vmem)] * 4,
         out_specs=pl.BlockSpec(memory_space=vmem),
         scratch_shapes=[
             pltpu.VMEM((2, tiles, total, lanes), jnp.float32),
             pltpu.VMEM((4, tiles, total, lanes), jnp.float32),
         ],
         compiler_params=pltpu.CompilerParams(vmem_limit_bytes=48 * 1024 * 1024),
-    )(south, north, south_ok, north_ok, scale, u, fields, west, east)
+    )(*indices, scale, u, fields, from_prev, from_next)
 
 
 def on_device(
@@ -121,17 +136,12 @@
     backward = [(i + 1, i) for i in range(space_count - 1)]
     from_prev = lax.ppermute(layers[:, :, rows - HALO:, :], "space", forward)
     from_next = lax.ppermute(layers[:, :, :HALO, :], "space", backward)
-    zero_tile = jnp.zeros_like(from_prev[:, :1])
-    from_prev = jnp.concatenate([from_prev, zero_tile], axis=1)
-    from_next = jnp.concatenate([from_next, zero_tile], axis=1)
     west_nb = neighbors[:, 0]
     east_nb = neighbors[:, 1]
-    west_index = jnp.where(west_nb == all_tiles, tile_count, west_nb - (block_base - tile_count))
-    east_index = jnp.where(east_nb == all_tiles, tile_count, east_nb - (block_base + tile_count))
-    west_index = jnp.clip(west_index, 0, tile_count)
-    east_index = jnp.clip(east_index, 0, tile_count)
-    west = jnp.take(from_prev, west_index, axis=1)
-    east = jnp.take(from_next, east_index, axis=1)
+    west_ok = (west_nb != all_tiles).astype(jnp.int32)
+    east_ok = (east_nb != all_tiles).astype(jnp.int32)
+    west_at = jnp.clip(west_nb - (block_base - tile_count), 0, tile_count - 1) * west_ok
+    east_at = jnp.clip(east_nb - (block_base + tile_count), 0, tile_count - 1) * east_ok
 
     south_nb = neighbors[:, 2]
     north_nb = neighbors[:, 3]
@@ -139,37 +149,60 @@
     north_ok = (north_nb != all_tiles).astype(jnp.int32)
     south = jnp.clip(south_nb - block_base, 0, tile_count - 1) * south_ok
     north = jnp.clip(north_nb - block_base, 0, tile_count - 1) * north_ok
+    indices = (south, north, south_ok, north_ok, west_at, east_at, west_ok, east_ok)
 
     fine_ends = jnp.stack(
         [
-            fine_propagate(
-                starts[n],
-                fields,
-                jnp.concatenate([west[n : n + 1], west[slice_count:]], axis=0),
-                jnp.concatenate([east[n : n + 1], east[slice_count:]], axis=0),
-                south,
-                north,
-                south_ok,
-                north_ok,
-                substep_scale,
-            )
+            fine_propagate(n, starts[n], fields, from_prev, from_next, indices, substep_scale)
             for n in range(slice_count)
         ],
         axis=0,
     )
     correction = fine_ends - prolong(apply_coarse(restrict(starts), coarse_x, coarse_y))
     coarse_jump = restrict(correction)
-    first_coarse = spread(restrict(starts[0]), "tm", 0)
-    every_jump = lax.all_gather(coarse_jump, "tm", axis=0, tiled=True)
-
-    def sweep(state_now, jump):
-        return (apply_coarse(state_now, coarse_x, coarse_y) + jump, state_now)
-
-    last_state, history = lax.scan(sweep, first_coarse, every_jump)
-    own_coarse = lax.dynamic_slice_in_dim(
-        history, lax.axis_index("tm") * slice_count, slice_count, 0
-    )
-    slice_ends = prolong(apply_coarse(own_coarse, coarse_x, coarse_y)) + correction
+    tm_index = lax.axis_index("tm")
+    tm_count = lax.axis_size("tm")
+    first_coarse = restrict(starts[0])
+
+    def prefix_over_tm(total, power_x, power_y):
+        distance = 1
+        while distance < tm_count:
+            received = passed_along(total, "tm", distance)
+            total = total + jnp.where(
+                tm_index >= distance, apply_coarse(received, power_x, power_y), 0.0
+            )
+            distance *= 2
+            if distance < tm_count:
+                power_x = jnp.einsum("tij,tjk->tik", power_x, power_x, precision=exact_precision)
+                power_y = jnp.einsum("tij,tjk->tik", power_y, power_y, precision=exact_precision)
+        return total
+
+    if slice_count == 1:
+        seed = jnp.where(tm_index == 0, apply_coarse(first_coarse, coarse_x, coarse_y), 0.0)
+        reached = prefix_over_tm(coarse_jump[0] + seed, coarse_x, coarse_y)
+        coarse_applied = (reached - coarse_jump[0])[None]
+    else:
+        shifted_jump = jnp.concatenate(
+            [passed_along(coarse_jump[-1:], "tm", 1), coarse_jump[:-1]], axis=0
+        )
+        head = jnp.where(tm_index == 0, first_coarse[None], shifted_jump[:1])
+        local = jnp.concatenate([head, shifted_jump[1:]], axis=0)
+        states = [local[0]]
+        for n in range(1, slice_count):
+            states.append(apply_coarse(states[-1], coarse_x, coarse_y) + local[n])
+        power_x = coarse_x
+        power_y = coarse_y
+        for n in range(1, slice_count):
+            power_x = jnp.einsum("tij,tjk->tik", power_x, coarse_x, precision=exact_precision)
+            power_y = jnp.einsum("tij,tjk->tik", power_y, coarse_y, precision=exact_precision)
+        total = prefix_over_tm(states[-1], power_x, power_y)
+        earlier = jnp.where(tm_index > 0, passed_along(total, "tm", 1), 0.0)
+        own_coarse = []
+        for n in range(slice_count):
+            earlier = apply_coarse(earlier, coarse_x, coarse_y)
+            own_coarse.append(states[n] + earlier)
+        coarse_applied = apply_coarse(jnp.stack(own_coarse, axis=0), coarse_x, coarse_y)
+    slice_ends = prolong(coarse_applied) + correction
     previous = passed_along(slice_ends[-1], "tm", 1)
     first_step = jnp.where(
         lax.axis_index("tm") == 0, jnp.zeros_like(previous), previous - starts[0]

time: 165 us -> 84.5 us (0.51)
  matrix products: 38.5 us -> 12.1 us
  local copies, waits for them, and re-layouts: 25.9 us -> 2.83 us
  waiting for transfers between devices: 50.9 us -> 28.9 us
  between operations: 14.4 us -> 1.02 us
  starting transfers between devices: 8.04 us -> 13.5 us
    all_gather x1 -> x0, waiting for transfers between devices: 30.2 us -> none  [on_device(): every_jump = lax.all_gather(coarse_jump, 'tm', axis=0, tiled=True)]
    dot_general x10 -> x5, matrix products: 25.2 us -> 6.31 us  [apply_coarse(): jnp.einsum('...tik,tlk->...til', mixed_x, matrix_y, precision=exact_preci...]
    ppermute x1 -> x4, waiting for transfers between devices: 9.26 us -> 27.8 us  [passed_along(): return lax.ppermute(block, axis, route)]
    dynamic_update_slice x8 -> x0, local copies, waits for them, and re-layouts: 13.4 us -> none  [on_device(): last_state, history = lax.scan(sweep, first_coarse, every_jump)]
    psum x1 -> x0, waiting for transfers between devices: 11.4 us -> none  [spread(): return lax.psum(kept, axis)]
    dot_general x10 -> x5, matrix products: 13.3 us -> 3.74 us  [apply_coarse(): jnp.einsum('tij,...tjk->...tik', matrix_x, coarse_values, precision=exact...]
    ppermute x1 -> x4, starting transfers between devices: 2.13 us -> 7.64 us  [passed_along(): return lax.ppermute(block, axis, route)]
    gather x2 -> x0, local copies, waits for them, and re-layouts: 4.54 us -> none  [the longest x1 2.28 us: on_device(): east = jnp.take(from_next, east_index, axis=1)]
  transfers between devices with their start and end apart: 5 -> 6, of which waited for: 3 -> 5; matrix products, arithmetic and copies ran while one was open for 11% -> 12% of each run, Pallas kernels for 12% -> 0%
where the time goes in v3:
time: 84.5 us; the launch traced here: 84.1 us
  waiting for transfers between devices  28.9 us (34%)
  Pallas kernels  19.9 us (24%)
  starting transfers between devices  13.5 us (16%)
  matrix products  12.1 us (14%)
  other arithmetic  5.88 us (7%)
  local copies, waits for them, and re-layouts  2.83 us (3%)
  between operations  1.02 us (1%)
    ppermute x4, waiting for transfers between devices, passed_along(): return lax.ppermute(block, axis, route)  27.8 us
    pallas_call x1, Pallas kernels, fine_propagate(): pl.pallas_call(functools.partial(fine_kernel, slice_at), out_shape=jax.Sh...  19.9 us
    ppermute x4, starting transfers between devices, passed_along(): return lax.ppermute(block, axis, route)  7.64 us
    dot_general x5, matrix products, apply_coarse(): jnp.einsum('...tik,tlk->...til', mixed_x, matrix_y, precision=exact_preci...  6.31 us
    dot_general x5, matrix products, apply_coarse(): jnp.einsum('tij,...tjk->...tik', matrix_x, coarse_values, precision=exact...  3.74 us
    ppermute x1, starting transfers between devices, on_device(): from_prev = lax.ppermute(layers[:, :, rows - HALO:, :], 'space', forward)  3.47 us
    another operation x2, other arithmetic, on_device(): jnp.stack([diffusivity, velocity[0], velocity[1], open_cells], axis=0)  2.68 us
    ppermute x1, starting transfers between devices, on_device(): from_next = lax.ppermute(layers[:, :, :HALO, :], 'space', backward)  2.38 us
  transfers between devices with their start and end apart: 6, of which 5 were waited for; matrix products, arithmetic and copies ran while one was open for 12% of the time, Pallas kernels for 0%

profile of v3, /device:TPU:12, one launch (start us, length us, event | category | flops | bytes accessed | tf_op | source)
XLA Modules:
  0.0 84.1 jit_solution(6290274347308836880)
XLA Ops:
  0.7 1.2 %subtract_bitcast_fusion = f32[1,8,128,128]{3,2,1,0:T(8,128)S(1)} fusion(s32[8,128,128]{2,1,0:T(8,128)} %param.11), kind=kLoop, calls=%fused_computation.12 | loop fusion | flops 262144 | bytes 1048576 | tf_op jit(solution)/shard_map/stack | solution.py:132
  1.9 2.2 %pad_maximum_fusion.1 = (f32[5,8,16,128]{3,2,1,0:T(8,128)}, f32[5,8,16,128]{3,2,1,0:T(8,128)}) fusion(f32[1,8,128,128]{3,2,1,0:T(8,128)S(1)} %subtract_bitcast_fusion, f32[2,8,128,128]{3,2,1,0:T(8,128)} %param.10, f32[1,8,128,128]{3,2,1,0:T(8,128)} %bitcast.72, f32[1,8,128,128]{3,2,1,0:T(8,128)} %param.8), kind=kLoop, calls=%fused_computation.13 | loop fusion | flops 491520 | bytes 3276800 | tf_op jit(solution)/shard_map/concatenate | solution.py:133
  4.1 3.5 %collective-permute-start = (f32[5,8,16,128]{3,2,1,0:T(8,128)}, f32[5,8,16,128]{3,2,1,0:T(8,128)S(1)}, u32[]{:S(2)}, u32[]{:S(2)}) collective-permute-start(f32[5,8,16,128]{3,2,1,0:T(8,128)} %get-tuple-element.3), channel_id=1, source_target_pairs={{0,1},{1,2},{2,3},{4,5},{5,6},{6,7},{8,9},{9,10},{10,11},{12,13},{... | collective-permute-start | bytes 983048 | tf_op jit(solution)/shard_map/ppermute | solution.py:137
  7.5 2.4 %collective-permute-start.1 = (f32[5,8,16,128]{3,2,1,0:T(8,128)}, f32[5,8,16,128]{3,2,1,0:T(8,128)}, u32[]{:S(2)}, u32[]{:S(2)}) collective-permute-start(f32[5,8,16,128]{3,2,1,0:T(8,128)} %get-tuple-element.2), channel_id=1, source_target_pairs={{1,0},{2,1},{3,2},{5,4},{6,5},{7,6},{9,8},{10,9},{11,10},{13,12},{... | collective-permute-start | bytes 983048 | tf_op jit(solution)/shard_map/ppermute | solution.py:138
  10.2 0.4 convolution_bitcast_fusion
  10.7 1.8 %fusion.23 = f32[8,64,128]{2,1,0:T(8,128)} fusion(f32[8,64,128]{2,1,0:T(8,128)S(1)} %convolution_bitcast_fusion, f32[8,128,128]{2,1,0:T(8,128)S(1)} %copy-done), kind=kOutput, calls=%fused_computation.44 | convolution fusion | flops 100663296 | bytes 1048576 | tf_op jit(solution)/shard_map/...tik,tlk->...til/dot_general | solution.py:38
  12.5 1.5 %pad_maximum_fusion.fields_ref = f32[4,8,128,128]{3,2,1,0:T(8,128)S(1)} fusion(f32[1,8,128,128]{3,2,1,0:T(8,128)S(1)} %copy-done.6, f32[2,8,128,128]{3,2,1,0:T(8,128)} %param.10, f32[1,8,128,128]{3,2,1,0:T(8,128)} %bitcast.73), kind=kLoop, calls=%fused_computation | loop fusion | flops 1048576 | bytes 4194304 | tf_op jit(solution)/shard_map/stack | solution.py:132
  14.0 0.8 slice.50
  14.8 0.8 slice.51
  15.5 2.2 %fusion.6 = f32[8,128,64]{1,2,0:T(8,128)} fusion(f32[8,64,64]{2,1,0:T(8,128)} %param.14, f32[8,64,128]{2,1,0:T(8,128)} %slice.50, f32[8,64,128]{2,1,0:T(8,128)} %slice.51), kind=kOutput, calls=%fused_computation.18 | convolution fusion | flops 50462720 | bytes 917504 | tf_op jit(solution)/shard_map/tij,...tjk->...tik/dot_general | solution.py:37
  17.7 1.2 %collective-permute-done.1.next_ref = f32[5,8,16,128]{3,2,1,0:T(8,128)} collective-permute-done((f32[5,8,16,128]{3,2,1,0:T(8,128)}, f32[5,8,16,128]{3,2,1,0:T(8,128)}, u32[]{:S(2)}, u32[]{:S(2)}) %collective-permute-start.1) | collective-permute-done | bytes 327712 | tf_op jit(solution)/shard_map/ppermute | solution.py:138
  18.9 19.9 %shard_map.95 = f32[8,128,128]{2,1,0:T(8,128)S(1)} custom-call(s32[8]{0:T(128)S(1)} %get-tuple-element.10.south_ref, s32[8]{0:T(128)S(1)} %get-tuple-element.9.north_ref, s32[8]{0:T(128)S(1)} %get-tuple-element.5.south_ok_ref, s32[8]{0:T(128)S(1)} %get-tuple-element.6.north_ok_ref, s32[8]{0:T(128)S(1)} %get-tuple-element.11.west_at_ref, ...), custom_call_target="tpu_custom_call" | custom-call | tf_op jit(solution)/shard_map/pallas_call | solution.py:109
  39.4 0.4 copy-done.8
  39.8 1.1 %fusion = f32[8,64,128]{2,1,0:T(8,128)S(1)} fusion(f32[8,128,64]{1,2,0:T(8,128)S(1)} %copy-done.8, f32[8,128,128]{2,1,0:T(8,128)S(1)} %copy-done, pred[]{:T(512)S(6)} %eq.4, f32[1,8,64,128]{3,2,1,0:T(8,128)S(1)} %slice.48, f32[1,8,64,128]{3,2,1,0:T(8,128)S(1)} %slice.49), kind=kOutput, calls=%fused_computation.6 | convolution fusion | flops 100925440 | bytes 1572865 | tf_op jit(solution)/shard_map/...tik,tlk->...til/dot_general | solution.py:38
  40.9 1.9 %collective-permute-start.2 = (f32[8,64,128]{2,1,0:T(8,128)S(1)}, f32[8,64,128]{2,1,0:T(8,128)S(1)}, u32[]{:S(2)}, u32[]{:S(2)}) collective-permute-start(f32[8,64,128]{2,1,0:T(8,128)S(1)} %fusion), channel_id=1, source_target_pairs={{0,4},{4,8},{8,12},{12,16},{16,20},{20,24},{24,28},{1,5},{5,9},{9,... | collective-permute-start | bytes 786440 | tf_op jit(solution)/shard_map/ppermute | solution.py:25
  42.9 0.4 fusion.25
  43.3 0.4 fusion.28
  43.6 5.9 %collective-permute-done.2 = f32[8,64,128]{2,1,0:T(8,128)S(1)} collective-permute-done((f32[8,64,128]{2,1,0:T(8,128)S(1)}, f32[8,64,128]{2,1,0:T(8,128)S(1)}, u32[]{:S(2)}, u32[]{:S(2)}) %collective-permute-start.2) | collective-permute-done | bytes 262176 | tf_op jit(solution)/shard_map/ppermute | solution.py:25
  49.9 1.1 %fusion.1 = f32[8,64,128]{2,1,0:T(8,128)S(1)} fusion(f32[8,64,128]{2,1,0:T(8,128)S(1)} %fusion, f32[8,128,64]{1,2,0:T(8,128)S(1)} %fusion.24, f32[8,128,128]{2,1,0:T(8,128)S(1)} %copy-done, pred[]{:T(512)S(6)} %ge.9), kind=kOutput, calls=%fused_computation.7 | convolution fusion | flops 100794368 | bytes 1310721 | tf_op jit(solution)/shard_map/...tik,tlk->...til/dot_general | solution.py:38
  51.0 2.5 %collective-permute-start.3 = (f32[8,64,128]{2,1,0:T(8,128)S(1)}, f32[8,64,128]{2,1,0:T(8,128)S(1)}, u32[]{:S(2)}, u32[]{:S(2)}) collective-permute-start(f32[8,64,128]{2,1,0:T(8,128)S(1)} %fusion.1), channel_id=1, source_target_pairs={{0,8},{4,12},{8,16},{12,20},{16,24},{20,28},{1,9},{5,13},{9,17},{1... | collective-permute-start | bytes 786440 | tf_op jit(solution)/shard_map/ppermute | solution.py:25
  53.5 0.6 fusion.27
  54.1 6.1 %collective-permute-done.3 = f32[8,64,128]{2,1,0:T(8,128)S(1)} collective-permute-done((f32[8,64,128]{2,1,0:T(8,128)S(1)}, f32[8,64,128]{2,1,0:T(8,128)S(1)}, u32[]{:S(2)}, u32[]{:S(2)}) %collective-permute-start.3) | collective-permute-done | bytes 262176 | tf_op jit(solution)/shard_map/ppermute | solution.py:25
  60.2 0.4 fusion.26
  60.6 1.1 %fusion.2 = f32[8,64,128]{2,1,0:T(8,128)S(1)} fusion(f32[8,64,128]{2,1,0:T(8,128)S(1)} %fusion.1, f32[8,64,128]{2,1,0:T(8,128)S(1)} %fusion.26, f32[8,128,128]{2,1,0:T(8,128)S(1)} %fusion.27, pred[]{:T(512)S(6)} %ge.10), kind=kOutput, calls=%fused_computation.8 | convolution fusion | flops 100794368 | bytes 1310721 | tf_op jit(solution)/shard_map/...tik,tlk->...til/dot_general | solution.py:38
  61.8 1.3 %collective-permute-start.4 = (f32[8,64,128]{2,1,0:T(8,128)S(1)}, f32[8,64,128]{2,1,0:T(8,128)S(1)}, u32[]{:S(2)}, u32[]{:S(2)}) collective-permute-start(f32[8,64,128]{2,1,0:T(8,128)S(1)} %fusion.2), channel_id=1, source_target_pairs={{0,16},{4,20},{8,24},{12,28},{1,17},{5,21},{9,25},{13,29},{2,18},{... | collective-permute-start | bytes 786440 | tf_op jit(solution)/shard_map/ppermute | solution.py:25
  63.1 0.6 fusion.30
  63.7 6.3 %collective-permute-done.4 = f32[8,64,128]{2,1,0:T(8,128)S(1)} collective-permute-done((f32[8,64,128]{2,1,0:T(8,128)S(1)}, f32[8,64,128]{2,1,0:T(8,128)S(1)}, u32[]{:S(2)}, u32[]{:S(2)}) %collective-permute-start.4) | collective-permute-done | bytes 262176 | tf_op jit(solution)/shard_map/ppermute | solution.py:25
  70.0 0.4 fusion.29
  70.4 1.1 %fusion.4 = f32[8,64,128]{2,1,0:T(8,128)S(1)} fusion(f32[8,64,128]{2,1,0:T(8,128)S(1)} %fusion.2, f32[8,64,128]{2,1,0:T(8,128)S(1)} %fusion.29, f32[8,128,128]{2,1,0:T(8,128)S(1)} %fusion.30, pred[]{:T(512)S(6)} %ge.11, f32[1,8,64,128]{3,2,1,0:T(8,128)S(1)} %slice.48, f32[1,8,64,128]{3,2,1,0:T(8,128)S(1)} %slice.49), kind=kOutput, calls=%fused_computation.10 | convolution fusion | flops 100990976 | bytes 1835009 | tf_op jit(solution)/shard_map/...tik,tlk->...til/dot_general | solution.py:38
  71.8 1.9 %collective-permute-start.5 = (f32[8,128,128]{2,1,0:T(8,128)S(1)}, f32[8,128,128]{2,1,0:T(8,128)S(1)}, u32[]{:S(2)}, u32[]{:S(2)}) collective-permute-start(f32[8,128,128]{2,1,0:T(8,128)S(1)} %add.39), channel_id=1, source_target_pairs={{0,4},{4,8},{8,12},{12,16},{16,20},{20,24},{24,28},{1,5},{5,9},{9,... | collective-permute-start | bytes 1572872 | tf_op jit(solution)/shard_map/ppermute | solution.py:25
  73.8 9.5 %collective-permute-done.5 = f32[8,128,128]{2,1,0:T(8,128)S(1)} collective-permute-done((f32[8,128,128]{2,1,0:T(8,128)S(1)}, f32[8,128,128]{2,1,0:T(8,128)S(1)}, u32[]{:S(2)}, u32[]{:S(2)}) %collective-permute-start.5) | collective-permute-done | bytes 524320 | tf_op jit(solution)/shard_map/ppermute | solution.py:25
  83.2 0.9 %select_bitcast_fusion = f32[1,8,128,128]{3,2,1,0:T(8,128)} fusion(f32[8,128,128]{2,1,0:T(8,128)S(1)} %collective-permute-done.5, pred[]{:T(512)S(6)} %eq.4, f32[1,8,128,128]{3,2,1,0:T(8,128)S(1)} %copy-done.1), kind=kLoop, calls=%fused_computation.11 | loop fusion | flops 262144 | bytes 1572865 | tf_op jit(solution)/shard_map/broadcast_in_dim | solution.py:210
  (33 shorter events, 1.4 us)
Async XLA Ops:
  0.6 10.0 %copy-start = (f32[8,128,128]{2,1,0:T(8,128)S(1)}, f32[8,128,128]{2,1,0:T(8,128)}, u32[]{:S(2)}) copy-start(f32[8,128,128]{2,1,0:T(8,128)} %param.15) | copy-start | bytes 1572868
  0.6 9.3 %copy-start.1 = (f32[1,8,128,128]{3,2,1,0:T(8,128)S(1)}, f32[1,8,128,128]{3,2,1,0:T(8,128)}, u32[]{:S(2)}) copy-start(f32[1,8,128,128]{3,2,1,0:T(8,128)} %param.8) | copy-start | bytes 1572868
  1.8 2.2 %copy-start.5 = (f32[1,8,128,128]{3,2,1,0:T(8,128)}, f32[1,8,128,128]{3,2,1,0:T(8,128)S(1)}, u32[]{:S(2)}) copy-start(f32[1,8,128,128]{3,2,1,0:T(8,128)S(1)} %subtract_bitcast_fusion) | copy-start | bytes 1572868
  1.8 8.3 %copy-start.10 = (s32[8,4]{0,1:T(4,128)S(1)}, s32[8,4]{0,1:T(4,128)}, u32[]{:S(2)}) copy-start(s32[8,4]{0,1:T(4,128)} %param.13) | copy-start | bytes 388
  1.9 8.4 %copy-start.3 = (f32[8,64,64]{2,1,0:T(8,128)S(1)}, f32[8,64,64]{2,1,0:T(8,128)}, u32[]{:S(2)}) copy-start(f32[8,64,64]{2,1,0:T(8,128)} %param.14) | copy-start | bytes 393220
  4.1 13.7 %collective-permute-start = (f32[5,8,16,128]{3,2,1,0:T(8,128)}, f32[5,8,16,128]{3,2,1,0:T(8,128)S(1)}, u32[]{:S(2)}, u32[]{:S(2)}) collective-permute-start(f32[5,8,16,128]{3,2,1,0:T(8,128)} %get-tuple-element.3), channel_id=1, source_target_pairs={{0,1},{1,2},{2,3},{4,5},{5,6},{6,7},{8,9},{9,10},{10,11},{12,13},{... | collective-permute-start | bytes 983048 | tf_op jit(solution)/shard_map/ppermute | solution.py:137
  7.5 11.4 %collective-permute-start.1 = (f32[5,8,16,128]{3,2,1,0:T(8,128)}, f32[5,8,16,128]{3,2,1,0:T(8,128)}, u32[]{:S(2)}, u32[]{:S(2)}) collective-permute-start(f32[5,8,16,128]{3,2,1,0:T(8,128)} %get-tuple-element.2), channel_id=1, source_target_pairs={{1,0},{2,1},{3,2},{5,4},{6,5},{7,6},{9,8},{10,9},{11,10},{13,12},{... | collective-permute-start | bytes 983048 | tf_op jit(solution)/shard_map/ppermute | solution.py:138
  10.2 2.3 %copy-start.6 = (f32[1,8,128,128]{3,2,1,0:T(8,128)S(1)}, f32[1,8,128,128]{3,2,1,0:T(8,128)}, u32[]{:S(2)}) copy-start(f32[1,8,128,128]{3,2,1,0:T(8,128)} %copy-done.5) | copy-start | bytes 1572868
  14.0 4.9 %copy-start.2 = (f32[12]{0:T(128)S(1)}, f32[12]{0:T(128)}, u32[]{:S(2)}) copy-start(f32[12]{0:T(128)} %scale_ref.1) | copy-start | bytes 148
  17.7 21.1 %copy-start.7 = (f32[8,64,128]{2,1,0:T(8,128)S(1)}, f32[8,64,128]{2,1,0:T(8,128)}, u32[]{:S(2)}) copy-start(f32[8,64,128]{2,1,0:T(8,128)} %fusion.23) | copy-start | bytes 786436
  38.8 1.0 %copy-start.8 = (f32[8,128,64]{1,2,0:T(8,128)S(1)}, f32[8,128,64]{1,2,0:T(8,128)}, u32[]{:S(2)}) copy-start(f32[8,128,64]{1,2,0:T(8,128)} %fusion.6) | copy-start | bytes 786436
  39.0 3.8 %copy-start.4 = (f32[8,64,64]{2,1,0:T(8,128)S(1)}, f32[8,64,64]{2,1,0:T(8,128)}, u32[]{:S(2)}) copy-start(f32[8,64,64]{2,1,0:T(8,128)} %param.14) | copy-start | bytes 393220
  40.9 8.6 %collective-permute-start.2 = (f32[8,64,128]{2,1,0:T(8,128)S(1)}, f32[8,64,128]{2,1,0:T(8,128)S(1)}, u32[]{:S(2)}, u32[]{:S(2)}) collective-permute-start(f32[8,64,128]{2,1,0:T(8,128)S(1)} %fusion), channel_id=1, source_target_pairs={{0,4},{4,8},{8,12},{12,16},{16,20},{20,24},{24,28},{1,5},{5,9},{9,... | collective-permute-start | bytes 786440 | tf_op jit(solution)/shard_map/ppermute | solution.py:25
  51.0 9.2 %collective-permute-start.3 = (f32[8,64,128]{2,1,0:T(8,128)S(1)}, f32[8,64,128]{2,1,0:T(8,128)S(1)}, u32[]{:S(2)}, u32[]{:S(2)}) collective-permute-start(f32[8,64,128]{2,1,0:T(8,128)S(1)} %fusion.1), channel_id=1, source_target_pairs={{0,8},{4,12},{8,16},{12,20},{16,24},{20,28},{1,9},{5,13},{9,17},{1... | collective-permute-start | bytes 786440 | tf_op jit(solution)/shard_map/ppermute | solution.py:25
  61.8 8.3 %collective-permute-start.4 = (f32[8,64,128]{2,1,0:T(8,128)S(1)}, f32[8,64,128]{2,1,0:T(8,128)S(1)}, u32[]{:S(2)}, u32[]{:S(2)}) collective-permute-start(f32[8,64,128]{2,1,0:T(8,128)S(1)} %fusion.2), channel_id=1, source_target_pairs={{0,16},{4,20},{8,24},{12,28},{1,17},{5,21},{9,25},{13,29},{2,18},{... | collective-permute-start | bytes 786440 | tf_op jit(solution)/shard_map/ppermute | solution.py:25
  71.8 12.3 %copy-start.9 = (f32[8,128,128]{2,1,0:T(8,128)}, f32[8,128,128]{2,1,0:T(8,128)S(1)}, u32[]{:S(2)}) copy-start(f32[8,128,128]{2,1,0:T(8,128)S(1)} %add.39) | copy-start | bytes 1572868
  71.8 11.4 %collective-permute-start.5 = (f32[8,128,128]{2,1,0:T(8,128)S(1)}, f32[8,128,128]{2,1,0:T(8,128)S(1)}, u32[]{:S(2)}, u32[]{:S(2)}) collective-permute-start(f32[8,128,128]{2,1,0:T(8,128)S(1)} %add.39), channel_id=1, source_target_pairs={{0,4},{4,8},{8,12},{12,16},{16,20},{20,24},{24,28},{1,5},{5,9},{9,... | collective-permute-start | bytes 1572872 | tf_op jit(solution)/shard_map/ppermute | solution.py:25

commit v4 on v3

--- a/solution.py
+++ b/solution.py
@@ -165,17 +165,32 @@
     first_coarse = restrict(starts[0])
 
     def prefix_over_tm(total, power_x, power_y):
+        distances = []
         distance = 1
         while distance < tm_count:
-            received = passed_along(total, "tm", distance)
-            total = total + jnp.where(
-                tm_index >= distance, apply_coarse(received, power_x, power_y), 0.0
-            )
+            distances.append(distance)
             distance *= 2
-            if distance < tm_count:
-                power_x = jnp.einsum("tij,tjk->tik", power_x, power_x, precision=exact_precision)
-                power_y = jnp.einsum("tij,tjk->tik", power_y, power_y, precision=exact_precision)
-        return total
+        powers = {}
+        for distance in distances:
+            powers[distance] = (power_x, power_y)
+            power_x = jnp.einsum("tij,tjk->tik", power_x, power_x, precision=exact_precision)
+            power_y = jnp.einsum("tij,tjk->tik", power_y, power_y, precision=exact_precision)
+        half = total.shape[0] // 2
+        parts = [(slice(0, half), distances[:1] + distances[1:]),
+                 (slice(half, None), distances[:1] + distances[1:][::-1])]
+        values = [total[part] for part, _ in parts]
+        for step in range(len(distances)):
+            if step == 0:
+                received = passed_along(total, "tm", distances[0])
+                received = [received[part] for part, _ in parts]
+            else:
+                received = [passed_along(values[k], "tm", parts[k][1][step]) for k in range(2)]
+            for k in range(2):
+                part, order = parts[k]
+                distance = order[step]
+                mixed = apply_coarse(received[k], powers[distance][0][part], powers[distance][1][part])
+                values[k] = values[k] + jnp.where(tm_index >= distance, mixed, 0.0)
+        return jnp.concatenate(values, axis=0)
 
     if slice_count == 1:
         seed = jnp.where(tm_index == 0, apply_coarse(first_coarse, coarse_x, coarse_y), 0.0)

time: 84.5 us -> 83.2 us (0.985)
  waiting for transfers between devices: 28.9 us -> 22.8 us
  starting transfers between devices: 13.5 us -> 17.9 us
  matrix products: 12.1 us -> 14.4 us
  other arithmetic: 5.88 us -> 4.62 us
    ppermute x4 -> x6, waiting for transfers between devices: 27.8 us -> 22.8 us  [passed_along(): return lax.ppermute(block, axis, route)]
    ppermute x4 -> x6, starting transfers between devices: 7.64 us -> 12.1 us  [passed_along(): return lax.ppermute(block, axis, route)]
    dot_general x2, matrix products: 1.26 us -> 3.29 us  [prefix_over_tm(): jnp.einsum('tij,tjk->tik', power_y, power_y, precision=exact_precision)]
    another operation x2, other arithmetic: 2.68 us -> 1.36 us  [on_device(): jnp.stack([diffusivity, velocity[0], velocity[1], open_cells], axis=0)]
    slice x6, local copies, waits for them, and re-layouts: 1.97 us -> 0.67 us  [restrict(): return 0.5 * (values[..., 0::2, :] + values[..., 1::2, :])]
    ppermute x1, waiting for transfers between devices: 1.17 us -> 0.01 us  [on_device(): from_next = lax.ppermute(layers[:, :, :HALO, :], 'space', backward)]
    unnamed x22 -> x36, local copies, waits for them, and re-layouts: 0.5 us -> 1.35 us
    dot_general x5 -> x8, matrix products: 3.74 us -> 3.06 us  [apply_coarse(): jnp.einsum('tij,...tjk->...tik', matrix_x, coarse_values, precision=exact...]
  transfers between devices with their start and end apart: 6 -> 8, of which waited for: 5 -> 6; matrix products, arithmetic and copies ran while one was open for 12% -> 15% of each run, Pallas kernels for 0% -> 0%
where the time goes in v4:
time: 83.2 us; the launch traced here: 82.8 us
  waiting for transfers between devices  22.8 us (27%)
  Pallas kernels  19.5 us (23%)
  starting transfers between devices  17.9 us (22%)
  matrix products  14.4 us (17%)
  other arithmetic  4.62 us (6%)
  local copies, waits for them, and re-layouts  2.39 us (3%)
  between operations  1.14 us (1%)
    ppermute x6, waiting for transfers between devices, passed_along(): return lax.ppermute(block, axis, route)  22.8 us
    pallas_call x1, Pallas kernels, fine_propagate(): pl.pallas_call(functools.partial(fine_kernel, slice_at), out_shape=jax.Sh...  19.5 us
    ppermute x6, starting transfers between devices, passed_along(): return lax.ppermute(block, axis, route)  12.1 us
    dot_general x8, matrix products, apply_coarse(): jnp.einsum('...tik,tlk->...til', mixed_x, matrix_y, precision=exact_preci...  6.61 us
    ppermute x1, starting transfers between devices, on_device(): from_prev = lax.ppermute(layers[:, :, rows - HALO:, :], 'space', forward)  3.47 us
    dot_general x2, matrix products, prefix_over_tm(): jnp.einsum('tij,tjk->tik', power_y, power_y, precision=exact_precision)  3.29 us
    dot_general x8, matrix products, apply_coarse(): jnp.einsum('tij,...tjk->...tik', matrix_x, coarse_values, precision=exact...  3.06 us
    ppermute x1, starting transfers between devices, on_device(): from_next = lax.ppermute(layers[:, :, :HALO, :], 'space', backward)  2.37 us
  transfers between devices with their start and end apart: 8, of which 6 were waited for; matrix products, arithmetic and copies ran while one was open for 15% of the time, Pallas kernels for 0%

profile of v4, /device:TPU:12, one launch (start us, length us, event | category | flops | bytes accessed | tf_op | source)
XLA Modules:
  0.0 82.8 jit_solution(5174583972063882753)
XLA Ops:
  0.6 1.1 %subtract_bitcast_fusion = f32[1,8,128,128]{3,2,1,0:T(8,128)S(1)} fusion(s32[8,128,128]{2,1,0:T(8,128)} %param.11), kind=kLoop, calls=%fused_computation.17 | loop fusion | flops 262144 | bytes 1048576 | tf_op jit(solution)/shard_map/stack | solution.py:132
  1.8 2.2 %pad_maximum_fusion.1 = (f32[5,8,16,128]{3,2,1,0:T(8,128)}, f32[5,8,16,128]{3,2,1,0:T(8,128)}) fusion(f32[1,8,128,128]{3,2,1,0:T(8,128)S(1)} %subtract_bitcast_fusion, f32[2,8,128,128]{3,2,1,0:T(8,128)} %param.10, f32[1,8,128,128]{3,2,1,0:T(8,128)} %bitcast.76, f32[1,8,128,128]{3,2,1,0:T(8,128)} %param.8), kind=kLoop, calls=%fused_computation.18 | loop fusion | flops 491520 | bytes 3276800 | tf_op jit(solution)/shard_map/concatenate | solution.py:133
  4.0 3.5 %collective-permute-start = (f32[5,8,16,128]{3,2,1,0:T(8,128)}, f32[5,8,16,128]{3,2,1,0:T(8,128)S(1)}, u32[]{:S(2)}, u32[]{:S(2)}) collective-permute-start(f32[5,8,16,128]{3,2,1,0:T(8,128)} %get-tuple-element.3), channel_id=1, source_target_pairs={{0,1},{1,2},{2,3},{4,5},{5,6},{6,7},{8,9},{9,10},{10,11},{12,13},{... | collective-permute-start | bytes 983048 | tf_op jit(solution)/shard_map/ppermute | solution.py:137
  7.5 2.4 %collective-permute-start.1 = (f32[5,8,16,128]{3,2,1,0:T(8,128)}, f32[5,8,16,128]{3,2,1,0:T(8,128)S(1)}, u32[]{:S(2)}, u32[]{:S(2)}) collective-permute-start(f32[5,8,16,128]{3,2,1,0:T(8,128)} %get-tuple-element.2), channel_id=1, source_target_pairs={{1,0},{2,1},{3,2},{5,4},{6,5},{7,6},{9,8},{10,9},{11,10},{13,12},{... | collective-permute-start | bytes 983048 | tf_op jit(solution)/shard_map/ppermute | solution.py:138
  10.8 0.7 copy-done.5
  11.5 1.1 %fusion.38 = f32[8,64,64]{2,1,0:T(8,128)} fusion(f32[8,64,64]{2,1,0:T(8,128)S(1)} %fusion.36), kind=kOutput, calls=%fused_computation.63 | convolution fusion | flops 25165824 | bytes 262144 | tf_op jit(solution)/shard_map/tij,tjk->tik/dot_general | solution.py:176
  12.6 0.4 convolution_bitcast_fusion
  13.0 1.8 %fusion.35 = f32[8,64,128]{2,1,0:T(8,128)} fusion(f32[8,64,128]{2,1,0:T(8,128)S(1)} %convolution_bitcast_fusion, f32[8,128,128]{2,1,0:T(8,128)S(1)} %copy-done.2), kind=kOutput, calls=%fused_computation.60 | convolution fusion | flops 100663296 | bytes 1048576 | tf_op jit(solution)/shard_map/...tik,tlk->...til/dot_general | solution.py:38
  14.9 1.1 %fusion.14 = f32[8,128,64]{1,2,0:T(8,128)} fusion(f32[8,64,64]{2,1,0:T(8,128)S(1)} %copy-done.7, f32[8,64,128]{2,1,0:T(8,128)S(1)} %slice.98, f32[8,64,128]{2,1,0:T(8,128)S(1)} %slice.99), kind=kOutput, calls=%fused_computation.30 | convolution fusion | flops 50462720 | bytes 917504 | tf_op jit(solution)/shard_map/tij,...tjk->...tik/dot_general | solution.py:37
  16.2 2.7 %fusion.37 = f32[8,128,128]{2,1,0:T(8,128)} fusion(f32[8,128,128]{2,1,0:T(8,128)} %param.15), kind=kOutput, calls=%fused_computation.62 | convolution fusion | flops 201326592 | bytes 1048576 | tf_op jit(solution)/shard_map/tij,tjk->tik/dot_general | solution.py:177
  18.9 19.5 %shard_map.95 = f32[8,128,128]{2,1,0:T(8,128)S(1)} custom-call(s32[8]{0:T(128)S(1)} %get-tuple-element.10.south_ref, s32[8]{0:T(128)S(1)} %get-tuple-element.9.north_ref, s32[8]{0:T(128)S(1)} %get-tuple-element.5.south_ok_ref, s32[8]{0:T(128)S(1)} %get-tuple-element.6.north_ok_ref, s32[8]{0:T(128)S(1)} %get-tuple-element.11.west_at_ref, ...), custom_call_target="tpu_custom_call" | custom-call | tf_op jit(solution)/shard_map/pallas_call | solution.py:109
  39.0 0.5 copy-done.3
  39.6 1.1 %fusion = f32[8,64,128]{2,1,0:T(8,128)S(1)} fusion(f32[8,128,64]{1,2,0:T(8,128)S(1)} %copy-done.15, f32[8,128,128]{2,1,0:T(8,128)S(1)} %copy-done.3, pred[]{:T(512)S(6)} %eq.4, f32[1,8,64,128]{3,2,1,0:T(8,128)S(1)} %slice.96, f32[1,8,64,128]{3,2,1,0:T(8,128)S(1)} %slice.97), kind=kOutput, calls=%fused_computation.3 | convolution fusion | flops 100925440 | bytes 1572865 | tf_op jit(solution)/shard_map/...tik,tlk->...til/dot_general | solution.py:38
  40.7 2.1 %collective-permute-start.2 = (f32[8,64,128]{2,1,0:T(8,128)S(1)}, f32[8,64,128]{2,1,0:T(8,128)S(1)}, u32[]{:S(2)}, u32[]{:S(2)}) collective-permute-start(f32[8,64,128]{2,1,0:T(8,128)S(1)} %fusion), channel_id=1, source_target_pairs={{0,4},{4,8},{8,12},{12,16},{16,20},{20,24},{24,28},{1,5},{5,9},{9,... | collective-permute-start | bytes 786440 | tf_op jit(solution)/shard_map/ppermute | solution.py:25
  42.8 0.6 fusion.39
  43.4 6.0 %collective-permute-done.2 = f32[8,64,128]{2,1,0:T(8,128)S(1)} collective-permute-done((f32[8,64,128]{2,1,0:T(8,128)S(1)}, f32[8,64,128]{2,1,0:T(8,128)S(1)}, u32[]{:S(2)}, u32[]{:S(2)}) %collective-permute-start.2) | collective-permute-done | bytes 262176 | tf_op jit(solution)/shard_map/ppermute | solution.py:25
  49.7 0.6 fusion.6
  50.3 2.5 %collective-permute-start.3 = (f32[4,64,128]{2,1,0:T(8,128)S(1)}, f32[4,64,128]{2,1,0:T(8,128)S(1)}, u32[]{:S(2)}, u32[]{:S(2)}) collective-permute-start(f32[4,64,128]{2,1,0:T(8,128)S(1)} %fusion.6), channel_id=1, source_target_pairs={{0,8},{4,12},{8,16},{12,20},{16,24},{20,28},{1,9},{5,13},{9,17},{1... | collective-permute-start | bytes 393224 | tf_op jit(solution)/shard_map/ppermute | solution.py:25
  53.1 0.6 fusion.3
  53.7 1.3 %collective-permute-start.5 = (f32[4,64,128]{2,1,0:T(8,128)S(1)}, f32[4,64,128]{2,1,0:T(8,128)S(1)}, u32[]{:S(2)}, u32[]{:S(2)}) collective-permute-start(f32[4,64,128]{2,1,0:T(8,128)S(1)} %fusion.3), channel_id=1, source_target_pairs={{0,16},{4,20},{8,24},{12,28},{1,17},{5,21},{9,25},{13,29},{2,18},{... | collective-permute-start | bytes 393224 | tf_op jit(solution)/shard_map/ppermute | solution.py:25
  55.0 3.2 %collective-permute-done.3 = f32[4,64,128]{2,1,0:T(8,128)S(1)} collective-permute-done((f32[4,64,128]{2,1,0:T(8,128)S(1)}, f32[4,64,128]{2,1,0:T(8,128)S(1)}, u32[]{:S(2)}, u32[]{:S(2)}) %collective-permute-start.3) | collective-permute-done | bytes 131104 | tf_op jit(solution)/shard_map/ppermute | solution.py:25
  58.5 0.6 fusion.5
  59.1 1.3 %collective-permute-start.4 = (f32[4,64,128]{2,1,0:T(8,128)S(1)}, f32[4,64,128]{2,1,0:T(8,128)S(1)}, u32[]{:S(2)}, u32[]{:S(2)}) collective-permute-start(f32[4,64,128]{2,1,0:T(8,128)S(1)} %fusion.5), channel_id=1, source_target_pairs={{0,16},{4,20},{8,24},{12,28},{1,17},{5,21},{9,25},{13,29},{2,18},{... | collective-permute-start | bytes 393224 | tf_op jit(solution)/shard_map/ppermute | solution.py:25
  60.9 0.6 fusion.2
  61.6 3.0 %collective-permute-start.6 = (f32[4,64,128]{2,1,0:T(8,128)S(1)}, f32[4,64,128]{2,1,0:T(8,128)S(1)}, u32[]{:S(2)}, u32[]{:S(2)}) collective-permute-start(f32[4,64,128]{2,1,0:T(8,128)S(1)} %fusion.2), channel_id=1, source_target_pairs={{0,8},{4,12},{8,16},{12,20},{16,24},{20,28},{1,9},{5,13},{9,17},{1... | collective-permute-start | bytes 393224 | tf_op jit(solution)/shard_map/ppermute | solution.py:25
  64.6 2.8 %collective-permute-done.4 = f32[4,64,128]{2,1,0:T(8,128)S(1)} collective-permute-done((f32[4,64,128]{2,1,0:T(8,128)S(1)}, f32[4,64,128]{2,1,0:T(8,128)S(1)}, u32[]{:S(2)}, u32[]{:S(2)}) %collective-permute-start.4) | collective-permute-done | bytes 131104 | tf_op jit(solution)/shard_map/ppermute | solution.py:25
  67.6 0.6 fusion.4
  68.2 1.1 %collective-permute-done.6 = f32[4,64,128]{2,1,0:T(8,128)S(1)} collective-permute-done((f32[4,64,128]{2,1,0:T(8,128)S(1)}, f32[4,64,128]{2,1,0:T(8,128)S(1)}, u32[]{:S(2)}, u32[]{:S(2)}) %collective-permute-start.6) | collective-permute-done | bytes 131104 | tf_op jit(solution)/shard_map/ppermute | solution.py:25
  69.6 0.6 fusion.1
  70.5 1.9 %collective-permute-start.7 = (f32[8,128,128]{2,1,0:T(8,128)S(1)}, f32[8,128,128]{2,1,0:T(8,128)S(1)}, u32[]{:S(2)}, u32[]{:S(2)}) collective-permute-start(f32[8,128,128]{2,1,0:T(8,128)S(1)} %add.51), channel_id=1, source_target_pairs={{0,4},{4,8},{8,12},{12,16},{16,20},{20,24},{24,28},{1,5},{5,9},{9,... | collective-permute-start | bytes 1572872 | tf_op jit(solution)/shard_map/ppermute | solution.py:25
  72.4 9.5 %collective-permute-done.7 = f32[8,128,128]{2,1,0:T(8,128)S(1)} collective-permute-done((f32[8,128,128]{2,1,0:T(8,128)S(1)}, f32[8,128,128]{2,1,0:T(8,128)S(1)}, u32[]{:S(2)}, u32[]{:S(2)}) %collective-permute-start.7) | collective-permute-done | bytes 524320 | tf_op jit(solution)/shard_map/ppermute | solution.py:25
  81.9 0.9 %select_bitcast_fusion = f32[1,8,128,128]{3,2,1,0:T(8,128)} fusion(f32[8,128,128]{2,1,0:T(8,128)S(1)} %collective-permute-done.7, pred[]{:T(512)S(6)} %eq.4, f32[1,8,128,128]{3,2,1,0:T(8,128)S(1)} %copy-done), kind=kLoop, calls=%fused_computation.16 | loop fusion | flops 262144 | bytes 1572865 | tf_op jit(solution)/shard_map/broadcast_in_dim | solution.py:225
  (58 shorter events, 3.8 us)
Async XLA Ops:
  0.6 9.3 %copy-start = (f32[1,8,128,128]{3,2,1,0:T(8,128)S(1)}, f32[1,8,128,128]{3,2,1,0:T(8,128)}, u32[]{:S(2)}) copy-start(f32[1,8,128,128]{3,2,1,0:T(8,128)} %param.8) | copy-start | bytes 1572868
  1.8 5.7 %copy-start.9 = (f32[1,8,128,128]{3,2,1,0:T(8,128)}, f32[1,8,128,128]{3,2,1,0:T(8,128)S(1)}, u32[]{:S(2)}) copy-start(f32[1,8,128,128]{3,2,1,0:T(8,128)S(1)} %subtract_bitcast_fusion) | copy-start | bytes 1572868
  1.8 8.6 %copy-start.17 = (s32[8,4]{0,1:T(4,128)S(1)}, s32[8,4]{0,1:T(4,128)}, u32[]{:S(2)}) copy-start(s32[8,4]{0,1:T(4,128)} %param.13) | copy-start | bytes 388
  1.8 8.6 %copy-start.7 = (f32[8,64,64]{2,1,0:T(8,128)S(1)}, f32[8,64,64]{2,1,0:T(8,128)}, u32[]{:S(2)}) copy-start(f32[8,64,64]{2,1,0:T(8,128)} %param.14) | copy-start | bytes 393220
  4.0 14.9 %collective-permute-start = (f32[5,8,16,128]{3,2,1,0:T(8,128)}, f32[5,8,16,128]{3,2,1,0:T(8,128)S(1)}, u32[]{:S(2)}, u32[]{:S(2)}) collective-permute-start(f32[5,8,16,128]{3,2,1,0:T(8,128)} %get-tuple-element.3), channel_id=1, source_target_pairs={{0,1},{1,2},{2,3},{4,5},{5,6},{6,7},{8,9},{9,10},{10,11},{12,13},{... | collective-permute-start | bytes 983048 | tf_op jit(solution)/shard_map/ppermute | solution.py:137
  7.5 11.4 %collective-permute-start.1 = (f32[5,8,16,128]{3,2,1,0:T(8,128)}, f32[5,8,16,128]{3,2,1,0:T(8,128)S(1)}, u32[]{:S(2)}, u32[]{:S(2)}) collective-permute-start(f32[5,8,16,128]{3,2,1,0:T(8,128)} %get-tuple-element.2), channel_id=1, source_target_pairs={{1,0},{2,1},{3,2},{5,4},{6,5},{7,6},{9,8},{10,9},{11,10},{13,12},{... | collective-permute-start | bytes 983048 | tf_op jit(solution)/shard_map/ppermute | solution.py:138
  10.0 3.0 %copy-start.2 = (f32[8,128,128]{2,1,0:T(8,128)S(1)}, f32[8,128,128]{2,1,0:T(8,128)}, u32[]{:S(2)}) copy-start(f32[8,128,128]{2,1,0:T(8,128)} %param.15) | copy-start | bytes 1572868
  10.8 0.7 copy-start.5
  11.5 4.5 %copy-start.10 = (f32[1,8,128,128]{3,2,1,0:T(8,128)S(1)}, f32[1,8,128,128]{3,2,1,0:T(8,128)}, u32[]{:S(2)}) copy-start(f32[1,8,128,128]{3,2,1,0:T(8,128)} %copy-done.9) | copy-start | bytes 1572868
  11.5 4.5 %copy-start.11 = (f32[2,8,128,128]{3,2,1,0:T(8,128)S(1)}, f32[2,8,128,128]{3,2,1,0:T(8,128)}, u32[]{:S(2)}) copy-start(f32[2,8,128,128]{3,2,1,0:T(8,128)} %param.10) | copy-start | bytes 3145732
  11.5 4.5 %copy-start.13 = (f32[8,128,128]{2,1,0:T(8,128)S(1)}, f32[8,128,128]{2,1,0:T(8,128)}, u32[]{:S(2)}) copy-start(f32[8,128,128]{2,1,0:T(8,128)} %param.9) | copy-start | bytes 1572868
  16.0 2.9 %copy-start.1 = (f32[12]{0:T(128)S(1)}, f32[12]{0:T(128)}, u32[]{:S(2)}) copy-start(f32[12]{0:T(128)} %scale_ref.1) | copy-start | bytes 148
  18.9 19.6 %copy-start.14 = (f32[8,64,128]{2,1,0:T(8,128)S(1)}, f32[8,64,128]{2,1,0:T(8,128)}, u32[]{:S(2)}) copy-start(f32[8,64,128]{2,1,0:T(8,128)} %fusion.35) | copy-start | bytes 786436
  38.5 1.0 %copy-start.3 = (f32[8,128,128]{2,1,0:T(8,128)S(1)}, f32[8,128,128]{2,1,0:T(8,128)}, u32[]{:S(2)}) copy-start(f32[8,128,128]{2,1,0:T(8,128)} %param.15) | copy-start | bytes 1572868
  38.5 1.1 %copy-start.15 = (f32[8,128,64]{1,2,0:T(8,128)S(1)}, f32[8,128,64]{1,2,0:T(8,128)}, u32[]{:S(2)}) copy-start(f32[8,128,64]{1,2,0:T(8,128)} %fusion.14) | copy-start | bytes 786436
  38.7 4.1 %copy-start.4 = (f32[8,128,128]{2,1,0:T(8,128)S(1)}, f32[8,128,128]{2,1,0:T(8,128)}, u32[]{:S(2)}) copy-start(f32[8,128,128]{2,1,0:T(8,128)} %fusion.37) | copy-start | bytes 1572868
  38.8 10.7 %copy-start.8 = (f32[8,64,64]{2,1,0:T(8,128)S(1)}, f32[8,64,64]{2,1,0:T(8,128)}, u32[]{:S(2)}) copy-start(f32[8,64,64]{2,1,0:T(8,128)} %param.14) | copy-start | bytes 393220
  40.7 17.5 %copy-start.6 = (f32[8,64,64]{2,1,0:T(8,128)S(1)}, f32[8,64,64]{2,1,0:T(8,128)}, u32[]{:S(2)}) copy-start(f32[8,64,64]{2,1,0:T(8,128)} %copy-done.5) | copy-start | bytes 393220
  40.7 8.7 %collective-permute-start.2 = (f32[8,64,128]{2,1,0:T(8,128)S(1)}, f32[8,64,128]{2,1,0:T(8,128)S(1)}, u32[]{:S(2)}, u32[]{:S(2)}) collective-permute-start(f32[8,64,128]{2,1,0:T(8,128)S(1)} %fusion), channel_id=1, source_target_pairs={{0,4},{4,8},{8,12},{12,16},{16,20},{20,24},{24,28},{1,5},{5,9},{9,... | collective-permute-start | bytes 786440 | tf_op jit(solution)/shard_map/ppermute | solution.py:25
  43.4 17.2 %copy-start.12 = (f32[8,64,64]{2,1,0:T(8,128)S(1)}, f32[8,64,64]{2,1,0:T(8,128)}, u32[]{:S(2)}) copy-start(f32[8,64,64]{2,1,0:T(8,128)} %fusion.38) | copy-start | bytes 393220
  50.3 7.9 %collective-permute-start.3 = (f32[4,64,128]{2,1,0:T(8,128)S(1)}, f32[4,64,128]{2,1,0:T(8,128)S(1)}, u32[]{:S(2)}, u32[]{:S(2)}) collective-permute-start(f32[4,64,128]{2,1,0:T(8,128)S(1)} %fusion.6), channel_id=1, source_target_pairs={{0,8},{4,12},{8,16},{12,20},{16,24},{20,28},{1,9},{5,13},{9,17},{1... | collective-permute-start | bytes 393224 | tf_op jit(solution)/shard_map/ppermute | solution.py:25
  53.7 6.9 %collective-permute-start.5 = (f32[4,64,128]{2,1,0:T(8,128)S(1)}, f32[4,64,128]{2,1,0:T(8,128)S(1)}, u32[]{:S(2)}, u32[]{:S(2)}) collective-permute-start(f32[4,64,128]{2,1,0:T(8,128)S(1)} %fusion.3), channel_id=1, source_target_pairs={{0,16},{4,20},{8,24},{12,28},{1,17},{5,21},{9,25},{13,29},{2,18},{... | collective-permute-start | bytes 393224 | tf_op jit(solution)/shard_map/ppermute | solution.py:25
  59.1 8.3 %collective-permute-start.4 = (f32[4,64,128]{2,1,0:T(8,128)S(1)}, f32[4,64,128]{2,1,0:T(8,128)S(1)}, u32[]{:S(2)}, u32[]{:S(2)}) collective-permute-start(f32[4,64,128]{2,1,0:T(8,128)S(1)} %fusion.5), channel_id=1, source_target_pairs={{0,16},{4,20},{8,24},{12,28},{1,17},{5,21},{9,25},{13,29},{2,18},{... | collective-permute-start | bytes 393224 | tf_op jit(solution)/shard_map/ppermute | solution.py:25
  61.6 7.8 %collective-permute-start.6 = (f32[4,64,128]{2,1,0:T(8,128)S(1)}, f32[4,64,128]{2,1,0:T(8,128)S(1)}, u32[]{:S(2)}, u32[]{:S(2)}) collective-permute-start(f32[4,64,128]{2,1,0:T(8,128)S(1)} %fusion.2), channel_id=1, source_target_pairs={{0,8},{4,12},{8,16},{12,20},{16,24},{20,28},{1,9},{5,13},{9,17},{1... | collective-permute-start | bytes 393224 | tf_op jit(solution)/shard_map/ppermute | solution.py:25
  70.5 12.3 %copy-start.16 = (f32[8,128,128]{2,1,0:T(8,128)}, f32[8,128,128]{2,1,0:T(8,128)S(1)}, u32[]{:S(2)}) copy-start(f32[8,128,128]{2,1,0:T(8,128)S(1)} %add.51) | copy-start | bytes 1572868
  70.5 11.4 %collective-permute-start.7 = (f32[8,128,128]{2,1,0:T(8,128)S(1)}, f32[8,128,128]{2,1,0:T(8,128)S(1)}, u32[]{:S(2)}, u32[]{:S(2)}) collective-permute-start(f32[8,128,128]{2,1,0:T(8,128)S(1)} %add.51), channel_id=1, source_target_pairs={{0,4},{4,8},{8,12},{12,16},{16,20},{20,24},{24,28},{1,5},{5,9},{9,... | collective-permute-start | bytes 1572872 | tf_op jit(solution)/shard_map/ppermute | solution.py:25

commit v5 on v4

--- a/solution.py
+++ b/solution.py
@@ -38,13 +38,16 @@
     return jnp.einsum("...tik,tlk->...til", mixed_x, matrix_y, precision=exact_precision)
 
 
-def fine_kernel(slice_at, south_ref, north_ref, south_ok_ref, north_ok_ref, west_at_ref, east_at_ref,
-                west_ok_ref, east_ok_ref, scale_ref, u_ref, fields_ref, prev_ref, next_ref,
+def fine_kernel(slice_at, south_ref, north_ref, west_at_ref, east_at_ref, west_ok_ref, east_ok_ref,
+                scale_ref, u_ref, diffusivity_ref, velocity_ref, obstacle_ref, prev_ref, next_ref,
                 out_ref, state_ref, field_ref):
     tiles = u_ref.shape[0]
     rows = u_ref.shape[1]
+    lanes = u_ref.shape[2]
     total = rows + 2 * HALO
     layers = prev_ref.shape[0]
+    for b in range(2):
+        state_ref[b, tiles] = jnp.zeros((total, lanes), jnp.float32)
     for i in range(tiles):
         west_at = west_at_ref[i]
         east_at = east_at_ref[i]
@@ -55,17 +58,22 @@
         state_ref[0, i, pl.ds(HALO + rows, HALO), :] = jnp.where(
             east_ok, next_ref[slice_at, east_at], 0.0
         )
+        own = (
+            diffusivity_ref[i],
+            velocity_ref[0, i],
+            velocity_ref[1, i],
+            1.0 - obstacle_ref[i].astype(jnp.float32),
+        )
         for f in range(4):
             field_at = layers - 4 + f
             field_ref[f, i, pl.ds(0, HALO), :] = jnp.where(
                 west_ok, prev_ref[field_at, west_at], 0.0
             )
-            field_ref[f, i, pl.ds(HALO, rows), :] = fields_ref[f, i]
+            field_ref[f, i, pl.ds(HALO, rows), :] = own[f]
             field_ref[f, i, pl.ds(HALO + rows, HALO), :] = jnp.where(
                 east_ok, next_ref[field_at, east_at], 0.0
             )
 
-    lanes = u_ref.shape[2]
     lane = lax.broadcasted_iota(jnp.int32, (total, lanes), 1)
     first_lane = lane == 0
     last_lane = lane == lanes - 1
@@ -78,12 +86,10 @@
             current = state_ref[src, i]
             south_tile = state_ref[src, south_ref[i]]
             north_tile = state_ref[src, north_ref[i]]
-            south_edge = jnp.where(south_ok_ref[i] > 0, pltpu.roll(south_tile, 1, 1), 0.0)
-            north_edge = jnp.where(north_ok_ref[i] > 0, pltpu.roll(north_tile, lanes - 1, 1), 0.0)
             from_west = pltpu.roll(current, 1, 0)
             from_east = pltpu.roll(current, total - 1, 0)
-            from_south = jnp.where(first_lane, south_edge, pltpu.roll(current, 1, 1))
-            from_north = jnp.where(last_lane, north_edge, pltpu.roll(current, lanes - 1, 1))
+            from_south = pltpu.roll(jnp.where(last_lane, south_tile, current), 1, 1)
+            from_north = pltpu.roll(jnp.where(first_lane, north_tile, current), lanes - 1, 1)
             diffusivity = field_ref[0, i]
             speed_x = field_ref[1, i]
             speed_y = field_ref[2, i]
@@ -101,7 +107,7 @@
         out_ref[i] = state_ref[last, i, pl.ds(HALO, rows), :]
 
 
-def fine_propagate(slice_at, u, fields, from_prev, from_next, indices, scale):
+def fine_propagate(slice_at, u, diffusivity, velocity, obstacle, from_prev, from_next, indices, scale):
     tiles, rows, lanes = u.shape
     total = rows + 2 * HALO
     vmem = pltpu.MemorySpace.VMEM
@@ -109,14 +115,14 @@
     return pl.pallas_call(
         functools.partial(fine_kernel, slice_at),
         out_shape=jax.ShapeDtypeStruct(u.shape, u.dtype),
-        in_specs=[pl.BlockSpec(memory_space=smem)] * 9 + [pl.BlockSpec(memory_space=vmem)] * 4,
+        in_specs=[pl.BlockSpec(memory_space=smem)] * 7 + [pl.BlockSpec(memory_space=vmem)] * 6,
         out_specs=pl.BlockSpec(memory_space=vmem),
         scratch_shapes=[
-            pltpu.VMEM((2, tiles, total, lanes), jnp.float32),
+            pltpu.VMEM((2, tiles + 1, total, lanes), jnp.float32),
             pltpu.VMEM((4, tiles, total, lanes), jnp.float32),
         ],
         compiler_params=pltpu.CompilerParams(vmem_limit_bytes=48 * 1024 * 1024),
-    )(*indices, scale, u, fields, from_prev, from_next)
+    )(*indices, scale, u, diffusivity, velocity, obstacle, from_prev, from_next)
 
 
 def on_device(
@@ -147,13 +153,16 @@
     north_nb = neighbors[:, 3]
     south_ok = (south_nb != all_tiles).astype(jnp.int32)
     north_ok = (north_nb != all_tiles).astype(jnp.int32)
-    south = jnp.clip(south_nb - block_base, 0, tile_count - 1) * south_ok
-    north = jnp.clip(north_nb - block_base, 0, tile_count - 1) * north_ok
-    indices = (south, north, south_ok, north_ok, west_at, east_at, west_ok, east_ok)
+    south = jnp.where(south_ok > 0, jnp.clip(south_nb - block_base, 0, tile_count - 1), tile_count)
+    north = jnp.where(north_ok > 0, jnp.clip(north_nb - block_base, 0, tile_count - 1), tile_count)
+    indices = (south, north, west_at, east_at, west_ok, east_ok)
 
     fine_ends = jnp.stack(
         [
-            fine_propagate(n, starts[n], fields, from_prev, from_next, indices, substep_scale)
+            fine_propagate(
+                n, starts[n], diffusivity, velocity, obstacle, from_prev, from_next, indices,
+                substep_scale,
+            )
             for n in range(slice_count)
         ],
         axis=0,

time: 83.2 us -> 79.2 us (0.952)
  Pallas kernels: 19.5 us -> 14.1 us
  local copies, waits for them, and re-layouts: 2.39 us -> 5.49 us
  matrix products: 14.4 us -> 13.2 us
    pallas_call x1, Pallas kernels: 19.5 us -> 14.1 us  [fine_propagate(): pl.pallas_call(functools.partial(fine_kernel, slice_at), out_shape=jax.Sh...]
    unnamed x36, local copies, waits for them, and re-layouts: 1.35 us -> 3.14 us
    slice x6, local copies, waits for them, and re-layouts: 0.67 us -> 1.99 us  [restrict(): return 0.5 * (values[..., 0::2, :] + values[..., 1::2, :])]
    dot_general x2, matrix products: 3.29 us -> 2.05 us  [prefix_over_tm(): jnp.einsum('tij,tjk->tik', power_y, power_y, precision=exact_precision)]
where the time goes in v5:
time: 79.2 us; the launch traced here: 78.7 us
  waiting for transfers between devices  22.8 us (29%)
  starting transfers between devices  17.9 us (23%)
  Pallas kernels  14.1 us (18%)
  matrix products  13.2 us (17%)
  local copies, waits for them, and re-layouts  5.49 us (7%)
  other arithmetic  4.14 us (5%)
  between operations  1.08 us (1%)
    ppermute x6, waiting for transfers between devices, passed_along(): return lax.ppermute(block, axis, route)  22.8 us
    pallas_call x1, Pallas kernels, fine_propagate(): pl.pallas_call(functools.partial(fine_kernel, slice_at), out_shape=jax.Sh...  14.1 us
    ppermute x6, starting transfers between devices, passed_along(): return lax.ppermute(block, axis, route)  12.1 us
    dot_general x8, matrix products, apply_coarse(): jnp.einsum('...tik,tlk->...til', mixed_x, matrix_y, precision=exact_preci...  6.62 us
    ppermute x1, starting transfers between devices, on_device(): from_prev = lax.ppermute(layers[:, :, rows - HALO:, :], 'space', forward)  3.47 us
    unnamed x36, local copies, waits for them, and re-layouts  3.14 us
    dot_general x8, matrix products, apply_coarse(): jnp.einsum('tij,...tjk->...tik', matrix_x, coarse_values, precision=exact...  3.07 us
    ppermute x1, starting transfers between devices, on_device(): from_next = lax.ppermute(layers[:, :, :HALO, :], 'space', backward)  2.37 us
  transfers between devices with their start and end apart: 8, of which 6 were waited for; matrix products, arithmetic and copies ran while one was open for 15% of the time, Pallas kernels for 0%

profile of v5, /device:TPU:12, one launch (start us, length us, event | category | flops | bytes accessed | tf_op | source)
XLA Modules:
  0.0 78.7 jit_solution(11617449631994174490)
XLA Ops:
  0.6 1.2 %subtract_bitcast_fusion = f32[1,8,128,128]{3,2,1,0:T(8,128)S(1)} fusion(s32[8,128,128]{2,1,0:T(8,128)} %obstacle_ref.1), kind=kLoop, calls=%fused_computation.16 | loop fusion | flops 262144 | bytes 1048576 | tf_op jit(solution)/shard_map/stack | solution.py:138
  2.0 1.9 %pad_maximum_fusion = (f32[5,8,16,128]{3,2,1,0:T(8,128)}, f32[5,8,16,128]{3,2,1,0:T(8,128)}) fusion(f32[1,8,128,128]{3,2,1,0:T(8,128)S(1)} %subtract_bitcast_fusion, f32[2,8,128,128]{3,2,1,0:T(8,128)} %velocity_ref.1, f32[1,8,128,128]{3,2,1,0:T(8,128)S(1)} %bitcast.68, f32[1,8,128,128]{3,2,1,0:T(8,128)S(1)} %copy-done), kind=kLoop, calls=%fused_computation.17 | loop fusion | flops 491520 | bytes 3276800 | tf_op jit(solution)/shard_map/concatenate | solution.py:139
  3.9 3.5 %collective-permute-start = (f32[5,8,16,128]{3,2,1,0:T(8,128)}, f32[5,8,16,128]{3,2,1,0:T(8,128)S(1)}, u32[]{:S(2)}, u32[]{:S(2)}) collective-permute-start(f32[5,8,16,128]{3,2,1,0:T(8,128)} %get-tuple-element.3), channel_id=1, source_target_pairs={{0,1},{1,2},{2,3},{4,5},{5,6},{6,7},{8,9},{9,10},{10,11},{12,13},{... | collective-permute-start | bytes 983048 | tf_op jit(solution)/shard_map/ppermute | solution.py:143
  7.3 2.4 %collective-permute-start.1 = (f32[5,8,16,128]{3,2,1,0:T(8,128)}, f32[5,8,16,128]{3,2,1,0:T(8,128)S(1)}, u32[]{:S(2)}, u32[]{:S(2)}) collective-permute-start(f32[5,8,16,128]{3,2,1,0:T(8,128)} %get-tuple-element.2), channel_id=1, source_target_pairs={{1,0},{2,1},{3,2},{5,4},{6,5},{7,6},{9,8},{10,9},{11,10},{13,12},{... | collective-permute-start | bytes 983048 | tf_op jit(solution)/shard_map/ppermute | solution.py:144
  9.7 0.8 slice.93
  10.5 0.8 slice.94
  11.5 0.8 %copy-done.9 = f32[8,64,64]{2,1,0:T(8,128)S(1)} copy-done((f32[8,64,64]{2,1,0:T(8,128)S(1)}, f32[8,64,64]{2,1,0:T(8,128)}, u32[]{:S(2)}) %copy-start.9) | copy-done | bytes 131096
  12.8 1.1 %fusion.36 = f32[8,64,64]{2,1,0:T(8,128)} fusion(f32[8,64,64]{2,1,0:T(8,128)S(1)} %fusion.34), kind=kOutput, calls=%fused_computation.60 | convolution fusion | flops 25165824 | bytes 262144 | tf_op jit(solution)/shard_map/tij,tjk->tik/dot_general | solution.py:185
  14.3 0.6 copy-done.5
  14.9 1.8 %fusion.33 = f32[8,64,128]{2,1,0:T(8,128)} fusion(f32[8,64,128]{2,1,0:T(8,128)S(1)} %convolution_bitcast_fusion, f32[8,128,128]{2,1,0:T(8,128)S(1)} %copy-done.5), kind=kOutput, calls=%fused_computation.57 | convolution fusion | flops 100663296 | bytes 1048576 | tf_op jit(solution)/shard_map/...tik,tlk->...til/dot_general | solution.py:38
  16.7 1.1 %fusion.14 = f32[8,128,64]{1,2,0:T(8,128)} fusion(f32[8,64,64]{2,1,0:T(8,128)S(1)} %copy-done.9, f32[8,64,128]{2,1,0:T(8,128)S(1)} %slice.97, f32[8,64,128]{2,1,0:T(8,128)S(1)} %slice.98), kind=kOutput, calls=%fused_computation.29 | convolution fusion | flops 50462720 | bytes 917504 | tf_op jit(solution)/shard_map/tij,...tjk->...tik/dot_general | solution.py:37
  17.9 1.4 %fusion.35 = f32[8,128,128]{2,1,0:T(8,128)} fusion(f32[8,128,128]{2,1,0:T(8,128)S(1)} %copy-done.5), kind=kOutput, calls=%fused_computation.59 | convolution fusion | flops 201326592 | bytes 1048576 | tf_op jit(solution)/shard_map/tij,tjk->tik/dot_general | solution.py:186
  19.4 0.6 copy-done.4
  20.0 14.1 %shard_map.95 = f32[8,128,128]{2,1,0:T(8,128)S(1)} custom-call(s32[8]{0:T(128)S(1)} %get-tuple-element.8.south_ref, s32[8]{0:T(128)S(1)} %get-tuple-element.7.north_ref, s32[8]{0:T(128)S(1)} %get-tuple-element.9.west_at_ref, s32[8]{0:T(128)S(1)} %get-tuple-element.6.east_at_ref, s32[8]{0:T(128)S(1)} %get-tuple-element.5.west_ok_ref, ...), custom_call_target="tpu_custom_call" | custom-call | tf_op jit(solution)/shard_map/pallas_call | solution.py:115
  34.7 0.8 %copy-done.15 = f32[8,128,64]{1,2,0:T(8,128)S(1)} copy-done((f32[8,128,64]{1,2,0:T(8,128)S(1)}, f32[8,128,64]{1,2,0:T(8,128)}, u32[]{:S(2)}) %copy-start.15) | copy-done | bytes 262168
  35.5 1.1 %fusion = f32[8,64,128]{2,1,0:T(8,128)S(1)} fusion(f32[8,128,64]{1,2,0:T(8,128)S(1)} %copy-done.15, f32[8,128,128]{2,1,0:T(8,128)S(1)} %copy-done.5, pred[]{:T(512)S(6)} %eq.4, f32[1,8,64,128]{3,2,1,0:T(8,128)S(1)} %slice.95, f32[1,8,64,128]{3,2,1,0:T(8,128)S(1)} %slice.96), kind=kOutput, calls=%fused_computation.2 | convolution fusion | flops 100925440 | bytes 1572865 | tf_op jit(solution)/shard_map/...tik,tlk->...til/dot_general | solution.py:38
  36.7 2.1 %collective-permute-start.2 = (f32[8,64,128]{2,1,0:T(8,128)S(1)}, f32[8,64,128]{2,1,0:T(8,128)S(1)}, u32[]{:S(2)}, u32[]{:S(2)}) collective-permute-start(f32[8,64,128]{2,1,0:T(8,128)S(1)} %fusion), channel_id=1, source_target_pairs={{0,4},{4,8},{8,12},{12,16},{16,20},{20,24},{24,28},{1,5},{5,9},{9,... | collective-permute-start | bytes 786440 | tf_op jit(solution)/shard_map/ppermute | solution.py:25
  38.7 0.6 fusion.37
  39.4 6.0 %collective-permute-done.2 = f32[8,64,128]{2,1,0:T(8,128)S(1)} collective-permute-done((f32[8,64,128]{2,1,0:T(8,128)S(1)}, f32[8,64,128]{2,1,0:T(8,128)S(1)}, u32[]{:S(2)}, u32[]{:S(2)}) %collective-permute-start.2) | collective-permute-done | bytes 262176 | tf_op jit(solution)/shard_map/ppermute | solution.py:25
  46.3 2.5 %collective-permute-start.3 = (f32[4,64,128]{2,1,0:T(8,128)S(1)}, f32[4,64,128]{2,1,0:T(8,128)S(1)}, u32[]{:S(2)}, u32[]{:S(2)}) collective-permute-start(f32[4,64,128]{2,1,0:T(8,128)S(1)} %fusion.6), channel_id=1, source_target_pairs={{0,8},{4,12},{8,16},{12,20},{16,24},{20,28},{1,9},{5,13},{9,17},{1... | collective-permute-start | bytes 393224 | tf_op jit(solution)/shard_map/ppermute | solution.py:25
  49.7 1.3 %collective-permute-start.5 = (f32[4,64,128]{2,1,0:T(8,128)S(1)}, f32[4,64,128]{2,1,0:T(8,128)S(1)}, u32[]{:S(2)}, u32[]{:S(2)}) collective-permute-start(f32[4,64,128]{2,1,0:T(8,128)S(1)} %fusion.3), channel_id=1, source_target_pairs={{0,16},{4,20},{8,24},{12,28},{1,17},{5,21},{9,25},{13,29},{2,18},{... | collective-permute-start | bytes 393224 | tf_op jit(solution)/shard_map/ppermute | solution.py:25
  51.0 3.1 %collective-permute-done.3 = f32[4,64,128]{2,1,0:T(8,128)S(1)} collective-permute-done((f32[4,64,128]{2,1,0:T(8,128)S(1)}, f32[4,64,128]{2,1,0:T(8,128)S(1)}, u32[]{:S(2)}, u32[]{:S(2)}) %collective-permute-start.3) | collective-permute-done | bytes 131104 | tf_op jit(solution)/shard_map/ppermute | solution.py:25
  54.4 0.6 fusion.5
  55.0 1.3 %collective-permute-start.4 = (f32[4,64,128]{2,1,0:T(8,128)S(1)}, f32[4,64,128]{2,1,0:T(8,128)S(1)}, u32[]{:S(2)}, u32[]{:S(2)}) collective-permute-start(f32[4,64,128]{2,1,0:T(8,128)S(1)} %fusion.5), channel_id=1, source_target_pairs={{0,16},{4,20},{8,24},{12,28},{1,17},{5,21},{9,25},{13,29},{2,18},{... | collective-permute-start | bytes 393224 | tf_op jit(solution)/shard_map/ppermute | solution.py:25
  56.9 0.6 fusion.2
  57.5 3.0 %collective-permute-start.6 = (f32[4,64,128]{2,1,0:T(8,128)S(1)}, f32[4,64,128]{2,1,0:T(8,128)S(1)}, u32[]{:S(2)}, u32[]{:S(2)}) collective-permute-start(f32[4,64,128]{2,1,0:T(8,128)S(1)} %fusion.2), channel_id=1, source_target_pairs={{0,8},{4,12},{8,16},{12,20},{16,24},{20,28},{1,9},{5,13},{9,17},{1... | collective-permute-start | bytes 393224 | tf_op jit(solution)/shard_map/ppermute | solution.py:25
  60.5 2.8 %collective-permute-done.4 = f32[4,64,128]{2,1,0:T(8,128)S(1)} collective-permute-done((f32[4,64,128]{2,1,0:T(8,128)S(1)}, f32[4,64,128]{2,1,0:T(8,128)S(1)}, u32[]{:S(2)}, u32[]{:S(2)}) %collective-permute-start.4) | collective-permute-done | bytes 131104 | tf_op jit(solution)/shard_map/ppermute | solution.py:25
  63.6 0.6 fusion.4
  64.2 1.1 %collective-permute-done.6 = f32[4,64,128]{2,1,0:T(8,128)S(1)} collective-permute-done((f32[4,64,128]{2,1,0:T(8,128)S(1)}, f32[4,64,128]{2,1,0:T(8,128)S(1)}, u32[]{:S(2)}, u32[]{:S(2)}) %collective-permute-start.6) | collective-permute-done | bytes 131104 | tf_op jit(solution)/shard_map/ppermute | solution.py:25
  66.5 1.9 %collective-permute-start.7 = (f32[8,128,128]{2,1,0:T(8,128)S(1)}, f32[8,128,128]{2,1,0:T(8,128)S(1)}, u32[]{:S(2)}, u32[]{:S(2)}) collective-permute-start(f32[8,128,128]{2,1,0:T(8,128)S(1)} %add.51), channel_id=1, source_target_pairs={{0,4},{4,8},{8,12},{12,16},{16,20},{20,24},{24,28},{1,5},{5,9},{9,... | collective-permute-start | bytes 1572872 | tf_op jit(solution)/shard_map/ppermute | solution.py:25
  68.4 9.5 %collective-permute-done.7 = f32[8,128,128]{2,1,0:T(8,128)S(1)} collective-permute-done((f32[8,128,128]{2,1,0:T(8,128)S(1)}, f32[8,128,128]{2,1,0:T(8,128)S(1)}, u32[]{:S(2)}, u32[]{:S(2)}) %collective-permute-start.7) | collective-permute-done | bytes 524320 | tf_op jit(solution)/shard_map/ppermute | solution.py:25
  77.9 0.9 %select_bitcast_fusion = f32[1,8,128,128]{3,2,1,0:T(8,128)} fusion(f32[8,128,128]{2,1,0:T(8,128)S(1)} %collective-permute-done.7, pred[]{:T(512)S(6)} %eq.4, f32[1,8,128,128]{3,2,1,0:T(8,128)S(1)} %copy-done), kind=kLoop, calls=%fused_computation.15 | loop fusion | flops 262144 | bytes 1572865 | tf_op jit(solution)/shard_map/broadcast_in_dim | solution.py:234
  (57 shorter events, 5.7 us)
Async XLA Ops:
  0.6 1.2 %copy-start = (f32[1,8,128,128]{3,2,1,0:T(8,128)S(1)}, f32[1,8,128,128]{3,2,1,0:T(8,128)}, u32[]{:S(2)}) copy-start(f32[1,8,128,128]{3,2,1,0:T(8,128)} %param.8) | copy-start | bytes 1572868
  0.6 1.3 %copy-start.2 = (f32[8,128,128]{2,1,0:T(8,128)S(1)}, f32[8,128,128]{2,1,0:T(8,128)}, u32[]{:S(2)}) copy-start(f32[8,128,128]{2,1,0:T(8,128)} %diffusivity_ref.1) | copy-start | bytes 1572868
  3.9 15.5 %collective-permute-start = (f32[5,8,16,128]{3,2,1,0:T(8,128)}, f32[5,8,16,128]{3,2,1,0:T(8,128)S(1)}, u32[]{:S(2)}, u32[]{:S(2)}) collective-permute-start(f32[5,8,16,128]{3,2,1,0:T(8,128)} %get-tuple-element.3), channel_id=1, source_target_pairs={{0,1},{1,2},{2,3},{4,5},{5,6},{6,7},{8,9},{9,10},{10,11},{12,13},{... | collective-permute-start | bytes 983048 | tf_op jit(solution)/shard_map/ppermute | solution.py:143
  7.3 12.0 %collective-permute-start.1 = (f32[5,8,16,128]{3,2,1,0:T(8,128)}, f32[5,8,16,128]{3,2,1,0:T(8,128)S(1)}, u32[]{:S(2)}, u32[]{:S(2)}) collective-permute-start(f32[5,8,16,128]{3,2,1,0:T(8,128)} %get-tuple-element.2), channel_id=1, source_target_pairs={{1,0},{2,1},{3,2},{5,4},{6,5},{7,6},{9,8},{10,9},{11,10},{13,12},{... | collective-permute-start | bytes 983048 | tf_op jit(solution)/shard_map/ppermute | solution.py:144
  11.4 1.0 %copy-start.9 = (f32[8,64,64]{2,1,0:T(8,128)S(1)}, f32[8,64,64]{2,1,0:T(8,128)}, u32[]{:S(2)}) copy-start(f32[8,64,64]{2,1,0:T(8,128)} %param.14) | copy-start | bytes 393220
  12.7 1.1 %copy-start.7 = (f32[8,64,64]{2,1,0:T(8,128)}, f32[8,64,64]{2,1,0:T(8,128)S(1)}, u32[]{:S(2)}) copy-start(f32[8,64,64]{2,1,0:T(8,128)S(1)} %fusion.34) | copy-start | bytes 393220
  12.7 1.1 %copy-start.13 = (f32[1,8,64,128]{3,2,1,0:T(8,128)S(1)}, f32[1,8,64,128]{3,2,1,0:T(8,128)}, u32[]{:S(2)}) copy-start(f32[1,8,64,128]{3,2,1,0:T(8,128)} %slice.93) | copy-start | bytes 786436
  12.8 1.1 %copy-start.14 = (f32[1,8,64,128]{3,2,1,0:T(8,128)S(1)}, f32[1,8,64,128]{3,2,1,0:T(8,128)}, u32[]{:S(2)}) copy-start(f32[1,8,64,128]{3,2,1,0:T(8,128)} %slice.94) | copy-start | bytes 786436
  13.9 1.0 %copy-start.5 = (f32[8,128,128]{2,1,0:T(8,128)S(1)}, f32[8,128,128]{2,1,0:T(8,128)}, u32[]{:S(2)}) copy-start(f32[8,128,128]{2,1,0:T(8,128)} %param.15) | copy-start | bytes 1572868
  16.7 1.1 %copy-start.17 = (s32[8,4]{0,1:T(4,128)S(1)}, s32[8,4]{0,1:T(4,128)}, u32[]{:S(2)}) copy-start(s32[8,4]{0,1:T(4,128)} %param.13) | copy-start | bytes 388
  17.9 1.5 %copy-start.1 = (f32[2,8,128,128]{3,2,1,0:T(8,128)S(1)}, f32[2,8,128,128]{3,2,1,0:T(8,128)}, u32[]{:S(2)}) copy-start(f32[2,8,128,128]{3,2,1,0:T(8,128)} %velocity_ref.1) | copy-start | bytes 3145732
  17.9 1.5 %copy-start.3 = (s32[8,128,128]{2,1,0:T(8,128)S(1)}, s32[8,128,128]{2,1,0:T(8,128)}, u32[]{:S(2)}) copy-start(s32[8,128,128]{2,1,0:T(8,128)} %obstacle_ref.1) | copy-start | bytes 1572868
  19.4 0.7 copy-start.4
  20.0 14.1 %copy-start.12 = (f32[8,64,128]{2,1,0:T(8,128)S(1)}, f32[8,64,128]{2,1,0:T(8,128)}, u32[]{:S(2)}) copy-start(f32[8,64,128]{2,1,0:T(8,128)} %fusion.33) | copy-start | bytes 786436
  34.6 1.0 %copy-start.15 = (f32[8,128,64]{1,2,0:T(8,128)S(1)}, f32[8,128,64]{1,2,0:T(8,128)}, u32[]{:S(2)}) copy-start(f32[8,128,64]{1,2,0:T(8,128)} %fusion.14) | copy-start | bytes 786436
  35.5 3.2 %copy-start.6 = (f32[8,128,128]{2,1,0:T(8,128)S(1)}, f32[8,128,128]{2,1,0:T(8,128)}, u32[]{:S(2)}) copy-start(f32[8,128,128]{2,1,0:T(8,128)} %fusion.35) | copy-start | bytes 1572868
  36.7 8.7 %copy-start.10 = (f32[8,64,64]{2,1,0:T(8,128)S(1)}, f32[8,64,64]{2,1,0:T(8,128)}, u32[]{:S(2)}) copy-start(f32[8,64,64]{2,1,0:T(8,128)} %param.14) | copy-start | bytes 393220
  36.7 8.7 %collective-permute-start.2 = (f32[8,64,128]{2,1,0:T(8,128)S(1)}, f32[8,64,128]{2,1,0:T(8,128)S(1)}, u32[]{:S(2)}, u32[]{:S(2)}) collective-permute-start(f32[8,64,128]{2,1,0:T(8,128)S(1)} %fusion), channel_id=1, source_target_pairs={{0,4},{4,8},{8,12},{12,16},{16,20},{20,24},{24,28},{1,5},{5,9},{9,... | collective-permute-start | bytes 786440 | tf_op jit(solution)/shard_map/ppermute | solution.py:25
  46.3 7.9 %collective-permute-start.3 = (f32[4,64,128]{2,1,0:T(8,128)S(1)}, f32[4,64,128]{2,1,0:T(8,128)S(1)}, u32[]{:S(2)}, u32[]{:S(2)}) collective-permute-start(f32[4,64,128]{2,1,0:T(8,128)S(1)} %fusion.6), channel_id=1, source_target_pairs={{0,8},{4,12},{8,16},{12,20},{16,24},{20,28},{1,9},{5,13},{9,17},{1... | collective-permute-start | bytes 393224 | tf_op jit(solution)/shard_map/ppermute | solution.py:25
  49.1 5.1 %copy-start.8 = (f32[8,64,64]{2,1,0:T(8,128)S(1)}, f32[8,64,64]{2,1,0:T(8,128)}, u32[]{:S(2)}) copy-start(f32[8,64,64]{2,1,0:T(8,128)} %copy-done.7) | copy-start | bytes 393220
  49.7 6.9 %collective-permute-start.5 = (f32[4,64,128]{2,1,0:T(8,128)S(1)}, f32[4,64,128]{2,1,0:T(8,128)S(1)}, u32[]{:S(2)}, u32[]{:S(2)}) collective-permute-start(f32[4,64,128]{2,1,0:T(8,128)S(1)} %fusion.3), channel_id=1, source_target_pairs={{0,16},{4,20},{8,24},{12,28},{1,17},{5,21},{9,25},{13,29},{2,18},{... | collective-permute-start | bytes 393224 | tf_op jit(solution)/shard_map/ppermute | solution.py:25
  54.4 2.2 %copy-start.11 = (f32[8,64,64]{2,1,0:T(8,128)S(1)}, f32[8,64,64]{2,1,0:T(8,128)}, u32[]{:S(2)}) copy-start(f32[8,64,64]{2,1,0:T(8,128)} %fusion.36) | copy-start | bytes 393220
  55.0 8.3 %collective-permute-start.4 = (f32[4,64,128]{2,1,0:T(8,128)S(1)}, f32[4,64,128]{2,1,0:T(8,128)S(1)}, u32[]{:S(2)}, u32[]{:S(2)}) collective-permute-start(f32[4,64,128]{2,1,0:T(8,128)S(1)} %fusion.5), channel_id=1, source_target_pairs={{0,16},{4,20},{8,24},{12,28},{1,17},{5,21},{9,25},{13,29},{2,18},{... | collective-permute-start | bytes 393224 | tf_op jit(solution)/shard_map/ppermute | solution.py:25
  57.5 7.8 %collective-permute-start.6 = (f32[4,64,128]{2,1,0:T(8,128)S(1)}, f32[4,64,128]{2,1,0:T(8,128)S(1)}, u32[]{:S(2)}, u32[]{:S(2)}) collective-permute-start(f32[4,64,128]{2,1,0:T(8,128)S(1)} %fusion.2), channel_id=1, source_target_pairs={{0,8},{4,12},{8,16},{12,20},{16,24},{20,28},{1,9},{5,13},{9,17},{1... | collective-permute-start | bytes 393224 | tf_op jit(solution)/shard_map/ppermute | solution.py:25
  66.5 12.3 %copy-start.16 = (f32[8,128,128]{2,1,0:T(8,128)}, f32[8,128,128]{2,1,0:T(8,128)S(1)}, u32[]{:S(2)}) copy-start(f32[8,128,128]{2,1,0:T(8,128)S(1)} %add.51) | copy-start | bytes 1572868
  66.5 11.4 %collective-permute-start.7 = (f32[8,128,128]{2,1,0:T(8,128)S(1)}, f32[8,128,128]{2,1,0:T(8,128)S(1)}, u32[]{:S(2)}, u32[]{:S(2)}) collective-permute-start(f32[8,128,128]{2,1,0:T(8,128)S(1)} %add.51), channel_id=1, source_target_pairs={{0,4},{4,8},{8,12},{12,16},{16,20},{20,24},{24,28},{1,5},{5,9},{9,... | collective-permute-start | bytes 1572872 | tf_op jit(solution)/shard_map/ppermute | solution.py:25

commit v6 on v5

--- a/solution.py
+++ b/solution.py
@@ -169,6 +169,7 @@
     )
     correction = fine_ends - prolong(apply_coarse(restrict(starts), coarse_x, coarse_y))
     coarse_jump = restrict(correction)
+    earlier_correction = passed_along(correction[-1], "tm", 1)
     tm_index = lax.axis_index("tm")
     tm_count = lax.axis_size("tm")
     first_coarse = restrict(starts[0])
@@ -227,7 +228,7 @@
             own_coarse.append(states[n] + earlier)
         coarse_applied = apply_coarse(jnp.stack(own_coarse, axis=0), coarse_x, coarse_y)
     slice_ends = prolong(coarse_applied) + correction
-    previous = passed_along(slice_ends[-1], "tm", 1)
+    previous = prolong(passed_along(coarse_applied[-1], "tm", 1)) + earlier_correction
     first_step = jnp.where(
         lax.axis_index("tm") == 0, jnp.zeros_like(previous), previous - starts[0]
     )

time: 79.2 us -> 76.4 us (0.965)
  waiting for transfers between devices: 22.8 us -> 16.4 us
  starting transfers between devices: 17.9 us -> 20.5 us
    ppermute x6 -> x7, waiting for transfers between devices: 22.8 us -> 16.3 us  [passed_along(): return lax.ppermute(block, axis, route)]
    ppermute x6 -> x7, starting transfers between devices: 12.1 us -> 14.7 us  [passed_along(): return lax.ppermute(block, axis, route)]
    add x1, other arithmetic: 0.06 us -> 0.85 us  [on_device(): slice_ends = prolong(coarse_applied) + correction]
    unnamed x36 -> x34, local copies, waits for them, and re-layouts: 3.14 us -> 3.13 us
  transfers between devices with their start and end apart: 8 -> 9, of which waited for: 6 -> 6; matrix products, arithmetic and copies ran while one was open for 15% -> 20% of each run, Pallas kernels for 0% -> 0%
where the time goes in v6:
time: 76.4 us; the launch traced here: 75.9 us
  starting transfers between devices  20.5 us (27%)
  waiting for transfers between devices  16.4 us (21%)
  Pallas kernels  14.1 us (18%)
  matrix products  13.2 us (17%)
  local copies, waits for them, and re-layouts  5.67 us (7%)
  other arithmetic  4.93 us (6%)
  between operations  1.07 us (1%)
    ppermute x7, waiting for transfers between devices, passed_along(): return lax.ppermute(block, axis, route)  16.3 us
    ppermute x7, starting transfers between devices, passed_along(): return lax.ppermute(block, axis, route)  14.7 us
    pallas_call x1, Pallas kernels, fine_propagate(): pl.pallas_call(functools.partial(fine_kernel, slice_at), out_shape=jax.Sh...  14.1 us
    dot_general x8, matrix products, apply_coarse(): jnp.einsum('...tik,tlk->...til', mixed_x, matrix_y, precision=exact_preci...  6.63 us
    ppermute x1, starting transfers between devices, on_device(): from_prev = lax.ppermute(layers[:, :, rows - HALO:, :], 'space', forward)  3.47 us
    unnamed x34, local copies, waits for them, and re-layouts  3.13 us
    dot_general x8, matrix products, apply_coarse(): jnp.einsum('tij,...tjk->...tik', matrix_x, coarse_values, precision=exact...  3.07 us
    ppermute x1, starting transfers between devices, on_device(): from_next = lax.ppermute(layers[:, :, :HALO, :], 'space', backward)  2.37 us
  transfers between devices with their start and end apart: 9, of which 6 were waited for; matrix products, arithmetic and copies ran while one was open for 20% of the time, Pallas kernels for 0%

profile of v6, /device:TPU:12, one launch (start us, length us, event | category | flops | bytes accessed | tf_op | source)
XLA Modules:
  0.0 75.9 jit_solution(11051665552583892560)
XLA Ops:
  0.6 1.2 %subtract_bitcast_fusion = f32[1,8,128,128]{3,2,1,0:T(8,128)S(1)} fusion(s32[8,128,128]{2,1,0:T(8,128)} %obstacle_ref.1), kind=kLoop, calls=%fused_computation.17 | loop fusion | flops 262144 | bytes 1048576 | tf_op jit(solution)/shard_map/stack | solution.py:138
  2.0 1.9 %pad_maximum_fusion = (f32[5,8,16,128]{3,2,1,0:T(8,128)}, f32[5,8,16,128]{3,2,1,0:T(8,128)}) fusion(f32[1,8,128,128]{3,2,1,0:T(8,128)S(1)} %subtract_bitcast_fusion, f32[2,8,128,128]{3,2,1,0:T(8,128)} %velocity_ref.1, f32[1,8,128,128]{3,2,1,0:T(8,128)S(1)} %bitcast.70, f32[1,8,128,128]{3,2,1,0:T(8,128)S(1)} %copy-done), kind=kLoop, calls=%fused_computation.18 | loop fusion | flops 491520 | bytes 3276800 | tf_op jit(solution)/shard_map/concatenate | solution.py:139
  3.9 3.5 %collective-permute-start = (f32[5,8,16,128]{3,2,1,0:T(8,128)}, f32[5,8,16,128]{3,2,1,0:T(8,128)S(1)}, u32[]{:S(2)}, u32[]{:S(2)}) collective-permute-start(f32[5,8,16,128]{3,2,1,0:T(8,128)} %get-tuple-element.3), channel_id=1, source_target_pairs={{0,1},{1,2},{2,3},{4,5},{5,6},{6,7},{8,9},{9,10},{10,11},{12,13},{... | collective-permute-start | bytes 983048 | tf_op jit(solution)/shard_map/ppermute | solution.py:143
  7.3 2.4 %collective-permute-start.1 = (f32[5,8,16,128]{3,2,1,0:T(8,128)}, f32[5,8,16,128]{3,2,1,0:T(8,128)S(1)}, u32[]{:S(2)}, u32[]{:S(2)}) collective-permute-start(f32[5,8,16,128]{3,2,1,0:T(8,128)} %get-tuple-element.2), channel_id=1, source_target_pairs={{1,0},{2,1},{3,2},{5,4},{6,5},{7,6},{9,8},{10,9},{11,10},{13,12},{... | collective-permute-start | bytes 983048 | tf_op jit(solution)/shard_map/ppermute | solution.py:144
  9.7 0.8 %slice.93 = f32[1,8,64,128]{3,2,1,0:T(8,128)} slice(f32[1,8,128,128]{3,2,1,0:T(8,128)S(1)} %copy-done), slice={[0:1:1], [0:8:1], [0:128:2], [0:128:1]} | slice | bytes 524288 | tf_op jit(solution)/shard_map/slice | solution.py:29
  10.5 0.8 %slice.94 = f32[1,8,64,128]{3,2,1,0:T(8,128)} slice(f32[1,8,128,128]{3,2,1,0:T(8,128)S(1)} %copy-done), slice={[0:1:1], [0:8:1], [1:128:2], [0:128:1]} | slice | bytes 524288 | tf_op jit(solution)/shard_map/slice | solution.py:29
  11.5 0.8 %copy-done.9 = f32[8,64,64]{2,1,0:T(8,128)S(1)} copy-done((f32[8,64,64]{2,1,0:T(8,128)S(1)}, f32[8,64,64]{2,1,0:T(8,128)}, u32[]{:S(2)}) %copy-start.9) | copy-done | bytes 131096
  12.8 1.1 %fusion.36 = f32[8,64,64]{2,1,0:T(8,128)} fusion(f32[8,64,64]{2,1,0:T(8,128)S(1)} %fusion.34), kind=kOutput, calls=%fused_computation.61 | convolution fusion | flops 25165824 | bytes 262144 | tf_op jit(solution)/shard_map/tij,tjk->tik/dot_general | solution.py:186
  14.3 0.6 copy-done.5
  14.9 1.8 %fusion.33 = f32[8,64,128]{2,1,0:T(8,128)} fusion(f32[8,64,128]{2,1,0:T(8,128)S(1)} %convolution_bitcast_fusion, f32[8,128,128]{2,1,0:T(8,128)S(1)} %copy-done.5), kind=kOutput, calls=%fused_computation.58 | convolution fusion | flops 100663296 | bytes 1048576 | tf_op jit(solution)/shard_map/...tik,tlk->...til/dot_general | solution.py:38
  16.7 1.1 %fusion.14 = f32[8,128,64]{1,2,0:T(8,128)} fusion(f32[8,64,64]{2,1,0:T(8,128)S(1)} %copy-done.9, f32[8,64,128]{2,1,0:T(8,128)S(1)} %slice.97, f32[8,64,128]{2,1,0:T(8,128)S(1)} %slice.98), kind=kOutput, calls=%fused_computation.30 | convolution fusion | flops 50462720 | bytes 917504 | tf_op jit(solution)/shard_map/tij,...tjk->...tik/dot_general | solution.py:37
  17.9 1.4 %fusion.35 = f32[8,128,128]{2,1,0:T(8,128)} fusion(f32[8,128,128]{2,1,0:T(8,128)S(1)} %copy-done.5), kind=kOutput, calls=%fused_computation.60 | convolution fusion | flops 201326592 | bytes 1048576 | tf_op jit(solution)/shard_map/tij,tjk->tik/dot_general | solution.py:187
  19.4 0.6 copy-done.4
  20.0 14.1 %shard_map.95 = f32[8,128,128]{2,1,0:T(8,128)S(1)} custom-call(s32[8]{0:T(128)S(1)} %get-tuple-element.8.south_ref, s32[8]{0:T(128)S(1)} %get-tuple-element.7.north_ref, s32[8]{0:T(128)S(1)} %get-tuple-element.9.west_at_ref, s32[8]{0:T(128)S(1)} %get-tuple-element.6.east_at_ref, s32[8]{0:T(128)S(1)} %get-tuple-element.5.west_ok_ref, ...), custom_call_target="tpu_custom_call" | custom-call | tf_op jit(solution)/shard_map/pallas_call | solution.py:115
  34.7 0.8 %copy-done.15 = f32[8,128,64]{1,2,0:T(8,128)S(1)} copy-done((f32[8,128,64]{1,2,0:T(8,128)S(1)}, f32[8,128,64]{1,2,0:T(8,128)}, u32[]{:S(2)}) %copy-start.15) | copy-done | bytes 262168
  35.5 1.1 %fusion = f32[8,64,128]{2,1,0:T(8,128)S(1)} fusion(f32[8,128,64]{1,2,0:T(8,128)S(1)} %copy-done.15, f32[8,128,128]{2,1,0:T(8,128)S(1)} %copy-done.5, pred[]{:T(512)S(6)} %eq.4, f32[1,8,64,128]{3,2,1,0:T(8,128)S(1)} %slice.95, f32[1,8,64,128]{3,2,1,0:T(8,128)S(1)} %slice.96), kind=kOutput, calls=%fused_computation.2 | convolution fusion | flops 100925440 | bytes 1572865 | tf_op jit(solution)/shard_map/...tik,tlk->...til/dot_general | solution.py:38
  36.7 2.1 %collective-permute-start.2 = (f32[8,64,128]{2,1,0:T(8,128)S(1)}, f32[8,64,128]{2,1,0:T(8,128)S(1)}, u32[]{:S(2)}, u32[]{:S(2)}) collective-permute-start(f32[8,64,128]{2,1,0:T(8,128)S(1)} %fusion), channel_id=1, source_target_pairs={{0,4},{4,8},{8,12},{12,16},{16,20},{20,24},{24,28},{1,5},{5,9},{9,... | collective-permute-start | bytes 786440 | tf_op jit(solution)/shard_map/ppermute | solution.py:25
  38.7 0.6 fusion.37
  39.4 3.5 %collective-permute-start.8 = (f32[8,128,128]{2,1,0:T(8,128)S(1)}, f32[8,128,128]{2,1,0:T(8,128)S(1)}, u32[]{:S(2)}, u32[]{:S(2)}) collective-permute-start(f32[8,128,128]{2,1,0:T(8,128)S(1)} %sub.57), channel_id=1, source_target_pairs={{0,4},{4,8},{8,12},{12,16},{16,20},{20,24},{24,28},{1,5},{5,9},{9,... | collective-permute-start | bytes 1572872 | tf_op jit(solution)/shard_map/ppermute | solution.py:25
  42.9 2.5 %collective-permute-done.2 = f32[8,64,128]{2,1,0:T(8,128)S(1)} collective-permute-done((f32[8,64,128]{2,1,0:T(8,128)S(1)}, f32[8,64,128]{2,1,0:T(8,128)S(1)}, u32[]{:S(2)}, u32[]{:S(2)}) %collective-permute-start.2) | collective-permute-done | bytes 262176 | tf_op jit(solution)/shard_map/ppermute | solution.py:25
  46.3 2.5 %collective-permute-start.3 = (f32[4,64,128]{2,1,0:T(8,128)S(1)}, f32[4,64,128]{2,1,0:T(8,128)S(1)}, u32[]{:S(2)}, u32[]{:S(2)}) collective-permute-start(f32[4,64,128]{2,1,0:T(8,128)S(1)} %fusion.6), channel_id=1, source_target_pairs={{0,8},{4,12},{8,16},{12,20},{16,24},{20,28},{1,9},{5,13},{9,17},{1... | collective-permute-start | bytes 393224 | tf_op jit(solution)/shard_map/ppermute | solution.py:25
  49.1 0.6 fusion.3
  49.7 1.3 %collective-permute-start.5 = (f32[4,64,128]{2,1,0:T(8,128)S(1)}, f32[4,64,128]{2,1,0:T(8,128)S(1)}, u32[]{:S(2)}, u32[]{:S(2)}) collective-permute-start(f32[4,64,128]{2,1,0:T(8,128)S(1)} %fusion.3), channel_id=1, source_target_pairs={{0,16},{4,20},{8,24},{12,28},{1,17},{5,21},{9,25},{13,29},{2,18},{... | collective-permute-start | bytes 393224 | tf_op jit(solution)/shard_map/ppermute | solution.py:25
  51.0 3.1 %collective-permute-done.3 = f32[4,64,128]{2,1,0:T(8,128)S(1)} collective-permute-done((f32[4,64,128]{2,1,0:T(8,128)S(1)}, f32[4,64,128]{2,1,0:T(8,128)S(1)}, u32[]{:S(2)}, u32[]{:S(2)}) %collective-permute-start.3) | collective-permute-done | bytes 131104 | tf_op jit(solution)/shard_map/ppermute | solution.py:25
  54.9 1.3 %collective-permute-start.4 = (f32[4,64,128]{2,1,0:T(8,128)S(1)}, f32[4,64,128]{2,1,0:T(8,128)S(1)}, u32[]{:S(2)}, u32[]{:S(2)}) collective-permute-start(f32[4,64,128]{2,1,0:T(8,128)S(1)} %fusion.5), channel_id=1, source_target_pairs={{0,16},{4,20},{8,24},{12,28},{1,17},{5,21},{9,25},{13,29},{2,18},{... | collective-permute-start | bytes 393224 | tf_op jit(solution)/shard_map/ppermute | solution.py:25
  57.5 2.1 %collective-permute-start.6 = (f32[4,64,128]{2,1,0:T(8,128)S(1)}, f32[4,64,128]{2,1,0:T(8,128)S(1)}, u32[]{:S(2)}, u32[]{:S(2)}) collective-permute-start(f32[4,64,128]{2,1,0:T(8,128)S(1)} %fusion.2), channel_id=1, source_target_pairs={{0,8},{4,12},{8,16},{12,20},{16,24},{20,28},{1,9},{5,13},{9,17},{1... | collective-permute-start | bytes 393224 | tf_op jit(solution)/shard_map/ppermute | solution.py:25
  59.6 3.6 %collective-permute-done.4 = f32[4,64,128]{2,1,0:T(8,128)S(1)} collective-permute-done((f32[4,64,128]{2,1,0:T(8,128)S(1)}, f32[4,64,128]{2,1,0:T(8,128)S(1)}, u32[]{:S(2)}, u32[]{:S(2)}) %collective-permute-start.4) | collective-permute-done | bytes 131104 | tf_op jit(solution)/shard_map/ppermute | solution.py:25
  64.1 1.2 %collective-permute-done.6 = f32[4,64,128]{2,1,0:T(8,128)S(1)} collective-permute-done((f32[4,64,128]{2,1,0:T(8,128)S(1)}, f32[4,64,128]{2,1,0:T(8,128)S(1)}, u32[]{:S(2)}, u32[]{:S(2)}) %collective-permute-start.6) | collective-permute-done | bytes 131104 | tf_op jit(solution)/shard_map/ppermute | solution.py:25
  66.2 1.9 %collective-permute-start.7 = (f32[8,64,128]{2,1,0:T(8,128)S(1)}, f32[8,64,128]{2,1,0:T(8,128)S(1)}, u32[]{:S(2)}, u32[]{:S(2)}) collective-permute-start(f32[8,64,128]{2,1,0:T(8,128)S(1)} %maximum_subtract_fusion), channel_id=1, source_target_pairs={{0,4},{4,8},{8,12},{12,16},{16,20},{20,24},{24,28},{1,5},{5,9},{9,... | collective-permute-start | bytes 786440 | tf_op jit(solution)/shard_map/ppermute | solution.py:25
  68.3 0.9 %add_bitcast_fusion = f32[1,8,128,128]{3,2,1,0:T(8,128)} fusion(f32[8,128,128]{2,1,0:T(8,128)S(1)} %bitcast.75, f32[8,128,128]{2,1,0:T(8,128)S(1)} %sub.57), kind=kLoop, calls=%fused_computation.16 | loop fusion | flops 131072 | bytes 1572864 | tf_op jit(solution)/shard_map/add | solution.py:230
  69.2 5.6 %collective-permute-done.7 = f32[8,64,128]{2,1,0:T(8,128)S(1)} collective-permute-done((f32[8,64,128]{2,1,0:T(8,128)S(1)}, f32[8,64,128]{2,1,0:T(8,128)S(1)}, u32[]{:S(2)}, u32[]{:S(2)}) %collective-permute-start.7) | collective-permute-done | bytes 262176 | tf_op jit(solution)/shard_map/ppermute | solution.py:25
  75.0 0.9 %select_bitcast_fusion = f32[1,8,128,128]{3,2,1,0:T(8,128)} fusion(f32[8,128,128]{2,1,0:T(8,128)S(1)} %bitcast.73, f32[8,128,128]{2,1,0:T(8,128)S(1)} %collective-permute-done.8, pred[]{:T(512)S(6)} %eq.4, f32[1,8,128,128]{3,2,1,0:T(8,128)S(1)} %copy-done), kind=kLoop, calls=%fused_computation.15 | loop fusion | flops 393216 | bytes 2097153 | tf_op jit(solution)/shard_map/broadcast_in_dim | solution.py:235
  (58 shorter events, 7.1 us)
Async XLA Ops:
  0.6 1.2 %copy-start = (f32[1,8,128,128]{3,2,1,0:T(8,128)S(1)}, f32[1,8,128,128]{3,2,1,0:T(8,128)}, u32[]{:S(2)}) copy-start(f32[1,8,128,128]{3,2,1,0:T(8,128)} %param.8) | copy-start | bytes 1572868
  0.6 1.3 %copy-start.2 = (f32[8,128,128]{2,1,0:T(8,128)S(1)}, f32[8,128,128]{2,1,0:T(8,128)}, u32[]{:S(2)}) copy-start(f32[8,128,128]{2,1,0:T(8,128)} %diffusivity_ref.1) | copy-start | bytes 1572868
  3.9 15.5 %collective-permute-start = (f32[5,8,16,128]{3,2,1,0:T(8,128)}, f32[5,8,16,128]{3,2,1,0:T(8,128)S(1)}, u32[]{:S(2)}, u32[]{:S(2)}) collective-permute-start(f32[5,8,16,128]{3,2,1,0:T(8,128)} %get-tuple-element.3), channel_id=1, source_target_pairs={{0,1},{1,2},{2,3},{4,5},{5,6},{6,7},{8,9},{9,10},{10,11},{12,13},{... | collective-permute-start | bytes 983048 | tf_op jit(solution)/shard_map/ppermute | solution.py:143
  7.3 12.0 %collective-permute-start.1 = (f32[5,8,16,128]{3,2,1,0:T(8,128)}, f32[5,8,16,128]{3,2,1,0:T(8,128)S(1)}, u32[]{:S(2)}, u32[]{:S(2)}) collective-permute-start(f32[5,8,16,128]{3,2,1,0:T(8,128)} %get-tuple-element.2), channel_id=1, source_target_pairs={{1,0},{2,1},{3,2},{5,4},{6,5},{7,6},{9,8},{10,9},{11,10},{13,12},{... | collective-permute-start | bytes 983048 | tf_op jit(solution)/shard_map/ppermute | solution.py:144
  11.4 1.0 %copy-start.9 = (f32[8,64,64]{2,1,0:T(8,128)S(1)}, f32[8,64,64]{2,1,0:T(8,128)}, u32[]{:S(2)}) copy-start(f32[8,64,64]{2,1,0:T(8,128)} %param.14) | copy-start | bytes 393220
  12.7 1.1 %copy-start.7 = (f32[8,64,64]{2,1,0:T(8,128)}, f32[8,64,64]{2,1,0:T(8,128)S(1)}, u32[]{:S(2)}) copy-start(f32[8,64,64]{2,1,0:T(8,128)S(1)} %fusion.34) | copy-start | bytes 393220
  12.7 1.1 %copy-start.13 = (f32[1,8,64,128]{3,2,1,0:T(8,128)S(1)}, f32[1,8,64,128]{3,2,1,0:T(8,128)}, u32[]{:S(2)}) copy-start(f32[1,8,64,128]{3,2,1,0:T(8,128)} %slice.93) | copy-start | bytes 786436
  12.8 1.1 %copy-start.14 = (f32[1,8,64,128]{3,2,1,0:T(8,128)S(1)}, f32[1,8,64,128]{3,2,1,0:T(8,128)}, u32[]{:S(2)}) copy-start(f32[1,8,64,128]{3,2,1,0:T(8,128)} %slice.94) | copy-start | bytes 786436
  13.9 1.0 %copy-start.5 = (f32[8,128,128]{2,1,0:T(8,128)S(1)}, f32[8,128,128]{2,1,0:T(8,128)}, u32[]{:S(2)}) copy-start(f32[8,128,128]{2,1,0:T(8,128)} %param.15) | copy-start | bytes 1572868
  16.7 1.1 %copy-start.16 = (s32[8,4]{0,1:T(4,128)S(1)}, s32[8,4]{0,1:T(4,128)}, u32[]{:S(2)}) copy-start(s32[8,4]{0,1:T(4,128)} %param.13) | copy-start | bytes 388
  17.9 1.5 %copy-start.1 = (f32[2,8,128,128]{3,2,1,0:T(8,128)S(1)}, f32[2,8,128,128]{3,2,1,0:T(8,128)}, u32[]{:S(2)}) copy-start(f32[2,8,128,128]{3,2,1,0:T(8,128)} %velocity_ref.1) | copy-start | bytes 3145732
  17.9 1.5 %copy-start.3 = (s32[8,128,128]{2,1,0:T(8,128)S(1)}, s32[8,128,128]{2,1,0:T(8,128)}, u32[]{:S(2)}) copy-start(s32[8,128,128]{2,1,0:T(8,128)} %obstacle_ref.1) | copy-start | bytes 1572868
  19.4 0.7 copy-start.4
  20.0 14.1 %copy-start.12 = (f32[8,64,128]{2,1,0:T(8,128)S(1)}, f32[8,64,128]{2,1,0:T(8,128)}, u32[]{:S(2)}) copy-start(f32[8,64,128]{2,1,0:T(8,128)} %fusion.33) | copy-start | bytes 786436
  34.6 1.0 %copy-start.15 = (f32[8,128,64]{1,2,0:T(8,128)S(1)}, f32[8,128,64]{1,2,0:T(8,128)}, u32[]{:S(2)}) copy-start(f32[8,128,64]{1,2,0:T(8,128)} %fusion.14) | copy-start | bytes 786436
  35.5 3.2 %copy-start.6 = (f32[8,128,128]{2,1,0:T(8,128)S(1)}, f32[8,128,128]{2,1,0:T(8,128)}, u32[]{:S(2)}) copy-start(f32[8,128,128]{2,1,0:T(8,128)} %fusion.35) | copy-start | bytes 1572868
  36.7 8.7 %copy-start.10 = (f32[8,64,64]{2,1,0:T(8,128)S(1)}, f32[8,64,64]{2,1,0:T(8,128)}, u32[]{:S(2)}) copy-start(f32[8,64,64]{2,1,0:T(8,128)} %param.14) | copy-start | bytes 393220
  36.7 8.7 %collective-permute-start.2 = (f32[8,64,128]{2,1,0:T(8,128)S(1)}, f32[8,64,128]{2,1,0:T(8,128)S(1)}, u32[]{:S(2)}, u32[]{:S(2)}) collective-permute-start(f32[8,64,128]{2,1,0:T(8,128)S(1)} %fusion), channel_id=1, source_target_pairs={{0,4},{4,8},{8,12},{12,16},{16,20},{20,24},{24,28},{1,5},{5,9},{9,... | collective-permute-start | bytes 786440 | tf_op jit(solution)/shard_map/ppermute | solution.py:25
  39.4 29.8 %collective-permute-start.8 = (f32[8,128,128]{2,1,0:T(8,128)S(1)}, f32[8,128,128]{2,1,0:T(8,128)S(1)}, u32[]{:S(2)}, u32[]{:S(2)}) collective-permute-start(f32[8,128,128]{2,1,0:T(8,128)S(1)} %sub.57), channel_id=1, source_target_pairs={{0,4},{4,8},{8,12},{12,16},{16,20},{20,24},{24,28},{1,5},{5,9},{9,... | collective-permute-start | bytes 1572872 | tf_op jit(solution)/shard_map/ppermute | solution.py:25
  46.3 7.8 %collective-permute-start.3 = (f32[4,64,128]{2,1,0:T(8,128)S(1)}, f32[4,64,128]{2,1,0:T(8,128)S(1)}, u32[]{:S(2)}, u32[]{:S(2)}) collective-permute-start(f32[4,64,128]{2,1,0:T(8,128)S(1)} %fusion.6), channel_id=1, source_target_pairs={{0,8},{4,12},{8,16},{12,20},{16,24},{20,28},{1,9},{5,13},{9,17},{1... | collective-permute-start | bytes 393224 | tf_op jit(solution)/shard_map/ppermute | solution.py:25
  49.1 5.0 %copy-start.8 = (f32[8,64,64]{2,1,0:T(8,128)S(1)}, f32[8,64,64]{2,1,0:T(8,128)}, u32[]{:S(2)}) copy-start(f32[8,64,64]{2,1,0:T(8,128)} %copy-done.7) | copy-start | bytes 393220
  49.7 6.9 %collective-permute-start.5 = (f32[4,64,128]{2,1,0:T(8,128)S(1)}, f32[4,64,128]{2,1,0:T(8,128)S(1)}, u32[]{:S(2)}, u32[]{:S(2)}) collective-permute-start(f32[4,64,128]{2,1,0:T(8,128)S(1)} %fusion.3), channel_id=1, source_target_pairs={{0,16},{4,20},{8,24},{12,28},{1,17},{5,21},{9,25},{13,29},{2,18},{... | collective-permute-start | bytes 393224 | tf_op jit(solution)/shard_map/ppermute | solution.py:25
  54.3 2.3 %copy-start.11 = (f32[8,64,64]{2,1,0:T(8,128)S(1)}, f32[8,64,64]{2,1,0:T(8,128)}, u32[]{:S(2)}) copy-start(f32[8,64,64]{2,1,0:T(8,128)} %fusion.36) | copy-start | bytes 393220
  54.9 8.3 %collective-permute-start.4 = (f32[4,64,128]{2,1,0:T(8,128)S(1)}, f32[4,64,128]{2,1,0:T(8,128)S(1)}, u32[]{:S(2)}, u32[]{:S(2)}) collective-permute-start(f32[4,64,128]{2,1,0:T(8,128)S(1)} %fusion.5), channel_id=1, source_target_pairs={{0,16},{4,20},{8,24},{12,28},{1,17},{5,21},{9,25},{13,29},{2,18},{... | collective-permute-start | bytes 393224 | tf_op jit(solution)/shard_map/ppermute | solution.py:25
  57.5 7.8 %collective-permute-start.6 = (f32[4,64,128]{2,1,0:T(8,128)S(1)}, f32[4,64,128]{2,1,0:T(8,128)S(1)}, u32[]{:S(2)}, u32[]{:S(2)}) collective-permute-start(f32[4,64,128]{2,1,0:T(8,128)S(1)} %fusion.2), channel_id=1, source_target_pairs={{0,8},{4,12},{8,16},{12,20},{16,24},{20,28},{1,9},{5,13},{9,17},{1... | collective-permute-start | bytes 393224 | tf_op jit(solution)/shard_map/ppermute | solution.py:25
  66.2 8.6 %collective-permute-start.7 = (f32[8,64,128]{2,1,0:T(8,128)S(1)}, f32[8,64,128]{2,1,0:T(8,128)S(1)}, u32[]{:S(2)}, u32[]{:S(2)}) collective-permute-start(f32[8,64,128]{2,1,0:T(8,128)S(1)} %maximum_subtract_fusion), channel_id=1, source_target_pairs={{0,4},{4,8},{8,12},{12,16},{16,20},{20,24},{24,28},{1,5},{5,9},{9,... | collective-permute-start | bytes 786440 | tf_op jit(solution)/shard_map/ppermute | solution.py:25

commit v7 on v6

--- a/solution.py
+++ b/solution.py
@@ -133,15 +133,23 @@
     rows = starts.shape[2]
     all_tiles = tile_count * lax.axis_size("space")
     block_base = lax.axis_index("space") * tile_count
-    open_cells = 1.0 - obstacle.astype(jnp.float32)
-
-    fields = jnp.stack([diffusivity, velocity[0], velocity[1], open_cells], axis=0)
-    layers = jnp.concatenate([starts, fields], axis=0)
+
+    def edge_rows(part):
+        return jnp.concatenate(
+            [
+                starts[:, :, part, :],
+                diffusivity[None, :, part, :],
+                velocity[:, :, part, :],
+                1.0 - obstacle[None, :, part, :].astype(jnp.float32),
+            ],
+            axis=0,
+        )
+
     space_count = lax.axis_size("space")
     forward = [(i, i + 1) for i in range(space_count - 1)]
     backward = [(i + 1, i) for i in range(space_count - 1)]
-    from_prev = lax.ppermute(layers[:, :, rows - HALO:, :], "space", forward)
-    from_next = lax.ppermute(layers[:, :, :HALO, :], "space", backward)
+    from_prev = lax.ppermute(edge_rows(slice(rows - HALO, None)), "space", forward)
+    from_next = lax.ppermute(edge_rows(slice(0, HALO)), "space", backward)
     west_nb = neighbors[:, 0]
     east_nb = neighbors[:, 1]
     west_ok = (west_nb != all_tiles).astype(jnp.int32)
@@ -169,6 +177,7 @@
     )
     correction = fine_ends - prolong(apply_coarse(restrict(starts), coarse_x, coarse_y))
     coarse_jump = restrict(correction)
+    late_x, late_y, coarse_jump = lax.optimization_barrier((coarse_x, coarse_y, coarse_jump))
     earlier_correction = passed_along(correction[-1], "tm", 1)
     tm_index = lax.axis_index("tm")
     tm_count = lax.axis_size("tm")
@@ -204,7 +213,7 @@
 
     if slice_count == 1:
         seed = jnp.where(tm_index == 0, apply_coarse(first_coarse, coarse_x, coarse_y), 0.0)
-        reached = prefix_over_tm(coarse_jump[0] + seed, coarse_x, coarse_y)
+        reached = prefix_over_tm(coarse_jump[0] + seed, late_x, late_y)
         coarse_applied = (reached - coarse_jump[0])[None]
     else:
         shifted_jump = jnp.concatenate(
@@ -220,6 +229,7 @@
         for n in range(1, slice_count):
             power_x = jnp.einsum("tij,tjk->tik", power_x, coarse_x, precision=exact_precision)
             power_y = jnp.einsum("tij,tjk->tik", power_y, coarse_y, precision=exact_precision)
+        power_x, power_y, states = lax.optimization_barrier((power_x, power_y, states))
         total = prefix_over_tm(states[-1], power_x, power_y)
         earlier = jnp.where(tm_index > 0, passed_along(total, "tm", 1), 0.0)
         own_coarse = []

time: 76.4 us -> 80.2 us (1.050)
  waiting for transfers between devices: 16.4 us -> 20.4 us
  matrix products: 13.2 us -> 12.1 us
    ppermute x2, waiting for transfers between devices: 0.01 us -> 2.61 us  [the longest x1 2.61 us: on_device(): from_next = lax.ppermute(edge_rows(slice(0, HALO)), 'space', backward)]
    slice x0 -> x2, local copies, waits for them, and re-layouts: none -> 1.95 us  [the longest x1 1 us: edge_rows(): velocity[:, :, part, :]]
    ppermute x7, waiting for transfers between devices: 16.3 us -> 17.8 us  [passed_along(): return lax.ppermute(block, axis, route)]
    unnamed x34 -> x20, local copies, waits for them, and re-layouts: 3.13 us -> 1.95 us
    another operation x1 -> x0, other arithmetic: 1.17 us -> none  [on_device(): jnp.stack([diffusivity, velocity[0], velocity[1], open_cells], axis=0)]
    sub x0 -> x1, other arithmetic: none -> 0.9 us  [edge_rows(): 1.0 - obstacle[None, :, part, :].astype(jnp.float32)]
    ppermute x7, starting transfers between devices: 14.7 us -> 15.5 us  [passed_along(): return lax.ppermute(block, axis, route)]
    concatenate x1 -> x2, other arithmetic: 1.88 us -> 1.5 us  [edge_rows(): jnp.concatenate([starts[:, :, part, :], diffusivity[None, :, part, :], ve...]
  transfers between devices with their start and end apart: 9 -> 9, of which waited for: 6 -> 7; matrix products, arithmetic and copies ran while one was open for 20% -> 20% of each run, Pallas kernels for 0% -> 0%
where the time goes in v7:
time: 80.2 us; the launch traced here: 79.7 us
  starting transfers between devices  21.3 us (27%)
  waiting for transfers between devices  20.4 us (25%)
  Pallas kernels  14.1 us (18%)
  matrix products  12.1 us (15%)
  local copies, waits for them, and re-layouts  6.42 us (8%)
  other arithmetic  4.26 us (5%)
  between operations  1.05 us (1%)
    ppermute x7, waiting for transfers between devices, passed_along(): return lax.ppermute(block, axis, route)  17.8 us
    ppermute x7, starting transfers between devices, passed_along(): return lax.ppermute(block, axis, route)  15.5 us
    pallas_call x1, Pallas kernels, fine_propagate(): pl.pallas_call(functools.partial(fine_kernel, slice_at), out_shape=jax.Sh...  14.1 us
    dot_general x8, matrix products, apply_coarse(): jnp.einsum('...tik,tlk->...til', mixed_x, matrix_y, precision=exact_preci...  7.08 us
    ppermute x1, starting transfers between devices, on_device(): lax.ppermute(edge_rows(slice(rows - HALO, None)), 'space', forward)  3.47 us
    dot_general x8, matrix products, apply_coarse(): jnp.einsum('tij,...tjk->...tik', matrix_x, coarse_values, precision=exact...  3.03 us
    ppermute x1, waiting for transfers between devices, on_device(): from_next = lax.ppermute(edge_rows(slice(0, HALO)), 'space', backward)  2.61 us
    ppermute x1, starting transfers between devices, on_device(): from_next = lax.ppermute(edge_rows(slice(0, HALO)), 'space', backward)  2.36 us
  transfers between devices with their start and end apart: 9, of which 7 were waited for; matrix products, arithmetic and copies ran while one was open for 20% of the time, Pallas kernels for 0%

profile of v7, /device:TPU:12, one launch (start us, length us, event | category | flops | bytes accessed | tf_op | source)
XLA Modules:
  0.0 79.7 jit_solution(900778603827978248)
XLA Ops:
  0.7 1.0 %fusion.34 = (f32[1,8,16,128]{3,2,1,0:T(8,128)S(1)}, f32[1,8,16,128]{3,2,1,0:T(8,128)S(1)}) fusion(f32[1,8,128,128]{3,2,1,0:T(8,128)} %param.8), kind=kLoop, calls=%fused_computation.60 | loop fusion | bytes 262144 | tf_op jit(solution)/shard_map/slice | solution.py:140
  1.6 1.0 %fusion.33 = (f32[2,8,16,128]{3,2,1,0:T(8,128)S(1)}, f32[2,8,16,128]{3,2,1,0:T(8,128)S(1)}) fusion(f32[2,8,128,128]{3,2,1,0:T(8,128)} %velocity_ref.1), kind=kLoop, calls=%fused_computation.59 | loop fusion | bytes 524288 | tf_op jit(solution)/shard_map/slice | solution.py:142
  2.6 0.9 %subtract_bitcast_fusion = (f32[1,8,16,128]{3,2,1,0:T(8,128)S(1)}, f32[1,8,16,128]{3,2,1,0:T(8,128)S(1)}, f32[1,8,16,128]{3,2,1,0:T(8,128)S(1)}, f32[1,8,16,128]{3,2,1,0:T(8,128)S(1)}) fusion(s32[8,128,128]{2,1,0:T(8,128)} %obstacle_ref.1, f32[8,128,128]{2,1,0:T(8,128)S(1)} %copy-done.3), kind=kLoop, calls=%fused_computation.39 | loop fusion | flops 65536 | bytes 524288 | tf_op jit(solution)/shard_map/sub | solution.py:143
  3.5 0.7 pad_maximum_fusion
  4.3 3.5 %collective-permute-start = (f32[5,8,16,128]{3,2,1,0:T(8,128)}, f32[5,8,16,128]{3,2,1,0:T(8,128)S(1)}, u32[]{:S(2)}, u32[]{:S(2)}) collective-permute-start(f32[5,8,16,128]{3,2,1,0:T(8,128)} %pad_maximum_fusion), channel_id=1, source_target_pairs={{0,1},{1,2},{2,3},{4,5},{5,6},{6,7},{8,9},{9,10},{10,11},{12,13},{... | collective-permute-start | bytes 983048 | tf_op jit(solution)/shard_map/ppermute | solution.py:151
  7.8 0.7 pad_maximum_fusion.1
  8.5 2.4 %collective-permute-start.1 = (f32[5,8,16,128]{3,2,1,0:T(8,128)}, f32[5,8,16,128]{3,2,1,0:T(8,128)S(1)}, u32[]{:S(2)}, u32[]{:S(2)}) collective-permute-start(f32[5,8,16,128]{3,2,1,0:T(8,128)} %pad_maximum_fusion.1), channel_id=1, source_target_pairs={{1,0},{2,1},{3,2},{5,4},{6,5},{7,6},{9,8},{10,9},{11,10},{13,12},{... | collective-permute-start | bytes 983048 | tf_op jit(solution)/shard_map/ppermute | solution.py:152
  11.1 0.8 slice.115
  11.9 0.8 slice.114
  13.7 1.1 %convolution_bitcast_fusion = f32[8,64,128]{2,1,0:T(8,128)} fusion(f32[8,64,64]{2,1,0:T(8,128)S(1)} %copy-done, f32[1,8,64,128]{3,2,1,0:T(8,128)S(1)} %copy-done.8, f32[1,8,64,128]{3,2,1,0:T(8,128)S(1)} %copy-done.7), kind=kOutput, calls=%fused_computation.1 | convolution fusion | flops 50462720 | bytes 917504 | tf_op jit(solution)/shard_map/tij,...tjk->...tik/dot_general | solution.py:37
  14.9 2.3 %fusion.35 = f32[8,64,128]{2,1,0:T(8,128)S(1)} fusion(f32[8,64,128]{2,1,0:T(8,128)} %convolution_bitcast_fusion, f32[8,128,128]{2,1,0:T(8,128)} %param.15), kind=kOutput, calls=%fused_computation.61 | convolution fusion | flops 100663296 | bytes 1048576 | tf_op jit(solution)/shard_map/...tik,tlk->...til/dot_general | solution.py:38
  17.2 2.6 %collective-permute-done.1.next_ref = f32[5,8,16,128]{3,2,1,0:T(8,128)S(1)} collective-permute-done((f32[5,8,16,128]{3,2,1,0:T(8,128)}, f32[5,8,16,128]{3,2,1,0:T(8,128)S(1)}, u32[]{:S(2)}, u32[]{:S(2)}) %collective-permute-start.1) | collective-permute-done | bytes 327712 | tf_op jit(solution)/shard_map/ppermute | solution.py:152
  19.8 0.6 copy-done.5
  20.4 14.1 %shard_map.95 = f32[8,128,128]{2,1,0:T(8,128)S(1)} custom-call(s32[8]{0:T(128)S(1)} %get-tuple-element.20.south_ref, s32[8]{0:T(128)S(1)} %get-tuple-element.19.north_ref, s32[8]{0:T(128)S(1)} %get-tuple-element.21.west_at_ref, s32[8]{0:T(128)S(1)} %get-tuple-element.18.east_at_ref, s32[8]{0:T(128)S(1)} %get-tuple-element.17.west_ok_ref, ...), custom_call_target="tpu_custom_call" | custom-call | tf_op jit(solution)/shard_map/pallas_call | solution.py:115
  35.1 1.9 %collective-permute-start.8 = (f32[8,128,128]{2,1,0:T(8,128)S(1)}, f32[8,128,128]{2,1,0:T(8,128)S(1)}, u32[]{:S(2)}, u32[]{:S(2)}) collective-permute-start(f32[8,128,128]{2,1,0:T(8,128)S(1)} %sub.65), channel_id=1, source_target_pairs={{0,4},{4,8},{8,12},{12,16},{16,20},{20,24},{24,28},{1,5},{5,9},{9,... | collective-permute-start | bytes 1572872 | tf_op jit(solution)/shard_map/ppermute | solution.py:25
  37.8 0.6 copy-done.6
  38.5 1.1 %fusion = f32[8,64,128]{2,1,0:T(8,128)S(1)} fusion(f32[8,128,64]{1,2,0:T(8,128)S(1)} %fusion.14, f32[8,128,128]{2,1,0:T(8,128)S(1)} %copy-done.6, f32[1,8,64,128]{3,2,1,0:T(8,128)S(1)} %add_multiply_fusion, pred[]{:T(512)S(6)} %eq.4), kind=kOutput, calls=%fused_computation.2 | convolution fusion | flops 100794368 | bytes 1310721 | tf_op jit(solution)/shard_map/...tik,tlk->...til/dot_general | solution.py:38
  39.6 3.5 %collective-permute-start.2 = (f32[8,64,128]{2,1,0:T(8,128)S(1)}, f32[8,64,128]{2,1,0:T(8,128)S(1)}, u32[]{:S(2)}, u32[]{:S(2)}) collective-permute-start(f32[8,64,128]{2,1,0:T(8,128)S(1)} %fusion), channel_id=1, source_target_pairs={{0,4},{4,8},{8,12},{12,16},{16,20},{20,24},{24,28},{1,5},{5,9},{9,... | collective-permute-start | bytes 786440 | tf_op jit(solution)/shard_map/ppermute | solution.py:25
  43.1 0.6 fusion.37
  43.8 0.6 fusion.39
  44.4 4.9 %collective-permute-done.2 = f32[8,64,128]{2,1,0:T(8,128)S(1)} collective-permute-done((f32[8,64,128]{2,1,0:T(8,128)S(1)}, f32[8,64,128]{2,1,0:T(8,128)S(1)}, u32[]{:S(2)}, u32[]{:S(2)}) %collective-permute-start.2) | collective-permute-done | bytes 262176 | tf_op jit(solution)/shard_map/ppermute | solution.py:25
  50.2 2.5 %collective-permute-start.3 = (f32[4,64,128]{2,1,0:T(8,128)S(1)}, f32[4,64,128]{2,1,0:T(8,128)S(1)}, u32[]{:S(2)}, u32[]{:S(2)}) collective-permute-start(f32[4,64,128]{2,1,0:T(8,128)S(1)} %fusion.6), channel_id=1, source_target_pairs={{0,8},{4,12},{8,16},{12,20},{16,24},{20,28},{1,9},{5,13},{9,17},{1... | collective-permute-start | bytes 393224 | tf_op jit(solution)/shard_map/ppermute | solution.py:25
  53.5 1.3 %collective-permute-start.5 = (f32[4,64,128]{2,1,0:T(8,128)S(1)}, f32[4,64,128]{2,1,0:T(8,128)S(1)}, u32[]{:S(2)}, u32[]{:S(2)}) collective-permute-start(f32[4,64,128]{2,1,0:T(8,128)S(1)} %fusion.3), channel_id=1, source_target_pairs={{0,16},{4,20},{8,24},{12,28},{1,17},{5,21},{9,25},{13,29},{2,18},{... | collective-permute-start | bytes 393224 | tf_op jit(solution)/shard_map/ppermute | solution.py:25
  54.8 3.2 %collective-permute-done.3 = f32[4,64,128]{2,1,0:T(8,128)S(1)} collective-permute-done((f32[4,64,128]{2,1,0:T(8,128)S(1)}, f32[4,64,128]{2,1,0:T(8,128)S(1)}, u32[]{:S(2)}, u32[]{:S(2)}) %collective-permute-start.3) | collective-permute-done | bytes 131104 | tf_op jit(solution)/shard_map/ppermute | solution.py:25
  58.9 1.3 %collective-permute-start.4 = (f32[4,64,128]{2,1,0:T(8,128)S(1)}, f32[4,64,128]{2,1,0:T(8,128)S(1)}, u32[]{:S(2)}, u32[]{:S(2)}) collective-permute-start(f32[4,64,128]{2,1,0:T(8,128)S(1)} %fusion.5), channel_id=1, source_target_pairs={{0,16},{4,20},{8,24},{12,28},{1,17},{5,21},{9,25},{13,29},{2,18},{... | collective-permute-start | bytes 393224 | tf_op jit(solution)/shard_map/ppermute | solution.py:25
  61.3 3.0 %collective-permute-start.6 = (f32[4,64,128]{2,1,0:T(8,128)S(1)}, f32[4,64,128]{2,1,0:T(8,128)S(1)}, u32[]{:S(2)}, u32[]{:S(2)}) collective-permute-start(f32[4,64,128]{2,1,0:T(8,128)S(1)} %fusion.2), channel_id=1, source_target_pairs={{0,8},{4,12},{8,16},{12,20},{16,24},{20,28},{1,9},{5,13},{9,17},{1... | collective-permute-start | bytes 393224 | tf_op jit(solution)/shard_map/ppermute | solution.py:25
  64.4 2.8 %collective-permute-done.4 = f32[4,64,128]{2,1,0:T(8,128)S(1)} collective-permute-done((f32[4,64,128]{2,1,0:T(8,128)S(1)}, f32[4,64,128]{2,1,0:T(8,128)S(1)}, u32[]{:S(2)}, u32[]{:S(2)}) %collective-permute-start.4) | collective-permute-done | bytes 131104 | tf_op jit(solution)/shard_map/ppermute | solution.py:25
  68.0 1.0 %collective-permute-done.6 = f32[4,64,128]{2,1,0:T(8,128)S(1)} collective-permute-done((f32[4,64,128]{2,1,0:T(8,128)S(1)}, f32[4,64,128]{2,1,0:T(8,128)S(1)}, u32[]{:S(2)}, u32[]{:S(2)}) %collective-permute-start.6) | collective-permute-done | bytes 131104 | tf_op jit(solution)/shard_map/ppermute | solution.py:25
  70.0 1.9 %collective-permute-start.7 = (f32[8,64,128]{2,1,0:T(8,128)S(1)}, f32[8,64,128]{2,1,0:T(8,128)S(1)}, u32[]{:S(2)}, u32[]{:S(2)}) collective-permute-start(f32[8,64,128]{2,1,0:T(8,128)S(1)} %maximum_subtract_fusion), channel_id=1, source_target_pairs={{0,4},{4,8},{8,12},{12,16},{16,20},{20,24},{24,28},{1,5},{5,9},{9,... | collective-permute-start | bytes 786440 | tf_op jit(solution)/shard_map/ppermute | solution.py:25
  72.1 0.9 %add_bitcast_fusion = f32[1,8,128,128]{3,2,1,0:T(8,128)} fusion(f32[8,128,128]{2,1,0:T(8,128)S(1)} %bitcast.79, f32[8,128,128]{2,1,0:T(8,128)S(1)} %sub.65), kind=kLoop, calls=%fused_computation.16 | loop fusion | flops 131072 | bytes 1572864 | tf_op jit(solution)/shard_map/add | solution.py:240
  73.0 5.6 %collective-permute-done.7 = f32[8,64,128]{2,1,0:T(8,128)S(1)} collective-permute-done((f32[8,64,128]{2,1,0:T(8,128)S(1)}, f32[8,64,128]{2,1,0:T(8,128)S(1)}, u32[]{:S(2)}, u32[]{:S(2)}) %collective-permute-start.7) | collective-permute-done | bytes 262176 | tf_op jit(solution)/shard_map/ppermute | solution.py:25
  78.8 0.9 %select_bitcast_fusion = f32[1,8,128,128]{3,2,1,0:T(8,128)} fusion(f32[8,128,128]{2,1,0:T(8,128)S(1)} %bitcast.77, f32[8,128,128]{2,1,0:T(8,128)S(1)} %collective-permute-done.8, pred[]{:T(512)S(6)} %eq.4, f32[1,8,128,128]{3,2,1,0:T(8,128)S(1)} %copy-done.1), kind=kLoop, calls=%fused_computation.15 | loop fusion | flops 393216 | bytes 2097153 | tf_op jit(solution)/shard_map/broadcast_in_dim | solution.py:245
  (48 shorter events, 8.4 us)
Async XLA Ops:
  0.6 12.0 %copy-start = (f32[8,64,64]{2,1,0:T(8,128)S(1)}, f32[8,64,64]{2,1,0:T(8,128)}, u32[]{:S(2)}) copy-start(f32[8,64,64]{2,1,0:T(8,128)} %param.14) | copy-start | bytes 393220
  0.6 2.0 %copy-start.3 = (f32[8,128,128]{2,1,0:T(8,128)S(1)}, f32[8,128,128]{2,1,0:T(8,128)}, u32[]{:S(2)}) copy-start(f32[8,128,128]{2,1,0:T(8,128)} %diffusivity_ref.1) | copy-start | bytes 1572868
  3.5 7.4 %copy-start.1 = (f32[1,8,128,128]{3,2,1,0:T(8,128)S(1)}, f32[1,8,128,128]{3,2,1,0:T(8,128)}, u32[]{:S(2)}) copy-start(f32[1,8,128,128]{3,2,1,0:T(8,128)} %param.8) | copy-start | bytes 1572868
  4.3 12.9 %collective-permute-start = (f32[5,8,16,128]{3,2,1,0:T(8,128)}, f32[5,8,16,128]{3,2,1,0:T(8,128)S(1)}, u32[]{:S(2)}, u32[]{:S(2)}) collective-permute-start(f32[5,8,16,128]{3,2,1,0:T(8,128)} %pad_maximum_fusion), channel_id=1, source_target_pairs={{0,1},{1,2},{2,3},{4,5},{5,6},{6,7},{8,9},{9,10},{10,11},{12,13},{... | collective-permute-start | bytes 983048 | tf_op jit(solution)/shard_map/ppermute | solution.py:151
  8.5 11.3 %collective-permute-start.1 = (f32[5,8,16,128]{3,2,1,0:T(8,128)}, f32[5,8,16,128]{3,2,1,0:T(8,128)S(1)}, u32[]{:S(2)}, u32[]{:S(2)}) collective-permute-start(f32[5,8,16,128]{3,2,1,0:T(8,128)} %pad_maximum_fusion.1), channel_id=1, source_target_pairs={{1,0},{2,1},{3,2},{5,4},{6,5},{7,6},{9,8},{10,9},{11,10},{13,12},{... | collective-permute-start | bytes 983048 | tf_op jit(solution)/shard_map/ppermute | solution.py:152
  12.7 1.0 %copy-start.7 = (f32[1,8,64,128]{3,2,1,0:T(8,128)S(1)}, f32[1,8,64,128]{3,2,1,0:T(8,128)}, u32[]{:S(2)}) copy-start(f32[1,8,64,128]{3,2,1,0:T(8,128)} %slice.115) | copy-start | bytes 786436
  12.7 1.0 %copy-start.8 = (f32[1,8,64,128]{3,2,1,0:T(8,128)S(1)}, f32[1,8,64,128]{3,2,1,0:T(8,128)}, u32[]{:S(2)}) copy-start(f32[1,8,64,128]{3,2,1,0:T(8,128)} %slice.114) | copy-start | bytes 786436
  12.7 2.1 %copy-start.9 = (s32[8,4]{0,1:T(4,128)S(1)}, s32[8,4]{0,1:T(4,128)}, u32[]{:S(2)}) copy-start(s32[8,4]{0,1:T(4,128)} %param.13) | copy-start | bytes 388
  13.7 6.1 %copy-start.2 = (f32[2,8,128,128]{3,2,1,0:T(8,128)S(1)}, f32[2,8,128,128]{3,2,1,0:T(8,128)}, u32[]{:S(2)}) copy-start(f32[2,8,128,128]{3,2,1,0:T(8,128)} %velocity_ref.1) | copy-start | bytes 3145732
  14.8 4.9 %copy-start.4 = (s32[8,128,128]{2,1,0:T(8,128)S(1)}, s32[8,128,128]{2,1,0:T(8,128)}, u32[]{:S(2)}) copy-start(s32[8,128,128]{2,1,0:T(8,128)} %obstacle_ref.1) | copy-start | bytes 1572868
  19.8 0.7 copy-start.5
  35.1 37.9 %collective-permute-start.8 = (f32[8,128,128]{2,1,0:T(8,128)S(1)}, f32[8,128,128]{2,1,0:T(8,128)S(1)}, u32[]{:S(2)}, u32[]{:S(2)}) collective-permute-start(f32[8,128,128]{2,1,0:T(8,128)S(1)} %sub.65), channel_id=1, source_target_pairs={{0,4},{4,8},{8,12},{12,16},{16,20},{20,24},{24,28},{1,5},{5,9},{9,... | collective-permute-start | bytes 1572872 | tf_op jit(solution)/shard_map/ppermute | solution.py:25
  37.4 1.0 %copy-start.6 = (f32[8,128,128]{2,1,0:T(8,128)S(1)}, f32[8,128,128]{2,1,0:T(8,128)}, u32[]{:S(2)}) copy-start(f32[8,128,128]{2,1,0:T(8,128)} %param.15) | copy-start | bytes 1572868
  39.6 9.7 %collective-permute-start.2 = (f32[8,64,128]{2,1,0:T(8,128)S(1)}, f32[8,64,128]{2,1,0:T(8,128)S(1)}, u32[]{:S(2)}, u32[]{:S(2)}) collective-permute-start(f32[8,64,128]{2,1,0:T(8,128)S(1)} %fusion), channel_id=1, source_target_pairs={{0,4},{4,8},{8,12},{12,16},{16,20},{20,24},{24,28},{1,5},{5,9},{9,... | collective-permute-start | bytes 786440 | tf_op jit(solution)/shard_map/ppermute | solution.py:25
  50.2 7.9 %collective-permute-start.3 = (f32[4,64,128]{2,1,0:T(8,128)S(1)}, f32[4,64,128]{2,1,0:T(8,128)S(1)}, u32[]{:S(2)}, u32[]{:S(2)}) collective-permute-start(f32[4,64,128]{2,1,0:T(8,128)S(1)} %fusion.6), channel_id=1, source_target_pairs={{0,8},{4,12},{8,16},{12,20},{16,24},{20,28},{1,9},{5,13},{9,17},{1... | collective-permute-start | bytes 393224 | tf_op jit(solution)/shard_map/ppermute | solution.py:25
  53.5 6.9 %collective-permute-start.5 = (f32[4,64,128]{2,1,0:T(8,128)S(1)}, f32[4,64,128]{2,1,0:T(8,128)S(1)}, u32[]{:S(2)}, u32[]{:S(2)}) collective-permute-start(f32[4,64,128]{2,1,0:T(8,128)S(1)} %fusion.3), channel_id=1, source_target_pairs={{0,16},{4,20},{8,24},{12,28},{1,17},{5,21},{9,25},{13,29},{2,18},{... | collective-permute-start | bytes 393224 | tf_op jit(solution)/shard_map/ppermute | solution.py:25
  58.9 8.3 %collective-permute-start.4 = (f32[4,64,128]{2,1,0:T(8,128)S(1)}, f32[4,64,128]{2,1,0:T(8,128)S(1)}, u32[]{:S(2)}, u32[]{:S(2)}) collective-permute-start(f32[4,64,128]{2,1,0:T(8,128)S(1)} %fusion.5), channel_id=1, source_target_pairs={{0,16},{4,20},{8,24},{12,28},{1,17},{5,21},{9,25},{13,29},{2,18},{... | collective-permute-start | bytes 393224 | tf_op jit(solution)/shard_map/ppermute | solution.py:25
  61.3 7.8 %collective-permute-start.6 = (f32[4,64,128]{2,1,0:T(8,128)S(1)}, f32[4,64,128]{2,1,0:T(8,128)S(1)}, u32[]{:S(2)}, u32[]{:S(2)}) collective-permute-start(f32[4,64,128]{2,1,0:T(8,128)S(1)} %fusion.2), channel_id=1, source_target_pairs={{0,8},{4,12},{8,16},{12,20},{16,24},{20,28},{1,9},{5,13},{9,17},{1... | collective-permute-start | bytes 393224 | tf_op jit(solution)/shard_map/ppermute | solution.py:25
  70.0 8.6 %collective-permute-start.7 = (f32[8,64,128]{2,1,0:T(8,128)S(1)}, f32[8,64,128]{2,1,0:T(8,128)S(1)}, u32[]{:S(2)}, u32[]{:S(2)}) collective-permute-start(f32[8,64,128]{2,1,0:T(8,128)S(1)} %maximum_subtract_fusion), channel_id=1, source_target_pairs={{0,4},{4,8},{8,12},{12,16},{16,20},{20,24},{24,28},{1,5},{5,9},{9,... | collective-permute-start | bytes 786440 | tf_op jit(solution)/shard_map/ppermute | solution.py:25

commit v8 on v6

--- a/solution.py
+++ b/solution.py
@@ -9,6 +9,7 @@
 
 SUB = 12
 HALO = 16
+PAD = 8
 
 
 exact_precision = lax.Precision.HIGHEST
@@ -46,16 +47,15 @@
     lanes = u_ref.shape[2]
     total = rows + 2 * HALO
     layers = prev_ref.shape[0]
-    for b in range(2):
-        state_ref[b, tiles] = jnp.zeros((total, lanes), jnp.float32)
+    state_ref[...] = jnp.zeros(state_ref.shape, jnp.float32)
     for i in range(tiles):
         west_at = west_at_ref[i]
         east_at = east_at_ref[i]
         west_ok = west_ok_ref[i] > 0
         east_ok = east_ok_ref[i] > 0
-        state_ref[0, i, pl.ds(0, HALO), :] = jnp.where(west_ok, prev_ref[slice_at, west_at], 0.0)
-        state_ref[0, i, pl.ds(HALO, rows), :] = u_ref[i]
-        state_ref[0, i, pl.ds(HALO + rows, HALO), :] = jnp.where(
+        state_ref[0, i, pl.ds(PAD, HALO), :] = jnp.where(west_ok, prev_ref[slice_at, west_at], 0.0)
+        state_ref[0, i, pl.ds(PAD + HALO, rows), :] = u_ref[i]
+        state_ref[0, i, pl.ds(PAD + HALO + rows, HALO), :] = jnp.where(
             east_ok, next_ref[slice_at, east_at], 0.0
         )
         own = (
@@ -64,13 +64,14 @@
             velocity_ref[1, i],
             1.0 - obstacle_ref[i].astype(jnp.float32),
         )
+        factor = (1.0, 0.5, 0.5, 1.0)
         for f in range(4):
             field_at = layers - 4 + f
-            field_ref[f, i, pl.ds(0, HALO), :] = jnp.where(
+            field_ref[f, i, pl.ds(0, HALO), :] = factor[f] * jnp.where(
                 west_ok, prev_ref[field_at, west_at], 0.0
             )
-            field_ref[f, i, pl.ds(HALO, rows), :] = own[f]
-            field_ref[f, i, pl.ds(HALO + rows, HALO), :] = jnp.where(
+            field_ref[f, i, pl.ds(HALO, rows), :] = factor[f] * own[f]
+            field_ref[f, i, pl.ds(HALO + rows, HALO), :] = factor[f] * jnp.where(
                 east_ok, next_ref[field_at, east_at], 0.0
             )
 
@@ -83,28 +84,30 @@
         dst = 1 - src
         strength = scale_ref[s]
         for i in range(tiles):
-            current = state_ref[src, i]
-            south_tile = state_ref[src, south_ref[i]]
-            north_tile = state_ref[src, north_ref[i]]
-            from_west = pltpu.roll(current, 1, 0)
-            from_east = pltpu.roll(current, total - 1, 0)
+            current = state_ref[src, i, pl.ds(PAD, total), :]
+            south_tile = state_ref[src, south_ref[i], pl.ds(PAD, total), :]
+            north_tile = state_ref[src, north_ref[i], pl.ds(PAD, total), :]
+            from_west = state_ref[src, i, pl.ds(PAD - 1, total), :]
+            from_east = state_ref[src, i, pl.ds(PAD + 1, total), :]
             from_south = pltpu.roll(jnp.where(last_lane, south_tile, current), 1, 1)
             from_north = pltpu.roll(jnp.where(first_lane, north_tile, current), lanes - 1, 1)
             diffusivity = field_ref[0, i]
-            speed_x = field_ref[1, i]
-            speed_y = field_ref[2, i]
+            half_speed_x = field_ref[1, i]
+            half_speed_y = field_ref[2, i]
             open_cells = field_ref[3, i]
             laplace = from_west + from_east + from_south + from_north - 4.0 * current
-            transport = speed_x * (from_east - from_west) + speed_y * (from_north - from_south)
-            state_ref[dst, i] = open_cells * (
-                current + strength * diffusivity * laplace - 0.5 * transport
+            half_transport = half_speed_x * (from_east - from_west) + half_speed_y * (
+                from_north - from_south
+            )
+            state_ref[dst, i, pl.ds(PAD, total), :] = open_cells * (
+                current + strength * diffusivity * laplace - half_transport
             )
         return carry
 
     lax.fori_loop(0, SUB, substep, 0)
     last = SUB % 2
     for i in range(tiles):
-        out_ref[i] = state_ref[last, i, pl.ds(HALO, rows), :]
+        out_ref[i] = state_ref[last, i, pl.ds(PAD + HALO, rows), :]
 
 
 def fine_propagate(slice_at, u, diffusivity, velocity, obstacle, from_prev, from_next, indices, scale):
@@ -118,7 +121,7 @@
         in_specs=[pl.BlockSpec(memory_space=smem)] * 7 + [pl.BlockSpec(memory_space=vmem)] * 6,
         out_specs=pl.BlockSpec(memory_space=vmem),
         scratch_shapes=[
-            pltpu.VMEM((2, tiles + 1, total, lanes), jnp.float32),
+            pltpu.VMEM((2, tiles + 1, total + 2 * PAD, lanes), jnp.float32),
             pltpu.VMEM((4, tiles, total, lanes), jnp.float32),
         ],
         compiler_params=pltpu.CompilerParams(vmem_limit_bytes=48 * 1024 * 1024),

time: 76.4 us -> 76 us (level)
  no operation moved by 1% of the time
where the time goes in v8:
time: 76 us; the launch traced here: 75.5 us
  starting transfers between devices  20.5 us (27%)
  waiting for transfers between devices  16.4 us (22%)
  Pallas kernels  13.7 us (18%)
  matrix products  13.2 us (17%)
  local copies, waits for them, and re-layouts  5.67 us (7%)
  other arithmetic  4.93 us (6%)
  between operations  1.07 us (1%)
    ppermute x7, waiting for transfers between devices, passed_along(): return lax.ppermute(block, axis, route)  16.4 us
    ppermute x7, starting transfers between devices, passed_along(): return lax.ppermute(block, axis, route)  14.6 us
    pallas_call x1, Pallas kernels, fine_propagate(): pl.pallas_call(functools.partial(fine_kernel, slice_at), out_shape=jax.Sh...  13.7 us
    dot_general x8, matrix products, apply_coarse(): jnp.einsum('...tik,tlk->...til', mixed_x, matrix_y, precision=exact_preci...  6.62 us
    ppermute x1, starting transfers between devices, on_device(): from_prev = lax.ppermute(layers[:, :, rows - HALO:, :], 'space', forward)  3.47 us
    unnamed x34, local copies, waits for them, and re-layouts  3.13 us
    dot_general x8, matrix products, apply_coarse(): jnp.einsum('tij,...tjk->...tik', matrix_x, coarse_values, precision=exact...  3.07 us
    ppermute x1, starting transfers between devices, on_device(): from_next = lax.ppermute(layers[:, :, :HALO, :], 'space', backward)  2.37 us
  transfers between devices with their start and end apart: 9, of which 6 were waited for; matrix products, arithmetic and copies ran while one was open for 20% of the time, Pallas kernels for 0%

profile of v8, /device:TPU:12, one launch (start us, length us, event | category | flops | bytes accessed | tf_op | source)
XLA Modules:
  0.0 75.5 jit_solution(17481669075023247233)
XLA Ops:
  0.6 1.2 %subtract_bitcast_fusion = f32[1,8,128,128]{3,2,1,0:T(8,128)S(1)} fusion(s32[8,128,128]{2,1,0:T(8,128)} %obstacle_ref.1), kind=kLoop, calls=%fused_computation.17 | loop fusion | flops 262144 | bytes 1048576 | tf_op jit(solution)/shard_map/stack | solution.py:141
  2.0 1.9 %pad_maximum_fusion = (f32[5,8,16,128]{3,2,1,0:T(8,128)}, f32[5,8,16,128]{3,2,1,0:T(8,128)}) fusion(f32[1,8,128,128]{3,2,1,0:T(8,128)S(1)} %subtract_bitcast_fusion, f32[2,8,128,128]{3,2,1,0:T(8,128)} %velocity_ref.1, f32[1,8,128,128]{3,2,1,0:T(8,128)S(1)} %bitcast.70, f32[1,8,128,128]{3,2,1,0:T(8,128)S(1)} %copy-done), kind=kLoop, calls=%fused_computation.18 | loop fusion | flops 491520 | bytes 3276800 | tf_op jit(solution)/shard_map/concatenate | solution.py:142
  3.9 3.5 %collective-permute-start = (f32[5,8,16,128]{3,2,1,0:T(8,128)}, f32[5,8,16,128]{3,2,1,0:T(8,128)S(1)}, u32[]{:S(2)}, u32[]{:S(2)}) collective-permute-start(f32[5,8,16,128]{3,2,1,0:T(8,128)} %get-tuple-element.3), channel_id=1, source_target_pairs={{0,1},{1,2},{2,3},{4,5},{5,6},{6,7},{8,9},{9,10},{10,11},{12,13},{... | collective-permute-start | bytes 983048 | tf_op jit(solution)/shard_map/ppermute | solution.py:146
  7.3 2.4 %collective-permute-start.1 = (f32[5,8,16,128]{3,2,1,0:T(8,128)}, f32[5,8,16,128]{3,2,1,0:T(8,128)S(1)}, u32[]{:S(2)}, u32[]{:S(2)}) collective-permute-start(f32[5,8,16,128]{3,2,1,0:T(8,128)} %get-tuple-element.2), channel_id=1, source_target_pairs={{1,0},{2,1},{3,2},{5,4},{6,5},{7,6},{9,8},{10,9},{11,10},{13,12},{... | collective-permute-start | bytes 983048 | tf_op jit(solution)/shard_map/ppermute | solution.py:147
  9.7 0.8 %slice.93 = f32[1,8,64,128]{3,2,1,0:T(8,128)} slice(f32[1,8,128,128]{3,2,1,0:T(8,128)S(1)} %copy-done), slice={[0:1:1], [0:8:1], [0:128:2], [0:128:1]} | slice | bytes 524288 | tf_op jit(solution)/shard_map/slice | solution.py:30
  10.5 0.8 %slice.94 = f32[1,8,64,128]{3,2,1,0:T(8,128)} slice(f32[1,8,128,128]{3,2,1,0:T(8,128)S(1)} %copy-done), slice={[0:1:1], [0:8:1], [1:128:2], [0:128:1]} | slice | bytes 524288 | tf_op jit(solution)/shard_map/slice | solution.py:30
  11.5 0.8 %copy-done.9 = f32[8,64,64]{2,1,0:T(8,128)S(1)} copy-done((f32[8,64,64]{2,1,0:T(8,128)S(1)}, f32[8,64,64]{2,1,0:T(8,128)}, u32[]{:S(2)}) %copy-start.9) | copy-done | bytes 131096
  12.8 1.1 %fusion.36 = f32[8,64,64]{2,1,0:T(8,128)} fusion(f32[8,64,64]{2,1,0:T(8,128)S(1)} %fusion.34), kind=kOutput, calls=%fused_computation.61 | convolution fusion | flops 25165824 | bytes 262144 | tf_op jit(solution)/shard_map/tij,tjk->tik/dot_general | solution.py:189
  14.3 0.6 copy-done.5
  14.9 1.8 %fusion.33 = f32[8,64,128]{2,1,0:T(8,128)} fusion(f32[8,64,128]{2,1,0:T(8,128)S(1)} %convolution_bitcast_fusion, f32[8,128,128]{2,1,0:T(8,128)S(1)} %copy-done.5), kind=kOutput, calls=%fused_computation.58 | convolution fusion | flops 100663296 | bytes 1048576 | tf_op jit(solution)/shard_map/...tik,tlk->...til/dot_general | solution.py:39
  16.7 1.1 %fusion.14 = f32[8,128,64]{1,2,0:T(8,128)} fusion(f32[8,64,64]{2,1,0:T(8,128)S(1)} %copy-done.9, f32[8,64,128]{2,1,0:T(8,128)S(1)} %slice.97, f32[8,64,128]{2,1,0:T(8,128)S(1)} %slice.98), kind=kOutput, calls=%fused_computation.30 | convolution fusion | flops 50462720 | bytes 917504 | tf_op jit(solution)/shard_map/tij,...tjk->...tik/dot_general | solution.py:38
  17.9 1.4 %fusion.35 = f32[8,128,128]{2,1,0:T(8,128)} fusion(f32[8,128,128]{2,1,0:T(8,128)S(1)} %copy-done.5), kind=kOutput, calls=%fused_computation.60 | convolution fusion | flops 201326592 | bytes 1048576 | tf_op jit(solution)/shard_map/tij,tjk->tik/dot_general | solution.py:190
  19.4 0.6 copy-done.4
  20.0 13.7 %shard_map.95 = f32[8,128,128]{2,1,0:T(8,128)S(1)} custom-call(s32[8]{0:T(128)S(1)} %get-tuple-element.8.south_ref, s32[8]{0:T(128)S(1)} %get-tuple-element.7.north_ref, s32[8]{0:T(128)S(1)} %get-tuple-element.9.west_at_ref, s32[8]{0:T(128)S(1)} %get-tuple-element.6.east_at_ref, s32[8]{0:T(128)S(1)} %get-tuple-element.5.west_ok_ref, ...), custom_call_target="tpu_custom_call" | custom-call | tf_op jit(solution)/shard_map/pallas_call | solution.py:118
  34.3 0.8 %copy-done.15 = f32[8,128,64]{1,2,0:T(8,128)S(1)} copy-done((f32[8,128,64]{1,2,0:T(8,128)S(1)}, f32[8,128,64]{1,2,0:T(8,128)}, u32[]{:S(2)}) %copy-start.15) | copy-done | bytes 262168
  35.1 1.1 %fusion = f32[8,64,128]{2,1,0:T(8,128)S(1)} fusion(f32[8,128,64]{1,2,0:T(8,128)S(1)} %copy-done.15, f32[8,128,128]{2,1,0:T(8,128)S(1)} %copy-done.5, pred[]{:T(512)S(6)} %eq.4, f32[1,8,64,128]{3,2,1,0:T(8,128)S(1)} %slice.95, f32[1,8,64,128]{3,2,1,0:T(8,128)S(1)} %slice.96), kind=kOutput, calls=%fused_computation.2 | convolution fusion | flops 100925440 | bytes 1572865 | tf_op jit(solution)/shard_map/...tik,tlk->...til/dot_general | solution.py:39
  36.3 2.1 %collective-permute-start.2 = (f32[8,64,128]{2,1,0:T(8,128)S(1)}, f32[8,64,128]{2,1,0:T(8,128)S(1)}, u32[]{:S(2)}, u32[]{:S(2)}) collective-permute-start(f32[8,64,128]{2,1,0:T(8,128)S(1)} %fusion), channel_id=1, source_target_pairs={{0,4},{4,8},{8,12},{12,16},{16,20},{20,24},{24,28},{1,5},{5,9},{9,... | collective-permute-start | bytes 786440 | tf_op jit(solution)/shard_map/ppermute | solution.py:26
  38.3 0.6 fusion.37
  39.0 3.5 %collective-permute-start.8 = (f32[8,128,128]{2,1,0:T(8,128)S(1)}, f32[8,128,128]{2,1,0:T(8,128)S(1)}, u32[]{:S(2)}, u32[]{:S(2)}) collective-permute-start(f32[8,128,128]{2,1,0:T(8,128)S(1)} %sub.57), channel_id=1, source_target_pairs={{0,4},{4,8},{8,12},{12,16},{16,20},{20,24},{24,28},{1,5},{5,9},{9,... | collective-permute-start | bytes 1572872 | tf_op jit(solution)/shard_map/ppermute | solution.py:26
  42.5 2.5 %collective-permute-done.2 = f32[8,64,128]{2,1,0:T(8,128)S(1)} collective-permute-done((f32[8,64,128]{2,1,0:T(8,128)S(1)}, f32[8,64,128]{2,1,0:T(8,128)S(1)}, u32[]{:S(2)}, u32[]{:S(2)}) %collective-permute-start.2) | collective-permute-done | bytes 262176 | tf_op jit(solution)/shard_map/ppermute | solution.py:26
  45.9 2.5 %collective-permute-start.3 = (f32[4,64,128]{2,1,0:T(8,128)S(1)}, f32[4,64,128]{2,1,0:T(8,128)S(1)}, u32[]{:S(2)}, u32[]{:S(2)}) collective-permute-start(f32[4,64,128]{2,1,0:T(8,128)S(1)} %fusion.6), channel_id=1, source_target_pairs={{0,8},{4,12},{8,16},{12,20},{16,24},{20,28},{1,9},{5,13},{9,17},{1... | collective-permute-start | bytes 393224 | tf_op jit(solution)/shard_map/ppermute | solution.py:26
  49.3 1.3 %collective-permute-start.5 = (f32[4,64,128]{2,1,0:T(8,128)S(1)}, f32[4,64,128]{2,1,0:T(8,128)S(1)}, u32[]{:S(2)}, u32[]{:S(2)}) collective-permute-start(f32[4,64,128]{2,1,0:T(8,128)S(1)} %fusion.3), channel_id=1, source_target_pairs={{0,16},{4,20},{8,24},{12,28},{1,17},{5,21},{9,25},{13,29},{2,18},{... | collective-permute-start | bytes 393224 | tf_op jit(solution)/shard_map/ppermute | solution.py:26
  50.6 3.1 %collective-permute-done.3 = f32[4,64,128]{2,1,0:T(8,128)S(1)} collective-permute-done((f32[4,64,128]{2,1,0:T(8,128)S(1)}, f32[4,64,128]{2,1,0:T(8,128)S(1)}, u32[]{:S(2)}, u32[]{:S(2)}) %collective-permute-start.3) | collective-permute-done | bytes 131104 | tf_op jit(solution)/shard_map/ppermute | solution.py:26
  54.5 1.3 %collective-permute-start.4 = (f32[4,64,128]{2,1,0:T(8,128)S(1)}, f32[4,64,128]{2,1,0:T(8,128)S(1)}, u32[]{:S(2)}, u32[]{:S(2)}) collective-permute-start(f32[4,64,128]{2,1,0:T(8,128)S(1)} %fusion.5), channel_id=1, source_target_pairs={{0,16},{4,20},{8,24},{12,28},{1,17},{5,21},{9,25},{13,29},{2,18},{... | collective-permute-start | bytes 393224 | tf_op jit(solution)/shard_map/ppermute | solution.py:26
  57.1 2.1 %collective-permute-start.6 = (f32[4,64,128]{2,1,0:T(8,128)S(1)}, f32[4,64,128]{2,1,0:T(8,128)S(1)}, u32[]{:S(2)}, u32[]{:S(2)}) collective-permute-start(f32[4,64,128]{2,1,0:T(8,128)S(1)} %fusion.2), channel_id=1, source_target_pairs={{0,8},{4,12},{8,16},{12,20},{16,24},{20,28},{1,9},{5,13},{9,17},{1... | collective-permute-start | bytes 393224 | tf_op jit(solution)/shard_map/ppermute | solution.py:26
  59.2 3.6 %collective-permute-done.4 = f32[4,64,128]{2,1,0:T(8,128)S(1)} collective-permute-done((f32[4,64,128]{2,1,0:T(8,128)S(1)}, f32[4,64,128]{2,1,0:T(8,128)S(1)}, u32[]{:S(2)}, u32[]{:S(2)}) %collective-permute-start.4) | collective-permute-done | bytes 131104 | tf_op jit(solution)/shard_map/ppermute | solution.py:26
  63.7 1.2 %collective-permute-done.6 = f32[4,64,128]{2,1,0:T(8,128)S(1)} collective-permute-done((f32[4,64,128]{2,1,0:T(8,128)S(1)}, f32[4,64,128]{2,1,0:T(8,128)S(1)}, u32[]{:S(2)}, u32[]{:S(2)}) %collective-permute-start.6) | collective-permute-done | bytes 131104 | tf_op jit(solution)/shard_map/ppermute | solution.py:26
  65.1 0.6 fusion.1
  65.8 1.9 %collective-permute-start.7 = (f32[8,64,128]{2,1,0:T(8,128)S(1)}, f32[8,64,128]{2,1,0:T(8,128)S(1)}, u32[]{:S(2)}, u32[]{:S(2)}) collective-permute-start(f32[8,64,128]{2,1,0:T(8,128)S(1)} %maximum_subtract_fusion), channel_id=1, source_target_pairs={{0,4},{4,8},{8,12},{12,16},{16,20},{20,24},{24,28},{1,5},{5,9},{9,... | collective-permute-start | bytes 786440 | tf_op jit(solution)/shard_map/ppermute | solution.py:26
  67.9 0.9 %add_bitcast_fusion = f32[1,8,128,128]{3,2,1,0:T(8,128)} fusion(f32[8,128,128]{2,1,0:T(8,128)S(1)} %bitcast.75, f32[8,128,128]{2,1,0:T(8,128)S(1)} %sub.57), kind=kLoop, calls=%fused_computation.16 | loop fusion | flops 131072 | bytes 1572864 | tf_op jit(solution)/shard_map/add | solution.py:233
  68.8 5.6 %collective-permute-done.7 = f32[8,64,128]{2,1,0:T(8,128)S(1)} collective-permute-done((f32[8,64,128]{2,1,0:T(8,128)S(1)}, f32[8,64,128]{2,1,0:T(8,128)S(1)}, u32[]{:S(2)}, u32[]{:S(2)}) %collective-permute-start.7) | collective-permute-done | bytes 262176 | tf_op jit(solution)/shard_map/ppermute | solution.py:26
  74.6 0.9 %select_bitcast_fusion = f32[1,8,128,128]{3,2,1,0:T(8,128)} fusion(f32[8,128,128]{2,1,0:T(8,128)S(1)} %bitcast.73, f32[8,128,128]{2,1,0:T(8,128)S(1)} %collective-permute-done.8, pred[]{:T(512)S(6)} %eq.4, f32[1,8,128,128]{3,2,1,0:T(8,128)S(1)} %copy-done), kind=kLoop, calls=%fused_computation.15 | loop fusion | flops 393216 | bytes 2097153 | tf_op jit(solution)/shard_map/broadcast_in_dim | solution.py:238
  (58 shorter events, 7.1 us)
Async XLA Ops:
  0.6 1.2 %copy-start = (f32[1,8,128,128]{3,2,1,0:T(8,128)S(1)}, f32[1,8,128,128]{3,2,1,0:T(8,128)}, u32[]{:S(2)}) copy-start(f32[1,8,128,128]{3,2,1,0:T(8,128)} %param.8) | copy-start | bytes 1572868
  0.6 1.3 %copy-start.2 = (f32[8,128,128]{2,1,0:T(8,128)S(1)}, f32[8,128,128]{2,1,0:T(8,128)}, u32[]{:S(2)}) copy-start(f32[8,128,128]{2,1,0:T(8,128)} %diffusivity_ref.1) | copy-start | bytes 1572868
  3.9 15.5 %collective-permute-start = (f32[5,8,16,128]{3,2,1,0:T(8,128)}, f32[5,8,16,128]{3,2,1,0:T(8,128)S(1)}, u32[]{:S(2)}, u32[]{:S(2)}) collective-permute-start(f32[5,8,16,128]{3,2,1,0:T(8,128)} %get-tuple-element.3), channel_id=1, source_target_pairs={{0,1},{1,2},{2,3},{4,5},{5,6},{6,7},{8,9},{9,10},{10,11},{12,13},{... | collective-permute-start | bytes 983048 | tf_op jit(solution)/shard_map/ppermute | solution.py:146
  7.3 12.0 %collective-permute-start.1 = (f32[5,8,16,128]{3,2,1,0:T(8,128)}, f32[5,8,16,128]{3,2,1,0:T(8,128)S(1)}, u32[]{:S(2)}, u32[]{:S(2)}) collective-permute-start(f32[5,8,16,128]{3,2,1,0:T(8,128)} %get-tuple-element.2), channel_id=1, source_target_pairs={{1,0},{2,1},{3,2},{5,4},{6,5},{7,6},{9,8},{10,9},{11,10},{13,12},{... | collective-permute-start | bytes 983048 | tf_op jit(solution)/shard_map/ppermute | solution.py:147
  11.4 1.0 %copy-start.9 = (f32[8,64,64]{2,1,0:T(8,128)S(1)}, f32[8,64,64]{2,1,0:T(8,128)}, u32[]{:S(2)}) copy-start(f32[8,64,64]{2,1,0:T(8,128)} %param.14) | copy-start | bytes 393220
  12.7 1.1 %copy-start.7 = (f32[8,64,64]{2,1,0:T(8,128)}, f32[8,64,64]{2,1,0:T(8,128)S(1)}, u32[]{:S(2)}) copy-start(f32[8,64,64]{2,1,0:T(8,128)S(1)} %fusion.34) | copy-start | bytes 393220
  12.7 1.1 %copy-start.13 = (f32[1,8,64,128]{3,2,1,0:T(8,128)S(1)}, f32[1,8,64,128]{3,2,1,0:T(8,128)}, u32[]{:S(2)}) copy-start(f32[1,8,64,128]{3,2,1,0:T(8,128)} %slice.93) | copy-start | bytes 786436
  12.8 1.1 %copy-start.14 = (f32[1,8,64,128]{3,2,1,0:T(8,128)S(1)}, f32[1,8,64,128]{3,2,1,0:T(8,128)}, u32[]{:S(2)}) copy-start(f32[1,8,64,128]{3,2,1,0:T(8,128)} %slice.94) | copy-start | bytes 786436
  13.9 1.0 %copy-start.5 = (f32[8,128,128]{2,1,0:T(8,128)S(1)}, f32[8,128,128]{2,1,0:T(8,128)}, u32[]{:S(2)}) copy-start(f32[8,128,128]{2,1,0:T(8,128)} %param.15) | copy-start | bytes 1572868
  16.7 1.1 %copy-start.16 = (s32[8,4]{0,1:T(4,128)S(1)}, s32[8,4]{0,1:T(4,128)}, u32[]{:S(2)}) copy-start(s32[8,4]{0,1:T(4,128)} %param.13) | copy-start | bytes 388
  17.9 1.5 %copy-start.1 = (f32[2,8,128,128]{3,2,1,0:T(8,128)S(1)}, f32[2,8,128,128]{3,2,1,0:T(8,128)}, u32[]{:S(2)}) copy-start(f32[2,8,128,128]{3,2,1,0:T(8,128)} %velocity_ref.1) | copy-start | bytes 3145732
  17.9 1.5 %copy-start.3 = (s32[8,128,128]{2,1,0:T(8,128)S(1)}, s32[8,128,128]{2,1,0:T(8,128)}, u32[]{:S(2)}) copy-start(s32[8,128,128]{2,1,0:T(8,128)} %obstacle_ref.1) | copy-start | bytes 1572868
  19.4 0.7 copy-start.4
  20.0 13.7 %copy-start.12 = (f32[8,64,128]{2,1,0:T(8,128)S(1)}, f32[8,64,128]{2,1,0:T(8,128)}, u32[]{:S(2)}) copy-start(f32[8,64,128]{2,1,0:T(8,128)} %fusion.33) | copy-start | bytes 786436
  34.2 1.0 %copy-start.15 = (f32[8,128,64]{1,2,0:T(8,128)S(1)}, f32[8,128,64]{1,2,0:T(8,128)}, u32[]{:S(2)}) copy-start(f32[8,128,64]{1,2,0:T(8,128)} %fusion.14) | copy-start | bytes 786436
  35.1 3.2 %copy-start.6 = (f32[8,128,128]{2,1,0:T(8,128)S(1)}, f32[8,128,128]{2,1,0:T(8,128)}, u32[]{:S(2)}) copy-start(f32[8,128,128]{2,1,0:T(8,128)} %fusion.35) | copy-start | bytes 1572868
  36.2 8.7 %copy-start.10 = (f32[8,64,64]{2,1,0:T(8,128)S(1)}, f32[8,64,64]{2,1,0:T(8,128)}, u32[]{:S(2)}) copy-start(f32[8,64,64]{2,1,0:T(8,128)} %param.14) | copy-start | bytes 393220
  36.3 8.7 %collective-permute-start.2 = (f32[8,64,128]{2,1,0:T(8,128)S(1)}, f32[8,64,128]{2,1,0:T(8,128)S(1)}, u32[]{:S(2)}, u32[]{:S(2)}) collective-permute-start(f32[8,64,128]{2,1,0:T(8,128)S(1)} %fusion), channel_id=1, source_target_pairs={{0,4},{4,8},{8,12},{12,16},{16,20},{20,24},{24,28},{1,5},{5,9},{9,... | collective-permute-start | bytes 786440 | tf_op jit(solution)/shard_map/ppermute | solution.py:26
  39.0 29.8 %collective-permute-start.8 = (f32[8,128,128]{2,1,0:T(8,128)S(1)}, f32[8,128,128]{2,1,0:T(8,128)S(1)}, u32[]{:S(2)}, u32[]{:S(2)}) collective-permute-start(f32[8,128,128]{2,1,0:T(8,128)S(1)} %sub.57), channel_id=1, source_target_pairs={{0,4},{4,8},{8,12},{12,16},{16,20},{20,24},{24,28},{1,5},{5,9},{9,... | collective-permute-start | bytes 1572872 | tf_op jit(solution)/shard_map/ppermute | solution.py:26
  45.9 7.8 %collective-permute-start.3 = (f32[4,64,128]{2,1,0:T(8,128)S(1)}, f32[4,64,128]{2,1,0:T(8,128)S(1)}, u32[]{:S(2)}, u32[]{:S(2)}) collective-permute-start(f32[4,64,128]{2,1,0:T(8,128)S(1)} %fusion.6), channel_id=1, source_target_pairs={{0,8},{4,12},{8,16},{12,20},{16,24},{20,28},{1,9},{5,13},{9,17},{1... | collective-permute-start | bytes 393224 | tf_op jit(solution)/shard_map/ppermute | solution.py:26
  48.6 5.0 %copy-start.8 = (f32[8,64,64]{2,1,0:T(8,128)S(1)}, f32[8,64,64]{2,1,0:T(8,128)}, u32[]{:S(2)}) copy-start(f32[8,64,64]{2,1,0:T(8,128)} %copy-done.7) | copy-start | bytes 393220
  49.3 6.9 %collective-permute-start.5 = (f32[4,64,128]{2,1,0:T(8,128)S(1)}, f32[4,64,128]{2,1,0:T(8,128)S(1)}, u32[]{:S(2)}, u32[]{:S(2)}) collective-permute-start(f32[4,64,128]{2,1,0:T(8,128)S(1)} %fusion.3), channel_id=1, source_target_pairs={{0,16},{4,20},{8,24},{12,28},{1,17},{5,21},{9,25},{13,29},{2,18},{... | collective-permute-start | bytes 393224 | tf_op jit(solution)/shard_map/ppermute | solution.py:26
  53.9 2.3 %copy-start.11 = (f32[8,64,64]{2,1,0:T(8,128)S(1)}, f32[8,64,64]{2,1,0:T(8,128)}, u32[]{:S(2)}) copy-start(f32[8,64,64]{2,1,0:T(8,128)} %fusion.36) | copy-start | bytes 393220
  54.5 8.3 %collective-permute-start.4 = (f32[4,64,128]{2,1,0:T(8,128)S(1)}, f32[4,64,128]{2,1,0:T(8,128)S(1)}, u32[]{:S(2)}, u32[]{:S(2)}) collective-permute-start(f32[4,64,128]{2,1,0:T(8,128)S(1)} %fusion.5), channel_id=1, source_target_pairs={{0,16},{4,20},{8,24},{12,28},{1,17},{5,21},{9,25},{13,29},{2,18},{... | collective-permute-start | bytes 393224 | tf_op jit(solution)/shard_map/ppermute | solution.py:26
  57.1 7.8 %collective-permute-start.6 = (f32[4,64,128]{2,1,0:T(8,128)S(1)}, f32[4,64,128]{2,1,0:T(8,128)S(1)}, u32[]{:S(2)}, u32[]{:S(2)}) collective-permute-start(f32[4,64,128]{2,1,0:T(8,128)S(1)} %fusion.2), channel_id=1, source_target_pairs={{0,8},{4,12},{8,16},{12,20},{16,24},{20,28},{1,9},{5,13},{9,17},{1... | collective-permute-start | bytes 393224 | tf_op jit(solution)/shard_map/ppermute | solution.py:26
  65.8 8.6 %collective-permute-start.7 = (f32[8,64,128]{2,1,0:T(8,128)S(1)}, f32[8,64,128]{2,1,0:T(8,128)S(1)}, u32[]{:S(2)}, u32[]{:S(2)}) collective-permute-start(f32[8,64,128]{2,1,0:T(8,128)S(1)} %maximum_subtract_fusion), channel_id=1, source_target_pairs={{0,4},{4,8},{8,12},{12,16},{16,20},{20,24},{24,28},{1,5},{5,9},{9,... | collective-permute-start | bytes 786440 | tf_op jit(solution)/shard_map/ppermute | solution.py:26

commit v9 on v8

--- a/solution.py
+++ b/solution.py
@@ -75,7 +75,8 @@
                 east_ok, next_ref[field_at, east_at], 0.0
             )
 
-    lane = lax.broadcasted_iota(jnp.int32, (total, lanes), 1)
+    chunk = 16
+    lane = lax.broadcasted_iota(jnp.int32, (chunk, lanes), 1)
     first_lane = lane == 0
     last_lane = lane == lanes - 1
 
@@ -84,24 +85,28 @@
         dst = 1 - src
         strength = scale_ref[s]
         for i in range(tiles):
-            current = state_ref[src, i, pl.ds(PAD, total), :]
-            south_tile = state_ref[src, south_ref[i], pl.ds(PAD, total), :]
-            north_tile = state_ref[src, north_ref[i], pl.ds(PAD, total), :]
-            from_west = state_ref[src, i, pl.ds(PAD - 1, total), :]
-            from_east = state_ref[src, i, pl.ds(PAD + 1, total), :]
-            from_south = pltpu.roll(jnp.where(last_lane, south_tile, current), 1, 1)
-            from_north = pltpu.roll(jnp.where(first_lane, north_tile, current), lanes - 1, 1)
-            diffusivity = field_ref[0, i]
-            half_speed_x = field_ref[1, i]
-            half_speed_y = field_ref[2, i]
-            open_cells = field_ref[3, i]
-            laplace = from_west + from_east + from_south + from_north - 4.0 * current
-            half_transport = half_speed_x * (from_east - from_west) + half_speed_y * (
-                from_north - from_south
-            )
-            state_ref[dst, i, pl.ds(PAD, total), :] = open_cells * (
-                current + strength * diffusivity * laplace - half_transport
-            )
+            south_at = south_ref[i]
+            north_at = north_ref[i]
+            for start in range(0, total, chunk):
+                rows_at = pl.ds(PAD + start, chunk)
+                current = state_ref[src, i, rows_at, :]
+                south_tile = state_ref[src, south_at, rows_at, :]
+                north_tile = state_ref[src, north_at, rows_at, :]
+                from_west = state_ref[src, i, pl.ds(PAD + start - 1, chunk), :]
+                from_east = state_ref[src, i, pl.ds(PAD + start + 1, chunk), :]
+                from_south = pltpu.roll(jnp.where(last_lane, south_tile, current), 1, 1)
+                from_north = pltpu.roll(jnp.where(first_lane, north_tile, current), lanes - 1, 1)
+                diffusivity = field_ref[0, i, pl.ds(start, chunk), :]
+                half_speed_x = field_ref[1, i, pl.ds(start, chunk), :]
+                half_speed_y = field_ref[2, i, pl.ds(start, chunk), :]
+                open_cells = field_ref[3, i, pl.ds(start, chunk), :]
+                laplace = from_west + from_east + from_south + from_north - 4.0 * current
+                half_transport = half_speed_x * (from_east - from_west) + half_speed_y * (
+                    from_north - from_south
+                )
+                state_ref[dst, i, rows_at, :] = open_cells * (
+                    current + strength * diffusivity * laplace - half_transport
+                )
         return carry
 
     lax.fori_loop(0, SUB, substep, 0)

time: 76 us -> 138 us (1.82)
  Pallas kernels: 13.7 us -> 75.8 us
    pallas_call x1, Pallas kernels: 13.7 us -> 75.8 us  [fine_propagate(): pl.pallas_call(functools.partial(fine_kernel, slice_at), out_shape=jax.Sh...]
  transfers between devices with their start and end apart: 9 -> 9, of which waited for: 6 -> 6; matrix products, arithmetic and copies ran while one was open for 20% -> 11% of each run, Pallas kernels for 0% -> 0%
where the time goes in v9:
time: 138 us; the launch traced here: 137 us
  Pallas kernels  75.8 us (55%)
  starting transfers between devices  20.5 us (15%)
  waiting for transfers between devices  16.4 us (12%)
  matrix products  13.2 us (10%)
  local copies, waits for them, and re-layouts  5.67 us (4%)
  other arithmetic  4.93 us (4%)
    pallas_call x1, Pallas kernels, fine_propagate(): pl.pallas_call(functools.partial(fine_kernel, slice_at), out_shape=jax.Sh...  75.8 us
    ppermute x7, waiting for transfers between devices, passed_along(): return lax.ppermute(block, axis, route)  16.3 us
    ppermute x7, starting transfers between devices, passed_along(): return lax.ppermute(block, axis, route)  14.7 us
    dot_general x8, matrix products, apply_coarse(): jnp.einsum('...tik,tlk->...til', mixed_x, matrix_y, precision=exact_preci...  6.63 us
    ppermute x1, starting transfers between devices, on_device(): from_prev = lax.ppermute(layers[:, :, rows - HALO:, :], 'space', forward)  3.47 us
    unnamed x34, local copies, waits for them, and re-layouts  3.13 us
    dot_general x8, matrix products, apply_coarse(): jnp.einsum('tij,...tjk->...tik', matrix_x, coarse_values, precision=exact...  3.07 us
  transfers between devices with their start and end apart: 9, of which 6 were waited for; matrix products, arithmetic and copies ran while one was open for 11% of the time, Pallas kernels for 0%

profile of v9, /device:TPU:12, one launch (start us, length us, event | category | flops | bytes accessed | tf_op | source)
XLA Modules:
  0.0 137.5 jit_solution(15128140746685108217)
XLA Ops:
  0.6 1.2 subtract_bitcast_fusion
  2.0 1.9 %pad_maximum_fusion = (f32[5,8,16,128]{3,2,1,0:T(8,128)}, f32[5,8,16,128]{3,2,1,0:T(8,128)}) fusion(f32[1,8,128,128]{3,2,1,0:T(8,128)S(1)} %subtract_bitcast_fusion, f32[2,8,128,128]{3,2,1,0:T(8,128)} %velocity_ref.1, f32[1,8,128,128]{3,2,1,0:T(8,128)S(1)} %bitcast.70, f32[1,8,128,128]{3,2,1,0:T(8,128)S(1)} %copy-done), kind=kLoop, calls=%fused_computation.18 | loop fusion | flops 491520 | bytes 3276800 | tf_op jit(solution)/shard_map/concatenate | solution.py:147
  3.9 3.5 %collective-permute-start = (f32[5,8,16,128]{3,2,1,0:T(8,128)}, f32[5,8,16,128]{3,2,1,0:T(8,128)S(1)}, u32[]{:S(2)}, u32[]{:S(2)}) collective-permute-start(f32[5,8,16,128]{3,2,1,0:T(8,128)} %get-tuple-element.3), channel_id=1, source_target_pairs={{0,1},{1,2},{2,3},{4,5},{5,6},{6,7},{8,9},{9,10},{10,11},{12,13},{... | collective-permute-start | bytes 983048 | tf_op jit(solution)/shard_map/ppermute | solution.py:151
  7.3 2.4 %collective-permute-start.1 = (f32[5,8,16,128]{3,2,1,0:T(8,128)}, f32[5,8,16,128]{3,2,1,0:T(8,128)S(1)}, u32[]{:S(2)}, u32[]{:S(2)}) collective-permute-start(f32[5,8,16,128]{3,2,1,0:T(8,128)} %get-tuple-element.2), channel_id=1, source_target_pairs={{1,0},{2,1},{3,2},{5,4},{6,5},{7,6},{9,8},{10,9},{11,10},{13,12},{... | collective-permute-start | bytes 983048 | tf_op jit(solution)/shard_map/ppermute | solution.py:152
  9.7 0.8 slice.93
  10.5 0.8 slice.94
  11.5 0.8 copy-done.9
  12.8 1.1 fusion.36
  14.3 0.6 copy-done.5
  14.9 1.8 %fusion.33 = f32[8,64,128]{2,1,0:T(8,128)} fusion(f32[8,64,128]{2,1,0:T(8,128)S(1)} %convolution_bitcast_fusion, f32[8,128,128]{2,1,0:T(8,128)S(1)} %copy-done.5), kind=kOutput, calls=%fused_computation.58 | convolution fusion | flops 100663296 | bytes 1048576 | tf_op jit(solution)/shard_map/...tik,tlk->...til/dot_general | solution.py:39
  16.7 1.1 fusion.14
  17.9 1.4 %fusion.35 = f32[8,128,128]{2,1,0:T(8,128)} fusion(f32[8,128,128]{2,1,0:T(8,128)S(1)} %copy-done.5), kind=kOutput, calls=%fused_computation.60 | convolution fusion | flops 201326592 | bytes 1048576 | tf_op jit(solution)/shard_map/tij,tjk->tik/dot_general | solution.py:195
  19.4 0.6 copy-done.4
  20.0 75.8 %shard_map.95 = f32[8,128,128]{2,1,0:T(8,128)S(1)} custom-call(s32[8]{0:T(128)S(1)} %get-tuple-element.8.south_ref, s32[8]{0:T(128)S(1)} %get-tuple-element.7.north_ref, s32[8]{0:T(128)S(1)} %get-tuple-element.9.west_at_ref, s32[8]{0:T(128)S(1)} %get-tuple-element.6.east_at_ref, s32[8]{0:T(128)S(1)} %get-tuple-element.5.west_ok_ref, ...), custom_call_target="tpu_custom_call" | custom-call | tf_op jit(solution)/shard_map/pallas_call | solution.py:123
  96.3 0.8 copy-done.15
  97.1 1.1 fusion
  98.3 2.1 %collective-permute-start.2 = (f32[8,64,128]{2,1,0:T(8,128)S(1)}, f32[8,64,128]{2,1,0:T(8,128)S(1)}, u32[]{:S(2)}, u32[]{:S(2)}) collective-permute-start(f32[8,64,128]{2,1,0:T(8,128)S(1)} %fusion), channel_id=1, source_target_pairs={{0,4},{4,8},{8,12},{12,16},{16,20},{20,24},{24,28},{1,5},{5,9},{9,... | collective-permute-start | bytes 786440 | tf_op jit(solution)/shard_map/ppermute | solution.py:26
  100.4 0.6 fusion.37
  101.0 3.5 %collective-permute-start.8 = (f32[8,128,128]{2,1,0:T(8,128)S(1)}, f32[8,128,128]{2,1,0:T(8,128)S(1)}, u32[]{:S(2)}, u32[]{:S(2)}) collective-permute-start(f32[8,128,128]{2,1,0:T(8,128)S(1)} %sub.57), channel_id=1, source_target_pairs={{0,4},{4,8},{8,12},{12,16},{16,20},{20,24},{24,28},{1,5},{5,9},{9,... | collective-permute-start | bytes 1572872 | tf_op jit(solution)/shard_map/ppermute | solution.py:26
  104.5 2.5 %collective-permute-done.2 = f32[8,64,128]{2,1,0:T(8,128)S(1)} collective-permute-done((f32[8,64,128]{2,1,0:T(8,128)S(1)}, f32[8,64,128]{2,1,0:T(8,128)S(1)}, u32[]{:S(2)}, u32[]{:S(2)}) %collective-permute-start.2) | collective-permute-done | bytes 262176 | tf_op jit(solution)/shard_map/ppermute | solution.py:26
  107.9 2.5 %collective-permute-start.3 = (f32[4,64,128]{2,1,0:T(8,128)S(1)}, f32[4,64,128]{2,1,0:T(8,128)S(1)}, u32[]{:S(2)}, u32[]{:S(2)}) collective-permute-start(f32[4,64,128]{2,1,0:T(8,128)S(1)} %fusion.6), channel_id=1, source_target_pairs={{0,8},{4,12},{8,16},{12,20},{16,24},{20,28},{1,9},{5,13},{9,17},{1... | collective-permute-start | bytes 393224 | tf_op jit(solution)/shard_map/ppermute | solution.py:26
  110.7 0.6 fusion.3
  111.3 1.3 collective-permute-start.5
  112.6 3.1 %collective-permute-done.3 = f32[4,64,128]{2,1,0:T(8,128)S(1)} collective-permute-done((f32[4,64,128]{2,1,0:T(8,128)S(1)}, f32[4,64,128]{2,1,0:T(8,128)S(1)}, u32[]{:S(2)}, u32[]{:S(2)}) %collective-permute-start.3) | collective-permute-done | bytes 131104 | tf_op jit(solution)/shard_map/ppermute | solution.py:26
  116.6 1.3 collective-permute-start.4
  119.1 2.1 %collective-permute-start.6 = (f32[4,64,128]{2,1,0:T(8,128)S(1)}, f32[4,64,128]{2,1,0:T(8,128)S(1)}, u32[]{:S(2)}, u32[]{:S(2)}) collective-permute-start(f32[4,64,128]{2,1,0:T(8,128)S(1)} %fusion.2), channel_id=1, source_target_pairs={{0,8},{4,12},{8,16},{12,20},{16,24},{20,28},{1,9},{5,13},{9,17},{1... | collective-permute-start | bytes 393224 | tf_op jit(solution)/shard_map/ppermute | solution.py:26
  121.2 3.6 %collective-permute-done.4 = f32[4,64,128]{2,1,0:T(8,128)S(1)} collective-permute-done((f32[4,64,128]{2,1,0:T(8,128)S(1)}, f32[4,64,128]{2,1,0:T(8,128)S(1)}, u32[]{:S(2)}, u32[]{:S(2)}) %collective-permute-start.4) | collective-permute-done | bytes 131104 | tf_op jit(solution)/shard_map/ppermute | solution.py:26
  125.7 1.2 collective-permute-done.6
  127.8 1.9 %collective-permute-start.7 = (f32[8,64,128]{2,1,0:T(8,128)S(1)}, f32[8,64,128]{2,1,0:T(8,128)S(1)}, u32[]{:S(2)}, u32[]{:S(2)}) collective-permute-start(f32[8,64,128]{2,1,0:T(8,128)S(1)} %maximum_subtract_fusion), channel_id=1, source_target_pairs={{0,4},{4,8},{8,12},{12,16},{16,20},{20,24},{24,28},{1,5},{5,9},{9,... | collective-permute-start | bytes 786440 | tf_op jit(solution)/shard_map/ppermute | solution.py:26
  130.0 0.9 add_bitcast_fusion
  130.8 5.6 %collective-permute-done.7 = f32[8,64,128]{2,1,0:T(8,128)S(1)} collective-permute-done((f32[8,64,128]{2,1,0:T(8,128)S(1)}, f32[8,64,128]{2,1,0:T(8,128)S(1)}, u32[]{:S(2)}, u32[]{:S(2)}) %collective-permute-start.7) | collective-permute-done | bytes 262176 | tf_op jit(solution)/shard_map/ppermute | solution.py:26
  136.6 0.9 select_bitcast_fusion
  (58 shorter events, 7.1 us)
Async XLA Ops:
  0.6 1.2 copy-start
  0.6 1.3 copy-start.2
  3.9 15.5 %collective-permute-start = (f32[5,8,16,128]{3,2,1,0:T(8,128)}, f32[5,8,16,128]{3,2,1,0:T(8,128)S(1)}, u32[]{:S(2)}, u32[]{:S(2)}) collective-permute-start(f32[5,8,16,128]{3,2,1,0:T(8,128)} %get-tuple-element.3), channel_id=1, source_target_pairs={{0,1},{1,2},{2,3},{4,5},{5,6},{6,7},{8,9},{9,10},{10,11},{12,13},{... | collective-permute-start | bytes 983048 | tf_op jit(solution)/shard_map/ppermute | solution.py:151
  7.3 12.0 %collective-permute-start.1 = (f32[5,8,16,128]{3,2,1,0:T(8,128)}, f32[5,8,16,128]{3,2,1,0:T(8,128)S(1)}, u32[]{:S(2)}, u32[]{:S(2)}) collective-permute-start(f32[5,8,16,128]{3,2,1,0:T(8,128)} %get-tuple-element.2), channel_id=1, source_target_pairs={{1,0},{2,1},{3,2},{5,4},{6,5},{7,6},{9,8},{10,9},{11,10},{13,12},{... | collective-permute-start | bytes 983048 | tf_op jit(solution)/shard_map/ppermute | solution.py:152
  11.4 1.0 copy-start.9
  12.7 1.1 copy-start.7
  12.7 1.1 copy-start.13
  12.8 1.1 copy-start.14
  13.9 1.0 copy-start.5
  16.7 1.1 copy-start.16
  17.9 1.5 %copy-start.1 = (f32[2,8,128,128]{3,2,1,0:T(8,128)S(1)}, f32[2,8,128,128]{3,2,1,0:T(8,128)}, u32[]{:S(2)}) copy-start(f32[2,8,128,128]{3,2,1,0:T(8,128)} %velocity_ref.1) | copy-start | bytes 3145732
  17.9 1.5 %copy-start.3 = (s32[8,128,128]{2,1,0:T(8,128)S(1)}, s32[8,128,128]{2,1,0:T(8,128)}, u32[]{:S(2)}) copy-start(s32[8,128,128]{2,1,0:T(8,128)} %obstacle_ref.1) | copy-start | bytes 1572868
  19.4 0.7 copy-start.4
  20.0 75.8 %copy-start.12 = (f32[8,64,128]{2,1,0:T(8,128)S(1)}, f32[8,64,128]{2,1,0:T(8,128)}, u32[]{:S(2)}) copy-start(f32[8,64,128]{2,1,0:T(8,128)} %fusion.33) | copy-start | bytes 786436
  96.2 1.0 copy-start.15
  97.1 3.2 %copy-start.6 = (f32[8,128,128]{2,1,0:T(8,128)S(1)}, f32[8,128,128]{2,1,0:T(8,128)}, u32[]{:S(2)}) copy-start(f32[8,128,128]{2,1,0:T(8,128)} %fusion.35) | copy-start | bytes 1572868
  98.3 8.7 %copy-start.10 = (f32[8,64,64]{2,1,0:T(8,128)S(1)}, f32[8,64,64]{2,1,0:T(8,128)}, u32[]{:S(2)}) copy-start(f32[8,64,64]{2,1,0:T(8,128)} %param.14) | copy-start | bytes 393220
  98.3 8.7 %collective-permute-start.2 = (f32[8,64,128]{2,1,0:T(8,128)S(1)}, f32[8,64,128]{2,1,0:T(8,128)S(1)}, u32[]{:S(2)}, u32[]{:S(2)}) collective-permute-start(f32[8,64,128]{2,1,0:T(8,128)S(1)} %fusion), channel_id=1, source_target_pairs={{0,4},{4,8},{8,12},{12,16},{16,20},{20,24},{24,28},{1,5},{5,9},{9,... | collective-permute-start | bytes 786440 | tf_op jit(solution)/shard_map/ppermute | solution.py:26
  101.0 29.8 %collective-permute-start.8 = (f32[8,128,128]{2,1,0:T(8,128)S(1)}, f32[8,128,128]{2,1,0:T(8,128)S(1)}, u32[]{:S(2)}, u32[]{:S(2)}) collective-permute-start(f32[8,128,128]{2,1,0:T(8,128)S(1)} %sub.57), channel_id=1, source_target_pairs={{0,4},{4,8},{8,12},{12,16},{16,20},{20,24},{24,28},{1,5},{5,9},{9,... | collective-permute-start | bytes 1572872 | tf_op jit(solution)/shard_map/ppermute | solution.py:26
  107.9 7.8 %collective-permute-start.3 = (f32[4,64,128]{2,1,0:T(8,128)S(1)}, f32[4,64,128]{2,1,0:T(8,128)S(1)}, u32[]{:S(2)}, u32[]{:S(2)}) collective-permute-start(f32[4,64,128]{2,1,0:T(8,128)S(1)} %fusion.6), channel_id=1, source_target_pairs={{0,8},{4,12},{8,16},{12,20},{16,24},{20,28},{1,9},{5,13},{9,17},{1... | collective-permute-start | bytes 393224 | tf_op jit(solution)/shard_map/ppermute | solution.py:26
  110.7 5.0 %copy-start.8 = (f32[8,64,64]{2,1,0:T(8,128)S(1)}, f32[8,64,64]{2,1,0:T(8,128)}, u32[]{:S(2)}) copy-start(f32[8,64,64]{2,1,0:T(8,128)} %copy-done.7) | copy-start | bytes 393220
  111.3 6.9 %collective-permute-start.5 = (f32[4,64,128]{2,1,0:T(8,128)S(1)}, f32[4,64,128]{2,1,0:T(8,128)S(1)}, u32[]{:S(2)}, u32[]{:S(2)}) collective-permute-start(f32[4,64,128]{2,1,0:T(8,128)S(1)} %fusion.3), channel_id=1, source_target_pairs={{0,16},{4,20},{8,24},{12,28},{1,17},{5,21},{9,25},{13,29},{2,18},{... | collective-permute-start | bytes 393224 | tf_op jit(solution)/shard_map/ppermute | solution.py:26
  115.9 2.3 %copy-start.11 = (f32[8,64,64]{2,1,0:T(8,128)S(1)}, f32[8,64,64]{2,1,0:T(8,128)}, u32[]{:S(2)}) copy-start(f32[8,64,64]{2,1,0:T(8,128)} %fusion.36) | copy-start | bytes 393220
  116.6 8.3 %collective-permute-start.4 = (f32[4,64,128]{2,1,0:T(8,128)S(1)}, f32[4,64,128]{2,1,0:T(8,128)S(1)}, u32[]{:S(2)}, u32[]{:S(2)}) collective-permute-start(f32[4,64,128]{2,1,0:T(8,128)S(1)} %fusion.5), channel_id=1, source_target_pairs={{0,16},{4,20},{8,24},{12,28},{1,17},{5,21},{9,25},{13,29},{2,18},{... | collective-permute-start | bytes 393224 | tf_op jit(solution)/shard_map/ppermute | solution.py:26
  119.1 7.8 %collective-permute-start.6 = (f32[4,64,128]{2,1,0:T(8,128)S(1)}, f32[4,64,128]{2,1,0:T(8,128)S(1)}, u32[]{:S(2)}, u32[]{:S(2)}) collective-permute-start(f32[4,64,128]{2,1,0:T(8,128)S(1)} %fusion.2), channel_id=1, source_target_pairs={{0,8},{4,12},{8,16},{12,20},{16,24},{20,28},{1,9},{5,13},{9,17},{1... | collective-permute-start | bytes 393224 | tf_op jit(solution)/shard_map/ppermute | solution.py:26
  127.8 8.6 %collective-permute-start.7 = (f32[8,64,128]{2,1,0:T(8,128)S(1)}, f32[8,64,128]{2,1,0:T(8,128)S(1)}, u32[]{:S(2)}, u32[]{:S(2)}) collective-permute-start(f32[8,64,128]{2,1,0:T(8,128)S(1)} %maximum_subtract_fusion), channel_id=1, source_target_pairs={{0,4},{4,8},{8,12},{12,16},{16,20},{20,24},{24,28},{1,5},{5,9},{9,... | collective-permute-start | bytes 786440 | tf_op jit(solution)/shard_map/ppermute | solution.py:26

commit v10 on v9

--- a/solution.py
+++ b/solution.py
@@ -41,21 +41,22 @@
 
 def fine_kernel(slice_at, south_ref, north_ref, west_at_ref, east_at_ref, west_ok_ref, east_ok_ref,
                 scale_ref, u_ref, diffusivity_ref, velocity_ref, obstacle_ref, prev_ref, next_ref,
-                out_ref, state_ref, field_ref):
+                out_ref, state_ref, other_ref, field_ref):
     tiles = u_ref.shape[0]
     rows = u_ref.shape[1]
     lanes = u_ref.shape[2]
     total = rows + 2 * HALO
     layers = prev_ref.shape[0]
     state_ref[...] = jnp.zeros(state_ref.shape, jnp.float32)
+    other_ref[...] = jnp.zeros(other_ref.shape, jnp.float32)
     for i in range(tiles):
         west_at = west_at_ref[i]
         east_at = east_at_ref[i]
         west_ok = west_ok_ref[i] > 0
         east_ok = east_ok_ref[i] > 0
-        state_ref[0, i, pl.ds(PAD, HALO), :] = jnp.where(west_ok, prev_ref[slice_at, west_at], 0.0)
-        state_ref[0, i, pl.ds(PAD + HALO, rows), :] = u_ref[i]
-        state_ref[0, i, pl.ds(PAD + HALO + rows, HALO), :] = jnp.where(
+        state_ref[i, pl.ds(PAD, HALO), :] = jnp.where(west_ok, prev_ref[slice_at, west_at], 0.0)
+        state_ref[i, pl.ds(PAD + HALO, rows), :] = u_ref[i]
+        state_ref[i, pl.ds(PAD + HALO + rows, HALO), :] = jnp.where(
             east_ok, next_ref[slice_at, east_at], 0.0
         )
         own = (
@@ -80,20 +81,17 @@
     first_lane = lane == 0
     last_lane = lane == lanes - 1
 
-    def substep(s, carry):
-        src = s % 2
-        dst = 1 - src
-        strength = scale_ref[s]
+    def substep(strength, src_ref, dst_ref):
         for i in range(tiles):
             south_at = south_ref[i]
             north_at = north_ref[i]
             for start in range(0, total, chunk):
                 rows_at = pl.ds(PAD + start, chunk)
-                current = state_ref[src, i, rows_at, :]
-                south_tile = state_ref[src, south_at, rows_at, :]
-                north_tile = state_ref[src, north_at, rows_at, :]
-                from_west = state_ref[src, i, pl.ds(PAD + start - 1, chunk), :]
-                from_east = state_ref[src, i, pl.ds(PAD + start + 1, chunk), :]
+                current = src_ref[i, rows_at, :]
+                south_tile = src_ref[south_at, rows_at, :]
+                north_tile = src_ref[north_at, rows_at, :]
+                from_west = src_ref[i, pl.ds(PAD + start - 1, chunk), :]
+                from_east = src_ref[i, pl.ds(PAD + start + 1, chunk), :]
                 from_south = pltpu.roll(jnp.where(last_lane, south_tile, current), 1, 1)
                 from_north = pltpu.roll(jnp.where(first_lane, north_tile, current), lanes - 1, 1)
                 diffusivity = field_ref[0, i, pl.ds(start, chunk), :]
@@ -104,15 +102,22 @@
                 half_transport = half_speed_x * (from_east - from_west) + half_speed_y * (
                     from_north - from_south
                 )
-                state_ref[dst, i, rows_at, :] = open_cells * (
+                dst_ref[i, rows_at, :] = open_cells * (
                     current + strength * diffusivity * laplace - half_transport
                 )
+
+    def substep_pair(p, carry):
+        substep(scale_ref[2 * p], state_ref, other_ref)
+        substep(scale_ref[2 * p + 1], other_ref, state_ref)
         return carry
 
-    lax.fori_loop(0, SUB, substep, 0)
-    last = SUB % 2
+    lax.fori_loop(0, SUB // 2, substep_pair, 0)
+    final_ref = state_ref
+    if SUB % 2:
+        substep(scale_ref[SUB - 1], state_ref, other_ref)
+        final_ref = other_ref
     for i in range(tiles):
-        out_ref[i] = state_ref[last, i, pl.ds(PAD + HALO, rows), :]
+        out_ref[i] = final_ref[i, pl.ds(PAD + HALO, rows), :]
 
 
 def fine_propagate(slice_at, u, diffusivity, velocity, obstacle, from_prev, from_next, indices, scale):
@@ -126,7 +131,8 @@
         in_specs=[pl.BlockSpec(memory_space=smem)] * 7 + [pl.BlockSpec(memory_space=vmem)] * 6,
         out_specs=pl.BlockSpec(memory_space=vmem),
         scratch_shapes=[
-            pltpu.VMEM((2, tiles + 1, total + 2 * PAD, lanes), jnp.float32),
+            pltpu.VMEM((tiles + 1, total + 2 * PAD, lanes), jnp.float32),
+            pltpu.VMEM((tiles + 1, total + 2 * PAD, lanes), jnp.float32),
             pltpu.VMEM((4, tiles, total, lanes), jnp.float32),
         ],
         compiler_params=pltpu.CompilerParams(vmem_limit_bytes=48 * 1024 * 1024),

time: 138 us -> 69.2 us (0.50)
  Pallas kernels: 75.8 us -> 6.9 us
    pallas_call x1, Pallas kernels: 75.8 us -> 6.9 us  [fine_propagate(): pl.pallas_call(functools.partial(fine_kernel, slice_at), out_shape=jax.Sh...]
  transfers between devices with their start and end apart: 9 -> 9, of which waited for: 6 -> 6; matrix products, arithmetic and copies ran while one was open for 11% -> 22% of each run, Pallas kernels for 0% -> 0%
where the time goes in v10:
time: 69.2 us; the launch traced here: 68.6 us
  starting transfers between devices  20.5 us (30%)
  waiting for transfers between devices  16.4 us (24%)
  matrix products  13.2 us (19%)
  Pallas kernels  6.9 us (10%)
  local copies, waits for them, and re-layouts  5.67 us (8%)
  other arithmetic  4.93 us (7%)
  between operations  1.07 us (2%)
    ppermute x7, waiting for transfers between devices, passed_along(): return lax.ppermute(block, axis, route)  16.4 us
    ppermute x7, starting transfers between devices, passed_along(): return lax.ppermute(block, axis, route)  14.7 us
    pallas_call x1, Pallas kernels, fine_propagate(): pl.pallas_call(functools.partial(fine_kernel, slice_at), out_shape=jax.Sh...  6.9 us
    dot_general x8, matrix products, apply_coarse(): jnp.einsum('...tik,tlk->...til', mixed_x, matrix_y, precision=exact_preci...  6.62 us
    ppermute x1, starting transfers between devices, on_device(): from_prev = lax.ppermute(layers[:, :, rows - HALO:, :], 'space', forward)  3.47 us
    unnamed x34, local copies, waits for them, and re-layouts  3.13 us
    dot_general x8, matrix products, apply_coarse(): jnp.einsum('tij,...tjk->...tik', matrix_x, coarse_values, precision=exact...  3.07 us
    ppermute x1, starting transfers between devices, on_device(): from_next = lax.ppermute(layers[:, :, :HALO, :], 'space', backward)  2.37 us
  transfers between devices with their start and end apart: 9, of which 6 were waited for; matrix products, arithmetic and copies ran while one was open for 22% of the time, Pallas kernels for 0%

profile of v10, /device:TPU:12, one launch (start us, length us, event | category | flops | bytes accessed | tf_op | source)
XLA Modules:
  0.0 68.6 jit_solution(12999319189704641318)
XLA Ops:
  0.6 1.2 %subtract_bitcast_fusion = f32[1,8,128,128]{3,2,1,0:T(8,128)S(1)} fusion(s32[8,128,128]{2,1,0:T(8,128)} %obstacle_ref.1), kind=kLoop, calls=%fused_computation.17 | loop fusion | flops 262144 | bytes 1048576 | tf_op jit(solution)/shard_map/stack | solution.py:152
  2.0 1.9 %pad_maximum_fusion = (f32[5,8,16,128]{3,2,1,0:T(8,128)}, f32[5,8,16,128]{3,2,1,0:T(8,128)}) fusion(f32[1,8,128,128]{3,2,1,0:T(8,128)S(1)} %subtract_bitcast_fusion, f32[2,8,128,128]{3,2,1,0:T(8,128)} %velocity_ref.1, f32[1,8,128,128]{3,2,1,0:T(8,128)S(1)} %bitcast.70, f32[1,8,128,128]{3,2,1,0:T(8,128)S(1)} %copy-done), kind=kLoop, calls=%fused_computation.18 | loop fusion | flops 491520 | bytes 3276800 | tf_op jit(solution)/shard_map/concatenate | solution.py:153
  3.9 3.5 %collective-permute-start = (f32[5,8,16,128]{3,2,1,0:T(8,128)}, f32[5,8,16,128]{3,2,1,0:T(8,128)S(1)}, u32[]{:S(2)}, u32[]{:S(2)}) collective-permute-start(f32[5,8,16,128]{3,2,1,0:T(8,128)} %get-tuple-element.3), channel_id=1, source_target_pairs={{0,1},{1,2},{2,3},{4,5},{5,6},{6,7},{8,9},{9,10},{10,11},{12,13},{... | collective-permute-start | bytes 983048 | tf_op jit(solution)/shard_map/ppermute | solution.py:157
  7.3 2.4 %collective-permute-start.1 = (f32[5,8,16,128]{3,2,1,0:T(8,128)}, f32[5,8,16,128]{3,2,1,0:T(8,128)S(1)}, u32[]{:S(2)}, u32[]{:S(2)}) collective-permute-start(f32[5,8,16,128]{3,2,1,0:T(8,128)} %get-tuple-element.2), channel_id=1, source_target_pairs={{1,0},{2,1},{3,2},{5,4},{6,5},{7,6},{9,8},{10,9},{11,10},{13,12},{... | collective-permute-start | bytes 983048 | tf_op jit(solution)/shard_map/ppermute | solution.py:158
  9.7 0.8 %slice.93 = f32[1,8,64,128]{3,2,1,0:T(8,128)} slice(f32[1,8,128,128]{3,2,1,0:T(8,128)S(1)} %copy-done), slice={[0:1:1], [0:8:1], [0:128:2], [0:128:1]} | slice | bytes 524288 | tf_op jit(solution)/shard_map/slice | solution.py:30
  10.5 0.8 %slice.94 = f32[1,8,64,128]{3,2,1,0:T(8,128)} slice(f32[1,8,128,128]{3,2,1,0:T(8,128)S(1)} %copy-done), slice={[0:1:1], [0:8:1], [1:128:2], [0:128:1]} | slice | bytes 524288 | tf_op jit(solution)/shard_map/slice | solution.py:30
  11.5 0.8 %copy-done.9 = f32[8,64,64]{2,1,0:T(8,128)S(1)} copy-done((f32[8,64,64]{2,1,0:T(8,128)S(1)}, f32[8,64,64]{2,1,0:T(8,128)}, u32[]{:S(2)}) %copy-start.9) | copy-done | bytes 131096
  12.8 1.1 %fusion.36 = f32[8,64,64]{2,1,0:T(8,128)} fusion(f32[8,64,64]{2,1,0:T(8,128)S(1)} %fusion.34), kind=kOutput, calls=%fused_computation.61 | convolution fusion | flops 25165824 | bytes 262144 | tf_op jit(solution)/shard_map/tij,tjk->tik/dot_general | solution.py:200
  14.3 0.6 copy-done.5
  14.9 1.8 %fusion.33 = f32[8,64,128]{2,1,0:T(8,128)} fusion(f32[8,64,128]{2,1,0:T(8,128)S(1)} %convolution_bitcast_fusion, f32[8,128,128]{2,1,0:T(8,128)S(1)} %copy-done.5), kind=kOutput, calls=%fused_computation.58 | convolution fusion | flops 100663296 | bytes 1048576 | tf_op jit(solution)/shard_map/...tik,tlk->...til/dot_general | solution.py:39
  16.7 1.1 %fusion.14 = f32[8,128,64]{1,2,0:T(8,128)} fusion(f32[8,64,64]{2,1,0:T(8,128)S(1)} %copy-done.9, f32[8,64,128]{2,1,0:T(8,128)S(1)} %slice.97, f32[8,64,128]{2,1,0:T(8,128)S(1)} %slice.98), kind=kOutput, calls=%fused_computation.30 | convolution fusion | flops 50462720 | bytes 917504 | tf_op jit(solution)/shard_map/tij,...tjk->...tik/dot_general | solution.py:38
  17.9 1.4 %fusion.35 = f32[8,128,128]{2,1,0:T(8,128)} fusion(f32[8,128,128]{2,1,0:T(8,128)S(1)} %copy-done.5), kind=kOutput, calls=%fused_computation.60 | convolution fusion | flops 201326592 | bytes 1048576 | tf_op jit(solution)/shard_map/tij,tjk->tik/dot_general | solution.py:201
  19.4 0.6 copy-done.4
  20.0 6.9 %shard_map.95 = f32[8,128,128]{2,1,0:T(8,128)S(1)} custom-call(s32[8]{0:T(128)S(1)} %get-tuple-element.8.south_ref, s32[8]{0:T(128)S(1)} %get-tuple-element.7.north_ref, s32[8]{0:T(128)S(1)} %get-tuple-element.9.west_at_ref, s32[8]{0:T(128)S(1)} %get-tuple-element.6.east_at_ref, s32[8]{0:T(128)S(1)} %get-tuple-element.5.west_ok_ref, ...), custom_call_target="tpu_custom_call" | custom-call | tf_op jit(solution)/shard_map/pallas_call | solution.py:128
  27.5 0.8 %copy-done.15 = f32[8,128,64]{1,2,0:T(8,128)S(1)} copy-done((f32[8,128,64]{1,2,0:T(8,128)S(1)}, f32[8,128,64]{1,2,0:T(8,128)}, u32[]{:S(2)}) %copy-start.15) | copy-done | bytes 262168
  28.3 1.1 %fusion = f32[8,64,128]{2,1,0:T(8,128)S(1)} fusion(f32[8,128,64]{1,2,0:T(8,128)S(1)} %copy-done.15, f32[8,128,128]{2,1,0:T(8,128)S(1)} %copy-done.5, pred[]{:T(512)S(6)} %eq.4, f32[1,8,64,128]{3,2,1,0:T(8,128)S(1)} %slice.95, f32[1,8,64,128]{3,2,1,0:T(8,128)S(1)} %slice.96), kind=kOutput, calls=%fused_computation.2 | convolution fusion | flops 100925440 | bytes 1572865 | tf_op jit(solution)/shard_map/...tik,tlk->...til/dot_general | solution.py:39
  29.4 2.1 %collective-permute-start.2 = (f32[8,64,128]{2,1,0:T(8,128)S(1)}, f32[8,64,128]{2,1,0:T(8,128)S(1)}, u32[]{:S(2)}, u32[]{:S(2)}) collective-permute-start(f32[8,64,128]{2,1,0:T(8,128)S(1)} %fusion), channel_id=1, source_target_pairs={{0,4},{4,8},{8,12},{12,16},{16,20},{20,24},{24,28},{1,5},{5,9},{9,... | collective-permute-start | bytes 786440 | tf_op jit(solution)/shard_map/ppermute | solution.py:26
  31.5 0.6 fusion.37
  32.1 3.5 %collective-permute-start.8 = (f32[8,128,128]{2,1,0:T(8,128)S(1)}, f32[8,128,128]{2,1,0:T(8,128)S(1)}, u32[]{:S(2)}, u32[]{:S(2)}) collective-permute-start(f32[8,128,128]{2,1,0:T(8,128)S(1)} %sub.57), channel_id=1, source_target_pairs={{0,4},{4,8},{8,12},{12,16},{16,20},{20,24},{24,28},{1,5},{5,9},{9,... | collective-permute-start | bytes 1572872 | tf_op jit(solution)/shard_map/ppermute | solution.py:26
  35.6 2.5 %collective-permute-done.2 = f32[8,64,128]{2,1,0:T(8,128)S(1)} collective-permute-done((f32[8,64,128]{2,1,0:T(8,128)S(1)}, f32[8,64,128]{2,1,0:T(8,128)S(1)}, u32[]{:S(2)}, u32[]{:S(2)}) %collective-permute-start.2) | collective-permute-done | bytes 262176 | tf_op jit(solution)/shard_map/ppermute | solution.py:26
  39.1 2.5 %collective-permute-start.3 = (f32[4,64,128]{2,1,0:T(8,128)S(1)}, f32[4,64,128]{2,1,0:T(8,128)S(1)}, u32[]{:S(2)}, u32[]{:S(2)}) collective-permute-start(f32[4,64,128]{2,1,0:T(8,128)S(1)} %fusion.6), channel_id=1, source_target_pairs={{0,8},{4,12},{8,16},{12,20},{16,24},{20,28},{1,9},{5,13},{9,17},{1... | collective-permute-start | bytes 393224 | tf_op jit(solution)/shard_map/ppermute | solution.py:26
  42.5 1.3 %collective-permute-start.5 = (f32[4,64,128]{2,1,0:T(8,128)S(1)}, f32[4,64,128]{2,1,0:T(8,128)S(1)}, u32[]{:S(2)}, u32[]{:S(2)}) collective-permute-start(f32[4,64,128]{2,1,0:T(8,128)S(1)} %fusion.3), channel_id=1, source_target_pairs={{0,16},{4,20},{8,24},{12,28},{1,17},{5,21},{9,25},{13,29},{2,18},{... | collective-permute-start | bytes 393224 | tf_op jit(solution)/shard_map/ppermute | solution.py:26
  43.8 3.0 %collective-permute-done.3 = f32[4,64,128]{2,1,0:T(8,128)S(1)} collective-permute-done((f32[4,64,128]{2,1,0:T(8,128)S(1)}, f32[4,64,128]{2,1,0:T(8,128)S(1)}, u32[]{:S(2)}, u32[]{:S(2)}) %collective-permute-start.3) | collective-permute-done | bytes 131104 | tf_op jit(solution)/shard_map/ppermute | solution.py:26
  47.7 1.3 %collective-permute-start.4 = (f32[4,64,128]{2,1,0:T(8,128)S(1)}, f32[4,64,128]{2,1,0:T(8,128)S(1)}, u32[]{:S(2)}, u32[]{:S(2)}) collective-permute-start(f32[4,64,128]{2,1,0:T(8,128)S(1)} %fusion.5), channel_id=1, source_target_pairs={{0,16},{4,20},{8,24},{12,28},{1,17},{5,21},{9,25},{13,29},{2,18},{... | collective-permute-start | bytes 393224 | tf_op jit(solution)/shard_map/ppermute | solution.py:26
  50.3 2.1 %collective-permute-start.6 = (f32[4,64,128]{2,1,0:T(8,128)S(1)}, f32[4,64,128]{2,1,0:T(8,128)S(1)}, u32[]{:S(2)}, u32[]{:S(2)}) collective-permute-start(f32[4,64,128]{2,1,0:T(8,128)S(1)} %fusion.2), channel_id=1, source_target_pairs={{0,8},{4,12},{8,16},{12,20},{16,24},{20,28},{1,9},{5,13},{9,17},{1... | collective-permute-start | bytes 393224 | tf_op jit(solution)/shard_map/ppermute | solution.py:26
  52.4 3.6 %collective-permute-done.4 = f32[4,64,128]{2,1,0:T(8,128)S(1)} collective-permute-done((f32[4,64,128]{2,1,0:T(8,128)S(1)}, f32[4,64,128]{2,1,0:T(8,128)S(1)}, u32[]{:S(2)}, u32[]{:S(2)}) %collective-permute-start.4) | collective-permute-done | bytes 131104 | tf_op jit(solution)/shard_map/ppermute | solution.py:26
  56.9 1.2 %collective-permute-done.6 = f32[4,64,128]{2,1,0:T(8,128)S(1)} collective-permute-done((f32[4,64,128]{2,1,0:T(8,128)S(1)}, f32[4,64,128]{2,1,0:T(8,128)S(1)}, u32[]{:S(2)}, u32[]{:S(2)}) %collective-permute-start.6) | collective-permute-done | bytes 131104 | tf_op jit(solution)/shard_map/ppermute | solution.py:26
  58.3 0.6 fusion.1
  59.0 1.9 %collective-permute-start.7 = (f32[8,64,128]{2,1,0:T(8,128)S(1)}, f32[8,64,128]{2,1,0:T(8,128)S(1)}, u32[]{:S(2)}, u32[]{:S(2)}) collective-permute-start(f32[8,64,128]{2,1,0:T(8,128)S(1)} %maximum_subtract_fusion), channel_id=1, source_target_pairs={{0,4},{4,8},{8,12},{12,16},{16,20},{20,24},{24,28},{1,5},{5,9},{9,... | collective-permute-start | bytes 786440 | tf_op jit(solution)/shard_map/ppermute | solution.py:26
  61.1 0.9 %add_bitcast_fusion = f32[1,8,128,128]{3,2,1,0:T(8,128)} fusion(f32[8,128,128]{2,1,0:T(8,128)S(1)} %bitcast.75, f32[8,128,128]{2,1,0:T(8,128)S(1)} %sub.57), kind=kLoop, calls=%fused_computation.16 | loop fusion | flops 131072 | bytes 1572864 | tf_op jit(solution)/shard_map/add | solution.py:244
  62.0 5.6 %collective-permute-done.7 = f32[8,64,128]{2,1,0:T(8,128)S(1)} collective-permute-done((f32[8,64,128]{2,1,0:T(8,128)S(1)}, f32[8,64,128]{2,1,0:T(8,128)S(1)}, u32[]{:S(2)}, u32[]{:S(2)}) %collective-permute-start.7) | collective-permute-done | bytes 262176 | tf_op jit(solution)/shard_map/ppermute | solution.py:26
  67.8 0.9 %select_bitcast_fusion = f32[1,8,128,128]{3,2,1,0:T(8,128)} fusion(f32[8,128,128]{2,1,0:T(8,128)S(1)} %bitcast.73, f32[8,128,128]{2,1,0:T(8,128)S(1)} %collective-permute-done.8, pred[]{:T(512)S(6)} %eq.4, f32[1,8,128,128]{3,2,1,0:T(8,128)S(1)} %copy-done), kind=kLoop, calls=%fused_computation.15 | loop fusion | flops 393216 | bytes 2097153 | tf_op jit(solution)/shard_map/broadcast_in_dim | solution.py:249
  (58 shorter events, 7.1 us)
Async XLA Ops:
  0.6 1.2 %copy-start = (f32[1,8,128,128]{3,2,1,0:T(8,128)S(1)}, f32[1,8,128,128]{3,2,1,0:T(8,128)}, u32[]{:S(2)}) copy-start(f32[1,8,128,128]{3,2,1,0:T(8,128)} %param.8) | copy-start | bytes 1572868
  0.6 1.3 %copy-start.2 = (f32[8,128,128]{2,1,0:T(8,128)S(1)}, f32[8,128,128]{2,1,0:T(8,128)}, u32[]{:S(2)}) copy-start(f32[8,128,128]{2,1,0:T(8,128)} %diffusivity_ref.1) | copy-start | bytes 1572868
  3.9 15.5 %collective-permute-start = (f32[5,8,16,128]{3,2,1,0:T(8,128)}, f32[5,8,16,128]{3,2,1,0:T(8,128)S(1)}, u32[]{:S(2)}, u32[]{:S(2)}) collective-permute-start(f32[5,8,16,128]{3,2,1,0:T(8,128)} %get-tuple-element.3), channel_id=1, source_target_pairs={{0,1},{1,2},{2,3},{4,5},{5,6},{6,7},{8,9},{9,10},{10,11},{12,13},{... | collective-permute-start | bytes 983048 | tf_op jit(solution)/shard_map/ppermute | solution.py:157
  7.3 12.0 %collective-permute-start.1 = (f32[5,8,16,128]{3,2,1,0:T(8,128)}, f32[5,8,16,128]{3,2,1,0:T(8,128)S(1)}, u32[]{:S(2)}, u32[]{:S(2)}) collective-permute-start(f32[5,8,16,128]{3,2,1,0:T(8,128)} %get-tuple-element.2), channel_id=1, source_target_pairs={{1,0},{2,1},{3,2},{5,4},{6,5},{7,6},{9,8},{10,9},{11,10},{13,12},{... | collective-permute-start | bytes 983048 | tf_op jit(solution)/shard_map/ppermute | solution.py:158
  11.4 1.0 %copy-start.9 = (f32[8,64,64]{2,1,0:T(8,128)S(1)}, f32[8,64,64]{2,1,0:T(8,128)}, u32[]{:S(2)}) copy-start(f32[8,64,64]{2,1,0:T(8,128)} %param.14) | copy-start | bytes 393220
  12.7 1.1 %copy-start.7 = (f32[8,64,64]{2,1,0:T(8,128)}, f32[8,64,64]{2,1,0:T(8,128)S(1)}, u32[]{:S(2)}) copy-start(f32[8,64,64]{2,1,0:T(8,128)S(1)} %fusion.34) | copy-start | bytes 393220
  12.7 1.1 %copy-start.13 = (f32[1,8,64,128]{3,2,1,0:T(8,128)S(1)}, f32[1,8,64,128]{3,2,1,0:T(8,128)}, u32[]{:S(2)}) copy-start(f32[1,8,64,128]{3,2,1,0:T(8,128)} %slice.93) | copy-start | bytes 786436
  12.8 1.1 %copy-start.14 = (f32[1,8,64,128]{3,2,1,0:T(8,128)S(1)}, f32[1,8,64,128]{3,2,1,0:T(8,128)}, u32[]{:S(2)}) copy-start(f32[1,8,64,128]{3,2,1,0:T(8,128)} %slice.94) | copy-start | bytes 786436
  13.9 1.0 %copy-start.5 = (f32[8,128,128]{2,1,0:T(8,128)S(1)}, f32[8,128,128]{2,1,0:T(8,128)}, u32[]{:S(2)}) copy-start(f32[8,128,128]{2,1,0:T(8,128)} %param.15) | copy-start | bytes 1572868
  16.7 1.1 %copy-start.16 = (s32[8,4]{0,1:T(4,128)S(1)}, s32[8,4]{0,1:T(4,128)}, u32[]{:S(2)}) copy-start(s32[8,4]{0,1:T(4,128)} %param.13) | copy-start | bytes 388
  17.9 1.5 %copy-start.1 = (f32[2,8,128,128]{3,2,1,0:T(8,128)S(1)}, f32[2,8,128,128]{3,2,1,0:T(8,128)}, u32[]{:S(2)}) copy-start(f32[2,8,128,128]{3,2,1,0:T(8,128)} %velocity_ref.1) | copy-start | bytes 3145732
  17.9 1.5 %copy-start.3 = (s32[8,128,128]{2,1,0:T(8,128)S(1)}, s32[8,128,128]{2,1,0:T(8,128)}, u32[]{:S(2)}) copy-start(s32[8,128,128]{2,1,0:T(8,128)} %obstacle_ref.1) | copy-start | bytes 1572868
  19.4 0.7 copy-start.4
  20.0 6.9 %copy-start.12 = (f32[8,64,128]{2,1,0:T(8,128)S(1)}, f32[8,64,128]{2,1,0:T(8,128)}, u32[]{:S(2)}) copy-start(f32[8,64,128]{2,1,0:T(8,128)} %fusion.33) | copy-start | bytes 786436
  27.3 1.0 %copy-start.15 = (f32[8,128,64]{1,2,0:T(8,128)S(1)}, f32[8,128,64]{1,2,0:T(8,128)}, u32[]{:S(2)}) copy-start(f32[8,128,64]{1,2,0:T(8,128)} %fusion.14) | copy-start | bytes 786436
  28.3 3.2 %copy-start.6 = (f32[8,128,128]{2,1,0:T(8,128)S(1)}, f32[8,128,128]{2,1,0:T(8,128)}, u32[]{:S(2)}) copy-start(f32[8,128,128]{2,1,0:T(8,128)} %fusion.35) | copy-start | bytes 1572868
  29.4 8.7 %copy-start.10 = (f32[8,64,64]{2,1,0:T(8,128)S(1)}, f32[8,64,64]{2,1,0:T(8,128)}, u32[]{:S(2)}) copy-start(f32[8,64,64]{2,1,0:T(8,128)} %param.14) | copy-start | bytes 393220
  29.4 8.7 %collective-permute-start.2 = (f32[8,64,128]{2,1,0:T(8,128)S(1)}, f32[8,64,128]{2,1,0:T(8,128)S(1)}, u32[]{:S(2)}, u32[]{:S(2)}) collective-permute-start(f32[8,64,128]{2,1,0:T(8,128)S(1)} %fusion), channel_id=1, source_target_pairs={{0,4},{4,8},{8,12},{12,16},{16,20},{20,24},{24,28},{1,5},{5,9},{9,... | collective-permute-start | bytes 786440 | tf_op jit(solution)/shard_map/ppermute | solution.py:26
  32.1 29.8 %collective-permute-start.8 = (f32[8,128,128]{2,1,0:T(8,128)S(1)}, f32[8,128,128]{2,1,0:T(8,128)S(1)}, u32[]{:S(2)}, u32[]{:S(2)}) collective-permute-start(f32[8,128,128]{2,1,0:T(8,128)S(1)} %sub.57), channel_id=1, source_target_pairs={{0,4},{4,8},{8,12},{12,16},{16,20},{20,24},{24,28},{1,5},{5,9},{9,... | collective-permute-start | bytes 1572872 | tf_op jit(solution)/shard_map/ppermute | solution.py:26
  39.1 7.8 %collective-permute-start.3 = (f32[4,64,128]{2,1,0:T(8,128)S(1)}, f32[4,64,128]{2,1,0:T(8,128)S(1)}, u32[]{:S(2)}, u32[]{:S(2)}) collective-permute-start(f32[4,64,128]{2,1,0:T(8,128)S(1)} %fusion.6), channel_id=1, source_target_pairs={{0,8},{4,12},{8,16},{12,20},{16,24},{20,28},{1,9},{5,13},{9,17},{1... | collective-permute-start | bytes 393224 | tf_op jit(solution)/shard_map/ppermute | solution.py:26
  41.8 5.0 %copy-start.8 = (f32[8,64,64]{2,1,0:T(8,128)S(1)}, f32[8,64,64]{2,1,0:T(8,128)}, u32[]{:S(2)}) copy-start(f32[8,64,64]{2,1,0:T(8,128)} %copy-done.7) | copy-start | bytes 393220
  42.5 6.9 %collective-permute-start.5 = (f32[4,64,128]{2,1,0:T(8,128)S(1)}, f32[4,64,128]{2,1,0:T(8,128)S(1)}, u32[]{:S(2)}, u32[]{:S(2)}) collective-permute-start(f32[4,64,128]{2,1,0:T(8,128)S(1)} %fusion.3), channel_id=1, source_target_pairs={{0,16},{4,20},{8,24},{12,28},{1,17},{5,21},{9,25},{13,29},{2,18},{... | collective-permute-start | bytes 393224 | tf_op jit(solution)/shard_map/ppermute | solution.py:26
  47.1 2.3 %copy-start.11 = (f32[8,64,64]{2,1,0:T(8,128)S(1)}, f32[8,64,64]{2,1,0:T(8,128)}, u32[]{:S(2)}) copy-start(f32[8,64,64]{2,1,0:T(8,128)} %fusion.36) | copy-start | bytes 393220
  47.7 8.3 %collective-permute-start.4 = (f32[4,64,128]{2,1,0:T(8,128)S(1)}, f32[4,64,128]{2,1,0:T(8,128)S(1)}, u32[]{:S(2)}, u32[]{:S(2)}) collective-permute-start(f32[4,64,128]{2,1,0:T(8,128)S(1)} %fusion.5), channel_id=1, source_target_pairs={{0,16},{4,20},{8,24},{12,28},{1,17},{5,21},{9,25},{13,29},{2,18},{... | collective-permute-start | bytes 393224 | tf_op jit(solution)/shard_map/ppermute | solution.py:26
  50.3 7.8 %collective-permute-start.6 = (f32[4,64,128]{2,1,0:T(8,128)S(1)}, f32[4,64,128]{2,1,0:T(8,128)S(1)}, u32[]{:S(2)}, u32[]{:S(2)}) collective-permute-start(f32[4,64,128]{2,1,0:T(8,128)S(1)} %fusion.2), channel_id=1, source_target_pairs={{0,8},{4,12},{8,16},{12,20},{16,24},{20,28},{1,9},{5,13},{9,17},{1... | collective-permute-start | bytes 393224 | tf_op jit(solution)/shard_map/ppermute | solution.py:26
  59.0 8.6 %collective-permute-start.7 = (f32[8,64,128]{2,1,0:T(8,128)S(1)}, f32[8,64,128]{2,1,0:T(8,128)S(1)}, u32[]{:S(2)}, u32[]{:S(2)}) collective-permute-start(f32[8,64,128]{2,1,0:T(8,128)S(1)} %maximum_subtract_fusion), channel_id=1, source_target_pairs={{0,4},{4,8},{8,12},{12,16},{16,20},{20,24},{24,28},{1,5},{5,9},{9,... | collective-permute-start | bytes 786440 | tf_op jit(solution)/shard_map/ppermute | solution.py:26

commit v11 on v10

--- a/solution.py
+++ b/solution.py
@@ -47,8 +47,11 @@
     lanes = u_ref.shape[2]
     total = rows + 2 * HALO
     layers = prev_ref.shape[0]
-    state_ref[...] = jnp.zeros(state_ref.shape, jnp.float32)
-    other_ref[...] = jnp.zeros(other_ref.shape, jnp.float32)
+    for ref in (state_ref, other_ref):
+        ref[tiles] = jnp.zeros(ref.shape[1:], jnp.float32)
+        for i in range(tiles):
+            ref[i, pl.ds(0, PAD), :] = jnp.zeros((PAD, lanes), jnp.float32)
+            ref[i, pl.ds(PAD + total, PAD), :] = jnp.zeros((PAD, lanes), jnp.float32)
     for i in range(tiles):
         west_at = west_at_ref[i]
         east_at = east_at_ref[i]
@@ -181,7 +184,9 @@
         ],
         axis=0,
     )
-    correction = fine_ends - prolong(apply_coarse(restrict(starts), coarse_x, coarse_y))
+    restricting_x = 0.5 * jnp.repeat(coarse_x, 2, axis=2)
+    coarse_of_starts = apply_coarse(starts, restricting_x, coarse_y)
+    correction = fine_ends - prolong(coarse_of_starts)
     coarse_jump = restrict(correction)
     earlier_correction = passed_along(correction[-1], "tm", 1)
     tm_index = lax.axis_index("tm")
@@ -217,7 +222,7 @@
         return jnp.concatenate(values, axis=0)
 
     if slice_count == 1:
-        seed = jnp.where(tm_index == 0, apply_coarse(first_coarse, coarse_x, coarse_y), 0.0)
+        seed = jnp.where(tm_index == 0, coarse_of_starts[0], 0.0)
         reached = prefix_over_tm(coarse_jump[0] + seed, coarse_x, coarse_y)
         coarse_applied = (reached - coarse_jump[0])[None]
     else:

time: 69.2 us -> 67.3 us (0.973)
  local copies, waits for them, and re-layouts: 5.67 us -> 2.64 us
  waiting for transfers between devices: 16.4 us -> 18.5 us
  matrix products: 13.2 us -> 12.1 us
    ppermute x1, waiting for transfers between devices: 0.01 us -> 2.25 us  [on_device(): from_next = lax.ppermute(layers[:, :, :HALO, :], 'space', backward)]
    slice x6 -> x2, local copies, waits for them, and re-layouts: 1.99 us -> 0.22 us  [restrict(): return 0.5 * (values[..., 0::2, :] + values[..., 1::2, :])]
    unnamed x34 -> x30, local copies, waits for them, and re-layouts: 3.13 us -> 1.69 us
    dot_general x8 -> x7, matrix products: 6.62 us -> 5.48 us  [apply_coarse(): jnp.einsum('...tik,tlk->...til', mixed_x, matrix_y, precision=exact_preci...]
    dot_general x8 -> x7, matrix products: 3.07 us -> 2.58 us  [apply_coarse(): jnp.einsum('tij,...tjk->...tik', matrix_x, coarse_values, precision=exact...]
  transfers between devices with their start and end apart: 9 -> 9, of which waited for: 6 -> 7; matrix products, arithmetic and copies ran while one was open for 22% -> 20% of each run, Pallas kernels for 0% -> 0%
where the time goes in v11:
time: 67.3 us; the launch traced here: 66.8 us
  starting transfers between devices  20.6 us (31%)
  waiting for transfers between devices  18.5 us (27%)
  matrix products  12.1 us (18%)
  Pallas kernels  6.89 us (10%)
  other arithmetic  5.02 us (7%)
  local copies, waits for them, and re-layouts  2.64 us (4%)
  between operations  1.08 us (2%)
    ppermute x7, waiting for transfers between devices, passed_along(): return lax.ppermute(block, axis, route)  16.2 us
    ppermute x7, starting transfers between devices, passed_along(): return lax.ppermute(block, axis, route)  14.8 us
    pallas_call x1, Pallas kernels, fine_propagate(): pl.pallas_call(functools.partial(fine_kernel, slice_at), out_shape=jax.Sh...  6.89 us
    dot_general x7, matrix products, apply_coarse(): jnp.einsum('...tik,tlk->...til', mixed_x, matrix_y, precision=exact_preci...  5.48 us
    ppermute x1, starting transfers between devices, on_device(): from_prev = lax.ppermute(layers[:, :, rows - HALO:, :], 'space', forward)  3.47 us
    dot_general x7, matrix products, apply_coarse(): jnp.einsum('tij,...tjk->...tik', matrix_x, coarse_values, precision=exact...  2.58 us
    dot_general x2, matrix products, prefix_over_tm(): jnp.einsum('tij,tjk->tik', power_y, power_y, precision=exact_precision)  2.57 us
    ppermute x1, starting transfers between devices, on_device(): from_next = lax.ppermute(layers[:, :, :HALO, :], 'space', backward)  2.37 us
  transfers between devices with their start and end apart: 9, of which 7 were waited for; matrix products, arithmetic and copies ran while one was open for 20% of the time, Pallas kernels for 0%

profile of v11, /device:TPU:12, one launch (start us, length us, event | category | flops | bytes accessed | tf_op | source)
XLA Modules:
  0.0 66.8 jit_solution(4627071027762082992)
XLA Ops:
  0.6 1.2 %subtract_bitcast_fusion = f32[1,8,128,128]{3,2,1,0:T(8,128)S(1)} fusion(s32[8,128,128]{2,1,0:T(8,128)} %obstacle_ref.1), kind=kLoop, calls=%fused_computation.16 | loop fusion | flops 262144 | bytes 1048576 | tf_op jit(solution)/shard_map/stack | solution.py:155
  2.0 1.9 %pad_maximum_fusion = (f32[5,8,16,128]{3,2,1,0:T(8,128)}, f32[5,8,16,128]{3,2,1,0:T(8,128)}) fusion(f32[1,8,128,128]{3,2,1,0:T(8,128)S(1)} %subtract_bitcast_fusion, f32[2,8,128,128]{3,2,1,0:T(8,128)} %velocity_ref.1, f32[1,8,128,128]{3,2,1,0:T(8,128)S(1)} %bitcast.58, f32[1,8,128,128]{3,2,1,0:T(8,128)S(1)} %copy-done), kind=kLoop, calls=%fused_computation.17 | loop fusion | flops 491520 | bytes 3276800 | tf_op jit(solution)/shard_map/concatenate | solution.py:156
  3.9 3.5 %collective-permute-start = (f32[5,8,16,128]{3,2,1,0:T(8,128)}, f32[5,8,16,128]{3,2,1,0:T(8,128)S(1)}, u32[]{:S(2)}, u32[]{:S(2)}) collective-permute-start(f32[5,8,16,128]{3,2,1,0:T(8,128)} %get-tuple-element.3), channel_id=1, source_target_pairs={{0,1},{1,2},{2,3},{4,5},{5,6},{6,7},{8,9},{9,10},{10,11},{12,13},{... | collective-permute-start | bytes 983048 | tf_op jit(solution)/shard_map/ppermute | solution.py:160
  7.4 2.4 %collective-permute-start.1 = (f32[5,8,16,128]{3,2,1,0:T(8,128)}, f32[5,8,16,128]{3,2,1,0:T(8,128)S(1)}, u32[]{:S(2)}, u32[]{:S(2)}) collective-permute-start(f32[5,8,16,128]{3,2,1,0:T(8,128)} %get-tuple-element.2), channel_id=1, source_target_pairs={{1,0},{2,1},{3,2},{5,4},{6,5},{7,6},{9,8},{10,9},{11,10},{13,12},{... | collective-permute-start | bytes 983048 | tf_op jit(solution)/shard_map/ppermute | solution.py:161
  10.4 1.0 %fusion.6 = f32[8,64,128]{2,1,0:T(8,128)S(1)} fusion(f32[8,64,128]{1,0,2:T(8,128)S(1)} %bitcast.64, f32[1,8,128,128]{3,2,1,0:T(8,128)S(1)} %copy-done), kind=kOutput, calls=%fused_computation.12 | convolution fusion | flops 100663296 | bytes 1048576 | tf_op jit(solution)/shard_map/tij,...tjk->...tik/dot_general | solution.py:38
  11.5 1.1 %fusion.28 = f32[8,64,64]{2,1,0:T(8,128)} fusion(f32[8,64,64]{2,1,0:T(8,128)S(1)} %fusion.26), kind=kOutput, calls=%fused_computation.53 | convolution fusion | flops 25165824 | bytes 262144 | tf_op jit(solution)/shard_map/tij,tjk->tik/dot_general | solution.py:205
  12.6 1.8 %fusion.25 = f32[8,64,128]{2,1,0:T(8,128)} fusion(f32[8,64,128]{2,1,0:T(8,128)S(1)} %fusion.6, f32[8,128,128]{2,1,0:T(8,128)S(1)} %copy-done.5), kind=kOutput, calls=%fused_computation.50 | convolution fusion | flops 100663296 | bytes 1048576 | tf_op jit(solution)/shard_map/...tik,tlk->...til/dot_general | solution.py:39
  14.4 1.9 %fusion.27 = f32[8,128,128]{2,1,0:T(8,128)S(1)} fusion(f32[8,128,128]{2,1,0:T(8,128)} %param.15), kind=kOutput, calls=%fused_computation.52 | convolution fusion | flops 201326592 | bytes 1048576 | tf_op jit(solution)/shard_map/tij,tjk->tik/dot_general | solution.py:206
  16.4 2.3 %collective-permute-done.1.next_ref = f32[5,8,16,128]{3,2,1,0:T(8,128)S(1)} collective-permute-done((f32[5,8,16,128]{3,2,1,0:T(8,128)}, f32[5,8,16,128]{3,2,1,0:T(8,128)S(1)}, u32[]{:S(2)}, u32[]{:S(2)}) %collective-permute-start.1) | collective-permute-done | bytes 327712 | tf_op jit(solution)/shard_map/ppermute | solution.py:161
  18.7 0.6 copy-done.4
  19.3 6.9 %shard_map.95 = f32[8,128,128]{2,1,0:T(8,128)S(1)} custom-call(s32[8]{0:T(128)S(1)} %get-tuple-element.8.south_ref, s32[8]{0:T(128)S(1)} %get-tuple-element.7.north_ref, s32[8]{0:T(128)S(1)} %get-tuple-element.9.west_at_ref, s32[8]{0:T(128)S(1)} %get-tuple-element.6.east_at_ref, s32[8]{0:T(128)S(1)} %get-tuple-element.5.west_ok_ref, ...), custom_call_target="tpu_custom_call" | custom-call | tf_op jit(solution)/shard_map/pallas_call | solution.py:131
  26.7 0.8 %copy-done.13 = f32[8,64,128]{2,1,0:T(8,128)S(1)} copy-done((f32[8,64,128]{2,1,0:T(8,128)S(1)}, f32[8,64,128]{2,1,0:T(8,128)}, u32[]{:S(2)}) %copy-start.13) | copy-done | bytes 262168
  27.6 2.1 %collective-permute-start.2 = (f32[8,64,128]{2,1,0:T(8,128)S(1)}, f32[8,64,128]{2,1,0:T(8,128)S(1)}, u32[]{:S(2)}, u32[]{:S(2)}) collective-permute-start(f32[8,64,128]{2,1,0:T(8,128)S(1)} %bitcast_add_fusion), channel_id=1, source_target_pairs={{0,4},{4,8},{8,12},{12,16},{16,20},{20,24},{24,28},{1,5},{5,9},{9,... | collective-permute-start | bytes 786440 | tf_op jit(solution)/shard_map/ppermute | solution.py:26
  29.7 0.6 fusion.29
  30.3 3.6 %collective-permute-start.8 = (f32[8,128,128]{2,1,0:T(8,128)S(1)}, f32[8,128,128]{2,1,0:T(8,128)S(1)}, u32[]{:S(2)}, u32[]{:S(2)}) collective-permute-start(f32[8,128,128]{2,1,0:T(8,128)S(1)} %sub.57), channel_id=1, source_target_pairs={{0,4},{4,8},{8,12},{12,16},{16,20},{20,24},{24,28},{1,5},{5,9},{9,... | collective-permute-start | bytes 1572872 | tf_op jit(solution)/shard_map/ppermute | solution.py:26
  34.0 2.4 %collective-permute-done.2 = f32[8,64,128]{2,1,0:T(8,128)S(1)} collective-permute-done((f32[8,64,128]{2,1,0:T(8,128)S(1)}, f32[8,64,128]{2,1,0:T(8,128)S(1)}, u32[]{:S(2)}, u32[]{:S(2)}) %collective-permute-start.2) | collective-permute-done | bytes 262176 | tf_op jit(solution)/shard_map/ppermute | solution.py:26
  36.6 0.6 fusion.5
  37.3 2.5 %collective-permute-start.3 = (f32[4,64,128]{2,1,0:T(8,128)S(1)}, f32[4,64,128]{2,1,0:T(8,128)S(1)}, u32[]{:S(2)}, u32[]{:S(2)}) collective-permute-start(f32[4,64,128]{2,1,0:T(8,128)S(1)} %fusion.5), channel_id=1, source_target_pairs={{0,8},{4,12},{8,16},{12,20},{16,24},{20,28},{1,9},{5,13},{9,17},{1... | collective-permute-start | bytes 393224 | tf_op jit(solution)/shard_map/ppermute | solution.py:26
  40.0 0.6 fusion.2
  40.7 1.3 %collective-permute-start.5 = (f32[4,64,128]{2,1,0:T(8,128)S(1)}, f32[4,64,128]{2,1,0:T(8,128)S(1)}, u32[]{:S(2)}, u32[]{:S(2)}) collective-permute-start(f32[4,64,128]{2,1,0:T(8,128)S(1)} %fusion.2), channel_id=1, source_target_pairs={{0,16},{4,20},{8,24},{12,28},{1,17},{5,21},{9,25},{13,29},{2,18},{... | collective-permute-start | bytes 393224 | tf_op jit(solution)/shard_map/ppermute | solution.py:26
  42.0 3.1 %collective-permute-done.3 = f32[4,64,128]{2,1,0:T(8,128)S(1)} collective-permute-done((f32[4,64,128]{2,1,0:T(8,128)S(1)}, f32[4,64,128]{2,1,0:T(8,128)S(1)}, u32[]{:S(2)}, u32[]{:S(2)}) %collective-permute-start.3) | collective-permute-done | bytes 131104 | tf_op jit(solution)/shard_map/ppermute | solution.py:26
  45.3 0.6 fusion.4
  45.9 1.3 %collective-permute-start.4 = (f32[4,64,128]{2,1,0:T(8,128)S(1)}, f32[4,64,128]{2,1,0:T(8,128)S(1)}, u32[]{:S(2)}, u32[]{:S(2)}) collective-permute-start(f32[4,64,128]{2,1,0:T(8,128)S(1)} %fusion.4), channel_id=1, source_target_pairs={{0,16},{4,20},{8,24},{12,28},{1,17},{5,21},{9,25},{13,29},{2,18},{... | collective-permute-start | bytes 393224 | tf_op jit(solution)/shard_map/ppermute | solution.py:26
  47.8 0.6 fusion.1
  48.5 2.1 %collective-permute-start.6 = (f32[4,64,128]{2,1,0:T(8,128)S(1)}, f32[4,64,128]{2,1,0:T(8,128)S(1)}, u32[]{:S(2)}, u32[]{:S(2)}) collective-permute-start(f32[4,64,128]{2,1,0:T(8,128)S(1)} %fusion.1), channel_id=1, source_target_pairs={{0,8},{4,12},{8,16},{12,20},{16,24},{20,28},{1,9},{5,13},{9,17},{1... | collective-permute-start | bytes 393224 | tf_op jit(solution)/shard_map/ppermute | solution.py:26
  50.6 3.6 %collective-permute-done.4 = f32[4,64,128]{2,1,0:T(8,128)S(1)} collective-permute-done((f32[4,64,128]{2,1,0:T(8,128)S(1)}, f32[4,64,128]{2,1,0:T(8,128)S(1)}, u32[]{:S(2)}, u32[]{:S(2)}) %collective-permute-start.4) | collective-permute-done | bytes 131104 | tf_op jit(solution)/shard_map/ppermute | solution.py:26
  54.4 0.6 fusion.3
  55.1 1.2 %collective-permute-done.6 = f32[4,64,128]{2,1,0:T(8,128)S(1)} collective-permute-done((f32[4,64,128]{2,1,0:T(8,128)S(1)}, f32[4,64,128]{2,1,0:T(8,128)S(1)}, u32[]{:S(2)}, u32[]{:S(2)}) %collective-permute-start.6) | collective-permute-done | bytes 131104 | tf_op jit(solution)/shard_map/ppermute | solution.py:26
  57.2 1.9 %collective-permute-start.7 = (f32[8,64,128]{2,1,0:T(8,128)S(1)}, f32[8,64,128]{2,1,0:T(8,128)S(1)}, u32[]{:S(2)}, u32[]{:S(2)}) collective-permute-start(f32[8,64,128]{2,1,0:T(8,128)S(1)} %maximum_subtract_fusion), channel_id=1, source_target_pairs={{0,4},{4,8},{8,12},{12,16},{16,20},{20,24},{24,28},{1,5},{5,9},{9,... | collective-permute-start | bytes 786440 | tf_op jit(solution)/shard_map/ppermute | solution.py:26
  59.3 0.9 %add_bitcast_fusion = f32[1,8,128,128]{3,2,1,0:T(8,128)} fusion(f32[8,128,128]{2,1,0:T(8,128)S(1)} %bitcast.63, f32[8,128,128]{2,1,0:T(8,128)S(1)} %sub.57), kind=kLoop, calls=%fused_computation.15 | loop fusion | flops 131072 | bytes 1572864 | tf_op jit(solution)/shard_map/add | solution.py:249
  60.1 5.6 %collective-permute-done.7 = f32[8,64,128]{2,1,0:T(8,128)S(1)} collective-permute-done((f32[8,64,128]{2,1,0:T(8,128)S(1)}, f32[8,64,128]{2,1,0:T(8,128)S(1)}, u32[]{:S(2)}, u32[]{:S(2)}) %collective-permute-start.7) | collective-permute-done | bytes 262176 | tf_op jit(solution)/shard_map/ppermute | solution.py:26
  65.9 0.9 %select_bitcast_fusion = f32[1,8,128,128]{3,2,1,0:T(8,128)} fusion(f32[8,128,128]{2,1,0:T(8,128)S(1)} %bitcast.61, f32[8,128,128]{2,1,0:T(8,128)S(1)} %collective-permute-done.8, pred[]{:T(512)S(6)} %eq.4, f32[1,8,128,128]{3,2,1,0:T(8,128)S(1)} %copy-done), kind=kLoop, calls=%fused_computation.14 | loop fusion | flops 393216 | bytes 2097153 | tf_op jit(solution)/shard_map/broadcast_in_dim | solution.py:254
  (52 shorter events, 4.3 us)
Async XLA Ops:
  0.6 1.2 %copy-start.2 = (f32[8,128,128]{2,1,0:T(8,128)S(1)}, f32[8,128,128]{2,1,0:T(8,128)}, u32[]{:S(2)}) copy-start(f32[8,128,128]{2,1,0:T(8,128)} %diffusivity_ref.1) | copy-start | bytes 1572868
  0.6 1.3 %copy-start = (f32[1,8,128,128]{3,2,1,0:T(8,128)S(1)}, f32[1,8,128,128]{3,2,1,0:T(8,128)}, u32[]{:S(2)}) copy-start(f32[1,8,128,128]{3,2,1,0:T(8,128)} %param.8) | copy-start | bytes 1572868
  2.0 7.8 %copy-start.9 = (f32[8,64,64]{2,1,0:T(8,128)S(1)}, f32[8,64,64]{2,1,0:T(8,128)}, u32[]{:S(2)}) copy-start(f32[8,64,64]{2,1,0:T(8,128)} %param.14) | copy-start | bytes 393220
  3.9 12.5 %collective-permute-start = (f32[5,8,16,128]{3,2,1,0:T(8,128)}, f32[5,8,16,128]{3,2,1,0:T(8,128)S(1)}, u32[]{:S(2)}, u32[]{:S(2)}) collective-permute-start(f32[5,8,16,128]{3,2,1,0:T(8,128)} %get-tuple-element.3), channel_id=1, source_target_pairs={{0,1},{1,2},{2,3},{4,5},{5,6},{6,7},{8,9},{9,10},{10,11},{12,13},{... | collective-permute-start | bytes 983048 | tf_op jit(solution)/shard_map/ppermute | solution.py:160
  7.4 11.3 %collective-permute-start.1 = (f32[5,8,16,128]{3,2,1,0:T(8,128)}, f32[5,8,16,128]{3,2,1,0:T(8,128)S(1)}, u32[]{:S(2)}, u32[]{:S(2)}) collective-permute-start(f32[5,8,16,128]{3,2,1,0:T(8,128)} %get-tuple-element.2), channel_id=1, source_target_pairs={{1,0},{2,1},{3,2},{5,4},{6,5},{7,6},{9,8},{10,9},{11,10},{13,12},{... | collective-permute-start | bytes 983048 | tf_op jit(solution)/shard_map/ppermute | solution.py:161
  10.2 1.3 %copy-start.7 = (f32[8,64,64]{2,1,0:T(8,128)}, f32[8,64,64]{2,1,0:T(8,128)S(1)}, u32[]{:S(2)}) copy-start(f32[8,64,64]{2,1,0:T(8,128)S(1)} %fusion.26) | copy-start | bytes 393220
  11.5 1.1 %copy-start.5 = (f32[8,128,128]{2,1,0:T(8,128)S(1)}, f32[8,128,128]{2,1,0:T(8,128)}, u32[]{:S(2)}) copy-start(f32[8,128,128]{2,1,0:T(8,128)} %param.15) | copy-start | bytes 1572868
  12.6 1.8 %copy-start.14 = (s32[8,4]{0,1:T(4,128)S(1)}, s32[8,4]{0,1:T(4,128)}, u32[]{:S(2)}) copy-start(s32[8,4]{0,1:T(4,128)} %param.13) | copy-start | bytes 388
  14.4 4.3 %copy-start.1 = (f32[2,8,128,128]{3,2,1,0:T(8,128)S(1)}, f32[2,8,128,128]{3,2,1,0:T(8,128)}, u32[]{:S(2)}) copy-start(f32[2,8,128,128]{3,2,1,0:T(8,128)} %velocity_ref.1) | copy-start | bytes 3145732
  14.4 4.2 %copy-start.3 = (s32[8,128,128]{2,1,0:T(8,128)S(1)}, s32[8,128,128]{2,1,0:T(8,128)}, u32[]{:S(2)}) copy-start(s32[8,128,128]{2,1,0:T(8,128)} %obstacle_ref.1) | copy-start | bytes 1572868
  18.7 0.7 copy-start.4
  19.3 6.9 %copy-start.12 = (f32[8,64,128]{2,1,0:T(8,128)S(1)}, f32[8,64,128]{2,1,0:T(8,128)}, u32[]{:S(2)}) copy-start(f32[8,64,128]{2,1,0:T(8,128)} %fusion.25) | copy-start | bytes 786436
  26.6 1.0 %copy-start.13 = (f32[8,64,128]{2,1,0:T(8,128)S(1)}, f32[8,64,128]{2,1,0:T(8,128)}, u32[]{:S(2)}) copy-start(f32[8,64,128]{2,1,0:T(8,128)} %fusion.25) | copy-start | bytes 786436
  27.6 8.7 %copy-start.10 = (f32[8,64,64]{2,1,0:T(8,128)S(1)}, f32[8,64,64]{2,1,0:T(8,128)}, u32[]{:S(2)}) copy-start(f32[8,64,64]{2,1,0:T(8,128)} %param.14) | copy-start | bytes 393220
  27.6 8.7 %collective-permute-start.2 = (f32[8,64,128]{2,1,0:T(8,128)S(1)}, f32[8,64,128]{2,1,0:T(8,128)S(1)}, u32[]{:S(2)}, u32[]{:S(2)}) collective-permute-start(f32[8,64,128]{2,1,0:T(8,128)S(1)} %bitcast_add_fusion), channel_id=1, source_target_pairs={{0,4},{4,8},{8,12},{12,16},{16,20},{20,24},{24,28},{1,5},{5,9},{9,... | collective-permute-start | bytes 786440 | tf_op jit(solution)/shard_map/ppermute | solution.py:26
  30.3 6.3 %copy-start.6 = (f32[8,128,128]{2,1,0:T(8,128)S(1)}, f32[8,128,128]{2,1,0:T(8,128)}, u32[]{:S(2)}) copy-start(f32[8,128,128]{2,1,0:T(8,128)} %param.15) | copy-start | bytes 1572868
  30.3 29.8 %collective-permute-start.8 = (f32[8,128,128]{2,1,0:T(8,128)S(1)}, f32[8,128,128]{2,1,0:T(8,128)S(1)}, u32[]{:S(2)}, u32[]{:S(2)}) collective-permute-start(f32[8,128,128]{2,1,0:T(8,128)S(1)} %sub.57), channel_id=1, source_target_pairs={{0,4},{4,8},{8,12},{12,16},{16,20},{20,24},{24,28},{1,5},{5,9},{9,... | collective-permute-start | bytes 1572872 | tf_op jit(solution)/shard_map/ppermute | solution.py:26
  37.3 7.8 %collective-permute-start.3 = (f32[4,64,128]{2,1,0:T(8,128)S(1)}, f32[4,64,128]{2,1,0:T(8,128)S(1)}, u32[]{:S(2)}, u32[]{:S(2)}) collective-permute-start(f32[4,64,128]{2,1,0:T(8,128)S(1)} %fusion.5), channel_id=1, source_target_pairs={{0,8},{4,12},{8,16},{12,20},{16,24},{20,28},{1,9},{5,13},{9,17},{1... | collective-permute-start | bytes 393224 | tf_op jit(solution)/shard_map/ppermute | solution.py:26
  40.0 5.0 %copy-start.8 = (f32[8,64,64]{2,1,0:T(8,128)S(1)}, f32[8,64,64]{2,1,0:T(8,128)}, u32[]{:S(2)}) copy-start(f32[8,64,64]{2,1,0:T(8,128)} %copy-done.7) | copy-start | bytes 393220
  40.7 6.9 %collective-permute-start.5 = (f32[4,64,128]{2,1,0:T(8,128)S(1)}, f32[4,64,128]{2,1,0:T(8,128)S(1)}, u32[]{:S(2)}, u32[]{:S(2)}) collective-permute-start(f32[4,64,128]{2,1,0:T(8,128)S(1)} %fusion.2), channel_id=1, source_target_pairs={{0,16},{4,20},{8,24},{12,28},{1,17},{5,21},{9,25},{13,29},{2,18},{... | collective-permute-start | bytes 393224 | tf_op jit(solution)/shard_map/ppermute | solution.py:26
  45.3 2.3 %copy-start.11 = (f32[8,64,64]{2,1,0:T(8,128)S(1)}, f32[8,64,64]{2,1,0:T(8,128)}, u32[]{:S(2)}) copy-start(f32[8,64,64]{2,1,0:T(8,128)} %fusion.28) | copy-start | bytes 393220
  45.9 8.3 %collective-permute-start.4 = (f32[4,64,128]{2,1,0:T(8,128)S(1)}, f32[4,64,128]{2,1,0:T(8,128)S(1)}, u32[]{:S(2)}, u32[]{:S(2)}) collective-permute-start(f32[4,64,128]{2,1,0:T(8,128)S(1)} %fusion.4), channel_id=1, source_target_pairs={{0,16},{4,20},{8,24},{12,28},{1,17},{5,21},{9,25},{13,29},{2,18},{... | collective-permute-start | bytes 393224 | tf_op jit(solution)/shard_map/ppermute | solution.py:26
  48.5 7.8 %collective-permute-start.6 = (f32[4,64,128]{2,1,0:T(8,128)S(1)}, f32[4,64,128]{2,1,0:T(8,128)S(1)}, u32[]{:S(2)}, u32[]{:S(2)}) collective-permute-start(f32[4,64,128]{2,1,0:T(8,128)S(1)} %fusion.1), channel_id=1, source_target_pairs={{0,8},{4,12},{8,16},{12,20},{16,24},{20,28},{1,9},{5,13},{9,17},{1... | collective-permute-start | bytes 393224 | tf_op jit(solution)/shard_map/ppermute | solution.py:26
  57.2 8.6 %collective-permute-start.7 = (f32[8,64,128]{2,1,0:T(8,128)S(1)}, f32[8,64,128]{2,1,0:T(8,128)S(1)}, u32[]{:S(2)}, u32[]{:S(2)}) collective-permute-start(f32[8,64,128]{2,1,0:T(8,128)S(1)} %maximum_subtract_fusion), channel_id=1, source_target_pairs={{0,4},{4,8},{8,12},{12,16},{16,20},{20,24},{24,28},{1,5},{5,9},{9,... | collective-permute-start | bytes 786440 | tf_op jit(solution)/shard_map/ppermute | solution.py:26

commit v12 on v11

--- a/solution.py
+++ b/solution.py
@@ -188,12 +188,11 @@
     coarse_of_starts = apply_coarse(starts, restricting_x, coarse_y)
     correction = fine_ends - prolong(coarse_of_starts)
     coarse_jump = restrict(correction)
-    earlier_correction = passed_along(correction[-1], "tm", 1)
     tm_index = lax.axis_index("tm")
     tm_count = lax.axis_size("tm")
     first_coarse = restrict(starts[0])
 
-    def prefix_over_tm(total, power_x, power_y):
+    def prefix_over_tm(total, power_x, power_y, later):
         distances = []
         distance = 1
         while distance < tm_count:
@@ -211,6 +210,8 @@
         for step in range(len(distances)):
             if step == 0:
                 received = passed_along(total, "tm", distances[0])
+                later, received = lax.optimization_barrier((later, received))
+                later = passed_along(later, "tm", 1)
                 received = [received[part] for part, _ in parts]
             else:
                 received = [passed_along(values[k], "tm", parts[k][1][step]) for k in range(2)]
@@ -219,11 +220,13 @@
                 distance = order[step]
                 mixed = apply_coarse(received[k], powers[distance][0][part], powers[distance][1][part])
                 values[k] = values[k] + jnp.where(tm_index >= distance, mixed, 0.0)
-        return jnp.concatenate(values, axis=0)
+        return jnp.concatenate(values, axis=0), later
 
     if slice_count == 1:
         seed = jnp.where(tm_index == 0, coarse_of_starts[0], 0.0)
-        reached = prefix_over_tm(coarse_jump[0] + seed, coarse_x, coarse_y)
+        reached, earlier_correction = prefix_over_tm(
+            coarse_jump[0] + seed, coarse_x, coarse_y, correction[-1]
+        )
         coarse_applied = (reached - coarse_jump[0])[None]
     else:
         shifted_jump = jnp.concatenate(
@@ -239,7 +242,7 @@
         for n in range(1, slice_count):
             power_x = jnp.einsum("tij,tjk->tik", power_x, coarse_x, precision=exact_precision)
             power_y = jnp.einsum("tij,tjk->tik", power_y, coarse_y, precision=exact_precision)
-        total = prefix_over_tm(states[-1], power_x, power_y)
+        total, earlier_correction = prefix_over_tm(states[-1], power_x, power_y, correction[-1])
         earlier = jnp.where(tm_index > 0, passed_along(total, "tm", 1), 0.0)
         own_coarse = []
         for n in range(slice_count):

time: 67.3 us -> 71 us (1.055)
  waiting for transfers between devices: 18.5 us -> 23.8 us
  starting transfers between devices: 20.6 us -> 19 us
    ppermute x7, waiting for transfers between devices: 16.2 us -> 21.5 us  [passed_along(): return lax.ppermute(block, axis, route)]
    ppermute x7, starting transfers between devices: 14.8 us -> 13.2 us  [passed_along(): return lax.ppermute(block, axis, route)]
  transfers between devices with their start and end apart: 9 -> 9, of which waited for: 7 -> 5; matrix products, arithmetic and copies ran while one was open for 20% -> 17% of each run, Pallas kernels for 0% -> 0%
where the time goes in v12:
time: 71 us; the launch traced here: 70.5 us
  waiting for transfers between devices  23.8 us (34%)
  starting transfers between devices  19 us (27%)
  matrix products  12.1 us (17%)
  Pallas kernels  6.85 us (10%)
  other arithmetic  5.01 us (7%)
  local copies, waits for them, and re-layouts  2.64 us (4%)
  between operations  1.11 us (2%)
    ppermute x7, waiting for transfers between devices, passed_along(): return lax.ppermute(block, axis, route)  21.5 us
    ppermute x7, starting transfers between devices, passed_along(): return lax.ppermute(block, axis, route)  13.2 us
    pallas_call x1, Pallas kernels, fine_propagate(): pl.pallas_call(functools.partial(fine_kernel, slice_at), out_shape=jax.Sh...  6.85 us
    dot_general x7, matrix products, apply_coarse(): jnp.einsum('...tik,tlk->...til', mixed_x, matrix_y, precision=exact_preci...  5.49 us
    ppermute x1, starting transfers between devices, on_device(): from_prev = lax.ppermute(layers[:, :, rows - HALO:, :], 'space', forward)  3.47 us
    dot_general x7, matrix products, apply_coarse(): jnp.einsum('tij,...tjk->...tik', matrix_x, coarse_values, precision=exact...  2.58 us
    dot_general x2, matrix products, prefix_over_tm(): jnp.einsum('tij,tjk->tik', power_y, power_y, precision=exact_precision)  2.57 us
    ppermute x1, starting transfers between devices, on_device(): from_next = lax.ppermute(layers[:, :, :HALO, :], 'space', backward)  2.37 us
  transfers between devices with their start and end apart: 9, of which 5 were waited for; matrix products, arithmetic and copies ran while one was open for 17% of the time, Pallas kernels for 0%

profile of v12, /device:TPU:12, one launch (start us, length us, event | category | flops | bytes accessed | tf_op | source)
XLA Modules:
  0.0 70.5 jit_solution(4365422470254729814)
XLA Ops:
  0.6 1.2 %subtract_bitcast_fusion = f32[1,8,128,128]{3,2,1,0:T(8,128)S(1)} fusion(s32[8,128,128]{2,1,0:T(8,128)} %obstacle_ref.1), kind=kLoop, calls=%fused_computation.16 | loop fusion | flops 262144 | bytes 1048576 | tf_op jit(solution)/shard_map/stack | solution.py:155
  2.0 1.9 %pad_maximum_fusion = (f32[5,8,16,128]{3,2,1,0:T(8,128)}, f32[5,8,16,128]{3,2,1,0:T(8,128)}) fusion(f32[1,8,128,128]{3,2,1,0:T(8,128)S(1)} %subtract_bitcast_fusion, f32[2,8,128,128]{3,2,1,0:T(8,128)} %velocity_ref.1, f32[1,8,128,128]{3,2,1,0:T(8,128)S(1)} %bitcast.58, f32[1,8,128,128]{3,2,1,0:T(8,128)S(1)} %copy-done), kind=kLoop, calls=%fused_computation.17 | loop fusion | flops 491520 | bytes 3276800 | tf_op jit(solution)/shard_map/concatenate | solution.py:156
  3.9 3.5 %collective-permute-start = (f32[5,8,16,128]{3,2,1,0:T(8,128)}, f32[5,8,16,128]{3,2,1,0:T(8,128)S(1)}, u32[]{:S(2)}, u32[]{:S(2)}) collective-permute-start(f32[5,8,16,128]{3,2,1,0:T(8,128)} %get-tuple-element.7), channel_id=1, source_target_pairs={{0,1},{1,2},{2,3},{4,5},{5,6},{6,7},{8,9},{9,10},{10,11},{12,13},{... | collective-permute-start | bytes 983048 | tf_op jit(solution)/shard_map/ppermute | solution.py:160
  7.4 2.4 %collective-permute-start.1 = (f32[5,8,16,128]{3,2,1,0:T(8,128)}, f32[5,8,16,128]{3,2,1,0:T(8,128)S(1)}, u32[]{:S(2)}, u32[]{:S(2)}) collective-permute-start(f32[5,8,16,128]{3,2,1,0:T(8,128)} %get-tuple-element.6), channel_id=1, source_target_pairs={{1,0},{2,1},{3,2},{5,4},{6,5},{7,6},{9,8},{10,9},{11,10},{13,12},{... | collective-permute-start | bytes 983048 | tf_op jit(solution)/shard_map/ppermute | solution.py:161
  10.4 1.0 %fusion.6 = f32[8,64,128]{2,1,0:T(8,128)S(1)} fusion(f32[8,64,128]{1,0,2:T(8,128)S(1)} %bitcast.64, f32[1,8,128,128]{3,2,1,0:T(8,128)S(1)} %copy-done), kind=kOutput, calls=%fused_computation.12 | convolution fusion | flops 100663296 | bytes 1048576 | tf_op jit(solution)/shard_map/tij,...tjk->...tik/dot_general | solution.py:38
  11.5 1.1 %fusion.28 = f32[8,64,64]{2,1,0:T(8,128)} fusion(f32[8,64,64]{2,1,0:T(8,128)S(1)} %fusion.26), kind=kOutput, calls=%fused_computation.53 | convolution fusion | flops 25165824 | bytes 262144 | tf_op jit(solution)/shard_map/tij,tjk->tik/dot_general | solution.py:204
  12.6 1.8 %fusion.25 = f32[8,64,128]{2,1,0:T(8,128)} fusion(f32[8,64,128]{2,1,0:T(8,128)S(1)} %fusion.6, f32[8,128,128]{2,1,0:T(8,128)S(1)} %copy-done.5), kind=kOutput, calls=%fused_computation.50 | convolution fusion | flops 100663296 | bytes 1048576 | tf_op jit(solution)/shard_map/...tik,tlk->...til/dot_general | solution.py:39
  14.4 1.9 %fusion.27 = f32[8,128,128]{2,1,0:T(8,128)S(1)} fusion(f32[8,128,128]{2,1,0:T(8,128)} %param.15), kind=kOutput, calls=%fused_computation.52 | convolution fusion | flops 201326592 | bytes 1048576 | tf_op jit(solution)/shard_map/tij,tjk->tik/dot_general | solution.py:205
  16.4 2.3 %collective-permute-done.1.next_ref = f32[5,8,16,128]{3,2,1,0:T(8,128)S(1)} collective-permute-done((f32[5,8,16,128]{3,2,1,0:T(8,128)}, f32[5,8,16,128]{3,2,1,0:T(8,128)S(1)}, u32[]{:S(2)}, u32[]{:S(2)}) %collective-permute-start.1) | collective-permute-done | bytes 327712 | tf_op jit(solution)/shard_map/ppermute | solution.py:161
  18.7 0.6 copy-done.4
  19.3 6.9 %shard_map.95 = f32[8,128,128]{2,1,0:T(8,128)S(1)} custom-call(s32[8]{0:T(128)S(1)} %get-tuple-element.12.south_ref, s32[8]{0:T(128)S(1)} %get-tuple-element.11.north_ref, s32[8]{0:T(128)S(1)} %get-tuple-element.13.west_at_ref, s32[8]{0:T(128)S(1)} %get-tuple-element.10.east_at_ref, s32[8]{0:T(128)S(1)} %get-tuple-element.9.west_ok_ref, ...), custom_call_target="tpu_custom_call" | custom-call | tf_op jit(solution)/shard_map/pallas_call | solution.py:131
  26.7 0.8 %copy-done.13 = f32[8,64,128]{2,1,0:T(8,128)S(1)} copy-done((f32[8,64,128]{2,1,0:T(8,128)S(1)}, f32[8,64,128]{2,1,0:T(8,128)}, u32[]{:S(2)}) %copy-start.13) | copy-done | bytes 262168
  27.6 2.1 %collective-permute-start.2 = (f32[8,64,128]{2,1,0:T(8,128)S(1)}, f32[8,64,128]{2,1,0:T(8,128)S(1)}, u32[]{:S(2)}, u32[]{:S(2)}) collective-permute-start(f32[8,64,128]{2,1,0:T(8,128)S(1)} %bitcast_add_fusion), channel_id=1, source_target_pairs={{0,4},{4,8},{8,12},{12,16},{16,20},{20,24},{24,28},{1,5},{5,9},{9,... | collective-permute-start | bytes 786440 | tf_op jit(solution)/shard_map/ppermute | solution.py:26
  29.6 0.6 fusion.29
  30.3 6.0 %collective-permute-done.2 = f32[8,64,128]{2,1,0:T(8,128)S(1)} collective-permute-done((f32[8,64,128]{2,1,0:T(8,128)S(1)}, f32[8,64,128]{2,1,0:T(8,128)S(1)}, u32[]{:S(2)}, u32[]{:S(2)}) %collective-permute-start.2) | collective-permute-done | bytes 262176 | tf_op jit(solution)/shard_map/ppermute | solution.py:26
  36.9 0.6 fusion.5
  37.5 2.6 %collective-permute-start.3 = (f32[4,64,128]{2,1,0:T(8,128)S(1)}, f32[4,64,128]{2,1,0:T(8,128)S(1)}, u32[]{:S(2)}, u32[]{:S(2)}) collective-permute-start(f32[4,64,128]{2,1,0:T(8,128)S(1)} %fusion.5), channel_id=1, source_target_pairs={{0,8},{4,12},{8,16},{12,20},{16,24},{20,28},{1,9},{5,13},{9,17},{1... | collective-permute-start | bytes 393224 | tf_op jit(solution)/shard_map/ppermute | solution.py:26
  40.1 0.6 fusion.2
  40.8 1.3 %collective-permute-start.5 = (f32[4,64,128]{2,1,0:T(8,128)S(1)}, f32[4,64,128]{2,1,0:T(8,128)S(1)}, u32[]{:S(2)}, u32[]{:S(2)}) collective-permute-start(f32[4,64,128]{2,1,0:T(8,128)S(1)} %fusion.2), channel_id=1, source_target_pairs={{0,16},{4,20},{8,24},{12,28},{1,17},{5,21},{9,25},{13,29},{2,18},{... | collective-permute-start | bytes 393224 | tf_op jit(solution)/shard_map/ppermute | solution.py:26
  42.1 1.9 %collective-permute-start.8 = (f32[8,128,128]{2,1,0:T(8,128)S(1)}, f32[8,128,128]{2,1,0:T(8,128)S(1)}, u32[]{:S(2)}, u32[]{:S(2)}) collective-permute-start(f32[8,128,128]{2,1,0:T(8,128)S(1)} %sub.57), channel_id=1, source_target_pairs={{0,4},{4,8},{8,12},{12,16},{16,20},{20,24},{24,28},{1,5},{5,9},{9,... | collective-permute-start | bytes 1572872 | tf_op jit(solution)/shard_map/ppermute | solution.py:26
  44.0 1.5 %collective-permute-done.3 = f32[4,64,128]{2,1,0:T(8,128)S(1)} collective-permute-done((f32[4,64,128]{2,1,0:T(8,128)S(1)}, f32[4,64,128]{2,1,0:T(8,128)S(1)}, u32[]{:S(2)}, u32[]{:S(2)}) %collective-permute-start.3) | collective-permute-done | bytes 131104 | tf_op jit(solution)/shard_map/ppermute | solution.py:26
  45.8 0.6 fusion.4
  46.4 1.3 %collective-permute-start.4 = (f32[4,64,128]{2,1,0:T(8,128)S(1)}, f32[4,64,128]{2,1,0:T(8,128)S(1)}, u32[]{:S(2)}, u32[]{:S(2)}) collective-permute-start(f32[4,64,128]{2,1,0:T(8,128)S(1)} %fusion.4), channel_id=1, source_target_pairs={{0,16},{4,20},{8,24},{12,28},{1,17},{5,21},{9,25},{13,29},{2,18},{... | collective-permute-start | bytes 393224 | tf_op jit(solution)/shard_map/ppermute | solution.py:26
  48.0 0.6 fusion.1
  48.6 2.1 %collective-permute-start.6 = (f32[4,64,128]{2,1,0:T(8,128)S(1)}, f32[4,64,128]{2,1,0:T(8,128)S(1)}, u32[]{:S(2)}, u32[]{:S(2)}) collective-permute-start(f32[4,64,128]{2,1,0:T(8,128)S(1)} %fusion.1), channel_id=1, source_target_pairs={{0,8},{4,12},{8,16},{12,20},{16,24},{20,28},{1,9},{5,13},{9,17},{1... | collective-permute-start | bytes 393224 | tf_op jit(solution)/shard_map/ppermute | solution.py:26
  50.7 8.4 %collective-permute-done.4 = f32[4,64,128]{2,1,0:T(8,128)S(1)} collective-permute-done((f32[4,64,128]{2,1,0:T(8,128)S(1)}, f32[4,64,128]{2,1,0:T(8,128)S(1)}, u32[]{:S(2)}, u32[]{:S(2)}) %collective-permute-start.4) | collective-permute-done | bytes 131104 | tf_op jit(solution)/shard_map/ppermute | solution.py:26
  59.3 0.6 fusion.3
  60.2 0.6 fusion
  60.9 1.9 %collective-permute-start.7 = (f32[8,64,128]{2,1,0:T(8,128)S(1)}, f32[8,64,128]{2,1,0:T(8,128)S(1)}, u32[]{:S(2)}, u32[]{:S(2)}) collective-permute-start(f32[8,64,128]{2,1,0:T(8,128)S(1)} %maximum_subtract_fusion), channel_id=1, source_target_pairs={{0,4},{4,8},{8,12},{12,16},{16,20},{20,24},{24,28},{1,5},{5,9},{9,... | collective-permute-start | bytes 786440 | tf_op jit(solution)/shard_map/ppermute | solution.py:26
  63.0 0.9 %add_bitcast_fusion = f32[1,8,128,128]{3,2,1,0:T(8,128)} fusion(f32[8,128,128]{2,1,0:T(8,128)S(1)} %bitcast.63, f32[8,128,128]{2,1,0:T(8,128)S(1)} %sub.57), kind=kLoop, calls=%fused_computation.15 | loop fusion | flops 131072 | bytes 1572864 | tf_op jit(solution)/shard_map/add | solution.py:252
  63.9 5.6 %collective-permute-done.7 = f32[8,64,128]{2,1,0:T(8,128)S(1)} collective-permute-done((f32[8,64,128]{2,1,0:T(8,128)S(1)}, f32[8,64,128]{2,1,0:T(8,128)S(1)}, u32[]{:S(2)}, u32[]{:S(2)}) %collective-permute-start.7) | collective-permute-done | bytes 262176 | tf_op jit(solution)/shard_map/ppermute | solution.py:26
  69.7 0.9 %select_bitcast_fusion = f32[1,8,128,128]{3,2,1,0:T(8,128)} fusion(f32[8,128,128]{2,1,0:T(8,128)S(1)} %bitcast.61, f32[8,128,128]{2,1,0:T(8,128)S(1)} %collective-permute-done.8, pred[]{:T(512)S(6)} %eq.4, f32[1,8,128,128]{3,2,1,0:T(8,128)S(1)} %copy-done), kind=kLoop, calls=%fused_computation.14 | loop fusion | flops 393216 | bytes 2097153 | tf_op jit(solution)/shard_map/broadcast_in_dim | solution.py:257
  (52 shorter events, 3.3 us)
Async XLA Ops:
  0.6 1.2 %copy-start.2 = (f32[8,128,128]{2,1,0:T(8,128)S(1)}, f32[8,128,128]{2,1,0:T(8,128)}, u32[]{:S(2)}) copy-start(f32[8,128,128]{2,1,0:T(8,128)} %diffusivity_ref.1) | copy-start | bytes 1572868
  0.6 1.3 %copy-start = (f32[1,8,128,128]{3,2,1,0:T(8,128)S(1)}, f32[1,8,128,128]{3,2,1,0:T(8,128)}, u32[]{:S(2)}) copy-start(f32[1,8,128,128]{3,2,1,0:T(8,128)} %param.8) | copy-start | bytes 1572868
  2.0 7.8 %copy-start.9 = (f32[8,64,64]{2,1,0:T(8,128)S(1)}, f32[8,64,64]{2,1,0:T(8,128)}, u32[]{:S(2)}) copy-start(f32[8,64,64]{2,1,0:T(8,128)} %param.14) | copy-start | bytes 393220
  3.9 12.5 %collective-permute-start = (f32[5,8,16,128]{3,2,1,0:T(8,128)}, f32[5,8,16,128]{3,2,1,0:T(8,128)S(1)}, u32[]{:S(2)}, u32[]{:S(2)}) collective-permute-start(f32[5,8,16,128]{3,2,1,0:T(8,128)} %get-tuple-element.7), channel_id=1, source_target_pairs={{0,1},{1,2},{2,3},{4,5},{5,6},{6,7},{8,9},{9,10},{10,11},{12,13},{... | collective-permute-start | bytes 983048 | tf_op jit(solution)/shard_map/ppermute | solution.py:160
  7.4 11.3 %collective-permute-start.1 = (f32[5,8,16,128]{3,2,1,0:T(8,128)}, f32[5,8,16,128]{3,2,1,0:T(8,128)S(1)}, u32[]{:S(2)}, u32[]{:S(2)}) collective-permute-start(f32[5,8,16,128]{3,2,1,0:T(8,128)} %get-tuple-element.6), channel_id=1, source_target_pairs={{1,0},{2,1},{3,2},{5,4},{6,5},{7,6},{9,8},{10,9},{11,10},{13,12},{... | collective-permute-start | bytes 983048 | tf_op jit(solution)/shard_map/ppermute | solution.py:161
  10.2 1.3 %copy-start.7 = (f32[8,64,64]{2,1,0:T(8,128)}, f32[8,64,64]{2,1,0:T(8,128)S(1)}, u32[]{:S(2)}) copy-start(f32[8,64,64]{2,1,0:T(8,128)S(1)} %fusion.26) | copy-start | bytes 393220
  11.5 1.1 %copy-start.5 = (f32[8,128,128]{2,1,0:T(8,128)S(1)}, f32[8,128,128]{2,1,0:T(8,128)}, u32[]{:S(2)}) copy-start(f32[8,128,128]{2,1,0:T(8,128)} %param.15) | copy-start | bytes 1572868
  12.6 1.8 %copy-start.14 = (s32[8,4]{0,1:T(4,128)S(1)}, s32[8,4]{0,1:T(4,128)}, u32[]{:S(2)}) copy-start(s32[8,4]{0,1:T(4,128)} %param.13) | copy-start | bytes 388
  14.4 4.3 %copy-start.1 = (f32[2,8,128,128]{3,2,1,0:T(8,128)S(1)}, f32[2,8,128,128]{3,2,1,0:T(8,128)}, u32[]{:S(2)}) copy-start(f32[2,8,128,128]{3,2,1,0:T(8,128)} %velocity_ref.1) | copy-start | bytes 3145732
  14.4 4.2 %copy-start.3 = (s32[8,128,128]{2,1,0:T(8,128)S(1)}, s32[8,128,128]{2,1,0:T(8,128)}, u32[]{:S(2)}) copy-start(s32[8,128,128]{2,1,0:T(8,128)} %obstacle_ref.1) | copy-start | bytes 1572868
  18.7 0.7 copy-start.4
  19.3 6.9 %copy-start.12 = (f32[8,64,128]{2,1,0:T(8,128)S(1)}, f32[8,64,128]{2,1,0:T(8,128)}, u32[]{:S(2)}) copy-start(f32[8,64,128]{2,1,0:T(8,128)} %fusion.25) | copy-start | bytes 786436
  26.6 1.0 %copy-start.13 = (f32[8,64,128]{2,1,0:T(8,128)S(1)}, f32[8,64,128]{2,1,0:T(8,128)}, u32[]{:S(2)}) copy-start(f32[8,64,128]{2,1,0:T(8,128)} %fusion.25) | copy-start | bytes 786436
  27.6 8.7 %copy-start.10 = (f32[8,64,64]{2,1,0:T(8,128)S(1)}, f32[8,64,64]{2,1,0:T(8,128)}, u32[]{:S(2)}) copy-start(f32[8,64,64]{2,1,0:T(8,128)} %param.14) | copy-start | bytes 393220
  27.6 8.7 %collective-permute-start.2 = (f32[8,64,128]{2,1,0:T(8,128)S(1)}, f32[8,64,128]{2,1,0:T(8,128)S(1)}, u32[]{:S(2)}, u32[]{:S(2)}) collective-permute-start(f32[8,64,128]{2,1,0:T(8,128)S(1)} %bitcast_add_fusion), channel_id=1, source_target_pairs={{0,4},{4,8},{8,12},{12,16},{16,20},{20,24},{24,28},{1,5},{5,9},{9,... | collective-permute-start | bytes 786440 | tf_op jit(solution)/shard_map/ppermute | solution.py:26
  30.3 6.6 %copy-start.6 = (f32[8,128,128]{2,1,0:T(8,128)S(1)}, f32[8,128,128]{2,1,0:T(8,128)}, u32[]{:S(2)}) copy-start(f32[8,128,128]{2,1,0:T(8,128)} %param.15) | copy-start | bytes 1572868
  37.5 8.0 %copy-start.8 = (f32[8,64,64]{2,1,0:T(8,128)S(1)}, f32[8,64,64]{2,1,0:T(8,128)}, u32[]{:S(2)}) copy-start(f32[8,64,64]{2,1,0:T(8,128)} %copy-done.7) | copy-start | bytes 393220
  37.5 8.0 %collective-permute-start.3 = (f32[4,64,128]{2,1,0:T(8,128)S(1)}, f32[4,64,128]{2,1,0:T(8,128)S(1)}, u32[]{:S(2)}, u32[]{:S(2)}) collective-permute-start(f32[4,64,128]{2,1,0:T(8,128)S(1)} %fusion.5), channel_id=1, source_target_pairs={{0,8},{4,12},{8,16},{12,20},{16,24},{20,28},{1,9},{5,13},{9,17},{1... | collective-permute-start | bytes 393224 | tf_op jit(solution)/shard_map/ppermute | solution.py:26
  40.8 6.9 %collective-permute-start.5 = (f32[4,64,128]{2,1,0:T(8,128)S(1)}, f32[4,64,128]{2,1,0:T(8,128)S(1)}, u32[]{:S(2)}, u32[]{:S(2)}) collective-permute-start(f32[4,64,128]{2,1,0:T(8,128)S(1)} %fusion.2), channel_id=1, source_target_pairs={{0,16},{4,20},{8,24},{12,28},{1,17},{5,21},{9,25},{13,29},{2,18},{... | collective-permute-start | bytes 393224 | tf_op jit(solution)/shard_map/ppermute | solution.py:26
  42.1 21.8 %collective-permute-start.8 = (f32[8,128,128]{2,1,0:T(8,128)S(1)}, f32[8,128,128]{2,1,0:T(8,128)S(1)}, u32[]{:S(2)}, u32[]{:S(2)}) collective-permute-start(f32[8,128,128]{2,1,0:T(8,128)S(1)} %sub.57), channel_id=1, source_target_pairs={{0,4},{4,8},{8,12},{12,16},{16,20},{20,24},{24,28},{1,5},{5,9},{9,... | collective-permute-start | bytes 1572872 | tf_op jit(solution)/shard_map/ppermute | solution.py:26
  45.7 1.9 %copy-start.11 = (f32[8,64,64]{2,1,0:T(8,128)S(1)}, f32[8,64,64]{2,1,0:T(8,128)}, u32[]{:S(2)}) copy-start(f32[8,64,64]{2,1,0:T(8,128)} %fusion.28) | copy-start | bytes 393220
  46.4 12.7 %collective-permute-start.4 = (f32[4,64,128]{2,1,0:T(8,128)S(1)}, f32[4,64,128]{2,1,0:T(8,128)S(1)}, u32[]{:S(2)}, u32[]{:S(2)}) collective-permute-start(f32[4,64,128]{2,1,0:T(8,128)S(1)} %fusion.4), channel_id=1, source_target_pairs={{0,16},{4,20},{8,24},{12,28},{1,17},{5,21},{9,25},{13,29},{2,18},{... | collective-permute-start | bytes 393224 | tf_op jit(solution)/shard_map/ppermute | solution.py:26
  48.6 11.4 %collective-permute-start.6 = (f32[4,64,128]{2,1,0:T(8,128)S(1)}, f32[4,64,128]{2,1,0:T(8,128)S(1)}, u32[]{:S(2)}, u32[]{:S(2)}) collective-permute-start(f32[4,64,128]{2,1,0:T(8,128)S(1)} %fusion.1), channel_id=1, source_target_pairs={{0,8},{4,12},{8,16},{12,20},{16,24},{20,28},{1,9},{5,13},{9,17},{1... | collective-permute-start | bytes 393224 | tf_op jit(solution)/shard_map/ppermute | solution.py:26
  60.9 8.6 %collective-permute-start.7 = (f32[8,64,128]{2,1,0:T(8,128)S(1)}, f32[8,64,128]{2,1,0:T(8,128)S(1)}, u32[]{:S(2)}, u32[]{:S(2)}) collective-permute-start(f32[8,64,128]{2,1,0:T(8,128)S(1)} %maximum_subtract_fusion), channel_id=1, source_target_pairs={{0,4},{4,8},{8,12},{12,16},{16,20},{20,24},{24,28},{1,5},{5,9},{9,... | collective-permute-start | bytes 786440 | tf_op jit(solution)/shard_map/ppermute | solution.py:26

commit v13 on v11

--- a/solution.py
+++ b/solution.py
@@ -46,7 +46,7 @@
     rows = u_ref.shape[1]
     lanes = u_ref.shape[2]
     total = rows + 2 * HALO
-    layers = prev_ref.shape[0]
+    layers = prev_ref.shape[1] // HALO
     for ref in (state_ref, other_ref):
         ref[tiles] = jnp.zeros(ref.shape[1:], jnp.float32)
         for i in range(tiles):
@@ -57,10 +57,16 @@
         east_at = east_at_ref[i]
         west_ok = west_ok_ref[i] > 0
         east_ok = east_ok_ref[i] > 0
-        state_ref[i, pl.ds(PAD, HALO), :] = jnp.where(west_ok, prev_ref[slice_at, west_at], 0.0)
+        def west_layer(layer):
+            return prev_ref[west_at, pl.ds(layer * HALO, HALO), :]
+
+        def east_layer(layer):
+            return next_ref[east_at, pl.ds(layer * HALO, HALO), :]
+
+        state_ref[i, pl.ds(PAD, HALO), :] = jnp.where(west_ok, west_layer(slice_at), 0.0)
         state_ref[i, pl.ds(PAD + HALO, rows), :] = u_ref[i]
         state_ref[i, pl.ds(PAD + HALO + rows, HALO), :] = jnp.where(
-            east_ok, next_ref[slice_at, east_at], 0.0
+            east_ok, east_layer(slice_at), 0.0
         )
         own = (
             diffusivity_ref[i],
@@ -71,12 +77,15 @@
         factor = (1.0, 0.5, 0.5, 1.0)
         for f in range(4):
             field_at = layers - 4 + f
-            field_ref[f, i, pl.ds(0, HALO), :] = factor[f] * jnp.where(
-                west_ok, prev_ref[field_at, west_at], 0.0
-            )
+            west_rows = west_layer(field_at)
+            east_rows = east_layer(field_at)
+            if f == 3:
+                west_rows = 1.0 - west_rows
+                east_rows = 1.0 - east_rows
+            field_ref[f, i, pl.ds(0, HALO), :] = factor[f] * jnp.where(west_ok, west_rows, 0.0)
             field_ref[f, i, pl.ds(HALO, rows), :] = factor[f] * own[f]
             field_ref[f, i, pl.ds(HALO + rows, HALO), :] = factor[f] * jnp.where(
-                east_ok, next_ref[field_at, east_at], 0.0
+                east_ok, east_rows, 0.0
             )
 
     chunk = 16
@@ -150,15 +159,18 @@
     rows = starts.shape[2]
     all_tiles = tile_count * lax.axis_size("space")
     block_base = lax.axis_index("space") * tile_count
-    open_cells = 1.0 - obstacle.astype(jnp.float32)
-
-    fields = jnp.stack([diffusivity, velocity[0], velocity[1], open_cells], axis=0)
-    layers = jnp.concatenate([starts, fields], axis=0)
+
+    def edge_rows(part):
+        pieces = [starts[n][:, part, :] for n in range(slice_count)]
+        pieces += [diffusivity[:, part, :], velocity[0][:, part, :], velocity[1][:, part, :]]
+        pieces.append(obstacle[:, part, :].astype(jnp.float32))
+        return jnp.concatenate(pieces, axis=1)
+
     space_count = lax.axis_size("space")
     forward = [(i, i + 1) for i in range(space_count - 1)]
     backward = [(i + 1, i) for i in range(space_count - 1)]
-    from_prev = lax.ppermute(layers[:, :, rows - HALO:, :], "space", forward)
-    from_next = lax.ppermute(layers[:, :, :HALO, :], "space", backward)
+    from_prev = lax.ppermute(edge_rows(slice(rows - HALO, None)), "space", forward)
+    from_next = lax.ppermute(edge_rows(slice(0, HALO)), "space", backward)
     west_nb = neighbors[:, 0]
     east_nb = neighbors[:, 1]
     west_ok = (west_nb != all_tiles).astype(jnp.int32)

time: 67.3 us -> 69.6 us (1.034)
  local copies, waits for them, and re-layouts: 2.64 us -> 8.38 us
  other arithmetic: 5.02 us -> 2.61 us
  waiting for transfers between devices: 18.5 us -> 16.7 us
  matrix products: 12.1 us -> 12.9 us
    unnamed x30 -> x36, local copies, waits for them, and re-layouts: 1.69 us -> 6.07 us
    ppermute x2, waiting for transfers between devices: 2.25 us -> 0.48 us  [the longest x1 0.48 us: on_device(): from_next = lax.ppermute(edge_rows(slice(0, HALO)), 'space', backward)]
    squeeze x0 -> x1, local copies, waits for them, and re-layouts: none -> 1.35 us  [edge_rows(): velocity[1][:, part, :]]
    concatenate x1, other arithmetic: 1.91 us -> 0.66 us  [edge_rows(): return jnp.concatenate(pieces, axis=1)]
    another operation x1 -> x0, other arithmetic: 1.17 us -> none  [on_device(): jnp.stack([diffusivity, velocity[0], velocity[1], open_cells], axis=0)]
    dot_general x2, matrix products: 2.57 us -> 3.35 us  [prefix_over_tm(): jnp.einsum('tij,tjk->tik', power_y, power_y, precision=exact_precision)]
  transfers between devices with their start and end apart: 9 -> 9, of which waited for: 7 -> 7; matrix products, arithmetic and copies ran while one was open for 20% -> 21% of each run, Pallas kernels for 0% -> 0%
where the time goes in v13:
time: 69.6 us; the launch traced here: 69.1 us
  starting transfers between devices  20.6 us (30%)
  waiting for transfers between devices  16.7 us (24%)
  matrix products  12.9 us (19%)
  local copies, waits for them, and re-layouts  8.38 us (12%)
  Pallas kernels  6.81 us (10%)
  other arithmetic  2.61 us (4%)
  between operations  1.07 us (2%)
    ppermute x7, waiting for transfers between devices, passed_along(): return lax.ppermute(block, axis, route)  16.2 us
    ppermute x7, starting transfers between devices, passed_along(): return lax.ppermute(block, axis, route)  14.8 us
    pallas_call x1, Pallas kernels, fine_propagate(): pl.pallas_call(functools.partial(fine_kernel, slice_at), out_shape=jax.Sh...  6.81 us
    unnamed x36, local copies, waits for them, and re-layouts  6.07 us
    dot_general x7, matrix products, apply_coarse(): jnp.einsum('...tik,tlk->...til', mixed_x, matrix_y, precision=exact_preci...  5.5 us
    ppermute x1, starting transfers between devices, on_device(): lax.ppermute(edge_rows(slice(rows - HALO, None)), 'space', forward)  3.47 us
    dot_general x2, matrix products, prefix_over_tm(): jnp.einsum('tij,tjk->tik', power_y, power_y, precision=exact_precision)  3.35 us
    dot_general x7, matrix products, apply_coarse(): jnp.einsum('tij,...tjk->...tik', matrix_x, coarse_values, precision=exact...  2.59 us
  transfers between devices with their start and end apart: 9, of which 7 were waited for; matrix products, arithmetic and copies ran while one was open for 21% of the time, Pallas kernels for 0%

profile of v13, /device:TPU:12, one launch (start us, length us, event | category | flops | bytes accessed | tf_op | source)
XLA Modules:
  0.0 69.1 jit_solution(17181840399079508995)
XLA Ops:
  0.6 1.5 %slice_dynamic-update-slice_fusion.2 = (f32[8,80,128]{2,1,0:T(8,128)}, f32[8,80,128]{2,1,0:T(8,128)}) fusion(f32[8,128,128]{2,1,0:T(8,128)} %bitcast.58), kind=kLoop, calls=%fused_computation.34 | loop fusion | bytes 262144
  2.2 1.4 %slice_bitcast_fusion = (f32[8,128,128]{2,1,0:T(8,128)S(1)}, f32[8,128,128]{2,1,0:T(8,128)S(1)}) fusion(f32[2,8,128,128]{3,2,1,0:T(8,128)} %velocity_ref.1), kind=kLoop, calls=%fused_computation.16 | loop fusion | bytes 2097152 | tf_op jit(solution)/shard_map/squeeze | solution.py:165
  3.6 0.7 slice_dynamic-update-slice_fusion.6
  4.2 0.7 slice_dynamic-update-slice_fusion.1
  4.9 0.7 slice_dynamic-update-slice_fusion
  5.6 0.7 convert_dynamic-update-slice_fusion
  6.2 3.5 %collective-permute-start = (f32[8,80,128]{2,1,0:T(8,128)}, f32[8,80,128]{2,1,0:T(8,128)S(1)}, u32[]{:S(2)}, u32[]{:S(2)}) collective-permute-start(f32[8,80,128]{2,1,0:T(8,128)} %get-tuple-element.5), channel_id=1, source_target_pairs={{0,1},{1,2},{2,3},{4,5},{5,6},{6,7},{8,9},{9,10},{10,11},{12,13},{... | collective-permute-start | bytes 983048 | tf_op jit(solution)/shard_map/ppermute | solution.py:172
  9.7 2.4 %collective-permute-start.1 = (f32[8,80,128]{2,1,0:T(8,128)}, f32[8,80,128]{2,1,0:T(8,128)S(1)}, u32[]{:S(2)}, u32[]{:S(2)}) collective-permute-start(f32[8,80,128]{2,1,0:T(8,128)} %get-tuple-element.4), channel_id=1, source_target_pairs={{1,0},{2,1},{3,2},{5,4},{6,5},{7,6},{9,8},{10,9},{11,10},{13,12},{... | collective-permute-start | bytes 983048 | tf_op jit(solution)/shard_map/ppermute | solution.py:173
  12.7 1.0 %copy-done = f32[1,8,128,128]{3,2,1,0:T(8,128)S(1)} copy-done((f32[1,8,128,128]{3,2,1,0:T(8,128)S(1)}, f32[1,8,128,128]{3,2,1,0:T(8,128)}, u32[]{:S(2)}) %copy-start) | copy-done | bytes 524312
  13.7 1.0 %fusion.6 = f32[8,64,128]{2,1,0:T(8,128)S(1)} fusion(f32[8,64,128]{1,0,2:T(8,128)S(1)} %bitcast.65, f32[1,8,128,128]{3,2,1,0:T(8,128)S(1)} %copy-done), kind=kOutput, calls=%fused_computation.12 | convolution fusion | flops 100663296 | bytes 1048576 | tf_op jit(solution)/shard_map/tij,...tjk->...tik/dot_general | solution.py:38
  14.8 1.1 %fusion.28 = f32[8,64,64]{2,1,0:T(8,128)} fusion(f32[8,64,64]{2,1,0:T(8,128)S(1)} %fusion.26), kind=kOutput, calls=%fused_computation.60 | convolution fusion | flops 25165824 | bytes 262144 | tf_op jit(solution)/shard_map/tij,tjk->tik/dot_general | solution.py:217
  15.9 1.8 %fusion.25 = f32[8,64,128]{2,1,0:T(8,128)} fusion(f32[8,64,128]{2,1,0:T(8,128)S(1)} %fusion.6, f32[8,128,128]{2,1,0:T(8,128)S(1)} %copy-done.6), kind=kOutput, calls=%fused_computation.57 | convolution fusion | flops 100663296 | bytes 1048576 | tf_op jit(solution)/shard_map/...tik,tlk->...til/dot_general | solution.py:39
  17.8 2.7 %fusion.27 = f32[8,128,128]{2,1,0:T(8,128)} fusion(f32[8,128,128]{2,1,0:T(8,128)} %param.15), kind=kOutput, calls=%fused_computation.59 | convolution fusion | flops 201326592 | bytes 1048576 | tf_op jit(solution)/shard_map/tij,tjk->tik/dot_general | solution.py:218
  21.0 0.7 copy-done.4
  21.6 6.8 %shard_map.95 = f32[8,128,128]{2,1,0:T(8,128)S(1)} custom-call(s32[8]{0:T(128)S(1)} %get-tuple-element.18.south_ref, s32[8]{0:T(128)S(1)} %get-tuple-element.17.north_ref, s32[8]{0:T(128)S(1)} %get-tuple-element.19.west_at_ref, s32[8]{0:T(128)S(1)} %get-tuple-element.16.east_at_ref, s32[8]{0:T(128)S(1)} %get-tuple-element.15.west_ok_ref, ...), custom_call_target="tpu_custom_call" | custom-call | tf_op jit(solution)/shard_map/pallas_call | solution.py:140
  29.0 0.8 %copy-done.14 = f32[8,64,128]{2,1,0:T(8,128)S(1)} copy-done((f32[8,64,128]{2,1,0:T(8,128)S(1)}, f32[8,64,128]{2,1,0:T(8,128)}, u32[]{:S(2)}) %copy-start.14) | copy-done | bytes 262168
  29.9 2.1 %collective-permute-start.2 = (f32[8,64,128]{2,1,0:T(8,128)S(1)}, f32[8,64,128]{2,1,0:T(8,128)S(1)}, u32[]{:S(2)}, u32[]{:S(2)}) collective-permute-start(f32[8,64,128]{2,1,0:T(8,128)S(1)} %bitcast_add_fusion), channel_id=1, source_target_pairs={{0,4},{4,8},{8,12},{12,16},{16,20},{20,24},{24,28},{1,5},{5,9},{9,... | collective-permute-start | bytes 786440 | tf_op jit(solution)/shard_map/ppermute | solution.py:26
  31.9 0.6 fusion.29
  32.6 3.6 %collective-permute-start.8 = (f32[8,128,128]{2,1,0:T(8,128)S(1)}, f32[8,128,128]{2,1,0:T(8,128)S(1)}, u32[]{:S(2)}, u32[]{:S(2)}) collective-permute-start(f32[8,128,128]{2,1,0:T(8,128)S(1)} %sub.49), channel_id=1, source_target_pairs={{0,4},{4,8},{8,12},{12,16},{16,20},{20,24},{24,28},{1,5},{5,9},{9,... | collective-permute-start | bytes 1572872 | tf_op jit(solution)/shard_map/ppermute | solution.py:26
  36.2 2.4 %collective-permute-done.2 = f32[8,64,128]{2,1,0:T(8,128)S(1)} collective-permute-done((f32[8,64,128]{2,1,0:T(8,128)S(1)}, f32[8,64,128]{2,1,0:T(8,128)S(1)}, u32[]{:S(2)}, u32[]{:S(2)}) %collective-permute-start.2) | collective-permute-done | bytes 262176 | tf_op jit(solution)/shard_map/ppermute | solution.py:26
  39.5 2.5 %collective-permute-start.3 = (f32[4,64,128]{2,1,0:T(8,128)S(1)}, f32[4,64,128]{2,1,0:T(8,128)S(1)}, u32[]{:S(2)}, u32[]{:S(2)}) collective-permute-start(f32[4,64,128]{2,1,0:T(8,128)S(1)} %fusion.5), channel_id=1, source_target_pairs={{0,8},{4,12},{8,16},{12,20},{16,24},{20,28},{1,9},{5,13},{9,17},{1... | collective-permute-start | bytes 393224 | tf_op jit(solution)/shard_map/ppermute | solution.py:26
  42.3 0.6 fusion.2
  42.9 1.3 %collective-permute-start.5 = (f32[4,64,128]{2,1,0:T(8,128)S(1)}, f32[4,64,128]{2,1,0:T(8,128)S(1)}, u32[]{:S(2)}, u32[]{:S(2)}) collective-permute-start(f32[4,64,128]{2,1,0:T(8,128)S(1)} %fusion.2), channel_id=1, source_target_pairs={{0,16},{4,20},{8,24},{12,28},{1,17},{5,21},{9,25},{13,29},{2,18},{... | collective-permute-start | bytes 393224 | tf_op jit(solution)/shard_map/ppermute | solution.py:26
  44.2 3.0 %collective-permute-done.3 = f32[4,64,128]{2,1,0:T(8,128)S(1)} collective-permute-done((f32[4,64,128]{2,1,0:T(8,128)S(1)}, f32[4,64,128]{2,1,0:T(8,128)S(1)}, u32[]{:S(2)}, u32[]{:S(2)}) %collective-permute-start.3) | collective-permute-done | bytes 131104 | tf_op jit(solution)/shard_map/ppermute | solution.py:26
  48.1 1.3 %collective-permute-start.4 = (f32[4,64,128]{2,1,0:T(8,128)S(1)}, f32[4,64,128]{2,1,0:T(8,128)S(1)}, u32[]{:S(2)}, u32[]{:S(2)}) collective-permute-start(f32[4,64,128]{2,1,0:T(8,128)S(1)} %fusion.4), channel_id=1, source_target_pairs={{0,16},{4,20},{8,24},{12,28},{1,17},{5,21},{9,25},{13,29},{2,18},{... | collective-permute-start | bytes 393224 | tf_op jit(solution)/shard_map/ppermute | solution.py:26
  50.7 2.1 %collective-permute-start.6 = (f32[4,64,128]{2,1,0:T(8,128)S(1)}, f32[4,64,128]{2,1,0:T(8,128)S(1)}, u32[]{:S(2)}, u32[]{:S(2)}) collective-permute-start(f32[4,64,128]{2,1,0:T(8,128)S(1)} %fusion.1), channel_id=1, source_target_pairs={{0,8},{4,12},{8,16},{12,20},{16,24},{20,28},{1,9},{5,13},{9,17},{1... | collective-permute-start | bytes 393224 | tf_op jit(solution)/shard_map/ppermute | solution.py:26
  52.8 3.6 %collective-permute-done.4 = f32[4,64,128]{2,1,0:T(8,128)S(1)} collective-permute-done((f32[4,64,128]{2,1,0:T(8,128)S(1)}, f32[4,64,128]{2,1,0:T(8,128)S(1)}, u32[]{:S(2)}, u32[]{:S(2)}) %collective-permute-start.4) | collective-permute-done | bytes 131104 | tf_op jit(solution)/shard_map/ppermute | solution.py:26
  57.3 1.2 %collective-permute-done.6 = f32[4,64,128]{2,1,0:T(8,128)S(1)} collective-permute-done((f32[4,64,128]{2,1,0:T(8,128)S(1)}, f32[4,64,128]{2,1,0:T(8,128)S(1)}, u32[]{:S(2)}, u32[]{:S(2)}) %collective-permute-start.6) | collective-permute-done | bytes 131104 | tf_op jit(solution)/shard_map/ppermute | solution.py:26
  59.4 1.9 %collective-permute-start.7 = (f32[8,64,128]{2,1,0:T(8,128)S(1)}, f32[8,64,128]{2,1,0:T(8,128)S(1)}, u32[]{:S(2)}, u32[]{:S(2)}) collective-permute-start(f32[8,64,128]{2,1,0:T(8,128)S(1)} %maximum_subtract_fusion), channel_id=1, source_target_pairs={{0,4},{4,8},{8,12},{12,16},{16,20},{20,24},{24,28},{1,5},{5,9},{9,... | collective-permute-start | bytes 786440 | tf_op jit(solution)/shard_map/ppermute | solution.py:26
  61.5 0.9 %add_bitcast_fusion = f32[1,8,128,128]{3,2,1,0:T(8,128)} fusion(f32[8,128,128]{2,1,0:T(8,128)S(1)} %bitcast.64, f32[8,128,128]{2,1,0:T(8,128)S(1)} %sub.49), kind=kLoop, calls=%fused_computation.15 | loop fusion | flops 131072 | bytes 1572864 | tf_op jit(solution)/shard_map/add | solution.py:261
  62.4 5.6 %collective-permute-done.7 = f32[8,64,128]{2,1,0:T(8,128)S(1)} collective-permute-done((f32[8,64,128]{2,1,0:T(8,128)S(1)}, f32[8,64,128]{2,1,0:T(8,128)S(1)}, u32[]{:S(2)}, u32[]{:S(2)}) %collective-permute-start.7) | collective-permute-done | bytes 262176 | tf_op jit(solution)/shard_map/ppermute | solution.py:26
  68.2 0.9 %select_bitcast_fusion = f32[1,8,128,128]{3,2,1,0:T(8,128)} fusion(f32[8,128,128]{2,1,0:T(8,128)S(1)} %bitcast.62, f32[8,128,128]{2,1,0:T(8,128)S(1)} %collective-permute-done.8, pred[]{:T(512)S(6)} %eq.4, f32[1,8,128,128]{3,2,1,0:T(8,128)S(1)} %copy-done), kind=kLoop, calls=%fused_computation.14 | loop fusion | flops 393216 | bytes 2097153 | tf_op jit(solution)/shard_map/broadcast_in_dim | solution.py:266
  (58 shorter events, 7.1 us)
Async XLA Ops:
  2.2 1.4 %copy-start.2 = (f32[8,128,128]{2,1,0:T(8,128)S(1)}, f32[8,128,128]{2,1,0:T(8,128)}, u32[]{:S(2)}) copy-start(f32[8,128,128]{2,1,0:T(8,128)} %diffusivity_ref.1) | copy-start | bytes 1572868
  3.5 2.0 %copy-start.3 = (s32[8,128,128]{2,1,0:T(8,128)S(1)}, s32[8,128,128]{2,1,0:T(8,128)}, u32[]{:S(2)}) copy-start(s32[8,128,128]{2,1,0:T(8,128)} %obstacle_ref.1) | copy-start | bytes 1572868
  4.9 7.2 %copy-start.10 = (f32[8,64,64]{2,1,0:T(8,128)S(1)}, f32[8,64,64]{2,1,0:T(8,128)}, u32[]{:S(2)}) copy-start(f32[8,64,64]{2,1,0:T(8,128)} %param.14) | copy-start | bytes 393220
  6.2 14.3 %collective-permute-start = (f32[8,80,128]{2,1,0:T(8,128)}, f32[8,80,128]{2,1,0:T(8,128)S(1)}, u32[]{:S(2)}, u32[]{:S(2)}) collective-permute-start(f32[8,80,128]{2,1,0:T(8,128)} %get-tuple-element.5), channel_id=1, source_target_pairs={{0,1},{1,2},{2,3},{4,5},{5,6},{6,7},{8,9},{9,10},{10,11},{12,13},{... | collective-permute-start | bytes 983048 | tf_op jit(solution)/shard_map/ppermute | solution.py:172
  9.7 11.3 %collective-permute-start.1 = (f32[8,80,128]{2,1,0:T(8,128)}, f32[8,80,128]{2,1,0:T(8,128)S(1)}, u32[]{:S(2)}, u32[]{:S(2)}) collective-permute-start(f32[8,80,128]{2,1,0:T(8,128)} %get-tuple-element.4), channel_id=1, source_target_pairs={{1,0},{2,1},{3,2},{5,4},{6,5},{7,6},{9,8},{10,9},{11,10},{13,12},{... | collective-permute-start | bytes 983048 | tf_op jit(solution)/shard_map/ppermute | solution.py:173
  12.5 2.3 %copy-start.8 = (f32[8,64,64]{2,1,0:T(8,128)}, f32[8,64,64]{2,1,0:T(8,128)S(1)}, u32[]{:S(2)}) copy-start(f32[8,64,64]{2,1,0:T(8,128)S(1)} %fusion.26) | copy-start | bytes 393220
  12.7 1.0 %copy-start = (f32[1,8,128,128]{3,2,1,0:T(8,128)S(1)}, f32[1,8,128,128]{3,2,1,0:T(8,128)}, u32[]{:S(2)}) copy-start(f32[1,8,128,128]{3,2,1,0:T(8,128)} %param.8) | copy-start | bytes 1572868
  14.8 1.1 %copy-start.6 = (f32[8,128,128]{2,1,0:T(8,128)S(1)}, f32[8,128,128]{2,1,0:T(8,128)}, u32[]{:S(2)}) copy-start(f32[8,128,128]{2,1,0:T(8,128)} %param.15) | copy-start | bytes 1572868
  15.9 1.8 %copy-start.15 = (s32[8,4]{0,1:T(4,128)S(1)}, s32[8,4]{0,1:T(4,128)}, u32[]{:S(2)}) copy-start(s32[8,4]{0,1:T(4,128)} %param.13) | copy-start | bytes 388
  17.7 3.2 %copy-start.1 = (f32[2,8,128,128]{3,2,1,0:T(8,128)S(1)}, f32[2,8,128,128]{3,2,1,0:T(8,128)}, u32[]{:S(2)}) copy-start(f32[2,8,128,128]{3,2,1,0:T(8,128)} %velocity_ref.1) | copy-start | bytes 3145732
  21.0 0.7 copy-start.4
  21.6 6.8 %copy-start.13 = (f32[8,64,128]{2,1,0:T(8,128)S(1)}, f32[8,64,128]{2,1,0:T(8,128)}, u32[]{:S(2)}) copy-start(f32[8,64,128]{2,1,0:T(8,128)} %fusion.25) | copy-start | bytes 786436
  28.9 1.0 %copy-start.14 = (f32[8,64,128]{2,1,0:T(8,128)S(1)}, f32[8,64,128]{2,1,0:T(8,128)}, u32[]{:S(2)}) copy-start(f32[8,64,128]{2,1,0:T(8,128)} %fusion.25) | copy-start | bytes 786436
  29.8 2.1 %copy-start.5 = (f32[8,128,128]{2,1,0:T(8,128)S(1)}, f32[8,128,128]{2,1,0:T(8,128)}, u32[]{:S(2)}) copy-start(f32[8,128,128]{2,1,0:T(8,128)} %fusion.27) | copy-start | bytes 1572868
  29.9 8.7 %copy-start.11 = (f32[8,64,64]{2,1,0:T(8,128)S(1)}, f32[8,64,64]{2,1,0:T(8,128)}, u32[]{:S(2)}) copy-start(f32[8,64,64]{2,1,0:T(8,128)} %param.14) | copy-start | bytes 393220
  29.9 8.7 %collective-permute-start.2 = (f32[8,64,128]{2,1,0:T(8,128)S(1)}, f32[8,64,128]{2,1,0:T(8,128)S(1)}, u32[]{:S(2)}, u32[]{:S(2)}) collective-permute-start(f32[8,64,128]{2,1,0:T(8,128)S(1)} %bitcast_add_fusion), channel_id=1, source_target_pairs={{0,4},{4,8},{8,12},{12,16},{16,20},{20,24},{24,28},{1,5},{5,9},{9,... | collective-permute-start | bytes 786440 | tf_op jit(solution)/shard_map/ppermute | solution.py:26
  32.6 6.3 %copy-start.7 = (f32[8,128,128]{2,1,0:T(8,128)S(1)}, f32[8,128,128]{2,1,0:T(8,128)}, u32[]{:S(2)}) copy-start(f32[8,128,128]{2,1,0:T(8,128)} %param.15) | copy-start | bytes 1572868
  32.6 29.8 %collective-permute-start.8 = (f32[8,128,128]{2,1,0:T(8,128)S(1)}, f32[8,128,128]{2,1,0:T(8,128)S(1)}, u32[]{:S(2)}, u32[]{:S(2)}) collective-permute-start(f32[8,128,128]{2,1,0:T(8,128)S(1)} %sub.49), channel_id=1, source_target_pairs={{0,4},{4,8},{8,12},{12,16},{16,20},{20,24},{24,28},{1,5},{5,9},{9,... | collective-permute-start | bytes 1572872 | tf_op jit(solution)/shard_map/ppermute | solution.py:26
  39.5 7.8 %collective-permute-start.3 = (f32[4,64,128]{2,1,0:T(8,128)S(1)}, f32[4,64,128]{2,1,0:T(8,128)S(1)}, u32[]{:S(2)}, u32[]{:S(2)}) collective-permute-start(f32[4,64,128]{2,1,0:T(8,128)S(1)} %fusion.5), channel_id=1, source_target_pairs={{0,8},{4,12},{8,16},{12,20},{16,24},{20,28},{1,9},{5,13},{9,17},{1... | collective-permute-start | bytes 393224 | tf_op jit(solution)/shard_map/ppermute | solution.py:26
  42.3 5.0 %copy-start.9 = (f32[8,64,64]{2,1,0:T(8,128)S(1)}, f32[8,64,64]{2,1,0:T(8,128)}, u32[]{:S(2)}) copy-start(f32[8,64,64]{2,1,0:T(8,128)} %copy-done.8) | copy-start | bytes 393220
  42.9 6.9 %collective-permute-start.5 = (f32[4,64,128]{2,1,0:T(8,128)S(1)}, f32[4,64,128]{2,1,0:T(8,128)S(1)}, u32[]{:S(2)}, u32[]{:S(2)}) collective-permute-start(f32[4,64,128]{2,1,0:T(8,128)S(1)} %fusion.2), channel_id=1, source_target_pairs={{0,16},{4,20},{8,24},{12,28},{1,17},{5,21},{9,25},{13,29},{2,18},{... | collective-permute-start | bytes 393224 | tf_op jit(solution)/shard_map/ppermute | solution.py:26
  47.5 2.3 %copy-start.12 = (f32[8,64,64]{2,1,0:T(8,128)S(1)}, f32[8,64,64]{2,1,0:T(8,128)}, u32[]{:S(2)}) copy-start(f32[8,64,64]{2,1,0:T(8,128)} %fusion.28) | copy-start | bytes 393220
  48.1 8.3 %collective-permute-start.4 = (f32[4,64,128]{2,1,0:T(8,128)S(1)}, f32[4,64,128]{2,1,0:T(8,128)S(1)}, u32[]{:S(2)}, u32[]{:S(2)}) collective-permute-start(f32[4,64,128]{2,1,0:T(8,128)S(1)} %fusion.4), channel_id=1, source_target_pairs={{0,16},{4,20},{8,24},{12,28},{1,17},{5,21},{9,25},{13,29},{2,18},{... | collective-permute-start | bytes 393224 | tf_op jit(solution)/shard_map/ppermute | solution.py:26
  50.7 7.8 %collective-permute-start.6 = (f32[4,64,128]{2,1,0:T(8,128)S(1)}, f32[4,64,128]{2,1,0:T(8,128)S(1)}, u32[]{:S(2)}, u32[]{:S(2)}) collective-permute-start(f32[4,64,128]{2,1,0:T(8,128)S(1)} %fusion.1), channel_id=1, source_target_pairs={{0,8},{4,12},{8,16},{12,20},{16,24},{20,28},{1,9},{5,13},{9,17},{1... | collective-permute-start | bytes 393224 | tf_op jit(solution)/shard_map/ppermute | solution.py:26
  59.4 8.6 %collective-permute-start.7 = (f32[8,64,128]{2,1,0:T(8,128)S(1)}, f32[8,64,128]{2,1,0:T(8,128)S(1)}, u32[]{:S(2)}, u32[]{:S(2)}) collective-permute-start(f32[8,64,128]{2,1,0:T(8,128)S(1)} %maximum_subtract_fusion), channel_id=1, source_target_pairs={{0,4},{4,8},{8,12},{12,16},{16,20},{20,24},{24,28},{1,5},{5,9},{9,... | collective-permute-start | bytes 786440 | tf_op jit(solution)/shard_map/ppermute | solution.py:26

commit v14 on v11

--- a/solution.py
+++ b/solution.py
@@ -142,6 +142,50 @@
     )(*indices, scale, u, diffusivity, velocity, obstacle, from_prev, from_next)
 
 
+def payload_kernel(starts_hbm, diffusivity_hbm, velocity_hbm, obstacle_hbm, low_ref, high_ref,
+                   obstacle_rows, sems):
+    slices = starts_hbm.shape[0]
+    rows = starts_hbm.shape[2]
+    copies = []
+    for side, (out_ref, first) in enumerate(((low_ref, 0), (high_ref, rows - HALO))):
+        part = pl.ds(first, HALO)
+        sources = [starts_hbm.at[n, :, part, :] for n in range(slices)]
+        sources += [
+            diffusivity_hbm.at[:, part, :],
+            velocity_hbm.at[0, :, part, :],
+            velocity_hbm.at[1, :, part, :],
+        ]
+        for k, source in enumerate(sources):
+            copies.append(pltpu.make_async_copy(source, out_ref.at[k], sems.at[side, k]))
+        copies.append(
+            pltpu.make_async_copy(
+                obstacle_hbm.at[:, part, :], obstacle_rows.at[side], sems.at[side, len(sources)]
+            )
+        )
+    for copy in copies:
+        copy.start()
+    for copy in copies:
+        copy.wait()
+    for side, out_ref in enumerate((low_ref, high_ref)):
+        out_ref[slices + 3] = 1.0 - obstacle_rows[side].astype(jnp.float32)
+
+
+def edge_payload(starts, diffusivity, velocity, obstacle):
+    slices, tiles, rows, lanes = starts.shape
+    shape = jax.ShapeDtypeStruct((slices + 4, tiles, HALO, lanes), jnp.float32)
+    vmem = pltpu.MemorySpace.VMEM
+    return pl.pallas_call(
+        payload_kernel,
+        out_shape=(shape, shape),
+        in_specs=[pl.BlockSpec(memory_space=pl.ANY)] * 4,
+        out_specs=(pl.BlockSpec(memory_space=vmem), pl.BlockSpec(memory_space=vmem)),
+        scratch_shapes=[
+            pltpu.VMEM((2, tiles, HALO, lanes), jnp.int32),
+            pltpu.SemaphoreType.DMA((2, slices + 4)),
+        ],
+    )(starts, diffusivity, velocity, obstacle)
+
+
 def on_device(
     starts, diffusivity, velocity, obstacle, substep_scale, neighbors, coarse_x, coarse_y
 ):
@@ -150,15 +194,13 @@
     rows = starts.shape[2]
     all_tiles = tile_count * lax.axis_size("space")
     block_base = lax.axis_index("space") * tile_count
-    open_cells = 1.0 - obstacle.astype(jnp.float32)
-
-    fields = jnp.stack([diffusivity, velocity[0], velocity[1], open_cells], axis=0)
-    layers = jnp.concatenate([starts, fields], axis=0)
+
+    low_rows, high_rows = edge_payload(starts, diffusivity, velocity, obstacle)
     space_count = lax.axis_size("space")
     forward = [(i, i + 1) for i in range(space_count - 1)]
     backward = [(i + 1, i) for i in range(space_count - 1)]
-    from_prev = lax.ppermute(layers[:, :, rows - HALO:, :], "space", forward)
-    from_next = lax.ppermute(layers[:, :, :HALO, :], "space", backward)
+    from_prev = lax.ppermute(high_rows, "space", forward)
+    from_next = lax.ppermute(low_rows, "space", backward)
     west_nb = neighbors[:, 0]
     east_nb = neighbors[:, 1]
     west_ok = (west_nb != all_tiles).astype(jnp.int32)

time: 67.3 us -> 66.1 us (0.982)
  other arithmetic: 5.02 us -> 1.95 us
  Pallas kernels: 6.89 us -> 8.94 us
  waiting for transfers between devices: 18.5 us -> 17.4 us
  local copies, waits for them, and re-layouts: 2.64 us -> 3.47 us
    pallas_call x0 -> x1, Pallas kernels: none -> 2.08 us  [edge_payload(): pl.pallas_call(payload_kernel, out_shape=(shape, shape), in_specs=[pl.Blo...]
    concatenate x1 -> x0, other arithmetic: 1.91 us -> none  [on_device(): layers = jnp.concatenate([starts, fields], axis=0)]
    another operation x1 -> x0, other arithmetic: 1.17 us -> none  [on_device(): jnp.stack([diffusivity, velocity[0], velocity[1], open_cells], axis=0)]
    ppermute x2, waiting for transfers between devices: 2.25 us -> 1.25 us  [the longest x1 1.25 us: on_device(): from_next = lax.ppermute(low_rows, 'space', backward)]
    unnamed x30, local copies, waits for them, and re-layouts: 1.69 us -> 2.52 us
where the time goes in v14:
time: 66.1 us; the launch traced here: 65.6 us
  starting transfers between devices  20.6 us (31%)
  waiting for transfers between devices  17.4 us (26%)
  matrix products  12.1 us (18%)
  Pallas kernels  8.94 us (14%)
  local copies, waits for them, and re-layouts  3.47 us (5%)
  other arithmetic  1.95 us (3%)
  between operations  1.08 us (2%)
    ppermute x7, waiting for transfers between devices, passed_along(): return lax.ppermute(block, axis, route)  16.2 us
    ppermute x7, starting transfers between devices, passed_along(): return lax.ppermute(block, axis, route)  14.8 us
    pallas_call x1, Pallas kernels, fine_propagate(): pl.pallas_call(functools.partial(fine_kernel, slice_at), out_shape=jax.Sh...  6.86 us
    dot_general x7, matrix products, apply_coarse(): jnp.einsum('...tik,tlk->...til', mixed_x, matrix_y, precision=exact_preci...  5.48 us
    ppermute x1, starting transfers between devices, on_device(): from_prev = lax.ppermute(high_rows, 'space', forward)  3.48 us
    dot_general x7, matrix products, apply_coarse(): jnp.einsum('tij,...tjk->...tik', matrix_x, coarse_values, precision=exact...  2.59 us
    dot_general x2, matrix products, prefix_over_tm(): jnp.einsum('tij,tjk->tik', power_y, power_y, precision=exact_precision)  2.56 us
    unnamed x30, local copies, waits for them, and re-layouts  2.52 us
  transfers between devices with their start and end apart: 9, of which 7 were waited for; matrix products, arithmetic and copies ran while one was open for 20% of the time, Pallas kernels for 0%

profile of v14, /device:TPU:12, one launch (start us, length us, event | category | flops | bytes accessed | tf_op | source)
XLA Modules:
  0.0 65.6 jit_solution(15731367276935572695)
XLA Ops:
  0.6 2.1 %shard_map.95 = (f32[5,8,16,128]{3,2,1,0:T(8,128)}, f32[5,8,16,128]{3,2,1,0:T(8,128)}) custom-call(f32[1,8,128,128]{3,2,1,0:T(8,128)} %starts_hbm.1, f32[8,128,128]{2,1,0:T(8,128)} %diffusivity_ref.1, f32[2,8,128,128]{3,2,1,0:T(8,128)} %velocity_ref.1, s32[8,128,128]{2,1,0:T(8,128)} %obstacle_ref.1), custom_call_target="tpu_custom_call" | custom-call | tf_op jit(solution)/shard_map/pallas_call | solution.py:177
  2.7 3.5 %collective-permute-start = (f32[5,8,16,128]{3,2,1,0:T(8,128)}, f32[5,8,16,128]{3,2,1,0:T(8,128)S(1)}, u32[]{:S(2)}, u32[]{:S(2)}) collective-permute-start(f32[5,8,16,128]{3,2,1,0:T(8,128)} %get-tuple-element.4), channel_id=1, source_target_pairs={{0,1},{1,2},{2,3},{4,5},{5,6},{6,7},{8,9},{9,10},{10,11},{12,13},{... | collective-permute-start | bytes 983048 | tf_op jit(solution)/shard_map/ppermute | solution.py:202
  6.2 2.4 %collective-permute-start.1 = (f32[5,8,16,128]{3,2,1,0:T(8,128)}, f32[5,8,16,128]{3,2,1,0:T(8,128)S(1)}, u32[]{:S(2)}, u32[]{:S(2)}) collective-permute-start(f32[5,8,16,128]{3,2,1,0:T(8,128)} %get-tuple-element.5), channel_id=1, source_target_pairs={{1,0},{2,1},{3,2},{5,4},{6,5},{7,6},{9,8},{10,9},{11,10},{13,12},{... | collective-permute-start | bytes 983048 | tf_op jit(solution)/shard_map/ppermute | solution.py:203
  9.3 1.0 %copy-done = f32[1,8,128,128]{3,2,1,0:T(8,128)S(1)} copy-done((f32[1,8,128,128]{3,2,1,0:T(8,128)S(1)}, f32[1,8,128,128]{3,2,1,0:T(8,128)}, u32[]{:S(2)}) %copy-start) | copy-done | bytes 524312
  10.3 1.0 %fusion.6 = f32[8,64,128]{2,1,0:T(8,128)S(1)} fusion(f32[8,64,128]{1,0,2:T(8,128)S(1)} %bitcast.60, f32[1,8,128,128]{3,2,1,0:T(8,128)S(1)} %copy-done), kind=kOutput, calls=%fused_computation.12 | convolution fusion | flops 100663296 | bytes 1048576 | tf_op jit(solution)/shard_map/tij,...tjk->...tik/dot_general | solution.py:38
  11.3 1.1 %fusion.28 = f32[8,64,64]{2,1,0:T(8,128)} fusion(f32[8,64,64]{2,1,0:T(8,128)S(1)} %fusion.26), kind=kOutput, calls=%fused_computation.48 | convolution fusion | flops 25165824 | bytes 262144 | tf_op jit(solution)/shard_map/tij,tjk->tik/dot_general | solution.py:247
  12.4 1.8 %fusion.25 = f32[8,64,128]{2,1,0:T(8,128)} fusion(f32[8,64,128]{2,1,0:T(8,128)S(1)} %fusion.6, f32[8,128,128]{2,1,0:T(8,128)S(1)} %copy-done.5), kind=kOutput, calls=%fused_computation.45 | convolution fusion | flops 100663296 | bytes 1048576 | tf_op jit(solution)/shard_map/...tik,tlk->...til/dot_general | solution.py:39
  14.3 1.9 %fusion.27 = f32[8,128,128]{2,1,0:T(8,128)S(1)} fusion(f32[8,128,128]{2,1,0:T(8,128)} %param.15), kind=kOutput, calls=%fused_computation.47 | convolution fusion | flops 201326592 | bytes 1048576 | tf_op jit(solution)/shard_map/tij,tjk->tik/dot_general | solution.py:248
  16.2 1.2 %collective-permute-done.1.next_ref = f32[5,8,16,128]{3,2,1,0:T(8,128)S(1)} collective-permute-done((f32[5,8,16,128]{3,2,1,0:T(8,128)}, f32[5,8,16,128]{3,2,1,0:T(8,128)S(1)}, u32[]{:S(2)}, u32[]{:S(2)}) %collective-permute-start.1) | collective-permute-done | bytes 327712 | tf_op jit(solution)/shard_map/ppermute | solution.py:203
  17.5 0.6 copy-done.4
  18.2 6.9 %shard_map.96 = f32[8,128,128]{2,1,0:T(8,128)S(1)} custom-call(s32[8]{0:T(128)S(1)} %get-tuple-element.10.south_ref, s32[8]{0:T(128)S(1)} %get-tuple-element.9.north_ref, s32[8]{0:T(128)S(1)} %get-tuple-element.11.west_at_ref, s32[8]{0:T(128)S(1)} %get-tuple-element.8.east_at_ref, s32[8]{0:T(128)S(1)} %get-tuple-element.7.west_ok_ref, ...), custom_call_target="tpu_custom_call" | custom-call | tf_op jit(solution)/shard_map/pallas_call | solution.py:131
  25.6 0.8 %copy-done.13 = f32[8,64,128]{2,1,0:T(8,128)S(1)} copy-done((f32[8,64,128]{2,1,0:T(8,128)S(1)}, f32[8,64,128]{2,1,0:T(8,128)}, u32[]{:S(2)}) %copy-start.13) | copy-done | bytes 262168
  26.4 2.1 %collective-permute-start.2 = (f32[8,64,128]{2,1,0:T(8,128)S(1)}, f32[8,64,128]{2,1,0:T(8,128)S(1)}, u32[]{:S(2)}, u32[]{:S(2)}) collective-permute-start(f32[8,64,128]{2,1,0:T(8,128)S(1)} %bitcast_add_fusion), channel_id=1, source_target_pairs={{0,4},{4,8},{8,12},{12,16},{16,20},{20,24},{24,28},{1,5},{5,9},{9,... | collective-permute-start | bytes 786440 | tf_op jit(solution)/shard_map/ppermute | solution.py:26
  28.5 0.6 fusion.29
  29.1 3.6 %collective-permute-start.8 = (f32[8,128,128]{2,1,0:T(8,128)S(1)}, f32[8,128,128]{2,1,0:T(8,128)S(1)}, u32[]{:S(2)}, u32[]{:S(2)}) collective-permute-start(f32[8,128,128]{2,1,0:T(8,128)S(1)} %sub.49), channel_id=1, source_target_pairs={{0,4},{4,8},{8,12},{12,16},{16,20},{20,24},{24,28},{1,5},{5,9},{9,... | collective-permute-start | bytes 1572872 | tf_op jit(solution)/shard_map/ppermute | solution.py:26
  32.8 2.4 %collective-permute-done.2 = f32[8,64,128]{2,1,0:T(8,128)S(1)} collective-permute-done((f32[8,64,128]{2,1,0:T(8,128)S(1)}, f32[8,64,128]{2,1,0:T(8,128)S(1)}, u32[]{:S(2)}, u32[]{:S(2)}) %collective-permute-start.2) | collective-permute-done | bytes 262176 | tf_op jit(solution)/shard_map/ppermute | solution.py:26
  35.5 0.6 fusion.5
  36.1 2.5 %collective-permute-start.3 = (f32[4,64,128]{2,1,0:T(8,128)S(1)}, f32[4,64,128]{2,1,0:T(8,128)S(1)}, u32[]{:S(2)}, u32[]{:S(2)}) collective-permute-start(f32[4,64,128]{2,1,0:T(8,128)S(1)} %fusion.5), channel_id=1, source_target_pairs={{0,8},{4,12},{8,16},{12,20},{16,24},{20,28},{1,9},{5,13},{9,17},{1... | collective-permute-start | bytes 393224 | tf_op jit(solution)/shard_map/ppermute | solution.py:26
  38.9 0.6 fusion.2
  39.5 1.3 %collective-permute-start.5 = (f32[4,64,128]{2,1,0:T(8,128)S(1)}, f32[4,64,128]{2,1,0:T(8,128)S(1)}, u32[]{:S(2)}, u32[]{:S(2)}) collective-permute-start(f32[4,64,128]{2,1,0:T(8,128)S(1)} %fusion.2), channel_id=1, source_target_pairs={{0,16},{4,20},{8,24},{12,28},{1,17},{5,21},{9,25},{13,29},{2,18},{... | collective-permute-start | bytes 393224 | tf_op jit(solution)/shard_map/ppermute | solution.py:26
  40.8 3.0 %collective-permute-done.3 = f32[4,64,128]{2,1,0:T(8,128)S(1)} collective-permute-done((f32[4,64,128]{2,1,0:T(8,128)S(1)}, f32[4,64,128]{2,1,0:T(8,128)S(1)}, u32[]{:S(2)}, u32[]{:S(2)}) %collective-permute-start.3) | collective-permute-done | bytes 131104 | tf_op jit(solution)/shard_map/ppermute | solution.py:26
  44.1 0.6 fusion.4
  44.7 1.3 %collective-permute-start.4 = (f32[4,64,128]{2,1,0:T(8,128)S(1)}, f32[4,64,128]{2,1,0:T(8,128)S(1)}, u32[]{:S(2)}, u32[]{:S(2)}) collective-permute-start(f32[4,64,128]{2,1,0:T(8,128)S(1)} %fusion.4), channel_id=1, source_target_pairs={{0,16},{4,20},{8,24},{12,28},{1,17},{5,21},{9,25},{13,29},{2,18},{... | collective-permute-start | bytes 393224 | tf_op jit(solution)/shard_map/ppermute | solution.py:26
  46.7 0.6 fusion.1
  47.3 2.1 %collective-permute-start.6 = (f32[4,64,128]{2,1,0:T(8,128)S(1)}, f32[4,64,128]{2,1,0:T(8,128)S(1)}, u32[]{:S(2)}, u32[]{:S(2)}) collective-permute-start(f32[4,64,128]{2,1,0:T(8,128)S(1)} %fusion.1), channel_id=1, source_target_pairs={{0,8},{4,12},{8,16},{12,20},{16,24},{20,28},{1,9},{5,13},{9,17},{1... | collective-permute-start | bytes 393224 | tf_op jit(solution)/shard_map/ppermute | solution.py:26
  49.4 3.6 %collective-permute-done.4 = f32[4,64,128]{2,1,0:T(8,128)S(1)} collective-permute-done((f32[4,64,128]{2,1,0:T(8,128)S(1)}, f32[4,64,128]{2,1,0:T(8,128)S(1)}, u32[]{:S(2)}, u32[]{:S(2)}) %collective-permute-start.4) | collective-permute-done | bytes 131104 | tf_op jit(solution)/shard_map/ppermute | solution.py:26
  53.9 1.2 %collective-permute-done.6 = f32[4,64,128]{2,1,0:T(8,128)S(1)} collective-permute-done((f32[4,64,128]{2,1,0:T(8,128)S(1)}, f32[4,64,128]{2,1,0:T(8,128)S(1)}, u32[]{:S(2)}, u32[]{:S(2)}) %collective-permute-start.6) | collective-permute-done | bytes 131104 | tf_op jit(solution)/shard_map/ppermute | solution.py:26
  55.3 0.6 fusion
  56.0 1.9 %collective-permute-start.7 = (f32[8,64,128]{2,1,0:T(8,128)S(1)}, f32[8,64,128]{2,1,0:T(8,128)S(1)}, u32[]{:S(2)}, u32[]{:S(2)}) collective-permute-start(f32[8,64,128]{2,1,0:T(8,128)S(1)} %maximum_subtract_fusion), channel_id=1, source_target_pairs={{0,4},{4,8},{8,12},{12,16},{16,20},{20,24},{24,28},{1,5},{5,9},{9,... | collective-permute-start | bytes 786440 | tf_op jit(solution)/shard_map/ppermute | solution.py:26
  58.1 0.9 %add_bitcast_fusion = f32[1,8,128,128]{3,2,1,0:T(8,128)} fusion(f32[8,128,128]{2,1,0:T(8,128)S(1)} %bitcast.59, f32[8,128,128]{2,1,0:T(8,128)S(1)} %sub.49), kind=kLoop, calls=%fused_computation.15 | loop fusion | flops 131072 | bytes 1572864 | tf_op jit(solution)/shard_map/add | solution.py:291
  59.0 5.6 %collective-permute-done.7 = f32[8,64,128]{2,1,0:T(8,128)S(1)} collective-permute-done((f32[8,64,128]{2,1,0:T(8,128)S(1)}, f32[8,64,128]{2,1,0:T(8,128)S(1)}, u32[]{:S(2)}, u32[]{:S(2)}) %collective-permute-start.7) | collective-permute-done | bytes 262176 | tf_op jit(solution)/shard_map/ppermute | solution.py:26
  64.8 0.9 %select_bitcast_fusion = f32[1,8,128,128]{3,2,1,0:T(8,128)} fusion(f32[8,128,128]{2,1,0:T(8,128)S(1)} %bitcast.57, f32[8,128,128]{2,1,0:T(8,128)S(1)} %collective-permute-done.8, pred[]{:T(512)S(6)} %eq.4, f32[1,8,128,128]{3,2,1,0:T(8,128)S(1)} %copy-done), kind=kLoop, calls=%fused_computation.14 | loop fusion | flops 393216 | bytes 2097153 | tf_op jit(solution)/shard_map/broadcast_in_dim | solution.py:296
  (51 shorter events, 4.2 us)
Async XLA Ops:
  0.6 8.0 %copy-start.9 = (f32[8,64,64]{2,1,0:T(8,128)S(1)}, f32[8,64,64]{2,1,0:T(8,128)}, u32[]{:S(2)}) copy-start(f32[8,64,64]{2,1,0:T(8,128)} %param.14) | copy-start | bytes 393220
  2.7 13.5 %collective-permute-start = (f32[5,8,16,128]{3,2,1,0:T(8,128)}, f32[5,8,16,128]{3,2,1,0:T(8,128)S(1)}, u32[]{:S(2)}, u32[]{:S(2)}) collective-permute-start(f32[5,8,16,128]{3,2,1,0:T(8,128)} %get-tuple-element.4), channel_id=1, source_target_pairs={{0,1},{1,2},{2,3},{4,5},{5,6},{6,7},{8,9},{9,10},{10,11},{12,13},{... | collective-permute-start | bytes 983048 | tf_op jit(solution)/shard_map/ppermute | solution.py:202
  6.2 11.3 %collective-permute-start.1 = (f32[5,8,16,128]{3,2,1,0:T(8,128)}, f32[5,8,16,128]{3,2,1,0:T(8,128)S(1)}, u32[]{:S(2)}, u32[]{:S(2)}) collective-permute-start(f32[5,8,16,128]{3,2,1,0:T(8,128)} %get-tuple-element.5), channel_id=1, source_target_pairs={{1,0},{2,1},{3,2},{5,4},{6,5},{7,6},{9,8},{10,9},{11,10},{13,12},{... | collective-permute-start | bytes 983048 | tf_op jit(solution)/shard_map/ppermute | solution.py:203
  9.0 2.3 %copy-start.7 = (f32[8,64,64]{2,1,0:T(8,128)}, f32[8,64,64]{2,1,0:T(8,128)S(1)}, u32[]{:S(2)}) copy-start(f32[8,64,64]{2,1,0:T(8,128)S(1)} %fusion.26) | copy-start | bytes 393220
  9.2 1.0 %copy-start = (f32[1,8,128,128]{3,2,1,0:T(8,128)S(1)}, f32[1,8,128,128]{3,2,1,0:T(8,128)}, u32[]{:S(2)}) copy-start(f32[1,8,128,128]{3,2,1,0:T(8,128)} %starts_hbm.1) | copy-start | bytes 1572868
  11.3 1.1 %copy-start.5 = (f32[8,128,128]{2,1,0:T(8,128)S(1)}, f32[8,128,128]{2,1,0:T(8,128)}, u32[]{:S(2)}) copy-start(f32[8,128,128]{2,1,0:T(8,128)} %param.15) | copy-start | bytes 1572868
  12.4 1.8 %copy-start.14 = (s32[8,4]{0,1:T(4,128)S(1)}, s32[8,4]{0,1:T(4,128)}, u32[]{:S(2)}) copy-start(s32[8,4]{0,1:T(4,128)} %param.13) | copy-start | bytes 388
  12.4 5.1 %copy-start.3 = (s32[8,128,128]{2,1,0:T(8,128)S(1)}, s32[8,128,128]{2,1,0:T(8,128)}, u32[]{:S(2)}) copy-start(s32[8,128,128]{2,1,0:T(8,128)} %obstacle_ref.1) | copy-start | bytes 1572868
  14.2 3.3 %copy-start.1 = (f32[2,8,128,128]{3,2,1,0:T(8,128)S(1)}, f32[2,8,128,128]{3,2,1,0:T(8,128)}, u32[]{:S(2)}) copy-start(f32[2,8,128,128]{3,2,1,0:T(8,128)} %velocity_ref.1) | copy-start | bytes 3145732
  14.3 3.2 %copy-start.2 = (f32[8,128,128]{2,1,0:T(8,128)S(1)}, f32[8,128,128]{2,1,0:T(8,128)}, u32[]{:S(2)}) copy-start(f32[8,128,128]{2,1,0:T(8,128)} %diffusivity_ref.1) | copy-start | bytes 1572868
  17.5 0.7 copy-start.4
  18.2 6.9 %copy-start.12 = (f32[8,64,128]{2,1,0:T(8,128)S(1)}, f32[8,64,128]{2,1,0:T(8,128)}, u32[]{:S(2)}) copy-start(f32[8,64,128]{2,1,0:T(8,128)} %fusion.25) | copy-start | bytes 786436
  25.4 1.0 %copy-start.13 = (f32[8,64,128]{2,1,0:T(8,128)S(1)}, f32[8,64,128]{2,1,0:T(8,128)}, u32[]{:S(2)}) copy-start(f32[8,64,128]{2,1,0:T(8,128)} %fusion.25) | copy-start | bytes 786436
  26.4 8.7 %copy-start.10 = (f32[8,64,64]{2,1,0:T(8,128)S(1)}, f32[8,64,64]{2,1,0:T(8,128)}, u32[]{:S(2)}) copy-start(f32[8,64,64]{2,1,0:T(8,128)} %param.14) | copy-start | bytes 393220
  26.4 8.7 %collective-permute-start.2 = (f32[8,64,128]{2,1,0:T(8,128)S(1)}, f32[8,64,128]{2,1,0:T(8,128)S(1)}, u32[]{:S(2)}, u32[]{:S(2)}) collective-permute-start(f32[8,64,128]{2,1,0:T(8,128)S(1)} %bitcast_add_fusion), channel_id=1, source_target_pairs={{0,4},{4,8},{8,12},{12,16},{16,20},{20,24},{24,28},{1,5},{5,9},{9,... | collective-permute-start | bytes 786440 | tf_op jit(solution)/shard_map/ppermute | solution.py:26
  29.1 6.3 %copy-start.6 = (f32[8,128,128]{2,1,0:T(8,128)S(1)}, f32[8,128,128]{2,1,0:T(8,128)}, u32[]{:S(2)}) copy-start(f32[8,128,128]{2,1,0:T(8,128)} %param.15) | copy-start | bytes 1572868
  29.1 29.8 %collective-permute-start.8 = (f32[8,128,128]{2,1,0:T(8,128)S(1)}, f32[8,128,128]{2,1,0:T(8,128)S(1)}, u32[]{:S(2)}, u32[]{:S(2)}) collective-permute-start(f32[8,128,128]{2,1,0:T(8,128)S(1)} %sub.49), channel_id=1, source_target_pairs={{0,4},{4,8},{8,12},{12,16},{16,20},{20,24},{24,28},{1,5},{5,9},{9,... | collective-permute-start | bytes 1572872 | tf_op jit(solution)/shard_map/ppermute | solution.py:26
  36.1 7.8 %collective-permute-start.3 = (f32[4,64,128]{2,1,0:T(8,128)S(1)}, f32[4,64,128]{2,1,0:T(8,128)S(1)}, u32[]{:S(2)}, u32[]{:S(2)}) collective-permute-start(f32[4,64,128]{2,1,0:T(8,128)S(1)} %fusion.5), channel_id=1, source_target_pairs={{0,8},{4,12},{8,16},{12,20},{16,24},{20,28},{1,9},{5,13},{9,17},{1... | collective-permute-start | bytes 393224 | tf_op jit(solution)/shard_map/ppermute | solution.py:26
  38.9 5.0 %copy-start.8 = (f32[8,64,64]{2,1,0:T(8,128)S(1)}, f32[8,64,64]{2,1,0:T(8,128)}, u32[]{:S(2)}) copy-start(f32[8,64,64]{2,1,0:T(8,128)} %copy-done.7) | copy-start | bytes 393220
  39.5 6.9 %collective-permute-start.5 = (f32[4,64,128]{2,1,0:T(8,128)S(1)}, f32[4,64,128]{2,1,0:T(8,128)S(1)}, u32[]{:S(2)}, u32[]{:S(2)}) collective-permute-start(f32[4,64,128]{2,1,0:T(8,128)S(1)} %fusion.2), channel_id=1, source_target_pairs={{0,16},{4,20},{8,24},{12,28},{1,17},{5,21},{9,25},{13,29},{2,18},{... | collective-permute-start | bytes 393224 | tf_op jit(solution)/shard_map/ppermute | solution.py:26
  44.1 2.3 %copy-start.11 = (f32[8,64,64]{2,1,0:T(8,128)S(1)}, f32[8,64,64]{2,1,0:T(8,128)}, u32[]{:S(2)}) copy-start(f32[8,64,64]{2,1,0:T(8,128)} %fusion.28) | copy-start | bytes 393220
  44.7 8.3 %collective-permute-start.4 = (f32[4,64,128]{2,1,0:T(8,128)S(1)}, f32[4,64,128]{2,1,0:T(8,128)S(1)}, u32[]{:S(2)}, u32[]{:S(2)}) collective-permute-start(f32[4,64,128]{2,1,0:T(8,128)S(1)} %fusion.4), channel_id=1, source_target_pairs={{0,16},{4,20},{8,24},{12,28},{1,17},{5,21},{9,25},{13,29},{2,18},{... | collective-permute-start | bytes 393224 | tf_op jit(solution)/shard_map/ppermute | solution.py:26
  47.3 7.8 %collective-permute-start.6 = (f32[4,64,128]{2,1,0:T(8,128)S(1)}, f32[4,64,128]{2,1,0:T(8,128)S(1)}, u32[]{:S(2)}, u32[]{:S(2)}) collective-permute-start(f32[4,64,128]{2,1,0:T(8,128)S(1)} %fusion.1), channel_id=1, source_target_pairs={{0,8},{4,12},{8,16},{12,20},{16,24},{20,28},{1,9},{5,13},{9,17},{1... | collective-permute-start | bytes 393224 | tf_op jit(solution)/shard_map/ppermute | solution.py:26
  56.0 8.6 %collective-permute-start.7 = (f32[8,64,128]{2,1,0:T(8,128)S(1)}, f32[8,64,128]{2,1,0:T(8,128)S(1)}, u32[]{:S(2)}, u32[]{:S(2)}) collective-permute-start(f32[8,64,128]{2,1,0:T(8,128)S(1)} %maximum_subtract_fusion), channel_id=1, source_target_pairs={{0,4},{4,8},{8,12},{12,16},{16,20},{20,24},{24,28},{1,5},{5,9},{9,... | collective-permute-start | bytes 786440 | tf_op jit(solution)/shard_map/ppermute | solution.py:26

commit v15 on v14

--- a/solution.py
+++ b/solution.py
@@ -265,8 +265,34 @@
 
     if slice_count == 1:
         seed = jnp.where(tm_index == 0, coarse_of_starts[0], 0.0)
-        reached = prefix_over_tm(coarse_jump[0] + seed, coarse_x, coarse_y)
-        coarse_applied = (reached - coarse_jump[0])[None]
+        jump = coarse_jump[0]
+        total = jump + seed
+        distances = []
+        distance = 1
+        while distance < tm_count:
+            distances.append(distance)
+            distance *= 2
+        power_x = coarse_x
+        power_y = coarse_y
+        received = passed_along(jnp.stack([total, jump], axis=0), "tm", 1)
+        jump_before = received[1]
+        lagged = None
+        for step, distance in enumerate(distances):
+            if step > 0:
+                power_x = jnp.einsum("tij,tjk->tik", power_x, power_x, precision=exact_precision)
+                power_y = jnp.einsum("tij,tjk->tik", power_y, power_y, precision=exact_precision)
+            last = step == len(distances) - 1
+            if last:
+                before = passed_along(total, "tm", 1) if step > 0 else received[0]
+                before_far = passed_along(total, "tm", distance + 1)
+            incoming = received[0] if step == 0 else passed_along(total, "tm", distance)
+            if last:
+                far_mixed = apply_coarse(before_far, power_x, power_y)
+                lagged = before + jnp.where(tm_index - 1 >= distance, far_mixed, 0.0)
+            mixed = apply_coarse(incoming, power_x, power_y)
+            total = total + jnp.where(tm_index >= distance, mixed, 0.0)
+        coarse_applied = (total - jump)[None]
+        coarse_before = lagged - jump_before
     else:
         shifted_jump = jnp.concatenate(
             [passed_along(coarse_jump[-1:], "tm", 1), coarse_jump[:-1]], axis=0
@@ -288,8 +314,9 @@
             earlier = apply_coarse(earlier, coarse_x, coarse_y)
             own_coarse.append(states[n] + earlier)
         coarse_applied = apply_coarse(jnp.stack(own_coarse, axis=0), coarse_x, coarse_y)
+        coarse_before = passed_along(coarse_applied[-1], "tm", 1)
     slice_ends = prolong(coarse_applied) + correction
-    previous = prolong(passed_along(coarse_applied[-1], "tm", 1)) + earlier_correction
+    previous = prolong(coarse_before) + earlier_correction
     first_step = jnp.where(
         lax.axis_index("tm") == 0, jnp.zeros_like(previous), previous - starts[0]
     )

time: 66.1 us -> 73.4 us (1.11)
  the two profiles are of different devices: /device:TPU:12 before, /device:TPU:0 now
where the time goes in v15:
time: 73.4 us; the launch traced here: 73 us
  starting transfers between devices  28.9 us (39%)
  waiting for transfers between devices  17 us (23%)
  matrix products  11.9 us (16%)
  Pallas kernels  8.96 us (12%)
  local copies, waits for them, and re-layouts  3.3 us (4%)
  other arithmetic  1.92 us (3%)
  between operations  1 us (1%)
    ppermute x6, starting transfers between devices, passed_along(): return lax.ppermute(block, axis, route)  22.6 us
    ppermute x6, waiting for transfers between devices, passed_along(): return lax.ppermute(block, axis, route)  12.9 us
    pallas_call x1, Pallas kernels, fine_propagate(): pl.pallas_call(functools.partial(fine_kernel, slice_at), out_shape=jax.Sh...  6.85 us
    dot_general x5, matrix products, apply_coarse(): jnp.einsum('...tik,tlk->...til', mixed_x, matrix_y, precision=exact_preci...  6.63 us
    ppermute x1, starting transfers between devices, on_device(): from_prev = lax.ppermute(high_rows, 'space', forward)  4.98 us
    ppermute x1, waiting for transfers between devices, on_device(): from_next = lax.ppermute(low_rows, 'space', backward)  4.03 us
    dot_general x5, matrix products, apply_coarse(): jnp.einsum('tij,...tjk->...tik', matrix_x, coarse_values, precision=exact...  3.24 us
    unnamed x16, local copies, waits for them, and re-layouts  2.35 us
  transfers between devices with their start and end apart: 8, of which 6 were waited for; matrix products, arithmetic and copies ran while one was open for 14% of the time, Pallas kernels for 0%

profile of v15, /device:TPU:0, one launch (start us, length us, event | category | flops | bytes accessed | tf_op | source)
XLA Modules:
  0.0 73.0 jit_solution(2042664324652551916)
XLA Ops:
  0.7 2.1 %shard_map.95 = (f32[5,8,16,128]{3,2,1,0:T(8,128)}, f32[5,8,16,128]{3,2,1,0:T(8,128)}) custom-call(f32[1,8,128,128]{3,2,1,0:T(8,128)} %starts_hbm.1, f32[8,128,128]{2,1,0:T(8,128)} %diffusivity_ref.1, f32[2,8,128,128]{3,2,1,0:T(8,128)} %velocity_ref.1, s32[8,128,128]{2,1,0:T(8,128)} %obstacle_ref.1), custom_call_target="tpu_custom_call" | custom-call | tf_op jit(solution)/shard_map/pallas_call | solution.py:177
  2.8 5.0 %collective-permute-start = (f32[5,8,16,128]{3,2,1,0:T(8,128)}, f32[5,8,16,128]{3,2,1,0:T(8,128)S(1)}, u32[]{:S(2)}, u32[]{:S(2)}) collective-permute-start(f32[5,8,16,128]{3,2,1,0:T(8,128)} %get-tuple-element.4), channel_id=1, source_target_pairs={{0,1},{1,2},{2,3},{4,5},{5,6},{6,7},{8,9},{9,10},{10,11},{12,13},{... | collective-permute-start | bytes 983048 | tf_op jit(solution)/shard_map/ppermute | solution.py:202
  7.8 1.3 %collective-permute-start.1 = (f32[5,8,16,128]{3,2,1,0:T(8,128)}, f32[5,8,16,128]{3,2,1,0:T(8,128)S(1)}, u32[]{:S(2)}, u32[]{:S(2)}) collective-permute-start(f32[5,8,16,128]{3,2,1,0:T(8,128)} %get-tuple-element.5), channel_id=1, source_target_pairs={{1,0},{2,1},{3,2},{5,4},{6,5},{7,6},{9,8},{10,9},{11,10},{13,12},{... | collective-permute-start | bytes 983048 | tf_op jit(solution)/shard_map/ppermute | solution.py:203
  9.3 1.0 %copy-done.1 = f32[1,8,128,128]{3,2,1,0:T(8,128)S(1)} copy-done((f32[1,8,128,128]{3,2,1,0:T(8,128)S(1)}, f32[1,8,128,128]{3,2,1,0:T(8,128)}, u32[]{:S(2)}) %copy-start.1) | copy-done | bytes 524312
  10.3 1.7 %fusion.6 = f32[8,64,128]{2,1,0:T(8,128)} fusion(f32[8,64,128]{1,0,2:T(8,128)S(1)} %bitcast.74, f32[1,8,128,128]{3,2,1,0:T(8,128)S(1)} %copy-done.1), kind=kOutput, calls=%fused_computation.11 | convolution fusion | flops 100663296 | bytes 1048576 | tf_op jit(solution)/shard_map/tij,...tjk->...tik/dot_general | solution.py:38
  12.0 0.7 copy-done.7
  12.8 2.1 %fusion.16 = f32[8,64,128]{2,1,0:T(8,128)S(1)} fusion(f32[8,64,128]{2,1,0:T(8,128)} %fusion.6, f32[8,128,128]{2,1,0:T(8,128)S(1)} %copy-done), kind=kOutput, calls=%fused_computation.37 | convolution fusion | flops 100663296 | bytes 1048576 | tf_op jit(solution)/shard_map/...tik,tlk->...til/dot_general | solution.py:39
  15.0 4.0 %collective-permute-done.1.next_ref = f32[5,8,16,128]{3,2,1,0:T(8,128)S(1)} collective-permute-done((f32[5,8,16,128]{3,2,1,0:T(8,128)}, f32[5,8,16,128]{3,2,1,0:T(8,128)S(1)}, u32[]{:S(2)}, u32[]{:S(2)}) %collective-permute-start.1) | collective-permute-done | bytes 327712 | tf_op jit(solution)/shard_map/ppermute | solution.py:203
  19.0 0.6 copy-done.5
  19.7 6.8 %shard_map.96 = f32[8,128,128]{2,1,0:T(8,128)S(1)} custom-call(s32[8]{0:T(128)S(1)} %get-tuple-element.12.south_ref, s32[8]{0:T(128)S(1)} %get-tuple-element.11.north_ref, s32[8]{0:T(128)S(1)} %get-tuple-element.13.west_at_ref, s32[8]{0:T(128)S(1)} %get-tuple-element.10.east_at_ref, s32[8]{0:T(128)S(1)} %get-tuple-element.9.west_ok_ref, ...), custom_call_target="tpu_custom_call" | custom-call | tf_op jit(solution)/shard_map/pallas_call | solution.py:131
  27.2 1.3 %collective-permute-start.2 = (f32[2,8,64,128]{3,2,1,0:T(8,128)S(1)}, f32[2,8,64,128]{3,2,1,0:T(8,128)S(1)}, u32[]{:S(2)}, u32[]{:S(2)}) collective-permute-start(f32[2,8,64,128]{3,2,1,0:T(8,128)S(1)} %pad_maximum_fusion), channel_id=1, source_target_pairs={{0,4},{4,8},{8,12},{12,16},{16,20},{20,24},{24,28},{1,5},{5,9},{9,... | collective-permute-start | bytes 1572872 | tf_op jit(solution)/shard_map/ppermute | solution.py:26
  28.9 0.4 fusion.20
  29.3 0.7 collective-permute-done.2
  30.3 1.1 %fusion = f32[8,64,128]{2,1,0:T(8,128)S(1)} fusion(f32[8,128,64]{1,2,0:T(8,128)S(1)} %fusion.8, f32[8,128,128]{2,1,0:T(8,128)S(1)} %copy-done, f32[1,8,64,128]{3,2,1,0:T(8,128)S(1)} %get-tuple-element.7, f32[8,64,128]{2,1,0:T(8,128)S(1)} %fusion.16, pred[]{:T(512)S(6)} %ge.12, pred[]{:T(512)S(6)} %eq.4), kind=kOutput, calls=%fused_computation.4 | convolution fusion | flops 100925440 | bytes 1572866 | tf_op jit(solution)/shard_map/...tik,tlk->...til/dot_general | solution.py:39
  31.5 11.1 %collective-permute-start.3 = (f32[8,64,128]{2,1,0:T(8,128)S(1)}, f32[8,64,128]{2,1,0:T(8,128)S(1)}, u32[]{:S(2)}, u32[]{:S(2)}) collective-permute-start(f32[8,64,128]{2,1,0:T(8,128)S(1)} %fusion), channel_id=1, source_target_pairs={{0,8},{4,12},{8,16},{12,20},{16,24},{20,28},{1,9},{5,13},{9,17},{1... | collective-permute-start | bytes 786440 | tf_op jit(solution)/shard_map/ppermute | solution.py:26
  42.6 0.6 fusion.19
  43.2 4.2 %collective-permute-done.3 = f32[8,64,128]{2,1,0:T(8,128)S(1)} collective-permute-done((f32[8,64,128]{2,1,0:T(8,128)S(1)}, f32[8,64,128]{2,1,0:T(8,128)S(1)}, u32[]{:S(2)}, u32[]{:S(2)}) %collective-permute-start.3) | collective-permute-done | bytes 262176 | tf_op jit(solution)/shard_map/ppermute | solution.py:26
  47.4 0.4 fusion.18
  47.8 1.1 %fusion.1 = f32[8,64,128]{2,1,0:T(8,128)S(1)} fusion(f32[8,64,128]{2,1,0:T(8,128)S(1)} %fusion, f32[8,64,128]{2,1,0:T(8,128)S(1)} %fusion.18, f32[8,128,128]{2,1,0:T(8,128)S(1)} %fusion.19, pred[]{:T(512)S(6)} %ge.13), kind=kOutput, calls=%fused_computation.5 | convolution fusion | flops 100794368 | bytes 1310721 | tf_op jit(solution)/shard_map/...tik,tlk->...til/dot_general | solution.py:39
  48.9 5.3 %collective-permute-start.4 = (f32[8,64,128]{2,1,0:T(8,128)S(1)}, f32[8,64,128]{2,1,0:T(8,128)S(1)}, u32[]{:S(2)}, u32[]{:S(2)}) collective-permute-start(f32[8,64,128]{2,1,0:T(8,128)S(1)} %fusion.1), channel_id=1, source_target_pairs={{0,16},{4,20},{8,24},{12,28},{1,17},{5,21},{9,25},{13,29},{2,18},{... | collective-permute-start | bytes 786440 | tf_op jit(solution)/shard_map/ppermute | solution.py:26
  54.3 0.6 fusion.22
  54.9 1.3 %collective-permute-start.7 = (f32[8,128,128]{2,1,0:T(8,128)S(1)}, f32[8,128,128]{2,1,0:T(8,128)S(1)}, u32[]{:S(2)}, u32[]{:S(2)}) collective-permute-start(f32[8,128,128]{2,1,0:T(8,128)S(1)} %sub.55), channel_id=1, source_target_pairs={{0,4},{4,8},{8,12},{12,16},{16,20},{20,24},{24,28},{1,5},{5,9},{9,... | collective-permute-start | bytes 1572872 | tf_op jit(solution)/shard_map/ppermute | solution.py:26
  56.2 2.2 %collective-permute-start.5 = (f32[8,64,128]{2,1,0:T(8,128)S(1)}, f32[8,64,128]{2,1,0:T(8,128)S(1)}, u32[]{:S(2)}, u32[]{:S(2)}) collective-permute-start(f32[8,64,128]{2,1,0:T(8,128)S(1)} %fusion.1), channel_id=1, source_target_pairs={{0,4},{4,8},{8,12},{12,16},{16,20},{20,24},{24,28},{1,5},{5,9},{9,... | collective-permute-start | bytes 786440 | tf_op jit(solution)/shard_map/ppermute | solution.py:26
  58.5 1.3 %collective-permute-start.6 = (f32[8,64,128]{2,1,0:T(8,128)S(1)}, f32[8,64,128]{2,1,0:T(8,128)S(1)}, u32[]{:S(2)}, u32[]{:S(2)}) collective-permute-start(f32[8,64,128]{2,1,0:T(8,128)S(1)} %fusion.1), channel_id=1, source_target_pairs={{0,20},{4,24},{8,28},{1,21},{5,25},{9,29},{2,22},{6,26},{10,30},{3... | collective-permute-start | bytes 786440 | tf_op jit(solution)/shard_map/ppermute | solution.py:26
  59.8 6.8 %collective-permute-done.4 = f32[8,64,128]{2,1,0:T(8,128)S(1)} collective-permute-done((f32[8,64,128]{2,1,0:T(8,128)S(1)}, f32[8,64,128]{2,1,0:T(8,128)S(1)}, u32[]{:S(2)}, u32[]{:S(2)}) %collective-permute-start.4) | collective-permute-done | bytes 262176 | tf_op jit(solution)/shard_map/ppermute | solution.py:26
  66.6 0.4 fusion.21
  67.0 1.1 %fusion.3 = f32[8,64,128]{2,1,0:T(8,128)S(1)} fusion(f32[8,64,128]{2,1,0:T(8,128)S(1)} %fusion.1, f32[8,64,128]{2,1,0:T(8,128)S(1)} %fusion.21, f32[8,128,128]{2,1,0:T(8,128)S(1)} %fusion.22, f32[1,8,64,128]{3,2,1,0:T(8,128)S(1)} %get-tuple-element.7, pred[]{:T(512)S(6)} %ge.14), kind=kOutput, calls=%fused_computation.7 | convolution fusion | flops 100859904 | bytes 1572865 | tf_op jit(solution)/shard_map/...tik,tlk->...til/dot_general | solution.py:39
  68.1 1.3 %collective-permute-done.6 = f32[8,64,128]{2,1,0:T(8,128)S(1)} collective-permute-done((f32[8,64,128]{2,1,0:T(8,128)S(1)}, f32[8,64,128]{2,1,0:T(8,128)S(1)}, u32[]{:S(2)}, u32[]{:S(2)}) %collective-permute-start.6) | collective-permute-done | bytes 262176 | tf_op jit(solution)/shard_map/ppermute | solution.py:26
  69.3 0.4 fusion.23
  69.9 0.9 %add_bitcast_fusion = f32[1,8,128,128]{3,2,1,0:T(8,128)} fusion(f32[8,128,128]{2,1,0:T(8,128)S(1)} %bitcast.73, f32[8,128,128]{2,1,0:T(8,128)S(1)} %sub.55), kind=kLoop, calls=%fused_computation.14 | loop fusion | flops 131072 | bytes 1572864 | tf_op jit(solution)/shard_map/add | solution.py:318
  70.8 1.1 %fusion.5 = f32[8,64,128]{2,1,0:T(8,128)S(1)} fusion(f32[8,64,128]{2,1,0:T(8,128)S(1)} %collective-permute-done.5, f32[8,64,128]{2,1,0:T(8,128)S(1)} %fusion.23, f32[8,128,128]{2,1,0:T(8,128)S(1)} %fusion.22, f32[2,8,64,128]{3,2,1,0:T(8,128)S(1)} %collective-permute-done.2, pred[]{:T(512)S(6)} %ge.15), kind=kOutput, calls=%fused_computation.9 | convolution fusion | flops 100859904 | bytes 1572865 | tf_op jit(solution)/shard_map/...tik,tlk->...til/dot_general | solution.py:39
  72.1 0.9 %select_bitcast_fusion = f32[1,8,128,128]{3,2,1,0:T(8,128)} fusion(f32[8,128,128]{2,1,0:T(8,128)S(1)} %bitcast.71, f32[8,128,128]{2,1,0:T(8,128)S(1)} %collective-permute-done.7, pred[]{:T(512)S(6)} %eq.4, f32[1,8,128,128]{3,2,1,0:T(8,128)S(1)} %copy-done.1), kind=kLoop, calls=%fused_computation.13 | loop fusion | flops 393216 | bytes 2097153 | tf_op jit(solution)/shard_map/broadcast_in_dim | solution.py:323
  (31 shorter events, 2.0 us)
Async XLA Ops:
  0.6 12.1 %copy-start = (f32[8,128,128]{2,1,0:T(8,128)S(1)}, f32[8,128,128]{2,1,0:T(8,128)}, u32[]{:S(2)}) copy-start(f32[8,128,128]{2,1,0:T(8,128)} %param.15) | copy-start | bytes 1572868
  0.6 8.4 %copy-start.6 = (f32[8,64,64]{2,1,0:T(8,128)S(1)}, f32[8,64,64]{2,1,0:T(8,128)}, u32[]{:S(2)}) copy-start(f32[8,64,64]{2,1,0:T(8,128)} %param.14) | copy-start | bytes 393220
  2.8 12.2 %collective-permute-start = (f32[5,8,16,128]{3,2,1,0:T(8,128)}, f32[5,8,16,128]{3,2,1,0:T(8,128)S(1)}, u32[]{:S(2)}, u32[]{:S(2)}) collective-permute-start(f32[5,8,16,128]{3,2,1,0:T(8,128)} %get-tuple-element.4), channel_id=1, source_target_pairs={{0,1},{1,2},{2,3},{4,5},{5,6},{6,7},{8,9},{9,10},{10,11},{12,13},{... | collective-permute-start | bytes 983048 | tf_op jit(solution)/shard_map/ppermute | solution.py:202
  7.8 11.3 %collective-permute-start.1 = (f32[5,8,16,128]{3,2,1,0:T(8,128)}, f32[5,8,16,128]{3,2,1,0:T(8,128)S(1)}, u32[]{:S(2)}, u32[]{:S(2)}) collective-permute-start(f32[5,8,16,128]{3,2,1,0:T(8,128)} %get-tuple-element.5), channel_id=1, source_target_pairs={{1,0},{2,1},{3,2},{5,4},{6,5},{7,6},{9,8},{10,9},{11,10},{13,12},{... | collective-permute-start | bytes 983048 | tf_op jit(solution)/shard_map/ppermute | solution.py:203
  9.3 1.0 %copy-start.1 = (f32[1,8,128,128]{3,2,1,0:T(8,128)S(1)}, f32[1,8,128,128]{3,2,1,0:T(8,128)}, u32[]{:S(2)}) copy-start(f32[1,8,128,128]{3,2,1,0:T(8,128)} %starts_hbm.1) | copy-start | bytes 1572868
  10.3 8.7 %copy-start.2 = (f32[2,8,128,128]{3,2,1,0:T(8,128)S(1)}, f32[2,8,128,128]{3,2,1,0:T(8,128)}, u32[]{:S(2)}) copy-start(f32[2,8,128,128]{3,2,1,0:T(8,128)} %velocity_ref.1) | copy-start | bytes 3145732
  12.0 0.7 copy-start.7
  12.8 6.3 %copy-start.3 = (f32[8,128,128]{2,1,0:T(8,128)S(1)}, f32[8,128,128]{2,1,0:T(8,128)}, u32[]{:S(2)}) copy-start(f32[8,128,128]{2,1,0:T(8,128)} %diffusivity_ref.1) | copy-start | bytes 1572868
  12.8 6.3 %copy-start.4 = (s32[8,128,128]{2,1,0:T(8,128)S(1)}, s32[8,128,128]{2,1,0:T(8,128)}, u32[]{:S(2)}) copy-start(s32[8,128,128]{2,1,0:T(8,128)} %obstacle_ref.1) | copy-start | bytes 1572868
  19.0 0.7 copy-start.5
  27.2 2.8 %collective-permute-start.2 = (f32[2,8,64,128]{3,2,1,0:T(8,128)S(1)}, f32[2,8,64,128]{3,2,1,0:T(8,128)S(1)}, u32[]{:S(2)}, u32[]{:S(2)}) collective-permute-start(f32[2,8,64,128]{3,2,1,0:T(8,128)S(1)} %pad_maximum_fusion), channel_id=1, source_target_pairs={{0,4},{4,8},{8,12},{12,16},{16,20},{20,24},{24,28},{1,5},{5,9},{9,... | collective-permute-start | bytes 1572872 | tf_op jit(solution)/shard_map/ppermute | solution.py:26
  31.5 15.9 %collective-permute-start.3 = (f32[8,64,128]{2,1,0:T(8,128)S(1)}, f32[8,64,128]{2,1,0:T(8,128)S(1)}, u32[]{:S(2)}, u32[]{:S(2)}) collective-permute-start(f32[8,64,128]{2,1,0:T(8,128)S(1)} %fusion), channel_id=1, source_target_pairs={{0,8},{4,12},{8,16},{12,20},{16,24},{20,28},{1,9},{5,13},{9,17},{1... | collective-permute-start | bytes 786440 | tf_op jit(solution)/shard_map/ppermute | solution.py:26
  48.9 17.7 %collective-permute-start.4 = (f32[8,64,128]{2,1,0:T(8,128)S(1)}, f32[8,64,128]{2,1,0:T(8,128)S(1)}, u32[]{:S(2)}, u32[]{:S(2)}) collective-permute-start(f32[8,64,128]{2,1,0:T(8,128)S(1)} %fusion.1), channel_id=1, source_target_pairs={{0,16},{4,20},{8,24},{12,28},{1,17},{5,21},{9,25},{13,29},{2,18},{... | collective-permute-start | bytes 786440 | tf_op jit(solution)/shard_map/ppermute | solution.py:26
  54.9 17.0 %collective-permute-start.7 = (f32[8,128,128]{2,1,0:T(8,128)S(1)}, f32[8,128,128]{2,1,0:T(8,128)S(1)}, u32[]{:S(2)}, u32[]{:S(2)}) collective-permute-start(f32[8,128,128]{2,1,0:T(8,128)S(1)} %sub.55), channel_id=1, source_target_pairs={{0,4},{4,8},{8,12},{12,16},{16,20},{20,24},{24,28},{1,5},{5,9},{9,... | collective-permute-start | bytes 1572872 | tf_op jit(solution)/shard_map/ppermute | solution.py:26
  56.2 14.6 %collective-permute-start.5 = (f32[8,64,128]{2,1,0:T(8,128)S(1)}, f32[8,64,128]{2,1,0:T(8,128)S(1)}, u32[]{:S(2)}, u32[]{:S(2)}) collective-permute-start(f32[8,64,128]{2,1,0:T(8,128)S(1)} %fusion.1), channel_id=1, source_target_pairs={{0,4},{4,8},{8,12},{12,16},{16,20},{20,24},{24,28},{1,5},{5,9},{9,... | collective-permute-start | bytes 786440 | tf_op jit(solution)/shard_map/ppermute | solution.py:26
  58.5 10.9 %collective-permute-start.6 = (f32[8,64,128]{2,1,0:T(8,128)S(1)}, f32[8,64,128]{2,1,0:T(8,128)S(1)}, u32[]{:S(2)}, u32[]{:S(2)}) collective-permute-start(f32[8,64,128]{2,1,0:T(8,128)S(1)} %fusion.1), channel_id=1, source_target_pairs={{0,20},{4,24},{8,28},{1,21},{5,25},{9,29},{2,22},{6,26},{10,30},{3... | collective-permute-start | bytes 786440 | tf_op jit(solution)/shard_map/ppermute | solution.py:26

commit v16 on v14

--- a/solution.py
+++ b/solution.py
@@ -41,7 +41,7 @@
 
 def fine_kernel(slice_at, south_ref, north_ref, west_at_ref, east_at_ref, west_ok_ref, east_ok_ref,
                 scale_ref, u_ref, diffusivity_ref, velocity_ref, obstacle_ref, prev_ref, next_ref,
-                out_ref, state_ref, other_ref, field_ref):
+                coarse_ref, out_ref, jump_ref, state_ref, other_ref, field_ref):
     tiles = u_ref.shape[0]
     rows = u_ref.shape[1]
     lanes = u_ref.shape[2]
@@ -119,27 +119,36 @@
     if SUB % 2:
         substep(scale_ref[SUB - 1], state_ref, other_ref)
         final_ref = other_ref
+    half_rows = rows // 2
     for i in range(tiles):
         out_ref[i] = final_ref[i, pl.ds(PAD + HALO, rows), :]
-
-
-def fine_propagate(slice_at, u, diffusivity, velocity, obstacle, from_prev, from_next, indices, scale):
+        even = final_ref[i, pl.ds(PAD + HALO, half_rows, stride=2), :]
+        odd = final_ref[i, pl.ds(PAD + HALO + 1, half_rows, stride=2), :]
+        coarse = coarse_ref[i]
+        jump_ref[i] = 0.5 * ((even - coarse) + (odd - coarse))
+
+
+def fine_propagate(slice_at, u, diffusivity, velocity, obstacle, from_prev, from_next, coarse,
+                   indices, scale):
     tiles, rows, lanes = u.shape
     total = rows + 2 * HALO
     vmem = pltpu.MemorySpace.VMEM
     smem = pltpu.MemorySpace.SMEM
     return pl.pallas_call(
         functools.partial(fine_kernel, slice_at),
-        out_shape=jax.ShapeDtypeStruct(u.shape, u.dtype),
-        in_specs=[pl.BlockSpec(memory_space=smem)] * 7 + [pl.BlockSpec(memory_space=vmem)] * 6,
-        out_specs=pl.BlockSpec(memory_space=vmem),
+        out_shape=(
+            jax.ShapeDtypeStruct(u.shape, u.dtype),
+            jax.ShapeDtypeStruct(coarse.shape, coarse.dtype),
+        ),
+        in_specs=[pl.BlockSpec(memory_space=smem)] * 7 + [pl.BlockSpec(memory_space=vmem)] * 7,
+        out_specs=(pl.BlockSpec(memory_space=vmem), pl.BlockSpec(memory_space=vmem)),
         scratch_shapes=[
             pltpu.VMEM((tiles + 1, total + 2 * PAD, lanes), jnp.float32),
             pltpu.VMEM((tiles + 1, total + 2 * PAD, lanes), jnp.float32),
             pltpu.VMEM((4, tiles, total, lanes), jnp.float32),
         ],
         compiler_params=pltpu.CompilerParams(vmem_limit_bytes=48 * 1024 * 1024),
-    )(*indices, scale, u, diffusivity, velocity, obstacle, from_prev, from_next)
+    )(*indices, scale, u, diffusivity, velocity, obstacle, from_prev, from_next, coarse)
 
 
 def payload_kernel(starts_hbm, diffusivity_hbm, velocity_hbm, obstacle_hbm, low_ref, high_ref,
@@ -216,20 +225,18 @@
     north = jnp.where(north_ok > 0, jnp.clip(north_nb - block_base, 0, tile_count - 1), tile_count)
     indices = (south, north, west_at, east_at, west_ok, east_ok)
 
-    fine_ends = jnp.stack(
-        [
-            fine_propagate(
-                n, starts[n], diffusivity, velocity, obstacle, from_prev, from_next, indices,
-                substep_scale,
-            )
-            for n in range(slice_count)
-        ],
-        axis=0,
-    )
     restricting_x = 0.5 * jnp.repeat(coarse_x, 2, axis=2)
     coarse_of_starts = apply_coarse(starts, restricting_x, coarse_y)
+    fine_results = [
+        fine_propagate(
+            n, starts[n], diffusivity, velocity, obstacle, from_prev, from_next,
+            coarse_of_starts[n], indices, substep_scale,
+        )
+        for n in range(slice_count)
+    ]
+    fine_ends = jnp.stack([result[0] for result in fine_results], axis=0)
+    coarse_jump = jnp.stack([result[1] for result in fine_results], axis=0)
     correction = fine_ends - prolong(coarse_of_starts)
-    coarse_jump = restrict(correction)
     earlier_correction = passed_along(correction[-1], "tm", 1)
     tm_index = lax.axis_index("tm")
     tm_count = lax.axis_size("tm")

time: 66.1 us -> 71.6 us (1.083)
  waiting for transfers between devices: 17.4 us -> 25.2 us
  local copies, waits for them, and re-layouts: 3.47 us -> 2.42 us
    ppermute x7, waiting for transfers between devices: 16.2 us -> 23.3 us  [passed_along(): return lax.ppermute(block, axis, route)]
    unnamed x30 -> x22, local copies, waits for them, and re-layouts: 2.52 us -> 1.69 us
  transfers between devices with their start and end apart: 9 -> 9, of which waited for: 7 -> 7; matrix products, arithmetic and copies ran while one was open for 20% -> 14% of each run, Pallas kernels for 0% -> 0%
where the time goes in v16:
time: 71.6 us; the launch traced here: 71.1 us
  waiting for transfers between devices  25.2 us (35%)
  starting transfers between devices  20.2 us (28%)
  matrix products  11.4 us (16%)
  Pallas kernels  8.94 us (12%)
  local copies, waits for them, and re-layouts  2.42 us (3%)
  other arithmetic  1.88 us (3%)
  between operations  1.05 us (1%)
    ppermute x7, waiting for transfers between devices, passed_along(): return lax.ppermute(block, axis, route)  23.3 us
    ppermute x7, starting transfers between devices, passed_along(): return lax.ppermute(block, axis, route)  14.3 us
    pallas_call x1, Pallas kernels, fine_propagate(): pl.pallas_call(functools.partial(fine_kernel, slice_at), out_shape=(jax.S...  6.86 us
    dot_general x7, matrix products, apply_coarse(): jnp.einsum('...tik,tlk->...til', mixed_x, matrix_y, precision=exact_preci...  4.79 us
    ppermute x1, starting transfers between devices, on_device(): from_prev = lax.ppermute(high_rows, 'space', forward)  3.48 us
    dot_general x7, matrix products, apply_coarse(): jnp.einsum('tij,...tjk->...tik', matrix_x, coarse_values, precision=exact...  2.58 us
    dot_general x2, matrix products, prefix_over_tm(): jnp.einsum('tij,tjk->tik', power_y, power_y, precision=exact_precision)  2.56 us
    ppermute x1, starting transfers between devices, on_device(): from_next = lax.ppermute(low_rows, 'space', backward)  2.37 us
  transfers between devices with their start and end apart: 9, of which 7 were waited for; matrix products, arithmetic and copies ran while one was open for 14% of the time, Pallas kernels for 0%

profile of v16, /device:TPU:12, one launch (start us, length us, event | category | flops | bytes accessed | tf_op | source)
XLA Modules:
  0.0 71.1 jit_solution(10905721560588351505)
XLA Ops:
  0.6 2.1 %shard_map.95 = (f32[5,8,16,128]{3,2,1,0:T(8,128)}, f32[5,8,16,128]{3,2,1,0:T(8,128)}) custom-call(f32[1,8,128,128]{3,2,1,0:T(8,128)} %starts_hbm.1, f32[8,128,128]{2,1,0:T(8,128)} %diffusivity_ref.1, f32[2,8,128,128]{3,2,1,0:T(8,128)} %velocity_ref.1, s32[8,128,128]{2,1,0:T(8,128)} %obstacle_ref.1), custom_call_target="tpu_custom_call" | custom-call | tf_op jit(solution)/shard_map/pallas_call | solution.py:186
  2.7 3.5 %collective-permute-start = (f32[5,8,16,128]{3,2,1,0:T(8,128)}, f32[5,8,16,128]{3,2,1,0:T(8,128)S(1)}, u32[]{:S(2)}, u32[]{:S(2)}) collective-permute-start(f32[5,8,16,128]{3,2,1,0:T(8,128)} %get-tuple-element.6), channel_id=1, source_target_pairs={{0,1},{1,2},{2,3},{4,5},{5,6},{6,7},{8,9},{9,10},{10,11},{12,13},{... | collective-permute-start | bytes 983048 | tf_op jit(solution)/shard_map/ppermute | solution.py:211
  6.2 2.4 %collective-permute-start.1 = (f32[5,8,16,128]{3,2,1,0:T(8,128)}, f32[5,8,16,128]{3,2,1,0:T(8,128)S(1)}, u32[]{:S(2)}, u32[]{:S(2)}) collective-permute-start(f32[5,8,16,128]{3,2,1,0:T(8,128)} %get-tuple-element.7), channel_id=1, source_target_pairs={{1,0},{2,1},{3,2},{5,4},{6,5},{7,6},{9,8},{10,9},{11,10},{13,12},{... | collective-permute-start | bytes 983048 | tf_op jit(solution)/shard_map/ppermute | solution.py:212
  9.3 1.0 %copy-done = f32[1,8,128,128]{3,2,1,0:T(8,128)S(1)} copy-done((f32[1,8,128,128]{3,2,1,0:T(8,128)S(1)}, f32[1,8,128,128]{3,2,1,0:T(8,128)}, u32[]{:S(2)}) %copy-start) | copy-done | bytes 524312
  10.2 1.0 %fusion.4 = f32[8,64,128]{2,1,0:T(8,128)S(1)} fusion(f32[8,64,128]{1,0,2:T(8,128)S(1)} %bitcast.54, f32[1,8,128,128]{3,2,1,0:T(8,128)S(1)} %copy-done), kind=kOutput, calls=%fused_computation.10 | convolution fusion | flops 100663296 | bytes 1048576 | tf_op jit(solution)/shard_map/tij,...tjk->...tik/dot_general | solution.py:38
  11.3 1.1 %fusion.30 = f32[8,64,64]{2,1,0:T(8,128)} fusion(f32[8,64,64]{2,1,0:T(8,128)S(1)} %fusion.28), kind=kOutput, calls=%fused_computation.47 | convolution fusion | flops 25165824 | bytes 262144 | tf_op jit(solution)/shard_map/tij,tjk->tik/dot_general | solution.py:254
  12.4 1.1 %fusion.27.coarse_ref = f32[8,64,128]{2,1,0:T(8,128)S(1)} fusion(f32[8,64,128]{2,1,0:T(8,128)S(1)} %fusion.4, f32[8,128,128]{2,1,0:T(8,128)S(1)} %copy-done.5), kind=kOutput, calls=%fused_computation.44 | convolution fusion | flops 100663296 | bytes 1048576 | tf_op jit(solution)/shard_map/...tik,tlk->...til/dot_general | solution.py:39
  13.6 1.9 %fusion.29 = f32[8,128,128]{2,1,0:T(8,128)S(1)} fusion(f32[8,128,128]{2,1,0:T(8,128)} %param.15), kind=kOutput, calls=%fused_computation.46 | convolution fusion | flops 201326592 | bytes 1048576 | tf_op jit(solution)/shard_map/tij,tjk->tik/dot_general | solution.py:255
  15.6 1.9 %collective-permute-done.1.next_ref = f32[5,8,16,128]{3,2,1,0:T(8,128)S(1)} collective-permute-done((f32[5,8,16,128]{3,2,1,0:T(8,128)}, f32[5,8,16,128]{3,2,1,0:T(8,128)S(1)}, u32[]{:S(2)}, u32[]{:S(2)}) %collective-permute-start.1) | collective-permute-done | bytes 327712 | tf_op jit(solution)/shard_map/ppermute | solution.py:212
  17.5 0.6 copy-done.4
  18.2 6.9 %shard_map.96 = (f32[8,128,128]{2,1,0:T(8,128)S(1)}, f32[8,64,128]{2,1,0:T(8,128)S(1)}) custom-call(s32[8]{0:T(128)S(1)} %get-tuple-element.16.south_ref, s32[8]{0:T(128)S(1)} %get-tuple-element.15.north_ref, s32[8]{0:T(128)S(1)} %get-tuple-element.17.west_at_ref, s32[8]{0:T(128)S(1)} %get-tuple-element.14.east_at_ref, s32[8]{0:T(128)S(1)} %get-tuple-element.13.west_ok_ref, ...), custom_call_target="tpu_custom_call" | custom-call | tf_op jit(solution)/shard_map/pallas_call | solution.py:137
  25.1 2.1 %collective-permute-start.2 = (f32[8,64,128]{2,1,0:T(8,128)S(1)}, f32[8,64,128]{2,1,0:T(8,128)S(1)}, u32[]{:S(2)}, u32[]{:S(2)}) collective-permute-start(f32[8,64,128]{2,1,0:T(8,128)S(1)} %select_add_fusion), channel_id=1, source_target_pairs={{0,4},{4,8},{8,12},{12,16},{16,20},{20,24},{24,28},{1,5},{5,9},{9,... | collective-permute-start | bytes 786440 | tf_op jit(solution)/shard_map/ppermute | solution.py:26
  27.1 0.6 fusion.31
  27.8 6.0 %collective-permute-done.2 = f32[8,64,128]{2,1,0:T(8,128)S(1)} collective-permute-done((f32[8,64,128]{2,1,0:T(8,128)S(1)}, f32[8,64,128]{2,1,0:T(8,128)S(1)}, u32[]{:S(2)}, u32[]{:S(2)}) %collective-permute-start.2) | collective-permute-done | bytes 262176 | tf_op jit(solution)/shard_map/ppermute | solution.py:26
  34.1 0.6 slice_add_fusion.1
  34.7 2.5 %collective-permute-start.3 = (f32[4,64,128]{2,1,0:T(8,128)S(1)}, f32[4,64,128]{2,1,0:T(8,128)S(1)}, u32[]{:S(2)}, u32[]{:S(2)}) collective-permute-start(f32[4,64,128]{2,1,0:T(8,128)S(1)} %slice_add_fusion.1), channel_id=1, source_target_pairs={{0,8},{4,12},{8,16},{12,20},{16,24},{20,28},{1,9},{5,13},{9,17},{1... | collective-permute-start | bytes 393224 | tf_op jit(solution)/shard_map/ppermute | solution.py:26
  37.5 0.6 slice_add_fusion
  38.1 1.3 %collective-permute-start.5 = (f32[4,64,128]{2,1,0:T(8,128)S(1)}, f32[4,64,128]{2,1,0:T(8,128)S(1)}, u32[]{:S(2)}, u32[]{:S(2)}) collective-permute-start(f32[4,64,128]{2,1,0:T(8,128)S(1)} %slice_add_fusion), channel_id=1, source_target_pairs={{0,16},{4,20},{8,24},{12,28},{1,17},{5,21},{9,25},{13,29},{2,18},{... | collective-permute-start | bytes 393224 | tf_op jit(solution)/shard_map/ppermute | solution.py:26
  39.4 3.2 %collective-permute-done.3 = f32[4,64,128]{2,1,0:T(8,128)S(1)} collective-permute-done((f32[4,64,128]{2,1,0:T(8,128)S(1)}, f32[4,64,128]{2,1,0:T(8,128)S(1)}, u32[]{:S(2)}, u32[]{:S(2)}) %collective-permute-start.3) | collective-permute-done | bytes 131104 | tf_op jit(solution)/shard_map/ppermute | solution.py:26
  42.8 0.6 fusion.3
  43.4 1.3 %collective-permute-start.4 = (f32[4,64,128]{2,1,0:T(8,128)S(1)}, f32[4,64,128]{2,1,0:T(8,128)S(1)}, u32[]{:S(2)}, u32[]{:S(2)}) collective-permute-start(f32[4,64,128]{2,1,0:T(8,128)S(1)} %fusion.3), channel_id=1, source_target_pairs={{0,16},{4,20},{8,24},{12,28},{1,17},{5,21},{9,25},{13,29},{2,18},{... | collective-permute-start | bytes 393224 | tf_op jit(solution)/shard_map/ppermute | solution.py:26
  45.3 0.6 fusion.1
  45.9 3.0 %collective-permute-start.6 = (f32[4,64,128]{2,1,0:T(8,128)S(1)}, f32[4,64,128]{2,1,0:T(8,128)S(1)}, u32[]{:S(2)}, u32[]{:S(2)}) collective-permute-start(f32[4,64,128]{2,1,0:T(8,128)S(1)} %fusion.1), channel_id=1, source_target_pairs={{0,8},{4,12},{8,16},{12,20},{16,24},{20,28},{1,9},{5,13},{9,17},{1... | collective-permute-start | bytes 393224 | tf_op jit(solution)/shard_map/ppermute | solution.py:26
  48.9 2.8 %collective-permute-done.4 = f32[4,64,128]{2,1,0:T(8,128)S(1)} collective-permute-done((f32[4,64,128]{2,1,0:T(8,128)S(1)}, f32[4,64,128]{2,1,0:T(8,128)S(1)}, u32[]{:S(2)}, u32[]{:S(2)}) %collective-permute-start.4) | collective-permute-done | bytes 131104 | tf_op jit(solution)/shard_map/ppermute | solution.py:26
  52.0 0.6 fusion.2
  52.6 1.0 %collective-permute-done.6 = f32[4,64,128]{2,1,0:T(8,128)S(1)} collective-permute-done((f32[4,64,128]{2,1,0:T(8,128)S(1)}, f32[4,64,128]{2,1,0:T(8,128)S(1)}, u32[]{:S(2)}, u32[]{:S(2)}) %collective-permute-start.6) | collective-permute-done | bytes 131104 | tf_op jit(solution)/shard_map/ppermute | solution.py:26
  53.9 0.6 fusion
  54.9 0.9 %add_bitcast_fusion = (f32[1,8,128,128]{3,2,1,0:T(8,128)}, f32[8,128,128]{2,1,0:T(8,128)S(1)}) fusion(f32[8,128,128]{2,1,0:T(8,128)S(1)} %bitcast.51, f32[8,128,128]{2,1,0:T(8,128)S(1)} %get-tuple-element.9, f32[8,128,128]{2,1,0:T(8,128)S(1)} %bitcast.52), kind=kLoop, calls=%fused_computation.13 | loop fusion | flops 262144 | bytes 2621440 | tf_op jit(solution)/shard_map/add | solution.py:298
  55.8 1.9 %collective-permute-start.8 = (f32[8,128,128]{2,1,0:T(8,128)S(1)}, f32[8,128,128]{2,1,0:T(8,128)S(1)}, u32[]{:S(2)}, u32[]{:S(2)}) collective-permute-start(f32[8,128,128]{2,1,0:T(8,128)S(1)} %get-tuple-element.11), channel_id=1, source_target_pairs={{0,4},{4,8},{8,12},{12,16},{16,20},{20,24},{24,28},{1,5},{5,9},{9,... | collective-permute-start | bytes 1572872 | tf_op jit(solution)/shard_map/ppermute | solution.py:26
  57.8 2.2 %collective-permute-start.7 = (f32[8,64,128]{2,1,0:T(8,128)S(1)}, f32[8,64,128]{2,1,0:T(8,128)S(1)}, u32[]{:S(2)}, u32[]{:S(2)}) collective-permute-start(f32[8,64,128]{2,1,0:T(8,128)S(1)} %maximum_subtract_fusion), channel_id=1, source_target_pairs={{0,4},{4,8},{8,12},{12,16},{16,20},{20,24},{24,28},{1,5},{5,9},{9,... | collective-permute-start | bytes 786440 | tf_op jit(solution)/shard_map/ppermute | solution.py:26
  60.0 10.0 %collective-permute-done.7 = f32[8,64,128]{2,1,0:T(8,128)S(1)} collective-permute-done((f32[8,64,128]{2,1,0:T(8,128)S(1)}, f32[8,64,128]{2,1,0:T(8,128)S(1)}, u32[]{:S(2)}, u32[]{:S(2)}) %collective-permute-start.7) | collective-permute-done | bytes 262176 | tf_op jit(solution)/shard_map/ppermute | solution.py:26
  70.2 0.9 %select_bitcast_fusion = f32[1,8,128,128]{3,2,1,0:T(8,128)} fusion(f32[8,128,128]{2,1,0:T(8,128)S(1)} %bitcast.53, f32[8,128,128]{2,1,0:T(8,128)S(1)} %collective-permute-done.8, pred[]{:T(512)S(6)} %eq.4, f32[1,8,128,128]{3,2,1,0:T(8,128)S(1)} %copy-done), kind=kLoop, calls=%fused_computation.12 | loop fusion | flops 393216 | bytes 2097153 | tf_op jit(solution)/shard_map/broadcast_in_dim | solution.py:303
  (40 shorter events, 3.1 us)
Async XLA Ops:
  0.6 8.0 %copy-start.7 = (f32[8,64,64]{2,1,0:T(8,128)S(1)}, f32[8,64,64]{2,1,0:T(8,128)}, u32[]{:S(2)}) copy-start(f32[8,64,64]{2,1,0:T(8,128)} %param.14) | copy-start | bytes 393220
  2.7 12.8 %collective-permute-start = (f32[5,8,16,128]{3,2,1,0:T(8,128)}, f32[5,8,16,128]{3,2,1,0:T(8,128)S(1)}, u32[]{:S(2)}, u32[]{:S(2)}) collective-permute-start(f32[5,8,16,128]{3,2,1,0:T(8,128)} %get-tuple-element.6), channel_id=1, source_target_pairs={{0,1},{1,2},{2,3},{4,5},{5,6},{6,7},{8,9},{9,10},{10,11},{12,13},{... | collective-permute-start | bytes 983048 | tf_op jit(solution)/shard_map/ppermute | solution.py:211
  6.2 11.3 %collective-permute-start.1 = (f32[5,8,16,128]{3,2,1,0:T(8,128)}, f32[5,8,16,128]{3,2,1,0:T(8,128)S(1)}, u32[]{:S(2)}, u32[]{:S(2)}) collective-permute-start(f32[5,8,16,128]{3,2,1,0:T(8,128)} %get-tuple-element.7), channel_id=1, source_target_pairs={{1,0},{2,1},{3,2},{5,4},{6,5},{7,6},{9,8},{10,9},{11,10},{13,12},{... | collective-permute-start | bytes 983048 | tf_op jit(solution)/shard_map/ppermute | solution.py:212
  9.2 1.0 %copy-start = (f32[1,8,128,128]{3,2,1,0:T(8,128)S(1)}, f32[1,8,128,128]{3,2,1,0:T(8,128)}, u32[]{:S(2)}) copy-start(f32[1,8,128,128]{3,2,1,0:T(8,128)} %starts_hbm.1) | copy-start | bytes 1572868
  11.3 1.1 %copy-start.5 = (f32[8,128,128]{2,1,0:T(8,128)S(1)}, f32[8,128,128]{2,1,0:T(8,128)}, u32[]{:S(2)}) copy-start(f32[8,128,128]{2,1,0:T(8,128)} %param.15) | copy-start | bytes 1572868
  12.4 1.1 %copy-start.10 = (s32[8,4]{0,1:T(4,128)S(1)}, s32[8,4]{0,1:T(4,128)}, u32[]{:S(2)}) copy-start(s32[8,4]{0,1:T(4,128)} %param.13) | copy-start | bytes 388
  12.4 5.1 %copy-start.3 = (s32[8,128,128]{2,1,0:T(8,128)S(1)}, s32[8,128,128]{2,1,0:T(8,128)}, u32[]{:S(2)}) copy-start(s32[8,128,128]{2,1,0:T(8,128)} %obstacle_ref.1) | copy-start | bytes 1572868
  13.6 4.0 %copy-start.1 = (f32[2,8,128,128]{3,2,1,0:T(8,128)S(1)}, f32[2,8,128,128]{3,2,1,0:T(8,128)}, u32[]{:S(2)}) copy-start(f32[2,8,128,128]{3,2,1,0:T(8,128)} %velocity_ref.1) | copy-start | bytes 3145732
  13.6 3.9 %copy-start.2 = (f32[8,128,128]{2,1,0:T(8,128)S(1)}, f32[8,128,128]{2,1,0:T(8,128)}, u32[]{:S(2)}) copy-start(f32[8,128,128]{2,1,0:T(8,128)} %diffusivity_ref.1) | copy-start | bytes 1572868
  17.5 0.7 copy-start.4
  25.1 8.7 %copy-start.8 = (f32[8,64,64]{2,1,0:T(8,128)S(1)}, f32[8,64,64]{2,1,0:T(8,128)}, u32[]{:S(2)}) copy-start(f32[8,64,64]{2,1,0:T(8,128)} %param.14) | copy-start | bytes 393220
  25.1 8.7 %collective-permute-start.2 = (f32[8,64,128]{2,1,0:T(8,128)S(1)}, f32[8,64,128]{2,1,0:T(8,128)S(1)}, u32[]{:S(2)}, u32[]{:S(2)}) collective-permute-start(f32[8,64,128]{2,1,0:T(8,128)S(1)} %select_add_fusion), channel_id=1, source_target_pairs={{0,4},{4,8},{8,12},{12,16},{16,20},{20,24},{24,28},{1,5},{5,9},{9,... | collective-permute-start | bytes 786440 | tf_op jit(solution)/shard_map/ppermute | solution.py:26
  27.8 6.3 %copy-start.6 = (f32[8,128,128]{2,1,0:T(8,128)S(1)}, f32[8,128,128]{2,1,0:T(8,128)}, u32[]{:S(2)}) copy-start(f32[8,128,128]{2,1,0:T(8,128)} %param.15) | copy-start | bytes 1572868
  34.7 7.9 %collective-permute-start.3 = (f32[4,64,128]{2,1,0:T(8,128)S(1)}, f32[4,64,128]{2,1,0:T(8,128)S(1)}, u32[]{:S(2)}, u32[]{:S(2)}) collective-permute-start(f32[4,64,128]{2,1,0:T(8,128)S(1)} %slice_add_fusion.1), channel_id=1, source_target_pairs={{0,8},{4,12},{8,16},{12,20},{16,24},{20,28},{1,9},{5,13},{9,17},{1... | collective-permute-start | bytes 393224 | tf_op jit(solution)/shard_map/ppermute | solution.py:26
  38.1 6.9 %collective-permute-start.5 = (f32[4,64,128]{2,1,0:T(8,128)S(1)}, f32[4,64,128]{2,1,0:T(8,128)S(1)}, u32[]{:S(2)}, u32[]{:S(2)}) collective-permute-start(f32[4,64,128]{2,1,0:T(8,128)S(1)} %slice_add_fusion), channel_id=1, source_target_pairs={{0,16},{4,20},{8,24},{12,28},{1,17},{5,21},{9,25},{13,29},{2,18},{... | collective-permute-start | bytes 393224 | tf_op jit(solution)/shard_map/ppermute | solution.py:26
  42.8 2.2 %copy-start.9 = (f32[8,64,64]{2,1,0:T(8,128)S(1)}, f32[8,64,64]{2,1,0:T(8,128)}, u32[]{:S(2)}) copy-start(f32[8,64,64]{2,1,0:T(8,128)} %fusion.30) | copy-start | bytes 393220
  43.4 8.3 %collective-permute-start.4 = (f32[4,64,128]{2,1,0:T(8,128)S(1)}, f32[4,64,128]{2,1,0:T(8,128)S(1)}, u32[]{:S(2)}, u32[]{:S(2)}) collective-permute-start(f32[4,64,128]{2,1,0:T(8,128)S(1)} %fusion.3), channel_id=1, source_target_pairs={{0,16},{4,20},{8,24},{12,28},{1,17},{5,21},{9,25},{13,29},{2,18},{... | collective-permute-start | bytes 393224 | tf_op jit(solution)/shard_map/ppermute | solution.py:26
  45.9 7.8 %collective-permute-start.6 = (f32[4,64,128]{2,1,0:T(8,128)S(1)}, f32[4,64,128]{2,1,0:T(8,128)S(1)}, u32[]{:S(2)}, u32[]{:S(2)}) collective-permute-start(f32[4,64,128]{2,1,0:T(8,128)S(1)} %fusion.1), channel_id=1, source_target_pairs={{0,8},{4,12},{8,16},{12,20},{16,24},{20,28},{1,9},{5,13},{9,17},{1... | collective-permute-start | bytes 393224 | tf_op jit(solution)/shard_map/ppermute | solution.py:26
  55.8 14.2 %collective-permute-start.8 = (f32[8,128,128]{2,1,0:T(8,128)S(1)}, f32[8,128,128]{2,1,0:T(8,128)S(1)}, u32[]{:S(2)}, u32[]{:S(2)}) collective-permute-start(f32[8,128,128]{2,1,0:T(8,128)S(1)} %get-tuple-element.11), channel_id=1, source_target_pairs={{0,4},{4,8},{8,12},{12,16},{16,20},{20,24},{24,28},{1,5},{5,9},{9,... | collective-permute-start | bytes 1572872 | tf_op jit(solution)/shard_map/ppermute | solution.py:26
  57.8 12.3 %collective-permute-start.7 = (f32[8,64,128]{2,1,0:T(8,128)S(1)}, f32[8,64,128]{2,1,0:T(8,128)S(1)}, u32[]{:S(2)}, u32[]{:S(2)}) collective-permute-start(f32[8,64,128]{2,1,0:T(8,128)S(1)} %maximum_subtract_fusion), channel_id=1, source_target_pairs={{0,4},{4,8},{8,12},{12,16},{16,20},{20,24},{24,28},{1,5},{5,9},{9,... | collective-permute-start | bytes 786440 | tf_op jit(solution)/shard_map/ppermute | solution.py:26

commit v17 on v16

--- a/solution.py
+++ b/solution.py
@@ -237,7 +237,8 @@
     fine_ends = jnp.stack([result[0] for result in fine_results], axis=0)
     coarse_jump = jnp.stack([result[1] for result in fine_results], axis=0)
     correction = fine_ends - prolong(coarse_of_starts)
-    earlier_correction = passed_along(correction[-1], "tm", 1)
+    last_correction, coarse_jump = lax.optimization_barrier((correction[-1], coarse_jump))
+    earlier_correction = passed_along(last_correction, "tm", 1)
     tm_index = lax.axis_index("tm")
     tm_count = lax.axis_size("tm")
     first_coarse = restrict(starts[0])

time: 71.6 us -> 65 us (0.908)
  waiting for transfers between devices: 25.2 us -> 18.2 us
    ppermute x7, waiting for transfers between devices: 23.3 us -> 16.2 us  [passed_along(): return lax.ppermute(block, axis, route)]
  transfers between devices with their start and end apart: 9 -> 9, of which waited for: 7 -> 7; matrix products, arithmetic and copies ran while one was open for 14% -> 20% of each run, Pallas kernels for 0% -> 0%
where the time goes in v17:
time: 65 us; the launch traced here: 64.6 us
  starting transfers between devices  20.6 us (32%)
  waiting for transfers between devices  18.2 us (28%)
  matrix products  11.4 us (18%)
  Pallas kernels  9.01 us (14%)
  local copies, waits for them, and re-layouts  2.42 us (4%)
  other arithmetic  1.89 us (3%)
  between operations  1.06 us (2%)
    ppermute x7, waiting for transfers between devices, passed_along(): return lax.ppermute(block, axis, route)  16.2 us
    ppermute x7, starting transfers between devices, passed_along(): return lax.ppermute(block, axis, route)  14.8 us
    pallas_call x1, Pallas kernels, fine_propagate(): pl.pallas_call(functools.partial(fine_kernel, slice_at), out_shape=(jax.S...  6.93 us
    dot_general x7, matrix products, apply_coarse(): jnp.einsum('...tik,tlk->...til', mixed_x, matrix_y, precision=exact_preci...  4.79 us
    ppermute x1, starting transfers between devices, on_device(): from_prev = lax.ppermute(high_rows, 'space', forward)  3.48 us
    dot_general x7, matrix products, apply_coarse(): jnp.einsum('tij,...tjk->...tik', matrix_x, coarse_values, precision=exact...  2.58 us
    dot_general x2, matrix products, prefix_over_tm(): jnp.einsum('tij,tjk->tik', power_y, power_y, precision=exact_precision)  2.56 us
    ppermute x1, starting transfers between devices, on_device(): from_next = lax.ppermute(low_rows, 'space', backward)  2.37 us
  transfers between devices with their start and end apart: 9, of which 7 were waited for; matrix products, arithmetic and copies ran while one was open for 20% of the time, Pallas kernels for 0%

profile of v17, /device:TPU:12, one launch (start us, length us, event | category | flops | bytes accessed | tf_op | source)
XLA Modules:
  0.0 64.6 jit_solution(4196372837949975450)
XLA Ops:
  0.6 2.1 %shard_map.95 = (f32[5,8,16,128]{3,2,1,0:T(8,128)}, f32[5,8,16,128]{3,2,1,0:T(8,128)}) custom-call(f32[1,8,128,128]{3,2,1,0:T(8,128)} %starts_hbm.1, f32[8,128,128]{2,1,0:T(8,128)} %diffusivity_ref.1, f32[2,8,128,128]{3,2,1,0:T(8,128)} %velocity_ref.1, s32[8,128,128]{2,1,0:T(8,128)} %obstacle_ref.1), custom_call_target="tpu_custom_call" | custom-call | tf_op jit(solution)/shard_map/pallas_call | solution.py:186
  2.7 3.5 %collective-permute-start = (f32[5,8,16,128]{3,2,1,0:T(8,128)}, f32[5,8,16,128]{3,2,1,0:T(8,128)S(1)}, u32[]{:S(2)}, u32[]{:S(2)}) collective-permute-start(f32[5,8,16,128]{3,2,1,0:T(8,128)} %get-tuple-element.8), channel_id=1, source_target_pairs={{0,1},{1,2},{2,3},{4,5},{5,6},{6,7},{8,9},{9,10},{10,11},{12,13},{... | collective-permute-start | bytes 983048 | tf_op jit(solution)/shard_map/ppermute | solution.py:211
  6.2 2.4 %collective-permute-start.1 = (f32[5,8,16,128]{3,2,1,0:T(8,128)}, f32[5,8,16,128]{3,2,1,0:T(8,128)S(1)}, u32[]{:S(2)}, u32[]{:S(2)}) collective-permute-start(f32[5,8,16,128]{3,2,1,0:T(8,128)} %get-tuple-element.9), channel_id=1, source_target_pairs={{1,0},{2,1},{3,2},{5,4},{6,5},{7,6},{9,8},{10,9},{11,10},{13,12},{... | collective-permute-start | bytes 983048 | tf_op jit(solution)/shard_map/ppermute | solution.py:212
  9.3 1.0 %copy-done = f32[1,8,128,128]{3,2,1,0:T(8,128)S(1)} copy-done((f32[1,8,128,128]{3,2,1,0:T(8,128)S(1)}, f32[1,8,128,128]{3,2,1,0:T(8,128)}, u32[]{:S(2)}) %copy-start) | copy-done | bytes 524312
  10.2 1.0 %fusion.6 = f32[8,64,128]{2,1,0:T(8,128)S(1)} fusion(f32[8,64,128]{1,0,2:T(8,128)S(1)} %bitcast.60, f32[1,8,128,128]{3,2,1,0:T(8,128)S(1)} %copy-done), kind=kOutput, calls=%fused_computation.12 | convolution fusion | flops 100663296 | bytes 1048576 | tf_op jit(solution)/shard_map/tij,...tjk->...tik/dot_general | solution.py:38
  11.3 1.1 %fusion.28 = f32[8,64,64]{2,1,0:T(8,128)} fusion(f32[8,64,64]{2,1,0:T(8,128)S(1)} %fusion.26), kind=kOutput, calls=%fused_computation.47 | convolution fusion | flops 25165824 | bytes 262144 | tf_op jit(solution)/shard_map/tij,tjk->tik/dot_general | solution.py:255
  12.4 1.1 %fusion.25.coarse_ref = f32[8,64,128]{2,1,0:T(8,128)S(1)} fusion(f32[8,64,128]{2,1,0:T(8,128)S(1)} %fusion.6, f32[8,128,128]{2,1,0:T(8,128)S(1)} %copy-done.5), kind=kOutput, calls=%fused_computation.44 | convolution fusion | flops 100663296 | bytes 1048576 | tf_op jit(solution)/shard_map/...tik,tlk->...til/dot_general | solution.py:39
  13.6 1.9 %fusion.27 = f32[8,128,128]{2,1,0:T(8,128)S(1)} fusion(f32[8,128,128]{2,1,0:T(8,128)} %param.15), kind=kOutput, calls=%fused_computation.46 | convolution fusion | flops 201326592 | bytes 1048576 | tf_op jit(solution)/shard_map/tij,tjk->tik/dot_general | solution.py:256
  15.6 1.9 %collective-permute-done.1.next_ref = f32[5,8,16,128]{3,2,1,0:T(8,128)S(1)} collective-permute-done((f32[5,8,16,128]{3,2,1,0:T(8,128)}, f32[5,8,16,128]{3,2,1,0:T(8,128)S(1)}, u32[]{:S(2)}, u32[]{:S(2)}) %collective-permute-start.1) | collective-permute-done | bytes 327712 | tf_op jit(solution)/shard_map/ppermute | solution.py:212
  17.5 0.6 copy-done.4
  18.2 6.9 %shard_map.96 = (f32[8,128,128]{2,1,0:T(8,128)S(1)}, f32[8,64,128]{2,1,0:T(8,128)S(1)}) custom-call(s32[8]{0:T(128)S(1)} %get-tuple-element.18.south_ref, s32[8]{0:T(128)S(1)} %get-tuple-element.17.north_ref, s32[8]{0:T(128)S(1)} %get-tuple-element.19.west_at_ref, s32[8]{0:T(128)S(1)} %get-tuple-element.16.east_at_ref, s32[8]{0:T(128)S(1)} %get-tuple-element.15.west_ok_ref, ...), custom_call_target="tpu_custom_call" | custom-call | tf_op jit(solution)/shard_map/pallas_call | solution.py:137
  25.4 2.1 %collective-permute-start.2 = (f32[8,64,128]{2,1,0:T(8,128)S(1)}, f32[8,64,128]{2,1,0:T(8,128)S(1)}, u32[]{:S(2)}, u32[]{:S(2)}) collective-permute-start(f32[8,64,128]{2,1,0:T(8,128)S(1)} %bitcast_add_fusion), channel_id=1, source_target_pairs={{0,4},{4,8},{8,12},{12,16},{16,20},{20,24},{24,28},{1,5},{5,9},{9,... | collective-permute-start | bytes 786440 | tf_op jit(solution)/shard_map/ppermute | solution.py:26
  27.5 0.6 fusion.29
  28.1 3.6 %collective-permute-start.8 = (f32[8,128,128]{2,1,0:T(8,128)S(1)}, f32[8,128,128]{2,1,0:T(8,128)S(1)}, u32[]{:S(2)}, u32[]{:S(2)}) collective-permute-start(f32[8,128,128]{2,1,0:T(8,128)S(1)} %sub.47), channel_id=1, source_target_pairs={{0,4},{4,8},{8,12},{12,16},{16,20},{20,24},{24,28},{1,5},{5,9},{9,... | collective-permute-start | bytes 1572872 | tf_op jit(solution)/shard_map/ppermute | solution.py:26
  31.7 2.4 %collective-permute-done.2 = f32[8,64,128]{2,1,0:T(8,128)S(1)} collective-permute-done((f32[8,64,128]{2,1,0:T(8,128)S(1)}, f32[8,64,128]{2,1,0:T(8,128)S(1)}, u32[]{:S(2)}, u32[]{:S(2)}) %collective-permute-start.2) | collective-permute-done | bytes 262176 | tf_op jit(solution)/shard_map/ppermute | solution.py:26
  34.4 0.6 fusion.5
  35.0 2.5 %collective-permute-start.3 = (f32[4,64,128]{2,1,0:T(8,128)S(1)}, f32[4,64,128]{2,1,0:T(8,128)S(1)}, u32[]{:S(2)}, u32[]{:S(2)}) collective-permute-start(f32[4,64,128]{2,1,0:T(8,128)S(1)} %fusion.5), channel_id=1, source_target_pairs={{0,8},{4,12},{8,16},{12,20},{16,24},{20,28},{1,9},{5,13},{9,17},{1... | collective-permute-start | bytes 393224 | tf_op jit(solution)/shard_map/ppermute | solution.py:26
  37.8 0.6 fusion.2
  38.4 1.3 %collective-permute-start.5 = (f32[4,64,128]{2,1,0:T(8,128)S(1)}, f32[4,64,128]{2,1,0:T(8,128)S(1)}, u32[]{:S(2)}, u32[]{:S(2)}) collective-permute-start(f32[4,64,128]{2,1,0:T(8,128)S(1)} %fusion.2), channel_id=1, source_target_pairs={{0,16},{4,20},{8,24},{12,28},{1,17},{5,21},{9,25},{13,29},{2,18},{... | collective-permute-start | bytes 393224 | tf_op jit(solution)/shard_map/ppermute | solution.py:26
  39.7 3.1 %collective-permute-done.3 = f32[4,64,128]{2,1,0:T(8,128)S(1)} collective-permute-done((f32[4,64,128]{2,1,0:T(8,128)S(1)}, f32[4,64,128]{2,1,0:T(8,128)S(1)}, u32[]{:S(2)}, u32[]{:S(2)}) %collective-permute-start.3) | collective-permute-done | bytes 131104 | tf_op jit(solution)/shard_map/ppermute | solution.py:26
  43.1 0.6 fusion.4
  43.7 1.3 %collective-permute-start.4 = (f32[4,64,128]{2,1,0:T(8,128)S(1)}, f32[4,64,128]{2,1,0:T(8,128)S(1)}, u32[]{:S(2)}, u32[]{:S(2)}) collective-permute-start(f32[4,64,128]{2,1,0:T(8,128)S(1)} %fusion.4), channel_id=1, source_target_pairs={{0,16},{4,20},{8,24},{12,28},{1,17},{5,21},{9,25},{13,29},{2,18},{... | collective-permute-start | bytes 393224 | tf_op jit(solution)/shard_map/ppermute | solution.py:26
  45.6 0.6 fusion.1
  46.2 2.1 %collective-permute-start.6 = (f32[4,64,128]{2,1,0:T(8,128)S(1)}, f32[4,64,128]{2,1,0:T(8,128)S(1)}, u32[]{:S(2)}, u32[]{:S(2)}) collective-permute-start(f32[4,64,128]{2,1,0:T(8,128)S(1)} %fusion.1), channel_id=1, source_target_pairs={{0,8},{4,12},{8,16},{12,20},{16,24},{20,28},{1,9},{5,13},{9,17},{1... | collective-permute-start | bytes 393224 | tf_op jit(solution)/shard_map/ppermute | solution.py:26
  48.3 3.6 %collective-permute-done.4 = f32[4,64,128]{2,1,0:T(8,128)S(1)} collective-permute-done((f32[4,64,128]{2,1,0:T(8,128)S(1)}, f32[4,64,128]{2,1,0:T(8,128)S(1)}, u32[]{:S(2)}, u32[]{:S(2)}) %collective-permute-start.4) | collective-permute-done | bytes 131104 | tf_op jit(solution)/shard_map/ppermute | solution.py:26
  52.2 0.6 fusion.3
  52.8 1.2 %collective-permute-done.6 = f32[4,64,128]{2,1,0:T(8,128)S(1)} collective-permute-done((f32[4,64,128]{2,1,0:T(8,128)S(1)}, f32[4,64,128]{2,1,0:T(8,128)S(1)}, u32[]{:S(2)}, u32[]{:S(2)}) %collective-permute-start.6) | collective-permute-done | bytes 131104 | tf_op jit(solution)/shard_map/ppermute | solution.py:26
  54.3 0.6 fusion
  54.9 1.9 %collective-permute-start.7 = (f32[8,64,128]{2,1,0:T(8,128)S(1)}, f32[8,64,128]{2,1,0:T(8,128)S(1)}, u32[]{:S(2)}, u32[]{:S(2)}) collective-permute-start(f32[8,64,128]{2,1,0:T(8,128)S(1)} %maximum_subtract_fusion), channel_id=1, source_target_pairs={{0,4},{4,8},{8,12},{12,16},{16,20},{20,24},{24,28},{1,5},{5,9},{9,... | collective-permute-start | bytes 786440 | tf_op jit(solution)/shard_map/ppermute | solution.py:26
  57.0 0.9 %add_bitcast_fusion = f32[1,8,128,128]{3,2,1,0:T(8,128)} fusion(f32[8,128,128]{2,1,0:T(8,128)S(1)} %bitcast.59, f32[8,128,128]{2,1,0:T(8,128)S(1)} %sub.47), kind=kLoop, calls=%fused_computation.15 | loop fusion | flops 131072 | bytes 1572864 | tf_op jit(solution)/shard_map/add | solution.py:299
  57.9 5.6 %collective-permute-done.7 = f32[8,64,128]{2,1,0:T(8,128)S(1)} collective-permute-done((f32[8,64,128]{2,1,0:T(8,128)S(1)}, f32[8,64,128]{2,1,0:T(8,128)S(1)}, u32[]{:S(2)}, u32[]{:S(2)}) %collective-permute-start.7) | collective-permute-done | bytes 262176 | tf_op jit(solution)/shard_map/ppermute | solution.py:26
  63.7 0.9 %select_bitcast_fusion = f32[1,8,128,128]{3,2,1,0:T(8,128)} fusion(f32[8,128,128]{2,1,0:T(8,128)S(1)} %bitcast.57, f32[8,128,128]{2,1,0:T(8,128)S(1)} %collective-permute-done.8, pred[]{:T(512)S(6)} %eq.4, f32[1,8,128,128]{3,2,1,0:T(8,128)S(1)} %copy-done), kind=kLoop, calls=%fused_computation.14 | loop fusion | flops 393216 | bytes 2097153 | tf_op jit(solution)/shard_map/broadcast_in_dim | solution.py:304
  (41 shorter events, 3.2 us)
Async XLA Ops:
  0.6 8.0 %copy-start.7 = (f32[8,64,64]{2,1,0:T(8,128)S(1)}, f32[8,64,64]{2,1,0:T(8,128)}, u32[]{:S(2)}) copy-start(f32[8,64,64]{2,1,0:T(8,128)} %param.14) | copy-start | bytes 393220
  2.7 12.8 %collective-permute-start = (f32[5,8,16,128]{3,2,1,0:T(8,128)}, f32[5,8,16,128]{3,2,1,0:T(8,128)S(1)}, u32[]{:S(2)}, u32[]{:S(2)}) collective-permute-start(f32[5,8,16,128]{3,2,1,0:T(8,128)} %get-tuple-element.8), channel_id=1, source_target_pairs={{0,1},{1,2},{2,3},{4,5},{5,6},{6,7},{8,9},{9,10},{10,11},{12,13},{... | collective-permute-start | bytes 983048 | tf_op jit(solution)/shard_map/ppermute | solution.py:211
  6.2 11.3 %collective-permute-start.1 = (f32[5,8,16,128]{3,2,1,0:T(8,128)}, f32[5,8,16,128]{3,2,1,0:T(8,128)S(1)}, u32[]{:S(2)}, u32[]{:S(2)}) collective-permute-start(f32[5,8,16,128]{3,2,1,0:T(8,128)} %get-tuple-element.9), channel_id=1, source_target_pairs={{1,0},{2,1},{3,2},{5,4},{6,5},{7,6},{9,8},{10,9},{11,10},{13,12},{... | collective-permute-start | bytes 983048 | tf_op jit(solution)/shard_map/ppermute | solution.py:212
  9.2 1.0 %copy-start = (f32[1,8,128,128]{3,2,1,0:T(8,128)S(1)}, f32[1,8,128,128]{3,2,1,0:T(8,128)}, u32[]{:S(2)}) copy-start(f32[1,8,128,128]{3,2,1,0:T(8,128)} %starts_hbm.1) | copy-start | bytes 1572868
  11.3 1.1 %copy-start.5 = (f32[8,128,128]{2,1,0:T(8,128)S(1)}, f32[8,128,128]{2,1,0:T(8,128)}, u32[]{:S(2)}) copy-start(f32[8,128,128]{2,1,0:T(8,128)} %param.15) | copy-start | bytes 1572868
  12.4 1.1 %copy-start.10 = (s32[8,4]{0,1:T(4,128)S(1)}, s32[8,4]{0,1:T(4,128)}, u32[]{:S(2)}) copy-start(s32[8,4]{0,1:T(4,128)} %param.13) | copy-start | bytes 388
  12.4 5.1 %copy-start.3 = (s32[8,128,128]{2,1,0:T(8,128)S(1)}, s32[8,128,128]{2,1,0:T(8,128)}, u32[]{:S(2)}) copy-start(s32[8,128,128]{2,1,0:T(8,128)} %obstacle_ref.1) | copy-start | bytes 1572868
  13.5 4.0 %copy-start.1 = (f32[2,8,128,128]{3,2,1,0:T(8,128)S(1)}, f32[2,8,128,128]{3,2,1,0:T(8,128)}, u32[]{:S(2)}) copy-start(f32[2,8,128,128]{3,2,1,0:T(8,128)} %velocity_ref.1) | copy-start | bytes 3145732
  13.6 3.9 %copy-start.2 = (f32[8,128,128]{2,1,0:T(8,128)S(1)}, f32[8,128,128]{2,1,0:T(8,128)}, u32[]{:S(2)}) copy-start(f32[8,128,128]{2,1,0:T(8,128)} %diffusivity_ref.1) | copy-start | bytes 1572868
  17.5 0.7 %copy-start.4 = (f32[12]{0:T(128)S(1)}, f32[12]{0:T(128)}, u32[]{:S(2)}) copy-start(f32[12]{0:T(128)} %scale_ref.1) | copy-start | bytes 148
  25.4 8.7 %copy-start.8 = (f32[8,64,64]{2,1,0:T(8,128)S(1)}, f32[8,64,64]{2,1,0:T(8,128)}, u32[]{:S(2)}) copy-start(f32[8,64,64]{2,1,0:T(8,128)} %param.14) | copy-start | bytes 393220
  25.4 8.7 %collective-permute-start.2 = (f32[8,64,128]{2,1,0:T(8,128)S(1)}, f32[8,64,128]{2,1,0:T(8,128)S(1)}, u32[]{:S(2)}, u32[]{:S(2)}) collective-permute-start(f32[8,64,128]{2,1,0:T(8,128)S(1)} %bitcast_add_fusion), channel_id=1, source_target_pairs={{0,4},{4,8},{8,12},{12,16},{16,20},{20,24},{24,28},{1,5},{5,9},{9,... | collective-permute-start | bytes 786440 | tf_op jit(solution)/shard_map/ppermute | solution.py:26
  28.1 6.3 %copy-start.6 = (f32[8,128,128]{2,1,0:T(8,128)S(1)}, f32[8,128,128]{2,1,0:T(8,128)}, u32[]{:S(2)}) copy-start(f32[8,128,128]{2,1,0:T(8,128)} %param.15) | copy-start | bytes 1572868
  28.1 29.8 %collective-permute-start.8 = (f32[8,128,128]{2,1,0:T(8,128)S(1)}, f32[8,128,128]{2,1,0:T(8,128)S(1)}, u32[]{:S(2)}, u32[]{:S(2)}) collective-permute-start(f32[8,128,128]{2,1,0:T(8,128)S(1)} %sub.47), channel_id=1, source_target_pairs={{0,4},{4,8},{8,12},{12,16},{16,20},{20,24},{24,28},{1,5},{5,9},{9,... | collective-permute-start | bytes 1572872 | tf_op jit(solution)/shard_map/ppermute | solution.py:26
  35.0 7.8 %collective-permute-start.3 = (f32[4,64,128]{2,1,0:T(8,128)S(1)}, f32[4,64,128]{2,1,0:T(8,128)S(1)}, u32[]{:S(2)}, u32[]{:S(2)}) collective-permute-start(f32[4,64,128]{2,1,0:T(8,128)S(1)} %fusion.5), channel_id=1, source_target_pairs={{0,8},{4,12},{8,16},{12,20},{16,24},{20,28},{1,9},{5,13},{9,17},{1... | collective-permute-start | bytes 393224 | tf_op jit(solution)/shard_map/ppermute | solution.py:26
  38.4 6.9 %collective-permute-start.5 = (f32[4,64,128]{2,1,0:T(8,128)S(1)}, f32[4,64,128]{2,1,0:T(8,128)S(1)}, u32[]{:S(2)}, u32[]{:S(2)}) collective-permute-start(f32[4,64,128]{2,1,0:T(8,128)S(1)} %fusion.2), channel_id=1, source_target_pairs={{0,16},{4,20},{8,24},{12,28},{1,17},{5,21},{9,25},{13,29},{2,18},{... | collective-permute-start | bytes 393224 | tf_op jit(solution)/shard_map/ppermute | solution.py:26
  43.1 2.3 %copy-start.9 = (f32[8,64,64]{2,1,0:T(8,128)S(1)}, f32[8,64,64]{2,1,0:T(8,128)}, u32[]{:S(2)}) copy-start(f32[8,64,64]{2,1,0:T(8,128)} %fusion.28) | copy-start | bytes 393220
  43.7 8.3 %collective-permute-start.4 = (f32[4,64,128]{2,1,0:T(8,128)S(1)}, f32[4,64,128]{2,1,0:T(8,128)S(1)}, u32[]{:S(2)}, u32[]{:S(2)}) collective-permute-start(f32[4,64,128]{2,1,0:T(8,128)S(1)} %fusion.4), channel_id=1, source_target_pairs={{0,16},{4,20},{8,24},{12,28},{1,17},{5,21},{9,25},{13,29},{2,18},{... | collective-permute-start | bytes 393224 | tf_op jit(solution)/shard_map/ppermute | solution.py:26
  46.2 7.8 %collective-permute-start.6 = (f32[4,64,128]{2,1,0:T(8,128)S(1)}, f32[4,64,128]{2,1,0:T(8,128)S(1)}, u32[]{:S(2)}, u32[]{:S(2)}) collective-permute-start(f32[4,64,128]{2,1,0:T(8,128)S(1)} %fusion.1), channel_id=1, source_target_pairs={{0,8},{4,12},{8,16},{12,20},{16,24},{20,28},{1,9},{5,13},{9,17},{1... | collective-permute-start | bytes 393224 | tf_op jit(solution)/shard_map/ppermute | solution.py:26
  54.9 8.6 %collective-permute-start.7 = (f32[8,64,128]{2,1,0:T(8,128)S(1)}, f32[8,64,128]{2,1,0:T(8,128)S(1)}, u32[]{:S(2)}, u32[]{:S(2)}) collective-permute-start(f32[8,64,128]{2,1,0:T(8,128)S(1)} %maximum_subtract_fusion), channel_id=1, source_target_pairs={{0,4},{4,8},{8,12},{12,16},{16,20},{20,24},{24,28},{1,5},{5,9},{9,... | collective-permute-start | bytes 786440 | tf_op jit(solution)/shard_map/ppermute | solution.py:26

commit v18 on v17

--- a/solution.py
+++ b/solution.py
@@ -254,17 +254,15 @@
             powers[distance] = (power_x, power_y)
             power_x = jnp.einsum("tij,tjk->tik", power_x, power_x, precision=exact_precision)
             power_y = jnp.einsum("tij,tjk->tik", power_y, power_y, precision=exact_precision)
-        half = total.shape[0] // 2
-        parts = [(slice(0, half), distances[:1] + distances[1:]),
-                 (slice(half, None), distances[:1] + distances[1:][::-1])]
+        parts = [(slice(0, None), distances)]
         values = [total[part] for part, _ in parts]
         for step in range(len(distances)):
             if step == 0:
                 received = passed_along(total, "tm", distances[0])
                 received = [received[part] for part, _ in parts]
             else:
-                received = [passed_along(values[k], "tm", parts[k][1][step]) for k in range(2)]
-            for k in range(2):
+                received = [passed_along(values[k], "tm", parts[k][1][step]) for k in range(len(parts))]
+            for k in range(len(parts)):
                 part, order = parts[k]
                 distance = order[step]
                 mixed = apply_coarse(received[k], powers[distance][0][part], powers[distance][1][part])

time: 65 us -> 71.7 us (1.10)
  waiting for transfers between devices: 18.2 us -> 33 us
  starting transfers between devices: 20.6 us -> 15.4 us
  matrix products: 11.4 us -> 8.67 us
    ppermute x7 -> x5, waiting for transfers between devices: 16.2 us -> 27.6 us  [passed_along(): return lax.ppermute(block, axis, route)]
    ppermute x7 -> x5, starting transfers between devices: 14.8 us -> 9.56 us  [passed_along(): return lax.ppermute(block, axis, route)]
    ppermute x1, waiting for transfers between devices: 0.01 us -> 2.17 us  [on_device(): from_prev = lax.ppermute(high_rows, 'space', forward)]
    dot_general x2, matrix products: 2.56 us -> 1.24 us  [prefix_over_tm(): jnp.einsum('tij,tjk->tik', power_y, power_y, precision=exact_precision)]
    ppermute x1, waiting for transfers between devices: 1.93 us -> 3.21 us  [on_device(): from_next = lax.ppermute(low_rows, 'space', backward)]
    dot_general x7 -> x4, matrix products: 2.58 us -> 2.19 us  [apply_coarse(): jnp.einsum('tij,...tjk->...tik', matrix_x, coarse_values, precision=exact...]
    dot_general x7 -> x4, matrix products: 4.79 us -> 4.47 us  [apply_coarse(): jnp.einsum('...tik,tlk->...til', mixed_x, matrix_y, precision=exact_preci...]
    unnamed x22 -> x16, local copies, waits for them, and re-layouts: 1.69 us -> 1.67 us
  transfers between devices with their start and end apart: 9 -> 7, of which waited for: 7 -> 6; matrix products, arithmetic and copies ran while one was open for 20% -> 10% of each run, Pallas kernels for 0% -> 0%
where the time goes in v18:
time: 71.7 us; the launch traced here: 71.3 us
  waiting for transfers between devices  33 us (46%)
  starting transfers between devices  15.4 us (21%)
  Pallas kernels  9.01 us (13%)
  matrix products  8.67 us (12%)
  local copies, waits for them, and re-layouts  2.4 us (3%)
  other arithmetic  1.87 us (3%)
  between operations  0.96 us (1%)
    ppermute x5, waiting for transfers between devices, passed_along(): return lax.ppermute(block, axis, route)  27.6 us
    ppermute x5, starting transfers between devices, passed_along(): return lax.ppermute(block, axis, route)  9.56 us
    pallas_call x1, Pallas kernels, fine_propagate(): pl.pallas_call(functools.partial(fine_kernel, slice_at), out_shape=(jax.S...  6.89 us
    dot_general x4, matrix products, apply_coarse(): jnp.einsum('...tik,tlk->...til', mixed_x, matrix_y, precision=exact_preci...  4.47 us
    ppermute x1, starting transfers between devices, on_device(): from_prev = lax.ppermute(high_rows, 'space', forward)  3.48 us
    ppermute x1, waiting for transfers between devices, on_device(): from_next = lax.ppermute(low_rows, 'space', backward)  3.21 us
    ppermute x1, starting transfers between devices, on_device(): from_next = lax.ppermute(low_rows, 'space', backward)  2.37 us
    dot_general x4, matrix products, apply_coarse(): jnp.einsum('tij,...tjk->...tik', matrix_x, coarse_values, precision=exact...  2.19 us
  transfers between devices with their start and end apart: 7, of which 6 were waited for; matrix products, arithmetic and copies ran while one was open for 10% of the time, Pallas kernels for 0%

profile of v18, /device:TPU:12, one launch (start us, length us, event | category | flops | bytes accessed | tf_op | source)
XLA Modules:
  0.0 71.3 jit_solution(10701060260219404912)
XLA Ops:
  0.7 2.1 %shard_map.95 = (f32[5,8,16,128]{3,2,1,0:T(8,128)}, f32[5,8,16,128]{3,2,1,0:T(8,128)}) custom-call(f32[1,8,128,128]{3,2,1,0:T(8,128)} %starts_hbm.1, f32[8,128,128]{2,1,0:T(8,128)} %diffusivity_ref.1, f32[2,8,128,128]{3,2,1,0:T(8,128)} %velocity_ref.1, s32[8,128,128]{2,1,0:T(8,128)} %obstacle_ref.1), custom_call_target="tpu_custom_call" | custom-call | tf_op jit(solution)/shard_map/pallas_call | solution.py:186
  2.8 3.5 %collective-permute-start = (f32[5,8,16,128]{3,2,1,0:T(8,128)}, f32[5,8,16,128]{3,2,1,0:T(8,128)S(1)}, u32[]{:S(2)}, u32[]{:S(2)}) collective-permute-start(f32[5,8,16,128]{3,2,1,0:T(8,128)} %get-tuple-element.8), channel_id=1, source_target_pairs={{0,1},{1,2},{2,3},{4,5},{5,6},{6,7},{8,9},{9,10},{10,11},{12,13},{... | collective-permute-start | bytes 983048 | tf_op jit(solution)/shard_map/ppermute | solution.py:211
  6.3 2.4 %collective-permute-start.1 = (f32[5,8,16,128]{3,2,1,0:T(8,128)}, f32[5,8,16,128]{3,2,1,0:T(8,128)S(1)}, u32[]{:S(2)}, u32[]{:S(2)}) collective-permute-start(f32[5,8,16,128]{3,2,1,0:T(8,128)} %get-tuple-element.9), channel_id=1, source_target_pairs={{1,0},{2,1},{3,2},{5,4},{6,5},{7,6},{9,8},{10,9},{11,10},{13,12},{... | collective-permute-start | bytes 983048 | tf_op jit(solution)/shard_map/ppermute | solution.py:212
  8.9 1.0 %copy-done.1 = f32[1,8,128,128]{3,2,1,0:T(8,128)S(1)} copy-done((f32[1,8,128,128]{3,2,1,0:T(8,128)S(1)}, f32[1,8,128,128]{3,2,1,0:T(8,128)}, u32[]{:S(2)}) %copy-start.1) | copy-done | bytes 524312
  9.9 1.0 %fusion.4 = f32[8,64,128]{2,1,0:T(8,128)S(1)} fusion(f32[8,64,128]{1,0,2:T(8,128)S(1)} %bitcast.56, f32[1,8,128,128]{3,2,1,0:T(8,128)S(1)} %copy-done.1), kind=kOutput, calls=%fused_computation.7 | convolution fusion | flops 100663296 | bytes 1048576 | tf_op jit(solution)/shard_map/tij,...tjk->...tik/dot_general | solution.py:38
  11.0 1.1 %fusion.13.coarse_ref = f32[8,64,128]{2,1,0:T(8,128)S(1)} fusion(f32[8,64,128]{2,1,0:T(8,128)S(1)} %fusion.4, f32[8,128,128]{2,1,0:T(8,128)S(1)} %copy-done), kind=kOutput, calls=%fused_computation.28 | convolution fusion | flops 100663296 | bytes 1048576 | tf_op jit(solution)/shard_map/...tik,tlk->...til/dot_general | solution.py:39
  12.2 2.2 %collective-permute-done.prev_ref = f32[5,8,16,128]{3,2,1,0:T(8,128)S(1)} collective-permute-done((f32[5,8,16,128]{3,2,1,0:T(8,128)}, f32[5,8,16,128]{3,2,1,0:T(8,128)S(1)}, u32[]{:S(2)}, u32[]{:S(2)}) %collective-permute-start) | collective-permute-done | bytes 327712 | tf_op jit(solution)/shard_map/ppermute | solution.py:211
  14.3 3.2 %collective-permute-done.1.next_ref = f32[5,8,16,128]{3,2,1,0:T(8,128)S(1)} collective-permute-done((f32[5,8,16,128]{3,2,1,0:T(8,128)}, f32[5,8,16,128]{3,2,1,0:T(8,128)S(1)}, u32[]{:S(2)}, u32[]{:S(2)}) %collective-permute-start.1) | collective-permute-done | bytes 327712 | tf_op jit(solution)/shard_map/ppermute | solution.py:212
  17.6 0.6 copy-done.5
  18.2 6.9 %shard_map.96 = (f32[8,128,128]{2,1,0:T(8,128)S(1)}, f32[8,64,128]{2,1,0:T(8,128)S(1)}) custom-call(s32[8]{0:T(128)S(1)} %get-tuple-element.18.south_ref, s32[8]{0:T(128)S(1)} %get-tuple-element.17.north_ref, s32[8]{0:T(128)S(1)} %get-tuple-element.19.west_at_ref, s32[8]{0:T(128)S(1)} %get-tuple-element.16.east_at_ref, s32[8]{0:T(128)S(1)} %get-tuple-element.15.west_ok_ref, ...), custom_call_target="tpu_custom_call" | custom-call | tf_op jit(solution)/shard_map/pallas_call | solution.py:137
  25.1 0.2 broadcast_in_dim.37
  25.4 1.9 %collective-permute-start.2 = (f32[8,64,128]{2,1,0:T(8,128)S(1)}, f32[8,64,128]{2,1,0:T(8,128)S(1)}, u32[]{:S(2)}, u32[]{:S(2)}) collective-permute-start(f32[8,64,128]{2,1,0:T(8,128)S(1)} %bitcast_add_fusion), channel_id=1, source_target_pairs={{0,4},{4,8},{8,12},{12,16},{16,20},{20,24},{24,28},{1,5},{5,9},{9,... | collective-permute-start | bytes 786440 | tf_op jit(solution)/shard_map/ppermute | solution.py:26
  27.3 0.4 fusion.15
  27.7 0.4 fusion.18
  28.1 5.9 %collective-permute-done.2 = f32[8,64,128]{2,1,0:T(8,128)S(1)} collective-permute-done((f32[8,64,128]{2,1,0:T(8,128)S(1)}, f32[8,64,128]{2,1,0:T(8,128)S(1)}, u32[]{:S(2)}, u32[]{:S(2)}) %collective-permute-start.2) | collective-permute-done | bytes 262176 | tf_op jit(solution)/shard_map/ppermute | solution.py:26
  34.0 0.4 fusion.14
  34.4 1.1 %fusion = f32[8,64,128]{2,1,0:T(8,128)S(1)} fusion(f32[8,64,128]{2,1,0:T(8,128)S(1)} %bitcast_add_fusion, f32[8,128,64]{1,2,0:T(8,128)S(1)} %fusion.14, f32[8,128,128]{2,1,0:T(8,128)S(1)} %copy-done, pred[]{:T(512)S(6)} %ge.9), kind=kOutput, calls=%fused_computation.3 | convolution fusion | flops 100794368 | bytes 1310721 | tf_op jit(solution)/shard_map/...tik,tlk->...til/dot_general | solution.py:39
  35.5 2.5 %collective-permute-start.3 = (f32[8,64,128]{2,1,0:T(8,128)S(1)}, f32[8,64,128]{2,1,0:T(8,128)S(1)}, u32[]{:S(2)}, u32[]{:S(2)}) collective-permute-start(f32[8,64,128]{2,1,0:T(8,128)S(1)} %fusion), channel_id=1, source_target_pairs={{0,8},{4,12},{8,16},{12,20},{16,24},{20,28},{1,9},{5,13},{9,17},{1... | collective-permute-start | bytes 786440 | tf_op jit(solution)/shard_map/ppermute | solution.py:26
  38.0 0.6 fusion.17
  38.6 6.1 %collective-permute-done.3 = f32[8,64,128]{2,1,0:T(8,128)S(1)} collective-permute-done((f32[8,64,128]{2,1,0:T(8,128)S(1)}, f32[8,64,128]{2,1,0:T(8,128)S(1)}, u32[]{:S(2)}, u32[]{:S(2)}) %collective-permute-start.3) | collective-permute-done | bytes 262176 | tf_op jit(solution)/shard_map/ppermute | solution.py:26
  44.7 0.4 fusion.16
  45.1 1.1 %fusion.1 = f32[8,64,128]{2,1,0:T(8,128)S(1)} fusion(f32[8,64,128]{2,1,0:T(8,128)S(1)} %fusion, f32[8,64,128]{2,1,0:T(8,128)S(1)} %fusion.16, f32[8,128,128]{2,1,0:T(8,128)S(1)} %fusion.17, pred[]{:T(512)S(6)} %ge.10), kind=kOutput, calls=%fused_computation.4 | convolution fusion | flops 100794368 | bytes 1310721 | tf_op jit(solution)/shard_map/...tik,tlk->...til/dot_general | solution.py:39
  46.2 1.3 %collective-permute-start.4 = (f32[8,64,128]{2,1,0:T(8,128)S(1)}, f32[8,64,128]{2,1,0:T(8,128)S(1)}, u32[]{:S(2)}, u32[]{:S(2)}) collective-permute-start(f32[8,64,128]{2,1,0:T(8,128)S(1)} %fusion.1), channel_id=1, source_target_pairs={{0,16},{4,20},{8,24},{12,28},{1,17},{5,21},{9,25},{13,29},{2,18},{... | collective-permute-start | bytes 786440 | tf_op jit(solution)/shard_map/ppermute | solution.py:26
  47.5 0.6 fusion.20
  48.2 1.9 %collective-permute-start.6 = (f32[8,128,128]{2,1,0:T(8,128)S(1)}, f32[8,128,128]{2,1,0:T(8,128)S(1)}, u32[]{:S(2)}, u32[]{:S(2)}) collective-permute-start(f32[8,128,128]{2,1,0:T(8,128)S(1)} %sub.47), channel_id=1, source_target_pairs={{0,4},{4,8},{8,12},{12,16},{16,20},{20,24},{24,28},{1,5},{5,9},{9,... | collective-permute-start | bytes 1572872 | tf_op jit(solution)/shard_map/ppermute | solution.py:26
  50.1 10.0 %collective-permute-done.4 = f32[8,64,128]{2,1,0:T(8,128)S(1)} collective-permute-done((f32[8,64,128]{2,1,0:T(8,128)S(1)}, f32[8,64,128]{2,1,0:T(8,128)S(1)}, u32[]{:S(2)}, u32[]{:S(2)}) %collective-permute-start.4) | collective-permute-done | bytes 262176 | tf_op jit(solution)/shard_map/ppermute | solution.py:26
  60.1 0.4 fusion.19
  60.5 1.1 %fusion.3 = f32[8,64,128]{2,1,0:T(8,128)S(1)} fusion(f32[8,64,128]{2,1,0:T(8,128)S(1)} %fusion.1, f32[8,64,128]{2,1,0:T(8,128)S(1)} %fusion.19, f32[8,128,128]{2,1,0:T(8,128)S(1)} %fusion.20, f32[1,8,64,128]{3,2,1,0:T(8,128)S(1)} %bitcast.52, pred[]{:T(512)S(6)} %ge.11), kind=kOutput, calls=%fused_computation.6 | convolution fusion | flops 100859904 | bytes 1572865 | tf_op jit(solution)/shard_map/...tik,tlk->...til/dot_general | solution.py:39
  61.7 1.9 %collective-permute-start.5 = (f32[8,64,128]{2,1,0:T(8,128)S(1)}, f32[8,64,128]{2,1,0:T(8,128)S(1)}, u32[]{:S(2)}, u32[]{:S(2)}) collective-permute-start(f32[8,64,128]{2,1,0:T(8,128)S(1)} %fusion.3), channel_id=1, source_target_pairs={{0,4},{4,8},{8,12},{12,16},{16,20},{20,24},{24,28},{1,5},{5,9},{9,... | collective-permute-start | bytes 786440 | tf_op jit(solution)/shard_map/ppermute | solution.py:26
  63.8 0.9 %add_bitcast_fusion = f32[1,8,128,128]{3,2,1,0:T(8,128)} fusion(f32[8,128,128]{2,1,0:T(8,128)S(1)} %bitcast.55, f32[8,128,128]{2,1,0:T(8,128)S(1)} %sub.47), kind=kLoop, calls=%fused_computation.10 | loop fusion | flops 131072 | bytes 1572864 | tf_op jit(solution)/shard_map/add | solution.py:297
  64.6 5.6 %collective-permute-done.5 = f32[8,64,128]{2,1,0:T(8,128)S(1)} collective-permute-done((f32[8,64,128]{2,1,0:T(8,128)S(1)}, f32[8,64,128]{2,1,0:T(8,128)S(1)}, u32[]{:S(2)}, u32[]{:S(2)}) %collective-permute-start.5) | collective-permute-done | bytes 262176 | tf_op jit(solution)/shard_map/ppermute | solution.py:26
  70.4 0.9 %select_bitcast_fusion = f32[1,8,128,128]{3,2,1,0:T(8,128)} fusion(f32[8,128,128]{2,1,0:T(8,128)S(1)} %bitcast.53, f32[8,128,128]{2,1,0:T(8,128)S(1)} %collective-permute-done.6, pred[]{:T(512)S(6)} %eq.4, f32[1,8,128,128]{3,2,1,0:T(8,128)S(1)} %copy-done.1), kind=kLoop, calls=%fused_computation.9 | loop fusion | flops 393216 | bytes 2097153 | tf_op jit(solution)/shard_map/broadcast_in_dim | solution.py:302
  (24 shorter events, 0.7 us)
Async XLA Ops:
  0.6 10.4 %copy-start = (f32[8,128,128]{2,1,0:T(8,128)S(1)}, f32[8,128,128]{2,1,0:T(8,128)}, u32[]{:S(2)}) copy-start(f32[8,128,128]{2,1,0:T(8,128)} %param.15) | copy-start | bytes 1572868
  0.6 8.0 %copy-start.6 = (f32[8,64,64]{2,1,0:T(8,128)S(1)}, f32[8,64,64]{2,1,0:T(8,128)}, u32[]{:S(2)}) copy-start(f32[8,64,64]{2,1,0:T(8,128)} %param.14) | copy-start | bytes 393220
  2.8 11.6 %collective-permute-start = (f32[5,8,16,128]{3,2,1,0:T(8,128)}, f32[5,8,16,128]{3,2,1,0:T(8,128)S(1)}, u32[]{:S(2)}, u32[]{:S(2)}) collective-permute-start(f32[5,8,16,128]{3,2,1,0:T(8,128)} %get-tuple-element.8), channel_id=1, source_target_pairs={{0,1},{1,2},{2,3},{4,5},{5,6},{6,7},{8,9},{9,10},{10,11},{12,13},{... | collective-permute-start | bytes 983048 | tf_op jit(solution)/shard_map/ppermute | solution.py:211
  6.3 11.3 %collective-permute-start.1 = (f32[5,8,16,128]{3,2,1,0:T(8,128)}, f32[5,8,16,128]{3,2,1,0:T(8,128)S(1)}, u32[]{:S(2)}, u32[]{:S(2)}) collective-permute-start(f32[5,8,16,128]{3,2,1,0:T(8,128)} %get-tuple-element.9), channel_id=1, source_target_pairs={{1,0},{2,1},{3,2},{5,4},{6,5},{7,6},{9,8},{10,9},{11,10},{13,12},{... | collective-permute-start | bytes 983048 | tf_op jit(solution)/shard_map/ppermute | solution.py:212
  8.8 1.0 %copy-start.1 = (f32[1,8,128,128]{3,2,1,0:T(8,128)S(1)}, f32[1,8,128,128]{3,2,1,0:T(8,128)}, u32[]{:S(2)}) copy-start(f32[1,8,128,128]{3,2,1,0:T(8,128)} %starts_hbm.1) | copy-start | bytes 1572868
  9.9 1.1 %copy-start.7 = (s32[8,4]{0,1:T(4,128)S(1)}, s32[8,4]{0,1:T(4,128)}, u32[]{:S(2)}) copy-start(s32[8,4]{0,1:T(4,128)} %param.13) | copy-start | bytes 388
  9.9 7.7 %copy-start.2 = (f32[2,8,128,128]{3,2,1,0:T(8,128)S(1)}, f32[2,8,128,128]{3,2,1,0:T(8,128)}, u32[]{:S(2)}) copy-start(f32[2,8,128,128]{3,2,1,0:T(8,128)} %velocity_ref.1) | copy-start | bytes 3145732
  11.0 6.5 %copy-start.3 = (f32[8,128,128]{2,1,0:T(8,128)S(1)}, f32[8,128,128]{2,1,0:T(8,128)}, u32[]{:S(2)}) copy-start(f32[8,128,128]{2,1,0:T(8,128)} %diffusivity_ref.1) | copy-start | bytes 1572868
  11.0 6.5 %copy-start.4 = (s32[8,128,128]{2,1,0:T(8,128)S(1)}, s32[8,128,128]{2,1,0:T(8,128)}, u32[]{:S(2)}) copy-start(s32[8,128,128]{2,1,0:T(8,128)} %obstacle_ref.1) | copy-start | bytes 1572868
  17.5 0.7 copy-start.5
  25.4 8.6 %collective-permute-start.2 = (f32[8,64,128]{2,1,0:T(8,128)S(1)}, f32[8,64,128]{2,1,0:T(8,128)S(1)}, u32[]{:S(2)}, u32[]{:S(2)}) collective-permute-start(f32[8,64,128]{2,1,0:T(8,128)S(1)} %bitcast_add_fusion), channel_id=1, source_target_pairs={{0,4},{4,8},{8,12},{12,16},{16,20},{20,24},{24,28},{1,5},{5,9},{9,... | collective-permute-start | bytes 786440 | tf_op jit(solution)/shard_map/ppermute | solution.py:26
  35.5 9.2 %collective-permute-start.3 = (f32[8,64,128]{2,1,0:T(8,128)S(1)}, f32[8,64,128]{2,1,0:T(8,128)S(1)}, u32[]{:S(2)}, u32[]{:S(2)}) collective-permute-start(f32[8,64,128]{2,1,0:T(8,128)S(1)} %fusion), channel_id=1, source_target_pairs={{0,8},{4,12},{8,16},{12,20},{16,24},{20,28},{1,9},{5,13},{9,17},{1... | collective-permute-start | bytes 786440 | tf_op jit(solution)/shard_map/ppermute | solution.py:26
  46.2 13.9 %collective-permute-start.4 = (f32[8,64,128]{2,1,0:T(8,128)S(1)}, f32[8,64,128]{2,1,0:T(8,128)S(1)}, u32[]{:S(2)}, u32[]{:S(2)}) collective-permute-start(f32[8,64,128]{2,1,0:T(8,128)S(1)} %fusion.1), channel_id=1, source_target_pairs={{0,16},{4,20},{8,24},{12,28},{1,17},{5,21},{9,25},{13,29},{2,18},{... | collective-permute-start | bytes 786440 | tf_op jit(solution)/shard_map/ppermute | solution.py:26
  48.2 16.5 %collective-permute-start.6 = (f32[8,128,128]{2,1,0:T(8,128)S(1)}, f32[8,128,128]{2,1,0:T(8,128)S(1)}, u32[]{:S(2)}, u32[]{:S(2)}) collective-permute-start(f32[8,128,128]{2,1,0:T(8,128)S(1)} %sub.47), channel_id=1, source_target_pairs={{0,4},{4,8},{8,12},{12,16},{16,20},{20,24},{24,28},{1,5},{5,9},{9,... | collective-permute-start | bytes 1572872 | tf_op jit(solution)/shard_map/ppermute | solution.py:26
  61.7 8.6 %collective-permute-start.5 = (f32[8,64,128]{2,1,0:T(8,128)S(1)}, f32[8,64,128]{2,1,0:T(8,128)S(1)}, u32[]{:S(2)}, u32[]{:S(2)}) collective-permute-start(f32[8,64,128]{2,1,0:T(8,128)S(1)} %fusion.3), channel_id=1, source_target_pairs={{0,4},{4,8},{8,12},{12,16},{16,20},{20,24},{24,28},{1,5},{5,9},{9,... | collective-permute-start | bytes 786440 | tf_op jit(solution)/shard_map/ppermute | solution.py:26

commit v19 on v17

--- a/solution.py
+++ b/solution.py
@@ -255,15 +255,11 @@
             power_x = jnp.einsum("tij,tjk->tik", power_x, power_x, precision=exact_precision)
             power_y = jnp.einsum("tij,tjk->tik", power_y, power_y, precision=exact_precision)
         half = total.shape[0] // 2
-        parts = [(slice(0, half), distances[:1] + distances[1:]),
-                 (slice(half, None), distances[:1] + distances[1:][::-1])]
+        parts = [(slice(0, half), distances),
+                 (slice(half, None), distances[1:] + distances[:1])]
         values = [total[part] for part, _ in parts]
         for step in range(len(distances)):
-            if step == 0:
-                received = passed_along(total, "tm", distances[0])
-                received = [received[part] for part, _ in parts]
-            else:
-                received = [passed_along(values[k], "tm", parts[k][1][step]) for k in range(2)]
+            received = [passed_along(values[k], "tm", parts[k][1][step]) for k in range(2)]
             for k in range(2):
                 part, order = parts[k]
                 distance = order[step]

time: 65 us -> 67.4 us (1.037)
  waiting for transfers between devices: 18.2 us -> 19.3 us
  starting transfers between devices: 20.6 us -> 21.7 us
    ppermute x7 -> x8, waiting for transfers between devices: 16.2 us -> 17.7 us  [passed_along(): return lax.ppermute(block, axis, route)]
    ppermute x7 -> x8, starting transfers between devices: 14.8 us -> 15.9 us  [passed_along(): return lax.ppermute(block, axis, route)]
    dot_general x2, matrix products: 2.56 us -> 3.37 us  [prefix_over_tm(): jnp.einsum('tij,tjk->tik', power_y, power_y, precision=exact_precision)]
    dot_general x2, matrix products: 1.47 us -> 0.77 us  [prefix_over_tm(): jnp.einsum('tij,tjk->tik', power_x, power_x, precision=exact_precision)]
  transfers between devices with their start and end apart: 9 -> 10, of which waited for: 7 -> 7; matrix products, arithmetic and copies ran while one was open for 20% -> 19% of each run, Pallas kernels for 0% -> 0%
where the time goes in v19:
time: 67.4 us; the launch traced here: 66.9 us
  starting transfers between devices  21.7 us (32%)
  waiting for transfers between devices  19.3 us (29%)
  matrix products  11.5 us (17%)
  Pallas kernels  8.98 us (13%)
  local copies, waits for them, and re-layouts  2.44 us (4%)
  other arithmetic  1.89 us (3%)
  between operations  1.1 us (2%)
    ppermute x8, waiting for transfers between devices, passed_along(): return lax.ppermute(block, axis, route)  17.7 us
    ppermute x8, starting transfers between devices, passed_along(): return lax.ppermute(block, axis, route)  15.9 us
    pallas_call x1, Pallas kernels, fine_propagate(): pl.pallas_call(functools.partial(fine_kernel, slice_at), out_shape=(jax.S...  6.9 us
    dot_general x7, matrix products, apply_coarse(): jnp.einsum('...tik,tlk->...til', mixed_x, matrix_y, precision=exact_preci...  4.79 us
    ppermute x1, starting transfers between devices, on_device(): from_prev = lax.ppermute(high_rows, 'space', forward)  3.48 us
    dot_general x2, matrix products, prefix_over_tm(): jnp.einsum('tij,tjk->tik', power_y, power_y, precision=exact_precision)  3.37 us
    dot_general x7, matrix products, apply_coarse(): jnp.einsum('tij,...tjk->...tik', matrix_x, coarse_values, precision=exact...  2.58 us
    ppermute x1, starting transfers between devices, on_device(): from_next = lax.ppermute(low_rows, 'space', backward)  2.37 us
  transfers between devices with their start and end apart: 10, of which 7 were waited for; matrix products, arithmetic and copies ran while one was open for 19% of the time, Pallas kernels for 0%

profile of v19, /device:TPU:12, one launch (start us, length us, event | category | flops | bytes accessed | tf_op | source)
XLA Modules:
  0.0 66.9 jit_solution(15544440386612986560)
XLA Ops:
  0.6 2.1 %shard_map.95 = (f32[5,8,16,128]{3,2,1,0:T(8,128)}, f32[5,8,16,128]{3,2,1,0:T(8,128)}) custom-call(f32[1,8,128,128]{3,2,1,0:T(8,128)} %starts_hbm.1, f32[8,128,128]{2,1,0:T(8,128)} %diffusivity_ref.1, f32[2,8,128,128]{3,2,1,0:T(8,128)} %velocity_ref.1, s32[8,128,128]{2,1,0:T(8,128)} %obstacle_ref.1), custom_call_target="tpu_custom_call" | custom-call | tf_op jit(solution)/shard_map/pallas_call | solution.py:186
  2.7 3.5 %collective-permute-start = (f32[5,8,16,128]{3,2,1,0:T(8,128)}, f32[5,8,16,128]{3,2,1,0:T(8,128)S(1)}, u32[]{:S(2)}, u32[]{:S(2)}) collective-permute-start(f32[5,8,16,128]{3,2,1,0:T(8,128)} %get-tuple-element.8), channel_id=1, source_target_pairs={{0,1},{1,2},{2,3},{4,5},{5,6},{6,7},{8,9},{9,10},{10,11},{12,13},{... | collective-permute-start | bytes 983048 | tf_op jit(solution)/shard_map/ppermute | solution.py:211
  6.2 2.4 %collective-permute-start.1 = (f32[5,8,16,128]{3,2,1,0:T(8,128)}, f32[5,8,16,128]{3,2,1,0:T(8,128)S(1)}, u32[]{:S(2)}, u32[]{:S(2)}) collective-permute-start(f32[5,8,16,128]{3,2,1,0:T(8,128)} %get-tuple-element.9), channel_id=1, source_target_pairs={{1,0},{2,1},{3,2},{5,4},{6,5},{7,6},{9,8},{10,9},{11,10},{13,12},{... | collective-permute-start | bytes 983048 | tf_op jit(solution)/shard_map/ppermute | solution.py:212
  9.2 1.0 %copy-done = f32[1,8,128,128]{3,2,1,0:T(8,128)S(1)} copy-done((f32[1,8,128,128]{3,2,1,0:T(8,128)S(1)}, f32[1,8,128,128]{3,2,1,0:T(8,128)}, u32[]{:S(2)}) %copy-start) | copy-done | bytes 524312
  10.2 1.0 %fusion.6 = f32[8,64,128]{2,1,0:T(8,128)S(1)} fusion(f32[8,64,128]{1,0,2:T(8,128)S(1)} %bitcast.60, f32[1,8,128,128]{3,2,1,0:T(8,128)S(1)} %copy-done), kind=kOutput, calls=%fused_computation.12 | convolution fusion | flops 100663296 | bytes 1048576 | tf_op jit(solution)/shard_map/tij,...tjk->...tik/dot_general | solution.py:38
  11.3 1.4 %fusion.28 = f32[8,128,128]{2,1,0:T(8,128)} fusion(f32[8,128,128]{2,1,0:T(8,128)S(1)} %copy-done.6), kind=kOutput, calls=%fused_computation.47 | convolution fusion | flops 201326592 | bytes 1048576 | tf_op jit(solution)/shard_map/tij,tjk->tik/dot_general | solution.py:256
  12.7 1.1 %fusion.26.coarse_ref = f32[8,64,128]{2,1,0:T(8,128)S(1)} fusion(f32[8,64,128]{2,1,0:T(8,128)S(1)} %fusion.6, f32[8,128,128]{2,1,0:T(8,128)S(1)} %copy-done.6), kind=kOutput, calls=%fused_computation.45 | convolution fusion | flops 100663296 | bytes 1048576 | tf_op jit(solution)/shard_map/...tik,tlk->...til/dot_general | solution.py:39
  13.9 1.9 %fusion.30 = f32[8,128,128]{2,1,0:T(8,128)S(1)} fusion(f32[8,128,128]{2,1,0:T(8,128)} %fusion.28), kind=kOutput, calls=%fused_computation.49 | convolution fusion | flops 201326592 | bytes 1048576 | tf_op jit(solution)/shard_map/tij,tjk->tik/dot_general | solution.py:256
  15.9 1.6 %collective-permute-done.1.next_ref = f32[5,8,16,128]{3,2,1,0:T(8,128)S(1)} collective-permute-done((f32[5,8,16,128]{3,2,1,0:T(8,128)}, f32[5,8,16,128]{3,2,1,0:T(8,128)S(1)}, u32[]{:S(2)}, u32[]{:S(2)}) %collective-permute-start.1) | collective-permute-done | bytes 327712 | tf_op jit(solution)/shard_map/ppermute | solution.py:212
  17.5 0.6 copy-done.4
  18.2 6.9 %shard_map.96 = (f32[8,128,128]{2,1,0:T(8,128)S(1)}, f32[8,64,128]{2,1,0:T(8,128)S(1)}) custom-call(s32[8]{0:T(128)S(1)} %get-tuple-element.20.south_ref, s32[8]{0:T(128)S(1)} %get-tuple-element.19.north_ref, s32[8]{0:T(128)S(1)} %get-tuple-element.21.west_at_ref, s32[8]{0:T(128)S(1)} %get-tuple-element.18.east_at_ref, s32[8]{0:T(128)S(1)} %get-tuple-element.17.west_ok_ref, ...), custom_call_target="tpu_custom_call" | custom-call | tf_op jit(solution)/shard_map/pallas_call | solution.py:137
  25.4 2.1 %collective-permute-start.2 = (f32[4,64,128]{2,1,0:T(8,128)S(1)}, f32[4,64,128]{2,1,0:T(8,128)S(1)}, u32[]{:S(2)}, u32[]{:S(2)}) collective-permute-start(f32[4,64,128]{2,1,0:T(8,128)S(1)} %get-tuple-element.14), channel_id=1, source_target_pairs={{0,4},{4,8},{8,12},{12,16},{16,20},{20,24},{24,28},{1,5},{5,9},{9,... | collective-permute-start | bytes 393224 | tf_op jit(solution)/shard_map/ppermute | solution.py:26
  27.9 3.4 %collective-permute-start.5 = (f32[4,64,128]{2,1,0:T(8,128)S(1)}, f32[4,64,128]{2,1,0:T(8,128)S(1)}, u32[]{:S(2)}, u32[]{:S(2)}) collective-permute-start(f32[4,64,128]{2,1,0:T(8,128)S(1)} %get-tuple-element.15), channel_id=1, source_target_pairs={{0,8},{4,12},{8,16},{12,20},{16,24},{20,28},{1,9},{5,13},{9,17},{1... | collective-permute-start | bytes 393224 | tf_op jit(solution)/shard_map/ppermute | solution.py:26
  31.3 2.0 %collective-permute-start.9 = (f32[8,128,128]{2,1,0:T(8,128)S(1)}, f32[8,128,128]{2,1,0:T(8,128)S(1)}, u32[]{:S(2)}, u32[]{:S(2)}) collective-permute-start(f32[8,128,128]{2,1,0:T(8,128)S(1)} %sub.47), channel_id=1, source_target_pairs={{0,4},{4,8},{8,12},{12,16},{16,20},{20,24},{24,28},{1,5},{5,9},{9,... | collective-permute-start | bytes 1572872 | tf_op jit(solution)/shard_map/ppermute | solution.py:26
  33.6 0.6 fusion.5
  34.2 1.9 %collective-permute-start.3 = (f32[4,64,128]{2,1,0:T(8,128)S(1)}, f32[4,64,128]{2,1,0:T(8,128)S(1)}, u32[]{:S(2)}, u32[]{:S(2)}) collective-permute-start(f32[4,64,128]{2,1,0:T(8,128)S(1)} %fusion.5), channel_id=1, source_target_pairs={{0,8},{4,12},{8,16},{12,20},{16,24},{20,28},{1,9},{5,13},{9,17},{1... | collective-permute-start | bytes 393224 | tf_op jit(solution)/shard_map/ppermute | solution.py:26
  36.7 0.6 fusion.2
  37.3 1.3 %collective-permute-start.6 = (f32[4,64,128]{2,1,0:T(8,128)S(1)}, f32[4,64,128]{2,1,0:T(8,128)S(1)}, u32[]{:S(2)}, u32[]{:S(2)}) collective-permute-start(f32[4,64,128]{2,1,0:T(8,128)S(1)} %fusion.2), channel_id=1, source_target_pairs={{0,16},{4,20},{8,24},{12,28},{1,17},{5,21},{9,25},{13,29},{2,18},{... | collective-permute-start | bytes 393224 | tf_op jit(solution)/shard_map/ppermute | solution.py:26
  38.6 4.9 %collective-permute-done.3 = f32[4,64,128]{2,1,0:T(8,128)S(1)} collective-permute-done((f32[4,64,128]{2,1,0:T(8,128)S(1)}, f32[4,64,128]{2,1,0:T(8,128)S(1)}, u32[]{:S(2)}, u32[]{:S(2)}) %collective-permute-start.3) | collective-permute-done | bytes 131104 | tf_op jit(solution)/shard_map/ppermute | solution.py:26
  43.8 0.6 fusion.4
  44.4 1.3 %collective-permute-start.4 = (f32[4,64,128]{2,1,0:T(8,128)S(1)}, f32[4,64,128]{2,1,0:T(8,128)S(1)}, u32[]{:S(2)}, u32[]{:S(2)}) collective-permute-start(f32[4,64,128]{2,1,0:T(8,128)S(1)} %fusion.4), channel_id=1, source_target_pairs={{0,16},{4,20},{8,24},{12,28},{1,17},{5,21},{9,25},{13,29},{2,18},{... | collective-permute-start | bytes 393224 | tf_op jit(solution)/shard_map/ppermute | solution.py:26
  45.7 2.6 %collective-permute-done.6 = f32[4,64,128]{2,1,0:T(8,128)S(1)} collective-permute-done((f32[4,64,128]{2,1,0:T(8,128)S(1)}, f32[4,64,128]{2,1,0:T(8,128)S(1)}, u32[]{:S(2)}, u32[]{:S(2)}) %collective-permute-start.6) | collective-permute-done | bytes 131104 | tf_op jit(solution)/shard_map/ppermute | solution.py:26
  48.5 0.6 fusion.1
  49.2 2.0 %collective-permute-start.7 = (f32[4,64,128]{2,1,0:T(8,128)S(1)}, f32[4,64,128]{2,1,0:T(8,128)S(1)}, u32[]{:S(2)}, u32[]{:S(2)}) collective-permute-start(f32[4,64,128]{2,1,0:T(8,128)S(1)} %fusion.1), channel_id=1, source_target_pairs={{0,4},{4,8},{8,12},{12,16},{16,20},{20,24},{24,28},{1,5},{5,9},{9,... | collective-permute-start | bytes 393224 | tf_op jit(solution)/shard_map/ppermute | solution.py:26
  51.1 0.6 collective-permute-done.4
  52.0 0.6 fusion.3
  52.6 3.8 %collective-permute-done.7 = f32[4,64,128]{2,1,0:T(8,128)S(1)} collective-permute-done((f32[4,64,128]{2,1,0:T(8,128)S(1)}, f32[4,64,128]{2,1,0:T(8,128)S(1)}, u32[]{:S(2)}, u32[]{:S(2)}) %collective-permute-start.7) | collective-permute-done | bytes 131104 | tf_op jit(solution)/shard_map/ppermute | solution.py:26
  56.6 0.6 fusion
  57.3 1.9 %collective-permute-start.8 = (f32[8,64,128]{2,1,0:T(8,128)S(1)}, f32[8,64,128]{2,1,0:T(8,128)S(1)}, u32[]{:S(2)}, u32[]{:S(2)}) collective-permute-start(f32[8,64,128]{2,1,0:T(8,128)S(1)} %maximum_subtract_fusion), channel_id=1, source_target_pairs={{0,4},{4,8},{8,12},{12,16},{16,20},{20,24},{24,28},{1,5},{5,9},{9,... | collective-permute-start | bytes 786440 | tf_op jit(solution)/shard_map/ppermute | solution.py:26
  59.4 0.9 %add_bitcast_fusion = f32[1,8,128,128]{3,2,1,0:T(8,128)} fusion(f32[8,128,128]{2,1,0:T(8,128)S(1)} %bitcast.59, f32[8,128,128]{2,1,0:T(8,128)S(1)} %sub.47), kind=kLoop, calls=%fused_computation.15 | loop fusion | flops 131072 | bytes 1572864 | tf_op jit(solution)/shard_map/add | solution.py:295
  60.3 5.6 %collective-permute-done.8 = f32[8,64,128]{2,1,0:T(8,128)S(1)} collective-permute-done((f32[8,64,128]{2,1,0:T(8,128)S(1)}, f32[8,64,128]{2,1,0:T(8,128)S(1)}, u32[]{:S(2)}, u32[]{:S(2)}) %collective-permute-start.8) | collective-permute-done | bytes 262176 | tf_op jit(solution)/shard_map/ppermute | solution.py:26
  66.1 0.9 %select_bitcast_fusion = f32[1,8,128,128]{3,2,1,0:T(8,128)} fusion(f32[8,128,128]{2,1,0:T(8,128)S(1)} %bitcast.57, f32[8,128,128]{2,1,0:T(8,128)S(1)} %collective-permute-done.9, pred[]{:T(512)S(6)} %eq.4, f32[1,8,128,128]{3,2,1,0:T(8,128)S(1)} %copy-done), kind=kLoop, calls=%fused_computation.14 | loop fusion | flops 393216 | bytes 2097153 | tf_op jit(solution)/shard_map/broadcast_in_dim | solution.py:300
  (44 shorter events, 3.5 us)
Async XLA Ops:
  0.6 8.0 %copy-start.8 = (f32[8,64,64]{2,1,0:T(8,128)S(1)}, f32[8,64,64]{2,1,0:T(8,128)}, u32[]{:S(2)}) copy-start(f32[8,64,64]{2,1,0:T(8,128)} %param.14) | copy-start | bytes 393220
  2.7 13.2 %collective-permute-start = (f32[5,8,16,128]{3,2,1,0:T(8,128)}, f32[5,8,16,128]{3,2,1,0:T(8,128)S(1)}, u32[]{:S(2)}, u32[]{:S(2)}) collective-permute-start(f32[5,8,16,128]{3,2,1,0:T(8,128)} %get-tuple-element.8), channel_id=1, source_target_pairs={{0,1},{1,2},{2,3},{4,5},{5,6},{6,7},{8,9},{9,10},{10,11},{12,13},{... | collective-permute-start | bytes 983048 | tf_op jit(solution)/shard_map/ppermute | solution.py:211
  6.2 11.3 %collective-permute-start.1 = (f32[5,8,16,128]{3,2,1,0:T(8,128)}, f32[5,8,16,128]{3,2,1,0:T(8,128)S(1)}, u32[]{:S(2)}, u32[]{:S(2)}) collective-permute-start(f32[5,8,16,128]{3,2,1,0:T(8,128)} %get-tuple-element.9), channel_id=1, source_target_pairs={{1,0},{2,1},{3,2},{5,4},{6,5},{7,6},{9,8},{10,9},{11,10},{13,12},{... | collective-permute-start | bytes 983048 | tf_op jit(solution)/shard_map/ppermute | solution.py:212
  9.2 1.0 %copy-start = (f32[1,8,128,128]{3,2,1,0:T(8,128)S(1)}, f32[1,8,128,128]{3,2,1,0:T(8,128)}, u32[]{:S(2)}) copy-start(f32[1,8,128,128]{3,2,1,0:T(8,128)} %starts_hbm.1) | copy-start | bytes 1572868
  10.2 1.1 %copy-start.6 = (f32[8,128,128]{2,1,0:T(8,128)S(1)}, f32[8,128,128]{2,1,0:T(8,128)}, u32[]{:S(2)}) copy-start(f32[8,128,128]{2,1,0:T(8,128)} %param.15) | copy-start | bytes 1572868
  12.7 1.1 %copy-start.10 = (s32[8,4]{0,1:T(4,128)S(1)}, s32[8,4]{0,1:T(4,128)}, u32[]{:S(2)}) copy-start(s32[8,4]{0,1:T(4,128)} %param.13) | copy-start | bytes 388
  12.7 4.8 %copy-start.3 = (s32[8,128,128]{2,1,0:T(8,128)S(1)}, s32[8,128,128]{2,1,0:T(8,128)}, u32[]{:S(2)}) copy-start(s32[8,128,128]{2,1,0:T(8,128)} %obstacle_ref.1) | copy-start | bytes 1572868
  13.9 3.6 %copy-start.1 = (f32[2,8,128,128]{3,2,1,0:T(8,128)S(1)}, f32[2,8,128,128]{3,2,1,0:T(8,128)}, u32[]{:S(2)}) copy-start(f32[2,8,128,128]{3,2,1,0:T(8,128)} %velocity_ref.1) | copy-start | bytes 3145732
  13.9 3.6 %copy-start.2 = (f32[8,128,128]{2,1,0:T(8,128)S(1)}, f32[8,128,128]{2,1,0:T(8,128)}, u32[]{:S(2)}) copy-start(f32[8,128,128]{2,1,0:T(8,128)} %diffusivity_ref.1) | copy-start | bytes 1572868
  17.5 0.7 copy-start.4
  25.4 7.9 %copy-start.9 = (f32[8,64,64]{2,1,0:T(8,128)S(1)}, f32[8,64,64]{2,1,0:T(8,128)}, u32[]{:S(2)}) copy-start(f32[8,64,64]{2,1,0:T(8,128)} %param.14) | copy-start | bytes 393220
  25.4 8.2 %copy-start.7 = (f32[8,128,128]{2,1,0:T(8,128)S(1)}, f32[8,128,128]{2,1,0:T(8,128)}, u32[]{:S(2)}) copy-start(f32[8,128,128]{2,1,0:T(8,128)} %param.15) | copy-start | bytes 1572868
  25.4 7.9 %collective-permute-start.2 = (f32[4,64,128]{2,1,0:T(8,128)S(1)}, f32[4,64,128]{2,1,0:T(8,128)S(1)}, u32[]{:S(2)}, u32[]{:S(2)}) collective-permute-start(f32[4,64,128]{2,1,0:T(8,128)S(1)} %get-tuple-element.14), channel_id=1, source_target_pairs={{0,4},{4,8},{8,12},{12,16},{16,20},{20,24},{24,28},{1,5},{5,9},{9,... | collective-permute-start | bytes 393224 | tf_op jit(solution)/shard_map/ppermute | solution.py:26
  27.9 8.5 %collective-permute-start.5 = (f32[4,64,128]{2,1,0:T(8,128)S(1)}, f32[4,64,128]{2,1,0:T(8,128)S(1)}, u32[]{:S(2)}, u32[]{:S(2)}) collective-permute-start(f32[4,64,128]{2,1,0:T(8,128)S(1)} %get-tuple-element.15), channel_id=1, source_target_pairs={{0,8},{4,12},{8,16},{12,20},{16,24},{20,28},{1,9},{5,13},{9,17},{1... | collective-permute-start | bytes 393224 | tf_op jit(solution)/shard_map/ppermute | solution.py:26
  31.3 29.0 %collective-permute-start.9 = (f32[8,128,128]{2,1,0:T(8,128)S(1)}, f32[8,128,128]{2,1,0:T(8,128)S(1)}, u32[]{:S(2)}, u32[]{:S(2)}) collective-permute-start(f32[8,128,128]{2,1,0:T(8,128)S(1)} %sub.47), channel_id=1, source_target_pairs={{0,4},{4,8},{8,12},{12,16},{16,20},{20,24},{24,28},{1,5},{5,9},{9,... | collective-permute-start | bytes 1572872 | tf_op jit(solution)/shard_map/ppermute | solution.py:26
  33.6 3.1 %copy-start.5 = (f32[8,128,128]{2,1,0:T(8,128)S(1)}, f32[8,128,128]{2,1,0:T(8,128)}, u32[]{:S(2)}) copy-start(f32[8,128,128]{2,1,0:T(8,128)} %fusion.28) | copy-start | bytes 1572868
  34.2 9.3 %collective-permute-start.3 = (f32[4,64,128]{2,1,0:T(8,128)S(1)}, f32[4,64,128]{2,1,0:T(8,128)S(1)}, u32[]{:S(2)}, u32[]{:S(2)}) collective-permute-start(f32[4,64,128]{2,1,0:T(8,128)S(1)} %fusion.5), channel_id=1, source_target_pairs={{0,8},{4,12},{8,16},{12,20},{16,24},{20,28},{1,9},{5,13},{9,17},{1... | collective-permute-start | bytes 393224 | tf_op jit(solution)/shard_map/ppermute | solution.py:26
  37.3 11.0 %collective-permute-start.6 = (f32[4,64,128]{2,1,0:T(8,128)S(1)}, f32[4,64,128]{2,1,0:T(8,128)S(1)}, u32[]{:S(2)}, u32[]{:S(2)}) collective-permute-start(f32[4,64,128]{2,1,0:T(8,128)S(1)} %fusion.2), channel_id=1, source_target_pairs={{0,16},{4,20},{8,24},{12,28},{1,17},{5,21},{9,25},{13,29},{2,18},{... | collective-permute-start | bytes 393224 | tf_op jit(solution)/shard_map/ppermute | solution.py:26
  44.4 7.3 %collective-permute-start.4 = (f32[4,64,128]{2,1,0:T(8,128)S(1)}, f32[4,64,128]{2,1,0:T(8,128)S(1)}, u32[]{:S(2)}, u32[]{:S(2)}) collective-permute-start(f32[4,64,128]{2,1,0:T(8,128)S(1)} %fusion.4), channel_id=1, source_target_pairs={{0,16},{4,20},{8,24},{12,28},{1,17},{5,21},{9,25},{13,29},{2,18},{... | collective-permute-start | bytes 393224 | tf_op jit(solution)/shard_map/ppermute | solution.py:26
  49.2 7.2 %collective-permute-start.7 = (f32[4,64,128]{2,1,0:T(8,128)S(1)}, f32[4,64,128]{2,1,0:T(8,128)S(1)}, u32[]{:S(2)}, u32[]{:S(2)}) collective-permute-start(f32[4,64,128]{2,1,0:T(8,128)S(1)} %fusion.1), channel_id=1, source_target_pairs={{0,4},{4,8},{8,12},{12,16},{16,20},{20,24},{24,28},{1,5},{5,9},{9,... | collective-permute-start | bytes 393224 | tf_op jit(solution)/shard_map/ppermute | solution.py:26
  57.3 8.6 %collective-permute-start.8 = (f32[8,64,128]{2,1,0:T(8,128)S(1)}, f32[8,64,128]{2,1,0:T(8,128)S(1)}, u32[]{:S(2)}, u32[]{:S(2)}) collective-permute-start(f32[8,64,128]{2,1,0:T(8,128)S(1)} %maximum_subtract_fusion), channel_id=1, source_target_pairs={{0,4},{4,8},{8,12},{12,16},{16,20},{20,24},{24,28},{1,5},{5,9},{9,... | collective-permute-start | bytes 786440 | tf_op jit(solution)/shard_map/ppermute | solution.py:26
